TPU v7x, 128 devices: a whole 4x4x4 slice. The times are simulated.
128 devices in a mesh: row: 16 (over z, x), col: 8 (over y, core).
Axes of the slice: x: 4, y: 4, z: 4, core: 2. Of those that a mesh axis runs over, the one named last changes fastest.
Arguments:
- front: bfloat16 [128, 96, 256, 256], P('row', 'col'), may hold values from -1.5 to 1.5
- pattern: int32 [128, 96], replicated, may hold values from 0 to 1
- pivots: int32 [2], replicated, may hold values from 0 to 95, as said below
- pivot_inv: bfloat16 [2, 256, 256], replicated, may hold values from -0.09375 to 0.09375
Outputs:
- factored: bfloat16 [128, 96, 256, 256], P('row', 'col')
Inputs may be any that keep to these rules, and one draw needn't show every extreme that they name: The two pivots are distinct front block indices below 96; one of them is 95, the last block column of the window.
All inputs are finite; a program needn't handle non-finite values.
Results may differ from a plain program's by a relative error of at most 0.0051.
Values may be sent and summed in bfloat16 or wider, within the bound.
No kernel may reach another device: no remote copies, remote signals or barrier semaphores. Data moves between devices by JAX's collectives and lax.ppermute only.
A program may use at most 128 MiB of HBM per device.

v0:
```python
import jax
import jax.numpy as jnp
from jax import lax
from jax.sharding import PartitionSpec as P


def from_root(value, axis, source):
    kept = jnp.where(lax.axis_index(axis) == source, value, 0).astype(value.dtype)
    return lax.psum(kept, axis)


def lower_panel(matrix, pivot, inverse, rows_ok, ncol):
    column = lax.dynamic_index_in_dim(matrix, pivot // ncol, 1, keepdims=False)
    lower = jnp.einsum("iab,bc->iac", column, inverse, preferred_element_type=jnp.float32)
    lower = jnp.where(rows_ok[:, None, None], lower, 0.0).astype(jnp.bfloat16)
    return from_root(lower, "col", pivot % ncol)


def eliminate(matrix, lower, upper, pivot, rows_ok, cols_ok, local, front_cols):
    product = jnp.einsum("iab,jbc->ijac", lower, upper, preferred_element_type=jnp.float32)
    update = rows_ok[:, None] & cols_ok[None, :] & (local > 0)
    changed = (matrix.astype(jnp.float32) - product).astype(jnp.bfloat16)
    result = jnp.where(update[:, :, None, None], changed, matrix)
    place = rows_ok[:, None] & (front_cols == pivot)[None, :]
    return jnp.where(place[:, :, None, None], lower[:, None], result)


def body(front, pattern, pivots, pivot_inv):
    rows_dev = front.shape[0]
    cols_dev = front.shape[1]
    nrow = lax.axis_size("row")
    ncol = lax.axis_size("col")
    row_index = lax.axis_index("row")
    col_index = lax.axis_index("col")
    grid = pattern.reshape(rows_dev, nrow, cols_dev, ncol)
    local = lax.dynamic_index_in_dim(grid, row_index, 1, keepdims=False)
    local = lax.dynamic_index_in_dim(local, col_index, 2, keepdims=False)
    front_rows = jnp.arange(rows_dev, dtype=jnp.int32) * nrow + row_index
    front_cols = jnp.arange(cols_dev, dtype=jnp.int32) * ncol + col_index
    matrix = jnp.where(local[:, :, None, None] > 0, front, jnp.zeros_like(front))
    first = pivots[0]
    second = pivots[1]
    rows_first = front_rows != first
    cols_first = front_cols != first
    lower_first = lower_panel(matrix, first, pivot_inv[0], rows_first, ncol)
    first_row = lax.dynamic_index_in_dim(matrix, first // nrow, 0, keepdims=False)
    upper_first = from_root(first_row, "row", first % nrow)
    matrix = eliminate(
        matrix, lower_first, upper_first, first, rows_first, cols_first, local, front_cols
    )
    second_row = lax.dynamic_index_in_dim(matrix, second // nrow, 0, keepdims=False)
    upper_second = from_root(second_row, "row", second % nrow)
    rows_second = rows_first & (front_rows != second)
    cols_second = cols_first & (front_cols != second)
    lower_second = lower_panel(matrix, second, pivot_inv[1], rows_second, ncol)
    matrix = eliminate(
        matrix, lower_second, upper_second, second, rows_second, cols_second, local, front_cols
    )
    return matrix


def solution(mesh):
    placed = (P("row", "col", None, None), P(), P(), P())
    return jax.shard_map(
        body, mesh=mesh, in_specs=placed, out_specs=P("row", "col", None, None), check_vma=False
    )
```

profile of v0, /device:TPU:6, one launch (start us, length us, event | category | flops | bytes accessed | tf_op | source)
XLA Modules:
  0.0 411.4 jit_solution(12664829645244328995)
XLA Ops:
  6.5 1.4 fusion.23
  10.3 0.6 fusion.22
  10.8 1.3 compare_and_fusion.1
  12.1 1.3 compare_and_fusion
  13.4 1.0 reshape.175
  14.4 0.1 constant_dynamic-slice_fusion
  14.5 0.1 copy.30
  14.6 16.6 %copy.22 = bf16[8,12,256,256]{2,3,1,0:T(8,128)(2,1)} copy(bf16[8,12,256,256]{3,2,1,0:T(8,128)(2,1)} %param.4) | data formatting | bytes 25165824 | tf_op args[0]
  31.2 0.1 and_and_fusion
  31.3 6.4 %broadcast_select_fusion = bf16[8,12,256,256]{2,3,1,0:T(8,128)(2,1)S(1)} fusion(bf16[8,12,256,256]{2,3,1,0:T(8,128)(2,1)} %copy.22, pred[8,12]{1,0:T(8,128)(4,1)S(1)} %get-tuple-element.6), kind=kLoop, calls=%fused_computation.8 | loop fusion | flops 6291456 | bytes 25165920 | tf_op jit(solution)/shard_map/jit(_where)/select_n | solution.py:40
  37.7 4.8 %copy-done = bf16[8,12,256,256]{2,3,1,0:T(8,128)(2,1)} copy-done((bf16[8,12,256,256]{2,3,1,0:T(8,128)(2,1)}, bf16[8,12,256,256]{2,3,1,0:T(8,128)(2,1)S(1)}, u32[]{:S(2)}) %copy-start) | copy-done | bytes 12582936
  42.5 1.6 fusion.8
  44.1 0.0 all-reduce.5.cloned.1.call-update
  44.1 0.0 all-reduce.7.cloned.1.call-start
  44.2 2.7 select_bitcast_fusion.1
  46.8 0.0 all-reduce.7.cloned.1.call-update
  46.9 0.0 all-reduce.9.cloned.1.call-start
  49.7 0.6 broadcast_compare_fusion
  50.3 0.1 broadcast_and_fusion
  50.4 58.6 %all-reduce.5.cloned.1.call-done = bf16[8,256,256]{2,1,0:T(8,128)(2,1)} async-done(((bf16[8,256,256]{2,1,0:T(8,128)(2,1)}), bf16[8,256,256]{2,1,0:T(8,128)(2,1)}) %all-reduce.5.cloned.1.call-update) | async-done | bytes 1048592 | tf_op jit(solution)/shard_map/psum | solution.py:9
  109.0 1.5 copy.24
  110.5 89.7 %all-reduce.7.cloned.1.call-done = bf16[12,256,256]{1,2,0:T(8,128)(2,1)} async-done(((bf16[12,256,256]{1,2,0:T(8,128)(2,1)}), bf16[12,256,256]{1,2,0:T(8,128)(2,1)}) %all-reduce.7.cloned.1.call-update) | async-done | bytes 1572880 | tf_op jit(solution)/shard_map/psum | solution.py:9
  200.2 16.1 %fusion.5 = bf16[8,12,256,256]{2,3,1,0:T(8,128)(2,1)} fusion(bf16[8,12,256,256]{2,3,1,0:T(8,128)(2,1)} %copy-done, pred[8,12]{1,0:T(8,128)(4,1)S(1)} %get-tuple-element.9, pred[8,12]{1,0:T(8,128)(4,1)S(1)} %get-tuple-element.8, bf16[8,256,256]{1,2,0:T(8,128)(2,1)S(1)} %copy.24, bf16[12,256,256]{1,2,0:T(8,128)(2,1)} %all-reduce.7.cloned.1.call-done, ...), kind=kOutput, calls=%fused_computation.7 | convolution fusion | flops 3252682752 | bytes 28836032 | tf_op jit(solution)/shard_map/iab,jbc->ijac/dot_general | solution.py:20
  216.3 2.8 fusion.9
  219.1 0.0 all-reduce.9.cloned.1.call-update
  219.1 0.0 all-reduce.11.cloned.1.call-start
  219.2 2.7 select_bitcast_fusion
  221.9 59.4 %all-reduce.9.cloned.1.call-done = bf16[8,256,256]{2,1,0:T(8,128)(2,1)} async-done(((bf16[8,256,256]{2,1,0:T(8,128)(2,1)}), bf16[8,256,256]{2,1,0:T(8,128)(2,1)}) %all-reduce.9.cloned.1.call-update) | async-done | bytes 1048592 | tf_op jit(solution)/shard_map/psum | solution.py:9
  281.3 1.5 copy.26
  282.7 89.4 %all-reduce.11.cloned.1.call-done = bf16[12,256,256]{1,2,0:T(8,128)(2,1)} async-done(((bf16[12,256,256]{1,2,0:T(8,128)(2,1)}), bf16[12,256,256]{1,2,0:T(8,128)(2,1)}) %all-reduce.11.cloned.1.call-update) | async-done | bytes 1572880 | tf_op jit(solution)/shard_map/psum | solution.py:9
  372.2 16.1 %fusion.4 = bf16[8,12,256,256]{2,3,1,0:T(8,128)(2,1)} fusion(bf16[8,12,256,256]{2,3,1,0:T(8,128)(2,1)} %fusion.5, pred[8,12]{1,0:T(8,128)(4,1)S(1)} %get-tuple-element.5, pred[8,12]{1,0:T(8,128)(4,1)S(1)} %get-tuple-element.7, bf16[8,256,256]{1,2,0:T(8,128)(2,1)S(1)} %copy.26, bf16[12,256,256]{1,2,0:T(8,128)(2,1)} %all-reduce.11.cloned.1.call-done, ...), kind=kOutput, calls=%fused_computation.6 | convolution fusion | flops 3252682752 | bytes 28836032 | tf_op jit(solution)/shard_map/iab,jbc->ijac/dot_general | solution.py:20
  388.3 16.6 %copy.27 = bf16[8,12,256,256]{3,2,1,0:T(8,128)(2,1)} copy(bf16[8,12,256,256]{2,3,1,0:T(8,128)(2,1)} %fusion.4) | data formatting | bytes 25165824 | tf_op jit(solution)/shard_map/jit(_where)/select_n | solution.py:25
  (5 shorter events, 0.0 us)
Async XLA Ops:
  6.5 102.5 %all-reduce.5.cloned.1.call-start = ((), (), s32[]{:S(2)}) async-start(), calls=%async_computation | async-start | bytes 2097152 | tf_op jit(solution)/shard_map/psum | solution.py:9
  31.3 11.2 %copy-start.1 = (bf16[2,256,256]{2,1,0:T(8,128)(2,1)S(1)}, bf16[2,256,256]{2,1,0:T(8,128)(2,1)}, u32[]{:S(2)}) copy-start(bf16[2,256,256]{2,1,0:T(8,128)(2,1)} %param.7) | copy-start | bytes 786436
  37.7 4.8 %copy-start = (bf16[8,12,256,256]{2,3,1,0:T(8,128)(2,1)}, bf16[8,12,256,256]{2,3,1,0:T(8,128)(2,1)S(1)}, u32[]{:S(2)}) copy-start(bf16[8,12,256,256]{2,3,1,0:T(8,128)(2,1)S(1)} %broadcast_select_fusion) | copy-start | bytes 37748740
  44.1 156.1 %all-reduce.7.cloned.1.call-start = ((), (), s32[]{:S(2)}) async-start(), calls=%async_computation.1 | async-start | bytes 3145728 | tf_op jit(solution)/shard_map/psum | solution.py:9
  46.9 234.4 %all-reduce.9.cloned.1.call-start = ((), (), s32[]{:S(2)}) async-start(), calls=%async_computation.2 | async-start | bytes 2097152 | tf_op jit(solution)/shard_map/psum | solution.py:9
  219.1 153.1 %all-reduce.11.cloned.1.call-start = ((), (), s32[]{:S(2)}) async-start(), calls=%async_computation.3 | async-start | bytes 3145728 | tf_op jit(solution)/shard_map/psum | solution.py:9
Sparse Core Ops, SparseCore 0:
  44.2 64.7 all-reduce.4
  112.3 87.7 all-reduce.6
  219.3 61.9 all-reduce.8
  284.4 87.7 all-reduce.10
where the time goes:
time: 413 us; the launch traced here: 411 us
  waiting for transfers between devices  297 us (72%)
  local copies, waits for them, and re-layouts  43.5 us (11%)
  matrix products  36.6 us (9%)
  between operations  18.4 us (4%)
  other arithmetic  15.6 us (4%)
    psum x4, waiting for transfers between devices, from_root(): return lax.psum(kept, axis)  297 us
    dot_general x2, matrix products, eliminate(): jnp.einsum('iab,jbc->ijac', lower, upper, preferred_element_type=jnp.floa...  32.2 us
    unnamed x6, local copies, waits for them, and re-layouts  21.5 us
    select_n x1, local copies, waits for them, and re-layouts, eliminate(): return jnp.where(place[:, :, None, None], lower[:, None], result)  16.6 us
  transfers between devices with their start and end apart: 4, of which 4 were waited for; matrix products, arithmetic and copies ran while one was open for 2% of the time, Pallas kernels for 0%

commit v1 on v0

--- a/solution.py
+++ b/solution.py
@@ -3,17 +3,90 @@
 from jax import lax
 from jax.sharding import PartitionSpec as P
 
-
-def from_root(value, axis, source):
-    kept = jnp.where(lax.axis_index(axis) == source, value, 0).astype(value.dtype)
-    return lax.psum(kept, axis)
+RING = 4
+CORES = 2
 
 
-def lower_panel(matrix, pivot, inverse, rows_ok, ncol):
-    column = lax.dynamic_index_in_dim(matrix, pivot // ncol, 1, keepdims=False)
+def pick(index, options):
+    out = options[-1]
+    for k in range(len(options) - 2, -1, -1):
+        out = jnp.where(index == k, options[k], out)
+    return out
+
+
+def ring_bcast(value, axis, plus, minus, me, root):
+    half = value.shape[0] // 2
+    first, second = value[:half], value[half:]
+    got_plus = lax.ppermute(first, axis, plus)
+    got_minus = lax.ppermute(second, axis, minus)
+    dist = (me - root) % RING
+    at_root = dist == 0
+    send_plus = jnp.where(at_root, second, got_plus)
+    send_minus = jnp.where(at_root, first, got_minus)
+    got_plus2 = lax.ppermute(send_plus, axis, plus)
+    got_minus2 = lax.ppermute(send_minus, axis, minus)
+    out_first = pick(dist, [first, got_plus, got_plus2, got_minus2])
+    out_second = pick(dist, [second, got_plus2, got_minus2, got_minus])
+    return jnp.concatenate([out_first, out_second], axis=0)
+
+
+def row_pairs(step_z, step_x):
+    return [
+        (RING * z + x, RING * ((z + step_z) % RING) + (x + step_x) % RING)
+        for z in range(RING)
+        for x in range(RING)
+    ]
+
+
+def row_bcast(value, root):
+    me = lax.axis_index("row")
+    mz, mx = me // RING, me % RING
+    rz, rx = root // RING, root % RING
+    xp, xm = row_pairs(0, 1), row_pairs(0, RING - 1)
+    zp, zm = row_pairs(1, 0), row_pairs(RING - 1, 0)
+    half = value.shape[0] // 2
+    along_x = value[:half]
+    along_z = value[half:]
+    along_x = ring_bcast(along_x, "row", xp, xm, mx, rx)
+    along_z = ring_bcast(along_z, "row", zp, zm, mz, rz)
+    along_x = ring_bcast(along_x, "row", zp, zm, mz, rz)
+    along_z = ring_bcast(along_z, "row", xp, xm, mx, rx)
+    return jnp.concatenate([along_x, along_z], axis=0)
+
+
+def col_bcast(value, root):
+    me = lax.axis_index("col")
+    my, mk = me // CORES, me % CORES
+    ry = root // CORES
+    swap = [(CORES * y + k, CORES * y + 1 - k) for y in range(RING) for k in range(CORES)]
+    hop = [(CORES * y, CORES * ((y + 1) % RING)) for y in range(RING)] + [
+        (CORES * y + 1, CORES * ((y - 1) % RING) + 1) for y in range(RING)
+    ]
+    got_swap = lax.ppermute(value, "col", swap)
+    on_root_chip = jnp.where(me == root, value, got_swap)
+    got_hop = lax.ppermute(on_root_chip, "col", hop)
+    dist = (my - ry) % RING
+    near = jnp.where(dist == 0, on_root_chip, got_hop)
+    got_swap2 = lax.ppermute(near, "col", swap)
+    half = value.shape[0] // 2
+    fwd = jnp.where(mk == 0, near[:half], near[half:])
+    got_fwd = lax.ppermute(fwd, "col", hop)
+    got_swap3 = lax.ppermute(got_fwd, "col", swap)
+    far = jnp.where(
+        mk == 0,
+        jnp.concatenate([got_fwd, got_swap3], axis=0),
+        jnp.concatenate([got_swap3, got_fwd], axis=0),
+    )
+    own_hop = (dist == 1) & (mk == 0) | (dist == 3) & (mk == 1)
+    other_hop = (dist == 1) & (mk == 1) | (dist == 3) & (mk == 0)
+    out = jnp.where(own_hop, got_hop, far)
+    out = jnp.where(other_hop, got_swap2, out)
+    return jnp.where(dist == 0, on_root_chip, out)
+
+
+def lower_local(column, inverse, rows_ok):
     lower = jnp.einsum("iab,bc->iac", column, inverse, preferred_element_type=jnp.float32)
-    lower = jnp.where(rows_ok[:, None, None], lower, 0.0).astype(jnp.bfloat16)
-    return from_root(lower, "col", pivot % ncol)
+    return jnp.where(rows_ok[:, None, None], lower, 0.0).astype(jnp.bfloat16)
 
 
 def eliminate(matrix, lower, upper, pivot, rows_ok, cols_ok, local, front_cols):
@@ -42,17 +115,44 @@
     second = pivots[1]
     rows_first = front_rows != first
     cols_first = front_cols != first
-    lower_first = lower_panel(matrix, first, pivot_inv[0], rows_first, ncol)
+    rows_second = rows_first & (front_rows != second)
+    cols_second = cols_first & (front_cols != second)
+
+    column_first = lax.dynamic_index_in_dim(matrix, first // ncol, 1, keepdims=False)
+    lower_first = col_bcast(lower_local(column_first, pivot_inv[0], rows_first), first % ncol)
     first_row = lax.dynamic_index_in_dim(matrix, first // nrow, 0, keepdims=False)
-    upper_first = from_root(first_row, "row", first % nrow)
+    upper_first = row_bcast(first_row, first % nrow)
+
+    a2 = second // nrow
+    row_before = lax.dynamic_slice_in_dim(matrix, a2, 1, 0)
+    row_after = eliminate(
+        row_before,
+        lax.dynamic_slice_in_dim(lower_first, a2, 1, 0),
+        upper_first,
+        first,
+        lax.dynamic_slice_in_dim(rows_first, a2, 1, 0),
+        cols_first,
+        lax.dynamic_slice_in_dim(local, a2, 1, 0),
+        front_cols,
+    )
+    upper_second = row_bcast(row_after[0], second % nrow)
+    b2 = second // ncol
+    col_before = lax.dynamic_slice_in_dim(matrix, b2, 1, 1)
+    col_after = eliminate(
+        col_before,
+        lower_first,
+        lax.dynamic_slice_in_dim(upper_first, b2, 1, 0),
+        first,
+        rows_first,
+        lax.dynamic_slice_in_dim(cols_first, b2, 1, 0),
+        lax.dynamic_slice_in_dim(local, b2, 1, 1),
+        lax.dynamic_slice_in_dim(front_cols, b2, 1, 0),
+    )
+    lower_second = col_bcast(lower_local(col_after[:, 0], pivot_inv[1], rows_second), second % ncol)
+
     matrix = eliminate(
         matrix, lower_first, upper_first, first, rows_first, cols_first, local, front_cols
     )
-    second_row = lax.dynamic_index_in_dim(matrix, second // nrow, 0, keepdims=False)
-    upper_second = from_root(second_row, "row", second % nrow)
-    rows_second = rows_first & (front_rows != second)
-    cols_second = cols_first & (front_cols != second)
-    lower_second = lower_panel(matrix, second, pivot_inv[1], rows_second, ncol)
     matrix = eliminate(
         matrix, lower_second, upper_second, second, rows_second, cols_second, local, front_cols
     )

time: 413 us -> 259 us (0.63)
  waiting for transfers between devices: 297 us -> 68.3 us
  starting transfers between devices: 0.13 us -> 55.2 us
  other arithmetic: 15.6 us -> 54.8 us
  local copies, waits for them, and re-layouts: 43.5 us -> 22.3 us
  between operations: 18.4 us -> 6.57 us
  matrix products: 36.6 us -> 48.3 us
    psum x4 -> x0, waiting for transfers between devices: 297 us -> none  [from_root(): return lax.psum(kept, axis)]
    ppermute x0 -> x42, waiting for transfers between devices: none -> 68.3 us  [the longest x8 30 us: ring_bcast(): got_minus = lax.ppermute(second, axis, minus)]
    ppermute x0 -> x42, starting transfers between devices: none -> 55.2 us  [the longest x8 18 us: ring_bcast(): got_minus = lax.ppermute(second, axis, minus)]
    select_n x2 -> x28, other arithmetic: 5.33 us -> 34.6 us  [the longest x6 9.73 us: ring_bcast(): send_minus = jnp.where(at_root, first, got_minus)]
    unnamed x6 -> x53, local copies, waits for them, and re-layouts: 21.5 us -> 2.59 us
    dot_general x2 -> x3, matrix products: 32.2 us -> 42.4 us  [eliminate(): jnp.einsum('iab,jbc->ijac', lower, upper, preferred_element_type=jnp.floa...]
    select_n x1, local copies, waits for them, and re-layouts: 16.6 us -> 10.6 us  [eliminate(): return jnp.where(place[:, :, None, None], lower[:, None], result)]
    select_n x1, other arithmetic: 6.39 us -> 10.6 us  [body(): jnp.where(local[:, :, None, None] > 0, front, jnp.zeros_like(front))]
  transfers between devices with their start and end apart: 4 -> 42, of which waited for: 4 -> 16; matrix products, arithmetic and copies ran while one was open for 2% -> 21% of each run, Pallas kernels for 0% -> 0%
where the time goes in v1:
time: 259 us; the launch traced here: 255 us
  waiting for transfers between devices  68.3 us (26%)
  starting transfers between devices  55.2 us (21%)
  other arithmetic  54.8 us (21%)
  matrix products  48.3 us (19%)
  local copies, waits for them, and re-layouts  22.3 us (9%)
  between operations  6.57 us (3%)
    dot_general x3, matrix products, eliminate(): jnp.einsum('iab,jbc->ijac', lower, upper, preferred_element_type=jnp.floa...  42.4 us
    ppermute x8, waiting for transfers between devices, ring_bcast(): got_minus = lax.ppermute(second, axis, minus)  30 us
    ppermute x8, waiting for transfers between devices, ring_bcast(): got_plus = lax.ppermute(first, axis, plus)  19.6 us
    ppermute x8, starting transfers between devices, ring_bcast(): got_minus = lax.ppermute(second, axis, minus)  18 us
    ppermute x8, starting transfers between devices, ring_bcast(): got_minus2 = lax.ppermute(send_minus, axis, minus)  15.1 us
    ppermute x8, waiting for transfers between devices, ring_bcast(): got_minus2 = lax.ppermute(send_minus, axis, minus)  11.8 us
    select_n x1, other arithmetic, body(): jnp.where(local[:, :, None, None] > 0, front, jnp.zeros_like(front))  10.6 us
    select_n x1, local copies, waits for them, and re-layouts, eliminate(): return jnp.where(place[:, :, None, None], lower[:, None], result)  10.6 us
  transfers between devices with their start and end apart: 42, of which 16 were waited for; matrix products, arithmetic and copies ran while one was open for 21% of the time, Pallas kernels for 0%

profile of v1, /device:TPU:6, one launch (start us, length us, event | category | flops | bytes accessed | tf_op | source)
XLA Modules:
  0.0 255.5 jit_solution(10411841612082035142)
XLA Ops:
  13.5 10.6 %copy_select_fusion = bf16[8,12,256,256]{3,2,0,1:T(8,128)(2,1)} fusion(bf16[8,12,256,256]{3,2,1,0:T(8,128)(2,1)} %param.4, pred[8,12]{0,1:T(8,128)(4,1)S(1)} %copy.71), kind=kLoop, calls=%fused_computation.8 | loop fusion | flops 6291456 | bytes 25165920 | tf_op jit(solution)/shard_map/jit(_where)/select_n | solution.py:113
  30.6 7.1 %collective-permute-done.5 = bf16[3,256,256]{2,1,0:T(8,128)(2,1)S(1)} collective-permute-done((bf16[3,256,256]{2,1,0:T(8,128)(2,1)}, bf16[3,256,256]{2,1,0:T(8,128)(2,1)S(1)}, u32[]{:S(2)}, u32[]{:S(2)}) %collective-permute-start.5) | collective-permute-done | bytes 393248 | tf_op jit(solution)/shard_map/ppermute | solution.py:20
  41.8 2.7 %select_convert_fusion.1 = bf16[8,256,256]{2,1,0:T(8,128)(2,1)} fusion(bf16[8,12,256,256]{3,2,0,1:T(8,128)(2,1)} %copy_select_fusion, s32[]{:T(128)S(6)} %select_n.561, pred[8]{0:T(512)(128)(4,1)S(1)} %get-tuple-element.14, bf16[2,256,256]{2,1,0:T(8,128)(2,1)S(1)} %copy-done.25), kind=kOutput, calls=%fused_computation.15 | convolution fusion | flops 269484032 | bytes 2228740 | tf_op jit(solution)/shard_map/iab,bc->iac/dot_general | solution.py:88
  46.4 4.2 %collective-permute-start.15 = (bf16[3,256,256]{2,1,0:T(8,128)(2,1)S(1)}, bf16[3,256,256]{2,1,0:T(8,128)(2,1)S(1)}, u32[]{:S(2)}, u32[]{:S(2)}) collective-permute-start(bf16[3,256,256]{2,1,0:T(8,128)(2,1)S(1)} %get-tuple-element.22), channel_id=1, source_target_pairs={{0,96},{8,104},{16,112},{24,120},{32,0},{40,8},{48,16},{56,24},{64... | collective-permute-start | bytes 1179656 | tf_op jit(solution)/shard_map/ppermute | solution.py:21
  51.5 4.3 %collective-permute-start.11 = (bf16[3,256,256]{2,1,0:T(8,128)(2,1)S(1)}, bf16[3,256,256]{2,1,0:T(8,128)(2,1)S(1)}, u32[]{:S(2)}, u32[]{:S(2)}) collective-permute-start(bf16[3,256,256]{2,1,0:T(8,128)(2,1)S(1)} %select_select_fusion.14), channel_id=1, source_target_pairs={{0,96},{8,104},{16,112},{24,120},{32,0},{40,8},{48,16},{56,24},{64... | collective-permute-start | bytes 1179656 | tf_op jit(solution)/shard_map/ppermute | solution.py:21
  55.9 4.2 %collective-permute-done.15 = bf16[3,256,256]{2,1,0:T(8,128)(2,1)S(1)} collective-permute-done((bf16[3,256,256]{2,1,0:T(8,128)(2,1)S(1)}, bf16[3,256,256]{2,1,0:T(8,128)(2,1)S(1)}, u32[]{:S(2)}, u32[]{:S(2)}) %collective-permute-start.15) | collective-permute-done | bytes 393248 | tf_op jit(solution)/shard_map/ppermute | solution.py:21
  60.1 8.0 %collective-permute-done.11 = bf16[3,256,256]{2,1,0:T(8,128)(2,1)S(1)} collective-permute-done((bf16[3,256,256]{2,1,0:T(8,128)(2,1)S(1)}, bf16[3,256,256]{2,1,0:T(8,128)(2,1)S(1)}, u32[]{:S(2)}, u32[]{:S(2)}) %collective-permute-start.11) | collective-permute-done | bytes 393248 | tf_op jit(solution)/shard_map/ppermute | solution.py:21
  68.1 2.2 broadcast_select_fusion.19
  70.4 3.7 %collective-permute-start.16 = (bf16[3,256,256]{2,1,0:T(8,128)(2,1)}, bf16[3,256,256]{2,1,0:T(8,128)(2,1)}, u32[]{:S(2)}, u32[]{:S(2)}) collective-permute-start(bf16[3,256,256]{2,1,0:T(8,128)(2,1)} %get-tuple-element.29), channel_id=1, source_target_pairs={{0,96},{8,104},{16,112},{24,120},{32,0},{40,8},{48,16},{56,24},{64... | collective-permute-start | bytes 1179656 | tf_op jit(solution)/shard_map/ppermute | solution.py:27
  77.8 4.8 %collective-permute-done.16 = bf16[3,256,256]{2,1,0:T(8,128)(2,1)} collective-permute-done((bf16[3,256,256]{2,1,0:T(8,128)(2,1)}, bf16[3,256,256]{2,1,0:T(8,128)(2,1)}, u32[]{:S(2)}, u32[]{:S(2)}) %collective-permute-start.16) | collective-permute-done | bytes 393248 | tf_op jit(solution)/shard_map/ppermute | solution.py:27
  84.2 3.7 %collective-permute-start.12 = (bf16[3,256,256]{2,1,0:T(8,128)(2,1)}, bf16[3,256,256]{2,1,0:T(8,128)(2,1)}, u32[]{:S(2)}, u32[]{:S(2)}) collective-permute-start(bf16[3,256,256]{2,1,0:T(8,128)(2,1)} %get-tuple-element.17), channel_id=1, source_target_pairs={{0,96},{8,104},{16,112},{24,120},{32,0},{40,8},{48,16},{56,24},{64... | collective-permute-start | bytes 1179656 | tf_op jit(solution)/shard_map/ppermute | solution.py:27
  87.9 7.1 %collective-permute-done.19 = bf16[3,256,256]{2,1,0:T(8,128)(2,1)} collective-permute-done((bf16[3,256,256]{2,1,0:T(8,128)(2,1)S(1)}, bf16[3,256,256]{2,1,0:T(8,128)(2,1)}, u32[]{:S(2)}, u32[]{:S(2)}) %collective-permute-start.19) | collective-permute-done | bytes 393248 | tf_op jit(solution)/shard_map/ppermute | solution.py:21
  102.6 3.7 %collective-permute-done.17 = bf16[3,256,256]{2,1,0:T(8,128)(2,1)S(1)} collective-permute-done((bf16[3,256,256]{2,1,0:T(8,128)(2,1)}, bf16[3,256,256]{2,1,0:T(8,128)(2,1)S(1)}, u32[]{:S(2)}, u32[]{:S(2)}) %collective-permute-start.17) | collective-permute-done | bytes 393248 | tf_op jit(solution)/shard_map/ppermute | solution.py:20
  107.2 2.5 collective-permute-start.18
  111.0 5.1 %collective-permute-done.10 = bf16[3,256,256]{2,1,0:T(8,128)(2,1)} collective-permute-done((bf16[3,256,256]{2,1,0:T(8,128)(2,1)}, bf16[3,256,256]{2,1,0:T(8,128)(2,1)}, u32[]{:S(2)}, u32[]{:S(2)}) %collective-permute-start.10) | collective-permute-done | bytes 393248 | tf_op jit(solution)/shard_map/ppermute | solution.py:26
  121.1 2.4 broadcast_select_fusion
  129.4 2.6 %pad_maximum_fusion = bf16[12,256,256]{2,1,0:T(8,128)(2,1)} fusion(bf16[3,256,256]{2,1,0:T(8,128)(2,1)} %copy-done.5, bf16[3,256,256]{2,1,0:T(8,128)(2,1)} %copy-done.3, bf16[3,256,256]{2,1,0:T(8,128)(2,1)S(1)} %get-tuple-element.40, bf16[3,256,256]{2,1,0:T(8,128)(2,1)S(1)} %get-tuple-element.39), kind=kLoop, calls=%fused_computation.16 | loop fusion | flops 2359296 | bytes 3145728 | tf_op jit(solution)/shard_map/concatenate | solution.py:54
  132.0 3.8 %collective-permute-done.26 = bf16[3,256,256]{2,1,0:T(8,128)(2,1)} collective-permute-done((bf16[3,256,256]{2,1,0:T(8,128)(2,1)}, bf16[3,256,256]{2,1,0:T(8,128)(2,1)}, u32[]{:S(2)}, u32[]{:S(2)}) %collective-permute-start.26) | collective-permute-done | bytes 393248 | tf_op jit(solution)/shard_map/ppermute | solution.py:20
  142.9 3.3 %select_convert_fusion = bf16[8,256,256]{2,1,0:T(8,128)(2,1)} fusion(bf16[8,256,256]{2,1,0:T(8,128)(2,1)S(1)} %copy-done.1, bf16[8,12,256,256]{3,2,0,1:T(8,128)(2,1)} %copy_select_fusion, s32[]{:T(128)S(6)} %select_n.549, pred[8]{0:T(512)(128)(4,1)S(1)} %fusion.47, pred[8]{0:T(512)(128)(4,1)S(1)} %get-tuple-element.13, ...), kind=kOutput, calls=%fused_computation.14 | convolution fusion | flops 540540928 | bytes 4459008 | tf_op jit(solution)/shard_map/iab,bc->iac/dot_general | solution.py:88
  147.9 3.2 %collective-permute-done.29 = bf16[3,256,256]{2,1,0:T(8,128)(2,1)} collective-permute-done((bf16[3,256,256]{2,1,0:T(8,128)(2,1)}, bf16[3,256,256]{2,1,0:T(8,128)(2,1)}, u32[]{:S(2)}, u32[]{:S(2)}) %collective-permute-start.29) | collective-permute-done | bytes 393248 | tf_op jit(solution)/shard_map/ppermute | solution.py:27
  153.8 2.3 collective-permute-start.35
  156.1 4.9 %collective-permute-done.32 = bf16[3,256,256]{2,1,0:T(8,128)(2,1)S(1)} collective-permute-done((bf16[3,256,256]{2,1,0:T(8,128)(2,1)S(1)}, bf16[3,256,256]{2,1,0:T(8,128)(2,1)S(1)}, u32[]{:S(2)}, u32[]{:S(2)}) %collective-permute-start.32) | collective-permute-done | bytes 393248 | tf_op jit(solution)/shard_map/ppermute | solution.py:21
  161.1 2.3 broadcast_select_fusion.11
  167.8 3.8 %collective-permute-done.37 = bf16[3,256,256]{2,1,0:T(8,128)(2,1)} collective-permute-done((bf16[3,256,256]{2,1,0:T(8,128)(2,1)}, bf16[3,256,256]{2,1,0:T(8,128)(2,1)}, u32[]{:S(2)}, u32[]{:S(2)}) %collective-permute-start.37) | collective-permute-done | bytes 393248 | tf_op jit(solution)/shard_map/ppermute | solution.py:27
  173.4 3.8 %collective-permute-start.40 = (bf16[3,256,256]{2,1,0:T(8,128)(2,1)}, bf16[3,256,256]{2,1,0:T(8,128)(2,1)}, u32[]{:S(2)}, u32[]{:S(2)}) collective-permute-start(bf16[3,256,256]{2,1,0:T(8,128)(2,1)} %select_select_fusion.2), channel_id=1, source_target_pairs={{0,24},{8,0},{16,8},{24,16},{32,56},{40,32},{48,40},{56,48},{64,88... | collective-permute-start | bytes 1179656 | tf_op jit(solution)/shard_map/ppermute | solution.py:21
  177.7 3.7 %collective-permute-start.33 = (bf16[3,256,256]{2,1,0:T(8,128)(2,1)}, bf16[3,256,256]{2,1,0:T(8,128)(2,1)S(1)}, u32[]{:S(2)}, u32[]{:S(2)}) collective-permute-start(bf16[3,256,256]{2,1,0:T(8,128)(2,1)} %get-tuple-element.5), channel_id=1, source_target_pairs={{0,96},{8,104},{16,112},{24,120},{32,0},{40,8},{48,16},{56,24},{64... | collective-permute-start | bytes 1179656 | tf_op jit(solution)/shard_map/ppermute | solution.py:27
  182.5 3.5 %collective-permute-done.40 = bf16[3,256,256]{2,1,0:T(8,128)(2,1)} collective-permute-done((bf16[3,256,256]{2,1,0:T(8,128)(2,1)}, bf16[3,256,256]{2,1,0:T(8,128)(2,1)}, u32[]{:S(2)}, u32[]{:S(2)}) %collective-permute-start.40) | collective-permute-done | bytes 393248 | tf_op jit(solution)/shard_map/ppermute | solution.py:21
  190.7 4.9 %collective-permute-done.38 = bf16[3,256,256]{2,1,0:T(8,128)(2,1)S(1)} collective-permute-done((bf16[3,256,256]{2,1,0:T(8,128)(2,1)S(1)}, bf16[3,256,256]{2,1,0:T(8,128)(2,1)S(1)}, u32[]{:S(2)}, u32[]{:S(2)}) %collective-permute-start.38) | collective-permute-done | bytes 393248 | tf_op jit(solution)/shard_map/ppermute | solution.py:20
  195.7 2.5 collective-permute-start.24
  201.1 10.1 %fusion.16 = f32[12,256,8,256]{1,3,2,0:T(8,128)} fusion(bf16[8,256,256]{2,1,0:T(8,128)(2,1)S(1)} %copy-done.2, bf16[3,256,256]{2,1,0:T(8,128)(2,1)S(1)} %copy-done.6, bf16[3,256,256]{2,1,0:T(8,128)(2,1)S(1)} %copy-done.4, bf16[3,256,256]{2,1,0:T(8,128)(2,1)S(1)} %get-tuple-element.40, bf16[3,256,256]{2,1,0:T(8,128)(2,1)S(1)} %get-tuple-element.39), kind=kOutput, calls=%fused_computation.25 | convolution fusion | flops 3227516928 | bytes 27787264 | tf_op jit(solution)/shard_map/iab,jbc->ijac/dot_general | solution.py:93
  215.1 29.8 %fusion.4 = bf16[8,12,256,256]{3,2,0,1:T(8,128)(2,1)} fusion(bf16[8,12,256,256]{3,2,0,1:T(8,128)(2,1)} %copy_select_fusion, f32[12,256,8,256]{1,3,2,0:T(8,128)} %fusion.16, pred[8,12]{0,1:T(8,128)(4,1)S(1)} %copy.80, pred[8,12]{0,1:T(8,128)(4,1)S(1)} %copy.79, pred[8,12]{0,1:T(8,128)(4,1)S(1)} %copy.78, pred[8,12]{0,1:T(8,128)(4,1)S(1)} %copy.69, ...), kind=kOutput, calls=%fused_computation.6 | convolution fusion | flops 3290431488 | bytes 54002048 | tf_op jit(solution)/shard_map/iab,jbc->ijac/dot_general | solution.py:93
  244.9 10.6 %copy.90 = bf16[8,12,256,256]{3,2,1,0:T(8,128)(2,1)} copy(bf16[8,12,256,256]{3,2,0,1:T(8,128)(2,1)} %fusion.4) | data formatting | bytes 25165824 | tf_op jit(solution)/shard_map/jit(_where)/select_n | solution.py:98
  (167 shorter events, 77.2 us)
Async XLA Ops:
  26.7 11.1 %collective-permute-start.5 = (bf16[3,256,256]{2,1,0:T(8,128)(2,1)}, bf16[3,256,256]{2,1,0:T(8,128)(2,1)S(1)}, u32[]{:S(2)}, u32[]{:S(2)}) collective-permute-start(bf16[3,256,256]{2,1,0:T(8,128)(2,1)} %get-tuple-element.34), channel_id=1, source_target_pairs={{0,8},{8,16},{16,24},{24,0},{32,40},{40,48},{48,56},{56,32},{64,72... | collective-permute-start | bytes 1179656 | tf_op jit(solution)/shard_map/ppermute | solution.py:20
  27.1 11.7 %collective-permute-start.7 = (bf16[3,256,256]{2,1,0:T(8,128)(2,1)S(1)}, bf16[3,256,256]{2,1,0:T(8,128)(2,1)S(1)}, u32[]{:S(2)}, u32[]{:S(2)}) collective-permute-start(bf16[3,256,256]{2,1,0:T(8,128)(2,1)S(1)} %get-tuple-element.32), channel_id=1, source_target_pairs={{0,24},{8,0},{16,8},{24,16},{32,56},{40,32},{48,40},{56,48},{64,88... | collective-permute-start | bytes 1179656 | tf_op jit(solution)/shard_map/ppermute | solution.py:21
  28.7 15.7 %collective-permute-start.13 = (bf16[3,256,256]{2,1,0:T(8,128)(2,1)}, bf16[3,256,256]{2,1,0:T(8,128)(2,1)S(1)}, u32[]{:S(2)}, u32[]{:S(2)}) collective-permute-start(bf16[3,256,256]{2,1,0:T(8,128)(2,1)} %get-tuple-element.33), channel_id=1, source_target_pairs={{0,32},{8,40},{16,48},{24,56},{32,64},{40,72},{48,80},{56,88},{64,... | collective-permute-start | bytes 1179656 | tf_op jit(solution)/shard_map/ppermute | solution.py:20
  39.8 10.9 %collective-permute-start.6 = (bf16[3,256,256]{2,1,0:T(8,128)(2,1)}, bf16[3,256,256]{2,1,0:T(8,128)(2,1)S(1)}, u32[]{:S(2)}, u32[]{:S(2)}) collective-permute-start(bf16[3,256,256]{2,1,0:T(8,128)(2,1)} %get-tuple-element.31), channel_id=1, source_target_pairs={{0,8},{8,16},{16,24},{24,0},{32,40},{40,48},{48,56},{56,32},{64,72... | collective-permute-start | bytes 1179656 | tf_op jit(solution)/shard_map/ppermute | solution.py:26
  40.2 11.2 %collective-permute-start.8 = (bf16[3,256,256]{2,1,0:T(8,128)(2,1)}, bf16[3,256,256]{2,1,0:T(8,128)(2,1)}, u32[]{:S(2)}, u32[]{:S(2)}) collective-permute-start(bf16[3,256,256]{2,1,0:T(8,128)(2,1)} %get-tuple-element.30), channel_id=1, source_target_pairs={{0,24},{8,0},{16,8},{24,16},{32,56},{40,32},{48,40},{56,48},{64,88... | collective-permute-start | bytes 1179656 | tf_op jit(solution)/shard_map/ppermute | solution.py:27
  44.4 29.6 %collective-permute-start = (bf16[8,256,256]{2,1,0:T(8,128)(2,1)}, bf16[8,256,256]{2,1,0:T(8,128)(2,1)}, u32[]{:S(2)}, u32[]{:S(2)}) collective-permute-start(bf16[8,256,256]{2,1,0:T(8,128)(2,1)} %select_convert_fusion.1), channel_id=1, source_target_pairs={{0,1},{1,0},{2,3},{3,2},{4,5},{5,4},{6,7},{7,6},{8,9},{9,8},{10,11... | collective-permute-start | bytes 3145736 | tf_op jit(solution)/shard_map/ppermute | solution.py:65
  46.4 13.7 %collective-permute-start.15 = (bf16[3,256,256]{2,1,0:T(8,128)(2,1)S(1)}, bf16[3,256,256]{2,1,0:T(8,128)(2,1)S(1)}, u32[]{:S(2)}, u32[]{:S(2)}) collective-permute-start(bf16[3,256,256]{2,1,0:T(8,128)(2,1)S(1)} %get-tuple-element.22), channel_id=1, source_target_pairs={{0,96},{8,104},{16,112},{24,120},{32,0},{40,8},{48,16},{56,24},{64... | collective-permute-start | bytes 1179656 | tf_op jit(solution)/shard_map/ppermute | solution.py:21
  51.5 16.6 %collective-permute-start.11 = (bf16[3,256,256]{2,1,0:T(8,128)(2,1)S(1)}, bf16[3,256,256]{2,1,0:T(8,128)(2,1)S(1)}, u32[]{:S(2)}, u32[]{:S(2)}) collective-permute-start(bf16[3,256,256]{2,1,0:T(8,128)(2,1)S(1)} %select_select_fusion.14), channel_id=1, source_target_pairs={{0,96},{8,104},{16,112},{24,120},{32,0},{40,8},{48,16},{56,24},{64... | collective-permute-start | bytes 1179656 | tf_op jit(solution)/shard_map/ppermute | solution.py:21
  55.9 21.2 %collective-permute-start.14 = (bf16[3,256,256]{2,1,0:T(8,128)(2,1)}, bf16[3,256,256]{2,1,0:T(8,128)(2,1)S(1)}, u32[]{:S(2)}, u32[]{:S(2)}) collective-permute-start(bf16[3,256,256]{2,1,0:T(8,128)(2,1)} %get-tuple-element.21), channel_id=1, source_target_pairs={{0,32},{8,40},{16,48},{24,56},{32,64},{40,72},{48,80},{56,88},{64,... | collective-permute-start | bytes 1179656 | tf_op jit(solution)/shard_map/ppermute | solution.py:26
  70.4 12.3 %collective-permute-start.16 = (bf16[3,256,256]{2,1,0:T(8,128)(2,1)}, bf16[3,256,256]{2,1,0:T(8,128)(2,1)}, u32[]{:S(2)}, u32[]{:S(2)}) collective-permute-start(bf16[3,256,256]{2,1,0:T(8,128)(2,1)} %get-tuple-element.29), channel_id=1, source_target_pairs={{0,96},{8,104},{16,112},{24,120},{32,0},{40,8},{48,16},{56,24},{64... | collective-permute-start | bytes 1179656 | tf_op jit(solution)/shard_map/ppermute | solution.py:27
  75.4 22.4 %collective-permute-start.1 = (bf16[8,256,256]{2,1,0:T(8,128)(2,1)S(1)}, bf16[8,256,256]{2,1,0:T(8,128)(2,1)}, u32[]{:S(2)}, u32[]{:S(2)}) collective-permute-start(bf16[8,256,256]{2,1,0:T(8,128)(2,1)S(1)} %broadcast_select_fusion.1), channel_id=1, source_target_pairs={{0,2},{2,4},{4,6},{6,0},{1,7},{3,1},{5,3},{7,5},{8,10},{10,12},{12... | collective-permute-start | bytes 3145736 | tf_op jit(solution)/shard_map/ppermute | solution.py:67
  83.8 11.2 %collective-permute-start.19 = (bf16[3,256,256]{2,1,0:T(8,128)(2,1)S(1)}, bf16[3,256,256]{2,1,0:T(8,128)(2,1)}, u32[]{:S(2)}, u32[]{:S(2)}) collective-permute-start(bf16[3,256,256]{2,1,0:T(8,128)(2,1)S(1)} %select_select_fusion.10), channel_id=1, source_target_pairs={{0,24},{8,0},{16,8},{24,16},{32,56},{40,32},{48,40},{56,48},{64,88... | collective-permute-start | bytes 1179656 | tf_op jit(solution)/shard_map/ppermute | solution.py:21
  84.2 17.4 %collective-permute-start.9 = (bf16[3,256,256]{2,1,0:T(8,128)(2,1)}, bf16[3,256,256]{2,1,0:T(8,128)(2,1)S(1)}, u32[]{:S(2)}, u32[]{:S(2)}) collective-permute-start(bf16[3,256,256]{2,1,0:T(8,128)(2,1)} %get-tuple-element.18), channel_id=1, source_target_pairs={{0,32},{8,40},{16,48},{24,56},{32,64},{40,72},{48,80},{56,88},{64,... | collective-permute-start | bytes 1179656 | tf_op jit(solution)/shard_map/ppermute | solution.py:20
  84.2 22.9 %collective-permute-start.12 = (bf16[3,256,256]{2,1,0:T(8,128)(2,1)}, bf16[3,256,256]{2,1,0:T(8,128)(2,1)}, u32[]{:S(2)}, u32[]{:S(2)}) collective-permute-start(bf16[3,256,256]{2,1,0:T(8,128)(2,1)} %get-tuple-element.17), channel_id=1, source_target_pairs={{0,96},{8,104},{16,112},{24,120},{32,0},{40,8},{48,16},{56,24},{64... | collective-permute-start | bytes 1179656 | tf_op jit(solution)/shard_map/ppermute | solution.py:27
  99.1 19.9 %collective-permute-start.2 = (bf16[8,256,256]{2,1,0:T(8,128)(2,1)S(1)}, bf16[8,256,256]{2,1,0:T(8,128)(2,1)}, u32[]{:S(2)}, u32[]{:S(2)}) collective-permute-start(bf16[8,256,256]{2,1,0:T(8,128)(2,1)S(1)} %broadcast_select_fusion.2), channel_id=1, source_target_pairs={{0,1},{1,0},{2,3},{3,2},{4,5},{5,4},{6,7},{7,6},{8,9},{9,8},{10,11... | collective-permute-start | bytes 3145736 | tf_op jit(solution)/shard_map/ppermute | solution.py:70
  102.6 13.6 %collective-permute-start.10 = (bf16[3,256,256]{2,1,0:T(8,128)(2,1)}, bf16[3,256,256]{2,1,0:T(8,128)(2,1)}, u32[]{:S(2)}, u32[]{:S(2)}) collective-permute-start(bf16[3,256,256]{2,1,0:T(8,128)(2,1)} %broadcast_select_fusion.20), channel_id=1, source_target_pairs={{0,32},{8,40},{16,48},{24,56},{32,64},{40,72},{48,80},{56,88},{64,... | collective-permute-start | bytes 1179656 | tf_op jit(solution)/shard_map/ppermute | solution.py:26
  106.3 11.3 %collective-permute-start.20 = (bf16[3,256,256]{2,1,0:T(8,128)(2,1)}, bf16[3,256,256]{2,1,0:T(8,128)(2,1)S(1)}, u32[]{:S(2)}, u32[]{:S(2)}) collective-permute-start(bf16[3,256,256]{2,1,0:T(8,128)(2,1)} %get-tuple-element.19), channel_id=1, source_target_pairs={{0,24},{8,0},{16,8},{24,16},{32,56},{40,32},{48,40},{56,48},{64,88... | collective-permute-start | bytes 1179656 | tf_op jit(solution)/shard_map/ppermute | solution.py:27
  124.6 11.2 %collective-permute-start.26 = (bf16[3,256,256]{2,1,0:T(8,128)(2,1)}, bf16[3,256,256]{2,1,0:T(8,128)(2,1)}, u32[]{:S(2)}, u32[]{:S(2)}) collective-permute-start(bf16[3,256,256]{2,1,0:T(8,128)(2,1)} %get-tuple-element.28), channel_id=1, source_target_pairs={{0,8},{8,16},{16,24},{24,0},{32,40},{40,48},{48,56},{56,32},{64,72... | collective-permute-start | bytes 1179656 | tf_op jit(solution)/shard_map/ppermute | solution.py:20
  125.5 11.5 %collective-permute-start.28 = (bf16[3,256,256]{2,1,0:T(8,128)(2,1)}, bf16[3,256,256]{2,1,0:T(8,128)(2,1)}, u32[]{:S(2)}, u32[]{:S(2)}) collective-permute-start(bf16[3,256,256]{2,1,0:T(8,128)(2,1)} %get-tuple-element.26), channel_id=1, source_target_pairs={{0,24},{8,0},{16,8},{24,16},{32,56},{40,32},{48,40},{56,48},{64,88... | collective-permute-start | bytes 1179656 | tf_op jit(solution)/shard_map/ppermute | solution.py:21
  139.8 11.3 %collective-permute-start.29 = (bf16[3,256,256]{2,1,0:T(8,128)(2,1)}, bf16[3,256,256]{2,1,0:T(8,128)(2,1)}, u32[]{:S(2)}, u32[]{:S(2)}) collective-permute-start(bf16[3,256,256]{2,1,0:T(8,128)(2,1)} %get-tuple-element.24), channel_id=1, source_target_pairs={{0,24},{8,0},{16,8},{24,16},{32,56},{40,32},{48,40},{56,48},{64,88... | collective-permute-start | bytes 1179656 | tf_op jit(solution)/shard_map/ppermute | solution.py:27
  140.9 15.3 %collective-permute-start.36 = (bf16[3,256,256]{2,1,0:T(8,128)(2,1)}, bf16[3,256,256]{2,1,0:T(8,128)(2,1)}, u32[]{:S(2)}, u32[]{:S(2)}) collective-permute-start(bf16[3,256,256]{2,1,0:T(8,128)(2,1)} %slice_bitcast_fusion), channel_id=1, source_target_pairs={{0,96},{8,104},{16,112},{24,120},{32,0},{40,8},{48,16},{56,24},{64... | collective-permute-start | bytes 1179656 | tf_op jit(solution)/shard_map/ppermute | solution.py:21
  146.2 19.2 %collective-permute-start.21 = (bf16[8,256,256]{2,1,0:T(8,128)(2,1)}, bf16[8,256,256]{2,1,0:T(8,128)(2,1)}, u32[]{:S(2)}, u32[]{:S(2)}) collective-permute-start(bf16[8,256,256]{2,1,0:T(8,128)(2,1)} %select_convert_fusion), channel_id=1, source_target_pairs={{0,1},{1,0},{2,3},{3,2},{4,5},{5,4},{6,7},{7,6},{8,9},{9,8},{10,11... | collective-permute-start | bytes 3145736 | tf_op jit(solution)/shard_map/ppermute | solution.py:65
  153.8 14.0 %collective-permute-start.35 = (bf16[3,256,256]{2,1,0:T(8,128)(2,1)}, bf16[3,256,256]{2,1,0:T(8,128)(2,1)}, u32[]{:S(2)}, u32[]{:S(2)}) collective-permute-start(bf16[3,256,256]{2,1,0:T(8,128)(2,1)} %broadcast_select_fusion.10), channel_id=1, source_target_pairs={{0,32},{8,40},{16,48},{24,56},{32,64},{40,72},{48,80},{56,88},{64,... | collective-permute-start | bytes 1179656 | tf_op jit(solution)/shard_map/ppermute | solution.py:26
  166.8 22.5 %collective-permute-start.22 = (bf16[8,256,256]{2,1,0:T(8,128)(2,1)S(1)}, bf16[8,256,256]{2,1,0:T(8,128)(2,1)}, u32[]{:S(2)}, u32[]{:S(2)}) collective-permute-start(bf16[8,256,256]{2,1,0:T(8,128)(2,1)S(1)} %broadcast_select_fusion.3), channel_id=1, source_target_pairs={{0,2},{2,4},{4,6},{6,0},{1,7},{3,1},{5,3},{7,5},{8,10},{10,12},{12... | collective-permute-start | bytes 3145736 | tf_op jit(solution)/shard_map/ppermute | solution.py:67
  167.8 13.6 %collective-permute-start.30 = (bf16[3,256,256]{2,1,0:T(8,128)(2,1)}, bf16[3,256,256]{2,1,0:T(8,128)(2,1)}, u32[]{:S(2)}, u32[]{:S(2)}) collective-permute-start(bf16[3,256,256]{2,1,0:T(8,128)(2,1)} %get-tuple-element.6), channel_id=1, source_target_pairs={{0,32},{8,40},{16,48},{24,56},{32,64},{40,72},{48,80},{56,88},{64,... | collective-permute-start | bytes 1179656 | tf_op jit(solution)/shard_map/ppermute | solution.py:20
  173.4 12.6 %collective-permute-start.40 = (bf16[3,256,256]{2,1,0:T(8,128)(2,1)}, bf16[3,256,256]{2,1,0:T(8,128)(2,1)}, u32[]{:S(2)}, u32[]{:S(2)}) collective-permute-start(bf16[3,256,256]{2,1,0:T(8,128)(2,1)} %select_select_fusion.2), channel_id=1, source_target_pairs={{0,24},{8,0},{16,8},{24,16},{32,56},{40,32},{48,40},{56,48},{64,88... | collective-permute-start | bytes 1179656 | tf_op jit(solution)/shard_map/ppermute | solution.py:21
  177.7 21.5 %collective-permute-start.33 = (bf16[3,256,256]{2,1,0:T(8,128)(2,1)}, bf16[3,256,256]{2,1,0:T(8,128)(2,1)S(1)}, u32[]{:S(2)}, u32[]{:S(2)}) collective-permute-start(bf16[3,256,256]{2,1,0:T(8,128)(2,1)} %get-tuple-element.5), channel_id=1, source_target_pairs={{0,96},{8,104},{16,112},{24,120},{32,0},{40,8},{48,16},{56,24},{64... | collective-permute-start | bytes 1179656 | tf_op jit(solution)/shard_map/ppermute | solution.py:27
  182.5 28.8 %collective-permute-start.31 = (bf16[3,256,256]{2,1,0:T(8,128)(2,1)S(1)}, bf16[3,256,256]{2,1,0:T(8,128)(2,1)S(1)}, u32[]{:S(2)}, u32[]{:S(2)}) collective-permute-start(bf16[3,256,256]{2,1,0:T(8,128)(2,1)S(1)} %broadcast_select_fusion.12), channel_id=1, source_target_pairs={{0,32},{8,40},{16,48},{24,56},{32,64},{40,72},{48,80},{56,88},{64,... | collective-permute-start | bytes 1179656 | tf_op jit(solution)/shard_map/ppermute | solution.py:26
  189.1 22.4 %collective-permute-start.41 = (bf16[3,256,256]{2,1,0:T(8,128)(2,1)S(1)}, bf16[3,256,256]{2,1,0:T(8,128)(2,1)S(1)}, u32[]{:S(2)}, u32[]{:S(2)}) collective-permute-start(bf16[3,256,256]{2,1,0:T(8,128)(2,1)S(1)} %get-tuple-element.7), channel_id=1, source_target_pairs={{0,24},{8,0},{16,8},{24,16},{32,56},{40,32},{48,40},{56,48},{64,88... | collective-permute-start | bytes 1179656 | tf_op jit(solution)/shard_map/ppermute | solution.py:27
  190.6 23.1 %collective-permute-start.23 = (bf16[8,256,256]{2,1,0:T(8,128)(2,1)S(1)}, bf16[8,256,256]{2,1,0:T(8,128)(2,1)S(1)}, u32[]{:S(2)}, u32[]{:S(2)}) collective-permute-start(bf16[8,256,256]{2,1,0:T(8,128)(2,1)S(1)} %broadcast_select_fusion.4), channel_id=1, source_target_pairs={{0,1},{1,0},{2,3},{3,2},{4,5},{5,4},{6,7},{7,6},{8,9},{9,8},{10,11... | collective-permute-start | bytes 3145736 | tf_op jit(solution)/shard_map/ppermute | solution.py:70
  195.7 15.6 %collective-permute-start.24 = (bf16[4,256,256]{2,1,0:T(8,128)(2,1)S(1)}, bf16[4,256,256]{2,1,0:T(8,128)(2,1)S(1)}, u32[]{:S(2)}, u32[]{:S(2)}) collective-permute-start(bf16[4,256,256]{2,1,0:T(8,128)(2,1)S(1)} %slice_select_fusion), channel_id=1, source_target_pairs={{0,2},{2,4},{4,6},{6,0},{1,7},{3,1},{5,3},{7,5},{8,10},{10,12},{12... | collective-permute-start | bytes 1572872 | tf_op jit(solution)/shard_map/ppermute | solution.py:73
  199.2 12.2 %collective-permute-start.39 = (bf16[3,256,256]{2,1,0:T(8,128)(2,1)S(1)}, bf16[3,256,256]{2,1,0:T(8,128)(2,1)S(1)}, u32[]{:S(2)}, u32[]{:S(2)}) collective-permute-start(bf16[3,256,256]{2,1,0:T(8,128)(2,1)S(1)} %broadcast_select_fusion.6), channel_id=1, source_target_pairs={{0,8},{8,16},{16,24},{24,0},{32,40},{40,48},{48,56},{56,32},{64,72... | collective-permute-start | bytes 1179656 | tf_op jit(solution)/shard_map/ppermute | solution.py:26
  (36 other events, 370.8 us)

commit v2 on v1

--- a/solution.py
+++ b/solution.py
@@ -1,6 +1,8 @@
 import jax
 import jax.numpy as jnp
 from jax import lax
+from jax.experimental import pallas as pl
+from jax.experimental.pallas import tpu as pltpu
 from jax.sharding import PartitionSpec as P
 
 RING = 4
@@ -98,6 +100,48 @@
     return jnp.where(place[:, :, None, None], lower[:, None], result)
 
 
+def update_kernel(codes, front_ref, l1_ref, l2_ref, u1_ref, u2_ref, out_ref):
+    i = pl.program_id(0)
+    lower1 = l1_ref[0]
+    lower2 = l2_ref[0]
+    for j in range(front_ref.shape[1]):
+        code = codes[i, j]
+        block = front_ref[0, j]
+        block = jnp.where((code & 1) != 0, block, jnp.zeros_like(block))
+        product = jnp.dot(lower1, u1_ref[j], preferred_element_type=jnp.float32)
+        changed = (block.astype(jnp.float32) - product).astype(jnp.bfloat16)
+        block = jnp.where((code & 2) != 0, changed, block)
+        block = jnp.where((code & 4) != 0, lower1, block)
+        product = jnp.dot(lower2, u2_ref[j], preferred_element_type=jnp.float32)
+        changed = (block.astype(jnp.float32) - product).astype(jnp.bfloat16)
+        block = jnp.where((code & 8) != 0, changed, block)
+        block = jnp.where((code & 16) != 0, lower2, block)
+        out_ref[0, j] = block
+
+
+def both_updates(front, codes, lower1, lower2, upper1, upper2):
+    rows, cols, bs, _ = front.shape
+    row_block = pl.BlockSpec((1, cols, bs, bs), lambda i, c: (i, 0, 0, 0))
+    lower_block = pl.BlockSpec((1, bs, bs), lambda i, c: (i, 0, 0))
+    upper_block = pl.BlockSpec((cols, bs, bs), lambda i, c: (0, 0, 0))
+    return pl.pallas_call(
+        update_kernel,
+        grid_spec=pltpu.PrefetchScalarGridSpec(
+            num_scalar_prefetch=1,
+            grid=(rows,),
+            in_specs=[row_block, lower_block, lower_block, upper_block, upper_block],
+            out_specs=row_block,
+        ),
+        out_shape=jax.ShapeDtypeStruct(front.shape, front.dtype),
+        compiler_params=pltpu.CompilerParams(dimension_semantics=("arbitrary",)),
+    )(codes, front, lower1, lower2, upper1, upper2)
+
+
+def masked(blocks, keep):
+    shape = keep.shape + (1,) * (blocks.ndim - keep.ndim)
+    return jnp.where(keep.reshape(shape) > 0, blocks, jnp.zeros_like(blocks))
+
+
 def body(front, pattern, pivots, pivot_inv):
     rows_dev = front.shape[0]
     cols_dev = front.shape[1]
@@ -110,7 +154,6 @@
     local = lax.dynamic_index_in_dim(local, col_index, 2, keepdims=False)
     front_rows = jnp.arange(rows_dev, dtype=jnp.int32) * nrow + row_index
     front_cols = jnp.arange(cols_dev, dtype=jnp.int32) * ncol + col_index
-    matrix = jnp.where(local[:, :, None, None] > 0, front, jnp.zeros_like(front))
     first = pivots[0]
     second = pivots[1]
     rows_first = front_rows != first
@@ -118,13 +161,22 @@
     rows_second = rows_first & (front_rows != second)
     cols_second = cols_first & (front_cols != second)
 
-    column_first = lax.dynamic_index_in_dim(matrix, first // ncol, 1, keepdims=False)
+    b1 = first // ncol
+    column_first = masked(
+        lax.dynamic_index_in_dim(front, b1, 1, keepdims=False),
+        lax.dynamic_index_in_dim(local, b1, 1, keepdims=False),
+    )
     lower_first = col_bcast(lower_local(column_first, pivot_inv[0], rows_first), first % ncol)
-    first_row = lax.dynamic_index_in_dim(matrix, first // nrow, 0, keepdims=False)
+    a1 = first // nrow
+    first_row = masked(
+        lax.dynamic_index_in_dim(front, a1, 0, keepdims=False),
+        lax.dynamic_index_in_dim(local, a1, 0, keepdims=False),
+    )
     upper_first = row_bcast(first_row, first % nrow)
 
     a2 = second // nrow
-    row_before = lax.dynamic_slice_in_dim(matrix, a2, 1, 0)
+    local_row = lax.dynamic_slice_in_dim(local, a2, 1, 0)
+    row_before = masked(lax.dynamic_slice_in_dim(front, a2, 1, 0), local_row)
     row_after = eliminate(
         row_before,
         lax.dynamic_slice_in_dim(lower_first, a2, 1, 0),
@@ -132,12 +184,13 @@
         first,
         lax.dynamic_slice_in_dim(rows_first, a2, 1, 0),
         cols_first,
-        lax.dynamic_slice_in_dim(local, a2, 1, 0),
+        local_row,
         front_cols,
     )
     upper_second = row_bcast(row_after[0], second % nrow)
     b2 = second // ncol
-    col_before = lax.dynamic_slice_in_dim(matrix, b2, 1, 1)
+    local_col = lax.dynamic_slice_in_dim(local, b2, 1, 1)
+    col_before = masked(lax.dynamic_slice_in_dim(front, b2, 1, 1), local_col)
     col_after = eliminate(
         col_before,
         lower_first,
@@ -145,18 +198,24 @@
         first,
         rows_first,
         lax.dynamic_slice_in_dim(cols_first, b2, 1, 0),
-        lax.dynamic_slice_in_dim(local, b2, 1, 1),
+        local_col,
         lax.dynamic_slice_in_dim(front_cols, b2, 1, 0),
     )
     lower_second = col_bcast(lower_local(col_after[:, 0], pivot_inv[1], rows_second), second % ncol)
 
-    matrix = eliminate(
-        matrix, lower_first, upper_first, first, rows_first, cols_first, local, front_cols
-    )
-    matrix = eliminate(
-        matrix, lower_second, upper_second, second, rows_second, cols_second, local, front_cols
-    )
-    return matrix
+    keep = local > 0
+    update_first = rows_first[:, None] & cols_first[None, :] & keep
+    place_first = rows_first[:, None] & (front_cols == first)[None, :]
+    update_second = rows_second[:, None] & cols_second[None, :] & keep
+    place_second = rows_second[:, None] & (front_cols == second)[None, :]
+    codes = (
+        keep.astype(jnp.int32)
+        + 2 * update_first.astype(jnp.int32)
+        + 4 * place_first.astype(jnp.int32)
+        + 8 * update_second.astype(jnp.int32)
+        + 16 * place_second.astype(jnp.int32)
+    )
+    return both_updates(front, codes, lower_first, lower_second, upper_first, upper_second)
 
 
 def solution(mesh):

time: 259 us -> 232 us (0.90)
  matrix products: 48.3 us -> 9.43 us
  waiting for transfers between devices: 68.3 us -> 98.4 us
  Pallas kernels: 0 us -> 16.7 us
  other arithmetic: 54.8 us -> 41.1 us
  local copies, waits for them, and re-layouts: 22.3 us -> 9.31 us
  starting transfers between devices: 55.2 us -> 46.4 us
    dot_general x3 -> x1, matrix products: 42.4 us -> 2.27 us  [eliminate(): jnp.einsum('iab,jbc->ijac', lower, upper, preferred_element_type=jnp.floa...]
    ppermute x8, waiting for transfers between devices: 30 us -> 46.7 us  [ring_bcast(): got_minus = lax.ppermute(second, axis, minus)]
    pallas_call x0 -> x1, Pallas kernels: none -> 16.7 us  [both_updates(): pl.pallas_call(update_kernel, grid_spec=pltpu.PrefetchScalarGridSpec(num_...]
    ppermute x8, waiting for transfers between devices: 6.87 us -> 20.2 us  [ring_bcast(): got_plus2 = lax.ppermute(send_plus, axis, plus)]
    select_n x1 -> x0, local copies, waits for them, and re-layouts: 10.6 us -> none  [eliminate(): return jnp.where(place[:, :, None, None], lower[:, None], result)]
    select_n x1, other arithmetic: 10.6 us -> 1.58 us  [masked(): return jnp.where(keep.reshape(shape) > 0, blocks, jnp.zeros_like(blocks))]
    ppermute x8, starting transfers between devices: 18 us -> 10.6 us  [ring_bcast(): got_minus = lax.ppermute(second, axis, minus)]
    ppermute x8, starting transfers between devices: 15.1 us -> 11.7 us  [ring_bcast(): got_minus2 = lax.ppermute(send_minus, axis, minus)]
  transfers between devices with their start and end apart: 42 -> 42, of which waited for: 16 -> 22; matrix products, arithmetic and copies ran while one was open for 21% -> 20% of each run, Pallas kernels for 0% -> 0%
where the time goes in v2:
time: 232 us; the launch traced here: 228 us
  waiting for transfers between devices  98.4 us (42%)
  starting transfers between devices  46.4 us (20%)
  other arithmetic  41.1 us (18%)
  Pallas kernels  16.7 us (7%)
  matrix products  9.43 us (4%)
  local copies, waits for them, and re-layouts  9.31 us (4%)
  between operations  6.91 us (3%)
    ppermute x8, waiting for transfers between devices, ring_bcast(): got_minus = lax.ppermute(second, axis, minus)  46.7 us
    ppermute x8, waiting for transfers between devices, ring_bcast(): got_plus = lax.ppermute(first, axis, plus)  20.6 us
    ppermute x8, waiting for transfers between devices, ring_bcast(): got_plus2 = lax.ppermute(send_plus, axis, plus)  20.2 us
    pallas_call x1, Pallas kernels, both_updates(): pl.pallas_call(update_kernel, grid_spec=pltpu.PrefetchScalarGridSpec(num_...  16.7 us
    ppermute x8, starting transfers between devices, ring_bcast(): got_minus2 = lax.ppermute(send_minus, axis, minus)  11.7 us
    ppermute x8, starting transfers between devices, ring_bcast(): got_plus2 = lax.ppermute(send_plus, axis, plus)  11 us
    ppermute x8, waiting for transfers between devices, ring_bcast(): got_minus2 = lax.ppermute(send_minus, axis, minus)  10.9 us
    ppermute x8, starting transfers between devices, ring_bcast(): got_minus = lax.ppermute(second, axis, minus)  10.6 us
  transfers between devices with their start and end apart: 42, of which 22 were waited for; matrix products, arithmetic and copies ran while one was open for 20% of the time, Pallas kernels for 0%

profile of v2, /device:TPU:6, one launch (start us, length us, event | category | flops | bytes accessed | tf_op | source)
XLA Modules:
  0.0 228.4 jit_solution(10788464413656865247)
XLA Ops:
  13.5 8.2 %collective-permute-done.7 = bf16[3,256,256]{2,1,0:T(8,128)(2,1)S(1)} collective-permute-done((bf16[3,256,256]{2,1,0:T(8,128)(2,1)S(1)}, bf16[3,256,256]{2,1,0:T(8,128)(2,1)S(1)}, u32[]{:S(2)}, u32[]{:S(2)}) %collective-permute-start.7) | collective-permute-done | bytes 393248 | tf_op jit(solution)/shard_map/ppermute | solution.py:23
  22.1 2.7 %select_convert_fusion.1 = bf16[8,256,256]{2,1,0:T(8,128)(2,1)} fusion(bf16[8,12,256,256]{3,2,1,0:T(8,128)(2,1)} %front_ref.1, s32[]{:T(128)S(6)} %select_n.561, pred[8]{0:T(512)(128)(4,1)S(1)} %get-tuple-element.46, pred[8]{0:T(512)(128)(4,1)S(1)} %get-tuple-element.22, bf16[2,256,256]{2,1,0:T(8,128)(2,1)} %param.7), kind=kOutput, calls=%fused_computation.6 | convolution fusion | flops 270008320 | bytes 2228244 | tf_op jit(solution)/shard_map/iab,bc->iac/dot_general | solution.py:90
  26.8 5.1 %collective-permute-done.5 = bf16[3,256,256]{2,1,0:T(8,128)(2,1)S(1)} collective-permute-done((bf16[3,256,256]{2,1,0:T(8,128)(2,1)S(1)}, bf16[3,256,256]{2,1,0:T(8,128)(2,1)S(1)}, u32[]{:S(2)}, u32[]{:S(2)}) %collective-permute-start.5) | collective-permute-done | bytes 393248 | tf_op jit(solution)/shard_map/ppermute | solution.py:22
  34.2 3.3 %collective-permute-done.8 = bf16[3,256,256]{2,1,0:T(8,128)(2,1)S(1)} collective-permute-done((bf16[3,256,256]{2,1,0:T(8,128)(2,1)S(1)}, bf16[3,256,256]{2,1,0:T(8,128)(2,1)S(1)}, u32[]{:S(2)}, u32[]{:S(2)}) %collective-permute-start.8) | collective-permute-done | bytes 393248 | tf_op jit(solution)/shard_map/ppermute | solution.py:29
  37.5 4.5 %collective-permute-done.6 = bf16[3,256,256]{2,1,0:T(8,128)(2,1)S(1)} collective-permute-done((bf16[3,256,256]{2,1,0:T(8,128)(2,1)}, bf16[3,256,256]{2,1,0:T(8,128)(2,1)S(1)}, u32[]{:S(2)}, u32[]{:S(2)}) %collective-permute-start.6) | collective-permute-done | bytes 393248 | tf_op jit(solution)/shard_map/ppermute | solution.py:28
  42.8 4.1 %collective-permute-start.11 = (bf16[3,256,256]{2,1,0:T(8,128)(2,1)S(1)}, bf16[3,256,256]{2,1,0:T(8,128)(2,1)S(1)}, u32[]{:S(2)}, u32[]{:S(2)}) collective-permute-start(bf16[3,256,256]{2,1,0:T(8,128)(2,1)S(1)} %select_select_fusion.14), channel_id=1, source_target_pairs={{0,96},{8,104},{16,112},{24,120},{32,0},{40,8},{48,16},{56,24},{64... | collective-permute-start | bytes 1179656 | tf_op jit(solution)/shard_map/ppermute | solution.py:23
  50.0 2.5 %collective-permute-done.11 = bf16[3,256,256]{2,1,0:T(8,128)(2,1)S(1)} collective-permute-done((bf16[3,256,256]{2,1,0:T(8,128)(2,1)S(1)}, bf16[3,256,256]{2,1,0:T(8,128)(2,1)S(1)}, u32[]{:S(2)}, u32[]{:S(2)}) %collective-permute-start.11) | collective-permute-done | bytes 393248 | tf_op jit(solution)/shard_map/ppermute | solution.py:23
  53.8 3.7 %collective-permute-start.15 = (bf16[3,256,256]{2,1,0:T(8,128)(2,1)S(1)}, bf16[3,256,256]{2,1,0:T(8,128)(2,1)S(1)}, u32[]{:S(2)}, u32[]{:S(2)}) collective-permute-start(bf16[3,256,256]{2,1,0:T(8,128)(2,1)S(1)} %get-tuple-element.31), channel_id=1, source_target_pairs={{0,96},{8,104},{16,112},{24,120},{32,0},{40,8},{48,16},{56,24},{64... | collective-permute-start | bytes 1179656 | tf_op jit(solution)/shard_map/ppermute | solution.py:23
  58.2 4.6 %collective-permute-done.15 = bf16[3,256,256]{2,1,0:T(8,128)(2,1)S(1)} collective-permute-done((bf16[3,256,256]{2,1,0:T(8,128)(2,1)S(1)}, bf16[3,256,256]{2,1,0:T(8,128)(2,1)S(1)}, u32[]{:S(2)}, u32[]{:S(2)}) %collective-permute-start.15) | collective-permute-done | bytes 393248 | tf_op jit(solution)/shard_map/ppermute | solution.py:23
  62.8 3.7 %collective-permute-done.13 = bf16[3,256,256]{2,1,0:T(8,128)(2,1)S(1)} collective-permute-done((bf16[3,256,256]{2,1,0:T(8,128)(2,1)S(1)}, bf16[3,256,256]{2,1,0:T(8,128)(2,1)S(1)}, u32[]{:S(2)}, u32[]{:S(2)}) %collective-permute-start.13) | collective-permute-done | bytes 393248 | tf_op jit(solution)/shard_map/ppermute | solution.py:22
  74.5 3.8 %collective-permute-done.16 = bf16[3,256,256]{2,1,0:T(8,128)(2,1)} collective-permute-done((bf16[3,256,256]{2,1,0:T(8,128)(2,1)}, bf16[3,256,256]{2,1,0:T(8,128)(2,1)}, u32[]{:S(2)}, u32[]{:S(2)}) %collective-permute-start.16) | collective-permute-done | bytes 393248 | tf_op jit(solution)/shard_map/ppermute | solution.py:29
  82.7 3.2 %collective-permute-done.9 = bf16[3,256,256]{2,1,0:T(8,128)(2,1)S(1)} collective-permute-done((bf16[3,256,256]{2,1,0:T(8,128)(2,1)}, bf16[3,256,256]{2,1,0:T(8,128)(2,1)S(1)}, u32[]{:S(2)}, u32[]{:S(2)}) %collective-permute-start.9) | collective-permute-done | bytes 393248 | tf_op jit(solution)/shard_map/ppermute | solution.py:22
  86.6 4.1 %collective-permute-done.19 = bf16[3,256,256]{2,1,0:T(8,128)(2,1)S(1)} collective-permute-done((bf16[3,256,256]{2,1,0:T(8,128)(2,1)S(1)}, bf16[3,256,256]{2,1,0:T(8,128)(2,1)S(1)}, u32[]{:S(2)}, u32[]{:S(2)}) %collective-permute-start.19) | collective-permute-done | bytes 393248 | tf_op jit(solution)/shard_map/ppermute | solution.py:23
  95.6 4.8 %collective-permute-done.17 = bf16[3,256,256]{2,1,0:T(8,128)(2,1)S(1)} collective-permute-done((bf16[3,256,256]{2,1,0:T(8,128)(2,1)S(1)}, bf16[3,256,256]{2,1,0:T(8,128)(2,1)S(1)}, u32[]{:S(2)}, u32[]{:S(2)}) %collective-permute-start.17) | collective-permute-done | bytes 393248 | tf_op jit(solution)/shard_map/ppermute | solution.py:22
  100.4 2.5 %collective-permute-start.18 = (bf16[3,256,256]{2,1,0:T(8,128)(2,1)S(1)}, bf16[3,256,256]{2,1,0:T(8,128)(2,1)S(1)}, u32[]{:S(2)}, u32[]{:S(2)}) collective-permute-start(bf16[3,256,256]{2,1,0:T(8,128)(2,1)S(1)} %broadcast_select_fusion.14), channel_id=1, source_target_pairs={{0,8},{8,16},{16,24},{24,0},{32,40},{40,48},{48,56},{56,32},{64,72... | collective-permute-start | bytes 1179656 | tf_op jit(solution)/shard_map/ppermute | solution.py:28
  104.5 3.8 %collective-permute-done.20 = bf16[3,256,256]{2,1,0:T(8,128)(2,1)S(1)} collective-permute-done((bf16[3,256,256]{2,1,0:T(8,128)(2,1)S(1)}, bf16[3,256,256]{2,1,0:T(8,128)(2,1)S(1)}, u32[]{:S(2)}, u32[]{:S(2)}) %collective-permute-start.20) | collective-permute-done | bytes 393248 | tf_op jit(solution)/shard_map/ppermute | solution.py:29
  108.4 2.3 broadcast_select_fusion
  112.0 3.4 %collective-permute-start.26 = (bf16[3,256,256]{2,1,0:T(8,128)(2,1)S(1)}, bf16[3,256,256]{2,1,0:T(8,128)(2,1)S(1)}, u32[]{:S(2)}, u32[]{:S(2)}) collective-permute-start(bf16[3,256,256]{2,1,0:T(8,128)(2,1)S(1)} %get-tuple-element.30), channel_id=1, source_target_pairs={{0,8},{8,16},{16,24},{24,0},{32,40},{40,48},{48,56},{56,32},{64,72... | collective-permute-start | bytes 1179656 | tf_op jit(solution)/shard_map/ppermute | solution.py:22
  118.4 5.2 %collective-permute-done.28 = bf16[3,256,256]{2,1,0:T(8,128)(2,1)S(1)} collective-permute-done((bf16[3,256,256]{2,1,0:T(8,128)(2,1)S(1)}, bf16[3,256,256]{2,1,0:T(8,128)(2,1)S(1)}, u32[]{:S(2)}, u32[]{:S(2)}) %collective-permute-start.28) | collective-permute-done | bytes 393248 | tf_op jit(solution)/shard_map/ppermute | solution.py:23
  124.7 3.2 %collective-permute-start.27 = (bf16[3,256,256]{2,1,0:T(8,128)(2,1)}, bf16[3,256,256]{2,1,0:T(8,128)(2,1)}, u32[]{:S(2)}, u32[]{:S(2)}) collective-permute-start(bf16[3,256,256]{2,1,0:T(8,128)(2,1)} %get-tuple-element.26), channel_id=1, source_target_pairs={{0,8},{8,16},{16,24},{24,0},{32,40},{40,48},{48,56},{56,32},{64,72... | collective-permute-start | bytes 1179656 | tf_op jit(solution)/shard_map/ppermute | solution.py:28
  129.3 4.5 %select_convert_fusion = bf16[8,256,256]{2,1,0:T(8,128)(2,1)} fusion(bf16[8,256,256]{2,1,0:T(8,128)(2,1)} %copy-done.1, bf16[8,12,256,256]{3,2,1,0:T(8,128)(2,1)} %front_ref.1, s32[]{:T(128)S(6)} %select_n.584, pred[8]{0:T(512)(128)(4,1)} %get-tuple-element.8, pred[8]{0:T(512)(128)(4,1)} %get-tuple-element.7, pred[8]{0:T(512)(128)(4,1)} %get-tuple-element.21, ...), kind=kOutput, calls=%fused_computation.5 | convolution fusion | flops 541065216 | bytes 4459520 | tf_op jit(solution)/shard_map/iab,bc->iac/dot_general | solution.py:90
  138.3 7.6 %collective-permute-done.36 = bf16[3,256,256]{2,1,0:T(8,128)(2,1)S(1)} collective-permute-done((bf16[3,256,256]{2,1,0:T(8,128)(2,1)}, bf16[3,256,256]{2,1,0:T(8,128)(2,1)S(1)}, u32[]{:S(2)}, u32[]{:S(2)}) %collective-permute-start.36) | collective-permute-done | bytes 393248 | tf_op jit(solution)/shard_map/ppermute | solution.py:23
  146.7 7.2 %collective-permute-done.32 = bf16[3,256,256]{2,1,0:T(8,128)(2,1)S(1)} collective-permute-done((bf16[3,256,256]{2,1,0:T(8,128)(2,1)S(1)}, bf16[3,256,256]{2,1,0:T(8,128)(2,1)S(1)}, u32[]{:S(2)}, u32[]{:S(2)}) %collective-permute-start.32) | collective-permute-done | bytes 393248 | tf_op jit(solution)/shard_map/ppermute | solution.py:23
  153.9 2.4 %broadcast_select_fusion.11 = (bf16[3,256,256]{2,1,0:T(8,128)(2,1)}, bf16[3,256,256]{2,1,0:T(8,128)(2,1)}, bf16[3,256,256]{2,1,0:T(8,128)(2,1)}, bf16[3,256,256]{2,1,0:T(8,128)(2,1)}) fusion(bf16[3,256,256]{2,1,0:T(8,128)(2,1)S(1)} %collective-permute-done.32, pred[]{:T(512)S(6)} %eq.192, bf16[3,256,256]{2,1,0:T(8,128)(2,1)S(1)} %collective-permute-done.26, ...), kind=kLoop, calls=%fused_computation.62 | loop fusion | flops 1179648 | bytes 5111812 | tf_op jit(solution)/shard_map/jit(_where)/select_n | solution.py:27
  156.4 3.2 %collective-permute-start.37 = (bf16[3,256,256]{2,1,0:T(8,128)(2,1)}, bf16[3,256,256]{2,1,0:T(8,128)(2,1)}, u32[]{:S(2)}, u32[]{:S(2)}) collective-permute-start(bf16[3,256,256]{2,1,0:T(8,128)(2,1)} %get-tuple-element.24), channel_id=1, source_target_pairs={{0,96},{8,104},{16,112},{24,120},{32,0},{40,8},{48,16},{56,24},{64... | collective-permute-start | bytes 1179656 | tf_op jit(solution)/shard_map/ppermute | solution.py:29
  161.9 6.5 %collective-permute-done.35 = bf16[3,256,256]{2,1,0:T(8,128)(2,1)S(1)} collective-permute-done((bf16[3,256,256]{2,1,0:T(8,128)(2,1)}, bf16[3,256,256]{2,1,0:T(8,128)(2,1)S(1)}, u32[]{:S(2)}, u32[]{:S(2)}) %collective-permute-start.35) | collective-permute-done | bytes 393248 | tf_op jit(solution)/shard_map/ppermute | solution.py:28
  172.2 2.3 collective-permute-start.33
  174.5 7.2 %collective-permute-done.40 = bf16[3,256,256]{2,1,0:T(8,128)(2,1)} collective-permute-done((bf16[3,256,256]{2,1,0:T(8,128)(2,1)S(1)}, bf16[3,256,256]{2,1,0:T(8,128)(2,1)}, u32[]{:S(2)}, u32[]{:S(2)}) %collective-permute-start.40) | collective-permute-done | bytes 393248 | tf_op jit(solution)/shard_map/ppermute | solution.py:23
  189.5 3.0 %collective-permute-done.38 = bf16[3,256,256]{2,1,0:T(8,128)(2,1)S(1)} collective-permute-done((bf16[3,256,256]{2,1,0:T(8,128)(2,1)S(1)}, bf16[3,256,256]{2,1,0:T(8,128)(2,1)S(1)}, u32[]{:S(2)}, u32[]{:S(2)}) %collective-permute-start.38) | collective-permute-done | bytes 393248 | tf_op jit(solution)/shard_map/ppermute | solution.py:22
  199.8 6.2 %collective-permute-done.39 = bf16[3,256,256]{2,1,0:T(8,128)(2,1)} collective-permute-done((bf16[3,256,256]{2,1,0:T(8,128)(2,1)}, bf16[3,256,256]{2,1,0:T(8,128)(2,1)}, u32[]{:S(2)}, u32[]{:S(2)}) %collective-permute-start.39) | collective-permute-done | bytes 393248 | tf_op jit(solution)/shard_map/ppermute | solution.py:28
  208.8 2.8 %fusion.9.l2_ref = bf16[8,256,256]{2,1,0:T(8,128)(2,1)} fusion(bf16[8,256,256]{2,1,0:T(8,128)(2,1)S(1)} %broadcast_select_fusion.1, bf16[8,256,256]{2,1,0:T(8,128)(2,1)} %collective-permute-done.23, bf16[8,256,256]{2,1,0:T(8,128)(2,1)} %collective-permute-done.22, bf16[4,256,256]{2,1,0:T(8,128)(2,1)S(1)} %collective-permute-done.25, ...), kind=kLoop, calls=%fused_computation.19 | loop fusion | flops 3145728 | bytes 5242884 | tf_op jit(solution)/shard_map/jit(_where)/select_n | solution.py:86
  211.6 16.7 %shard_map.46 = bf16[8,12,256,256]{3,2,1,0:T(8,128)(2,1)} custom-call(s32[8,12]{1,0:T(8,128)} %select_add_fusion.codes, bf16[8,12,256,256]{3,2,1,0:T(8,128)(2,1)} %front_ref.1, bf16[8,256,256]{2,1,0:T(8,128)(2,1)} %copy-done.1, bf16[8,256,256]{2,1,0:T(8,128)(2,1)} %fusion.9.l2_ref, bf16[12,256,256]{2,1,0:T(8,128)(2,1)} %copy-done, ...), custom_call_target="tpu_custom_call" | custom-call | tf_op jit(solution)/shard_map/pallas_call | solution.py:127
  (179 shorter events, 73.0 us)
Async XLA Ops:
  9.6 12.1 %collective-permute-start.7 = (bf16[3,256,256]{2,1,0:T(8,128)(2,1)S(1)}, bf16[3,256,256]{2,1,0:T(8,128)(2,1)S(1)}, u32[]{:S(2)}, u32[]{:S(2)}) collective-permute-start(bf16[3,256,256]{2,1,0:T(8,128)(2,1)S(1)} %slice.97), channel_id=1, source_target_pairs={{0,24},{8,0},{16,8},{24,16},{32,56},{40,32},{48,40},{56,48},{64,88... | collective-permute-start | bytes 1179656 | tf_op jit(solution)/shard_map/ppermute | solution.py:23
  21.8 10.1 %collective-permute-start.5 = (bf16[3,256,256]{2,1,0:T(8,128)(2,1)S(1)}, bf16[3,256,256]{2,1,0:T(8,128)(2,1)S(1)}, u32[]{:S(2)}, u32[]{:S(2)}) collective-permute-start(bf16[3,256,256]{2,1,0:T(8,128)(2,1)S(1)} %get-tuple-element.34), channel_id=1, source_target_pairs={{0,8},{8,16},{16,24},{24,0},{32,40},{40,48},{48,56},{56,32},{64,72... | collective-permute-start | bytes 1179656 | tf_op jit(solution)/shard_map/ppermute | solution.py:22
  24.8 22.2 %collective-permute-start = (bf16[8,256,256]{2,1,0:T(8,128)(2,1)}, bf16[8,256,256]{2,1,0:T(8,128)(2,1)}, u32[]{:S(2)}, u32[]{:S(2)}) collective-permute-start(bf16[8,256,256]{2,1,0:T(8,128)(2,1)} %select_convert_fusion.1), channel_id=1, source_target_pairs={{0,1},{1,0},{2,3},{3,2},{4,5},{5,4},{6,7},{7,6},{8,9},{9,8},{10,11... | collective-permute-start | bytes 3145736 | tf_op jit(solution)/shard_map/ppermute | solution.py:67
  24.8 12.7 %collective-permute-start.8 = (bf16[3,256,256]{2,1,0:T(8,128)(2,1)S(1)}, bf16[3,256,256]{2,1,0:T(8,128)(2,1)S(1)}, u32[]{:S(2)}, u32[]{:S(2)}) collective-permute-start(bf16[3,256,256]{2,1,0:T(8,128)(2,1)S(1)} %get-tuple-element.33), channel_id=1, source_target_pairs={{0,24},{8,0},{16,8},{24,16},{32,56},{40,32},{48,40},{56,48},{64,88... | collective-permute-start | bytes 1179656 | tf_op jit(solution)/shard_map/ppermute | solution.py:29
  48.4 24.6 %collective-permute-start.1 = (bf16[8,256,256]{2,1,0:T(8,128)(2,1)S(1)}, bf16[8,256,256]{2,1,0:T(8,128)(2,1)}, u32[]{:S(2)}, u32[]{:S(2)}) collective-permute-start(bf16[8,256,256]{2,1,0:T(8,128)(2,1)S(1)} %broadcast_select_fusion.3), channel_id=1, source_target_pairs={{0,2},{2,4},{4,6},{6,0},{1,7},{3,1},{5,3},{7,5},{8,10},{10,12},{12... | collective-permute-start | bytes 3145736 | tf_op jit(solution)/shard_map/ppermute | solution.py:69
  67.5 10.7 %collective-permute-start.16 = (bf16[3,256,256]{2,1,0:T(8,128)(2,1)}, bf16[3,256,256]{2,1,0:T(8,128)(2,1)}, u32[]{:S(2)}, u32[]{:S(2)}) collective-permute-start(bf16[3,256,256]{2,1,0:T(8,128)(2,1)} %get-tuple-element.35), channel_id=1, source_target_pairs={{0,96},{8,104},{16,112},{24,120},{32,0},{40,8},{48,16},{56,24},{64... | collective-permute-start | bytes 1179656 | tf_op jit(solution)/shard_map/ppermute | solution.py:29
  68.2 11.9 %collective-permute-start.14 = (bf16[3,256,256]{2,1,0:T(8,128)(2,1)}, bf16[3,256,256]{2,1,0:T(8,128)(2,1)}, u32[]{:S(2)}, u32[]{:S(2)}) collective-permute-start(bf16[3,256,256]{2,1,0:T(8,128)(2,1)} %get-tuple-element.36), channel_id=1, source_target_pairs={{0,32},{8,40},{16,48},{24,56},{32,64},{40,72},{48,80},{56,88},{64,... | collective-permute-start | bytes 1179656 | tf_op jit(solution)/shard_map/ppermute | solution.py:28
  70.9 24.3 %collective-permute-start.12 = (bf16[3,256,256]{2,1,0:T(8,128)(2,1)}, bf16[3,256,256]{2,1,0:T(8,128)(2,1)S(1)}, u32[]{:S(2)}, u32[]{:S(2)}) collective-permute-start(bf16[3,256,256]{2,1,0:T(8,128)(2,1)} %get-tuple-element.17), channel_id=1, source_target_pairs={{0,96},{8,104},{16,112},{24,120},{32,0},{40,8},{48,16},{56,24},{64... | collective-permute-start | bytes 1179656 | tf_op jit(solution)/shard_map/ppermute | solution.py:29
  72.9 13.0 %collective-permute-start.9 = (bf16[3,256,256]{2,1,0:T(8,128)(2,1)}, bf16[3,256,256]{2,1,0:T(8,128)(2,1)S(1)}, u32[]{:S(2)}, u32[]{:S(2)}) collective-permute-start(bf16[3,256,256]{2,1,0:T(8,128)(2,1)} %get-tuple-element.18), channel_id=1, source_target_pairs={{0,32},{8,40},{16,48},{24,56},{32,64},{40,72},{48,80},{56,88},{64,... | collective-permute-start | bytes 1179656 | tf_op jit(solution)/shard_map/ppermute | solution.py:22
  74.4 28.6 %collective-permute-start.2 = (bf16[8,256,256]{2,1,0:T(8,128)(2,1)S(1)}, bf16[8,256,256]{2,1,0:T(8,128)(2,1)S(1)}, u32[]{:S(2)}, u32[]{:S(2)}) collective-permute-start(bf16[8,256,256]{2,1,0:T(8,128)(2,1)S(1)} %broadcast_select_fusion.4), channel_id=1, source_target_pairs={{0,1},{1,0},{2,3},{3,2},{4,5},{5,4},{6,7},{7,6},{8,9},{9,8},{10,11... | collective-permute-start | bytes 3145736 | tf_op jit(solution)/shard_map/ppermute | solution.py:72
  81.4 13.7 %collective-permute-start.3 = (bf16[4,256,256]{2,1,0:T(8,128)(2,1)S(1)}, bf16[4,256,256]{2,1,0:T(8,128)(2,1)S(1)}, u32[]{:S(2)}, u32[]{:S(2)}) collective-permute-start(bf16[4,256,256]{2,1,0:T(8,128)(2,1)S(1)} %slice_select_fusion.1), channel_id=1, source_target_pairs={{0,2},{2,4},{4,6},{6,0},{1,7},{3,1},{5,3},{7,5},{8,10},{10,12},{12... | collective-permute-start | bytes 1572872 | tf_op jit(solution)/shard_map/ppermute | solution.py:75
  95.5 12.8 %collective-permute-start.20 = (bf16[3,256,256]{2,1,0:T(8,128)(2,1)S(1)}, bf16[3,256,256]{2,1,0:T(8,128)(2,1)S(1)}, u32[]{:S(2)}, u32[]{:S(2)}) collective-permute-start(bf16[3,256,256]{2,1,0:T(8,128)(2,1)S(1)} %get-tuple-element.19), channel_id=1, source_target_pairs={{0,24},{8,0},{16,8},{24,16},{32,56},{40,32},{48,40},{56,48},{64,88... | collective-permute-start | bytes 1179656 | tf_op jit(solution)/shard_map/ppermute | solution.py:29
  111.7 11.9 %collective-permute-start.28 = (bf16[3,256,256]{2,1,0:T(8,128)(2,1)S(1)}, bf16[3,256,256]{2,1,0:T(8,128)(2,1)S(1)}, u32[]{:S(2)}, u32[]{:S(2)}) collective-permute-start(bf16[3,256,256]{2,1,0:T(8,128)(2,1)S(1)} %get-tuple-element.27), channel_id=1, source_target_pairs={{0,24},{8,0},{16,8},{24,16},{32,56},{40,32},{48,40},{56,48},{64,88... | collective-permute-start | bytes 1179656 | tf_op jit(solution)/shard_map/ppermute | solution.py:23
  112.0 11.7 %collective-permute-start.26 = (bf16[3,256,256]{2,1,0:T(8,128)(2,1)S(1)}, bf16[3,256,256]{2,1,0:T(8,128)(2,1)S(1)}, u32[]{:S(2)}, u32[]{:S(2)}) collective-permute-start(bf16[3,256,256]{2,1,0:T(8,128)(2,1)S(1)} %get-tuple-element.30), channel_id=1, source_target_pairs={{0,8},{8,16},{16,24},{24,0},{32,40},{40,48},{48,56},{56,32},{64,72... | collective-permute-start | bytes 1179656 | tf_op jit(solution)/shard_map/ppermute | solution.py:22
  124.7 11.2 %collective-permute-start.29 = (bf16[3,256,256]{2,1,0:T(8,128)(2,1)}, bf16[3,256,256]{2,1,0:T(8,128)(2,1)}, u32[]{:S(2)}, u32[]{:S(2)}) collective-permute-start(bf16[3,256,256]{2,1,0:T(8,128)(2,1)} %get-tuple-element.25), channel_id=1, source_target_pairs={{0,24},{8,0},{16,8},{24,16},{32,56},{40,32},{48,40},{56,48},{64,88... | collective-permute-start | bytes 1179656 | tf_op jit(solution)/shard_map/ppermute | solution.py:29
  124.7 11.2 %collective-permute-start.27 = (bf16[3,256,256]{2,1,0:T(8,128)(2,1)}, bf16[3,256,256]{2,1,0:T(8,128)(2,1)}, u32[]{:S(2)}, u32[]{:S(2)}) collective-permute-start(bf16[3,256,256]{2,1,0:T(8,128)(2,1)} %get-tuple-element.26), channel_id=1, source_target_pairs={{0,8},{8,16},{16,24},{24,0},{32,40},{40,48},{48,56},{56,32},{64,72... | collective-permute-start | bytes 1179656 | tf_op jit(solution)/shard_map/ppermute | solution.py:28
  133.7 25.9 %collective-permute-start.21 = (bf16[8,256,256]{2,1,0:T(8,128)(2,1)}, bf16[8,256,256]{2,1,0:T(8,128)(2,1)}, u32[]{:S(2)}, u32[]{:S(2)}) collective-permute-start(bf16[8,256,256]{2,1,0:T(8,128)(2,1)} %select_convert_fusion), channel_id=1, source_target_pairs={{0,1},{1,0},{2,3},{3,2},{4,5},{5,4},{6,7},{7,6},{8,9},{9,8},{10,11... | collective-permute-start | bytes 3145736 | tf_op jit(solution)/shard_map/ppermute | solution.py:67
  133.7 12.2 %collective-permute-start.36 = (bf16[3,256,256]{2,1,0:T(8,128)(2,1)}, bf16[3,256,256]{2,1,0:T(8,128)(2,1)S(1)}, u32[]{:S(2)}, u32[]{:S(2)}) collective-permute-start(bf16[3,256,256]{2,1,0:T(8,128)(2,1)} %get-tuple-element.28), channel_id=1, source_target_pairs={{0,96},{8,104},{16,112},{24,120},{32,0},{40,8},{48,16},{56,24},{64... | collective-permute-start | bytes 1179656 | tf_op jit(solution)/shard_map/ppermute | solution.py:23
  133.8 12.9 %collective-permute-start.34 = (bf16[3,256,256]{2,1,0:T(8,128)(2,1)}, bf16[3,256,256]{2,1,0:T(8,128)(2,1)S(1)}, u32[]{:S(2)}, u32[]{:S(2)}) collective-permute-start(bf16[3,256,256]{2,1,0:T(8,128)(2,1)} %get-tuple-element.29), channel_id=1, source_target_pairs={{0,32},{8,40},{16,48},{24,56},{32,64},{40,72},{48,80},{56,88},{64,... | collective-permute-start | bytes 1179656 | tf_op jit(solution)/shard_map/ppermute | solution.py:22
  136.9 17.0 %collective-permute-start.32 = (bf16[3,256,256]{2,1,0:T(8,128)(2,1)S(1)}, bf16[3,256,256]{2,1,0:T(8,128)(2,1)S(1)}, u32[]{:S(2)}, u32[]{:S(2)}) collective-permute-start(bf16[3,256,256]{2,1,0:T(8,128)(2,1)S(1)} %select_select_fusion.6), channel_id=1, source_target_pairs={{0,96},{8,104},{16,112},{24,120},{32,0},{40,8},{48,16},{56,24},{64... | collective-permute-start | bytes 1179656 | tf_op jit(solution)/shard_map/ppermute | solution.py:23
  156.3 12.2 %collective-permute-start.35 = (bf16[3,256,256]{2,1,0:T(8,128)(2,1)}, bf16[3,256,256]{2,1,0:T(8,128)(2,1)S(1)}, u32[]{:S(2)}, u32[]{:S(2)}) collective-permute-start(bf16[3,256,256]{2,1,0:T(8,128)(2,1)} %get-tuple-element.23), channel_id=1, source_target_pairs={{0,32},{8,40},{16,48},{24,56},{32,64},{40,72},{48,80},{56,88},{64,... | collective-permute-start | bytes 1179656 | tf_op jit(solution)/shard_map/ppermute | solution.py:28
  156.4 12.8 %collective-permute-start.37 = (bf16[3,256,256]{2,1,0:T(8,128)(2,1)}, bf16[3,256,256]{2,1,0:T(8,128)(2,1)}, u32[]{:S(2)}, u32[]{:S(2)}) collective-permute-start(bf16[3,256,256]{2,1,0:T(8,128)(2,1)} %get-tuple-element.24), channel_id=1, source_target_pairs={{0,96},{8,104},{16,112},{24,120},{32,0},{40,8},{48,16},{56,24},{64... | collective-permute-start | bytes 1179656 | tf_op jit(solution)/shard_map/ppermute | solution.py:29
  161.0 23.3 %collective-permute-start.22 = (bf16[8,256,256]{2,1,0:T(8,128)(2,1)S(1)}, bf16[8,256,256]{2,1,0:T(8,128)(2,1)}, u32[]{:S(2)}, u32[]{:S(2)}) collective-permute-start(bf16[8,256,256]{2,1,0:T(8,128)(2,1)S(1)} %broadcast_select_fusion.1), channel_id=1, source_target_pairs={{0,2},{2,4},{4,6},{6,0},{1,7},{3,1},{5,3},{7,5},{8,10},{10,12},{12... | collective-permute-start | bytes 3145736 | tf_op jit(solution)/shard_map/ppermute | solution.py:69
  170.4 11.3 %collective-permute-start.40 = (bf16[3,256,256]{2,1,0:T(8,128)(2,1)S(1)}, bf16[3,256,256]{2,1,0:T(8,128)(2,1)}, u32[]{:S(2)}, u32[]{:S(2)}) collective-permute-start(bf16[3,256,256]{2,1,0:T(8,128)(2,1)S(1)} %select_select_fusion.2), channel_id=1, source_target_pairs={{0,24},{8,0},{16,8},{24,16},{32,56},{40,32},{48,40},{56,48},{64,88... | collective-permute-start | bytes 1179656 | tf_op jit(solution)/shard_map/ppermute | solution.py:23
  172.2 21.9 %collective-permute-start.33 = (bf16[3,256,256]{2,1,0:T(8,128)(2,1)}, bf16[3,256,256]{2,1,0:T(8,128)(2,1)S(1)}, u32[]{:S(2)}, u32[]{:S(2)}) collective-permute-start(bf16[3,256,256]{2,1,0:T(8,128)(2,1)} %get-tuple-element.9), channel_id=1, source_target_pairs={{0,96},{8,104},{16,112},{24,120},{32,0},{40,8},{48,16},{56,24},{64... | collective-permute-start | bytes 1179656 | tf_op jit(solution)/shard_map/ppermute | solution.py:29
  174.5 12.7 %collective-permute-start.30 = (bf16[3,256,256]{2,1,0:T(8,128)(2,1)}, bf16[3,256,256]{2,1,0:T(8,128)(2,1)S(1)}, u32[]{:S(2)}, u32[]{:S(2)}) collective-permute-start(bf16[3,256,256]{2,1,0:T(8,128)(2,1)} %get-tuple-element.10), channel_id=1, source_target_pairs={{0,32},{8,40},{16,48},{24,56},{32,64},{40,72},{48,80},{56,88},{64,... | collective-permute-start | bytes 1179656 | tf_op jit(solution)/shard_map/ppermute | solution.py:22
  186.4 10.9 %collective-permute-start.24 = (bf16[4,256,256]{2,1,0:T(8,128)(2,1)}, bf16[4,256,256]{2,1,0:T(8,128)(2,1)}, u32[]{:S(2)}, u32[]{:S(2)}) collective-permute-start(bf16[4,256,256]{2,1,0:T(8,128)(2,1)} %slice_select_fusion), channel_id=1, source_target_pairs={{0,2},{2,4},{4,6},{6,0},{1,7},{3,1},{5,3},{7,5},{8,10},{10,12},{12... | collective-permute-start | bytes 1572872 | tf_op jit(solution)/shard_map/ppermute | solution.py:75
  188.1 10.3 %collective-permute-start.31 = (bf16[3,256,256]{2,1,0:T(8,128)(2,1)}, bf16[3,256,256]{2,1,0:T(8,128)(2,1)}, u32[]{:S(2)}, u32[]{:S(2)}) collective-permute-start(bf16[3,256,256]{2,1,0:T(8,128)(2,1)} %broadcast_select_fusion.12), channel_id=1, source_target_pairs={{0,32},{8,40},{16,48},{24,56},{32,64},{40,72},{48,80},{56,88},{64,... | collective-permute-start | bytes 1179656 | tf_op jit(solution)/shard_map/ppermute | solution.py:28
  188.1 11.7 %collective-permute-start.41 = (bf16[3,256,256]{2,1,0:T(8,128)(2,1)}, bf16[3,256,256]{2,1,0:T(8,128)(2,1)}, u32[]{:S(2)}, u32[]{:S(2)}) collective-permute-start(bf16[3,256,256]{2,1,0:T(8,128)(2,1)} %get-tuple-element.11), channel_id=1, source_target_pairs={{0,24},{8,0},{16,8},{24,16},{32,56},{40,32},{48,40},{56,48},{64,88... | collective-permute-start | bytes 1179656 | tf_op jit(solution)/shard_map/ppermute | solution.py:29
  192.6 16.3 %collective-permute-start.23 = (bf16[8,256,256]{2,1,0:T(8,128)(2,1)S(1)}, bf16[8,256,256]{2,1,0:T(8,128)(2,1)}, u32[]{:S(2)}, u32[]{:S(2)}) collective-permute-start(bf16[8,256,256]{2,1,0:T(8,128)(2,1)S(1)} %broadcast_select_fusion.2), channel_id=1, source_target_pairs={{0,1},{1,0},{2,3},{3,2},{4,5},{5,4},{6,7},{7,6},{8,9},{9,8},{10,11... | collective-permute-start | bytes 3145736 | tf_op jit(solution)/shard_map/ppermute | solution.py:72
  194.9 11.1 %collective-permute-start.39 = (bf16[3,256,256]{2,1,0:T(8,128)(2,1)}, bf16[3,256,256]{2,1,0:T(8,128)(2,1)}, u32[]{:S(2)}, u32[]{:S(2)}) collective-permute-start(bf16[3,256,256]{2,1,0:T(8,128)(2,1)} %broadcast_select_fusion.6), channel_id=1, source_target_pairs={{0,8},{8,16},{16,24},{24,0},{32,40},{40,48},{48,56},{56,32},{64,72... | collective-permute-start | bytes 1179656 | tf_op jit(solution)/shard_map/ppermute | solution.py:28
  197.4 11.5 %collective-permute-start.25 = (bf16[4,256,256]{2,1,0:T(8,128)(2,1)}, bf16[4,256,256]{2,1,0:T(8,128)(2,1)S(1)}, u32[]{:S(2)}, u32[]{:S(2)}) collective-permute-start(bf16[4,256,256]{2,1,0:T(8,128)(2,1)} %collective-permute-done.24), channel_id=1, source_target_pairs={{0,1},{1,0},{2,3},{3,2},{4,5},{5,4},{6,7},{7,6},{8,9},{9,8},{10,11... | collective-permute-start | bytes 1572872 | tf_op jit(solution)/shard_map/ppermute | solution.py:76
  (46 other events, 381.3 us)

commit v3 on v2

--- a/solution.py
+++ b/solution.py
@@ -9,27 +9,31 @@
 CORES = 2
 
 
+def per_part(cond, a, b):
+    return jnp.where(cond.reshape((-1,) + (1,) * (a.ndim - 1)), a, b)
+
+
 def pick(index, options):
     out = options[-1]
     for k in range(len(options) - 2, -1, -1):
-        out = jnp.where(index == k, options[k], out)
+        out = per_part(index == k, options[k], out)
     return out
 
 
 def ring_bcast(value, axis, plus, minus, me, root):
-    half = value.shape[0] // 2
-    first, second = value[:half], value[half:]
+    half = value.shape[1] // 2
+    first, second = value[:, :half], value[:, half:]
     got_plus = lax.ppermute(first, axis, plus)
     got_minus = lax.ppermute(second, axis, minus)
     dist = (me - root) % RING
     at_root = dist == 0
-    send_plus = jnp.where(at_root, second, got_plus)
-    send_minus = jnp.where(at_root, first, got_minus)
+    send_plus = per_part(at_root, second, got_plus)
+    send_minus = per_part(at_root, first, got_minus)
     got_plus2 = lax.ppermute(send_plus, axis, plus)
     got_minus2 = lax.ppermute(send_minus, axis, minus)
     out_first = pick(dist, [first, got_plus, got_plus2, got_minus2])
     out_second = pick(dist, [second, got_plus2, got_minus2, got_minus])
-    return jnp.concatenate([out_first, out_second], axis=0)
+    return jnp.concatenate([out_first, out_second], axis=1)
 
 
 def row_pairs(step_z, step_x):
@@ -46,14 +50,14 @@
     rz, rx = root // RING, root % RING
     xp, xm = row_pairs(0, 1), row_pairs(0, RING - 1)
     zp, zm = row_pairs(1, 0), row_pairs(RING - 1, 0)
-    half = value.shape[0] // 2
-    along_x = value[:half]
-    along_z = value[half:]
+    half = value.shape[1] // 2
+    along_x = value[:, :half]
+    along_z = value[:, half:]
     along_x = ring_bcast(along_x, "row", xp, xm, mx, rx)
     along_z = ring_bcast(along_z, "row", zp, zm, mz, rz)
     along_x = ring_bcast(along_x, "row", zp, zm, mz, rz)
     along_z = ring_bcast(along_z, "row", xp, xm, mx, rx)
-    return jnp.concatenate([along_x, along_z], axis=0)
+    return jnp.concatenate([along_x, along_z], axis=1)
 
 
 def col_bcast(value, root):
@@ -65,25 +69,25 @@
         (CORES * y + 1, CORES * ((y - 1) % RING) + 1) for y in range(RING)
     ]
     got_swap = lax.ppermute(value, "col", swap)
-    on_root_chip = jnp.where(me == root, value, got_swap)
+    on_root_chip = per_part(me == root, value, got_swap)
     got_hop = lax.ppermute(on_root_chip, "col", hop)
     dist = (my - ry) % RING
-    near = jnp.where(dist == 0, on_root_chip, got_hop)
+    near = per_part(dist == 0, on_root_chip, got_hop)
     got_swap2 = lax.ppermute(near, "col", swap)
-    half = value.shape[0] // 2
-    fwd = jnp.where(mk == 0, near[:half], near[half:])
+    half = value.shape[1] // 2
+    fwd = jnp.where(mk == 0, near[:, :half], near[:, half:])
     got_fwd = lax.ppermute(fwd, "col", hop)
     got_swap3 = lax.ppermute(got_fwd, "col", swap)
     far = jnp.where(
         mk == 0,
-        jnp.concatenate([got_fwd, got_swap3], axis=0),
-        jnp.concatenate([got_swap3, got_fwd], axis=0),
+        jnp.concatenate([got_fwd, got_swap3], axis=1),
+        jnp.concatenate([got_swap3, got_fwd], axis=1),
     )
     own_hop = (dist == 1) & (mk == 0) | (dist == 3) & (mk == 1)
     other_hop = (dist == 1) & (mk == 1) | (dist == 3) & (mk == 0)
-    out = jnp.where(own_hop, got_hop, far)
-    out = jnp.where(other_hop, got_swap2, out)
-    return jnp.where(dist == 0, on_root_chip, out)
+    out = per_part(own_hop, got_hop, far)
+    out = per_part(other_hop, got_swap2, out)
+    return per_part(dist == 0, on_root_chip, out)
 
 
 def lower_local(column, inverse, rows_ok):
@@ -161,47 +165,63 @@
     rows_second = rows_first & (front_rows != second)
     cols_second = cols_first & (front_cols != second)
 
-    b1 = first // ncol
-    column_first = masked(
-        lax.dynamic_index_in_dim(front, b1, 1, keepdims=False),
-        lax.dynamic_index_in_dim(local, b1, 1, keepdims=False),
-    )
-    lower_first = col_bcast(lower_local(column_first, pivot_inv[0], rows_first), first % ncol)
-    a1 = first // nrow
-    first_row = masked(
-        lax.dynamic_index_in_dim(front, a1, 0, keepdims=False),
-        lax.dynamic_index_in_dim(local, a1, 0, keepdims=False),
-    )
-    upper_first = row_bcast(first_row, first % nrow)
-
-    a2 = second // nrow
-    local_row = lax.dynamic_slice_in_dim(local, a2, 1, 0)
-    row_before = masked(lax.dynamic_slice_in_dim(front, a2, 1, 0), local_row)
+    a1, b1 = first // nrow, first // ncol
+    a2, b2 = second // nrow, second // ncol
+    r1, c1 = first % nrow, first % ncol
+    r2, c2 = second % nrow, second % ncol
+
+    def local_row(a):
+        return masked(
+            lax.dynamic_index_in_dim(front, a, 0, keepdims=False),
+            lax.dynamic_index_in_dim(local, a, 0, keepdims=False),
+        )
+
+    def local_col(b):
+        return masked(
+            lax.dynamic_index_in_dim(front, b, 1, keepdims=False),
+            lax.dynamic_index_in_dim(local, b, 1, keepdims=False),
+        )
+
+    lower_first = lower_local(local_col(b1), pivot_inv[0], rows_first)
+    cols_sent = col_bcast(jnp.stack([lower_first, local_col(b2)]), jnp.stack([c1, c2]))
+    rows_sent = row_bcast(jnp.stack([local_row(a1), local_row(a2)]), jnp.stack([r1, r2]))
+    lower_first, second_col = cols_sent[0], cols_sent[1]
+    upper_first, second_row = rows_sent[0], rows_sent[1]
+
+    def one_block(a, b, r, c):
+        block = masked(front[a, b], local[a, b])
+        owner = (row_index == r) & (col_index == c)
+        return jnp.where(owner, block, jnp.zeros_like(block))
+
+    cross = lax.psum(
+        jnp.stack([one_block(a1, b2, r1, c2), one_block(a2, b1, r2, c1)]), ("row", "col")
+    )
+    first_at_second, second_at_first = cross[0], cross[1]
+
+    second_ok = (second != first)[None]
+    lower_first_at_second = lower_local(second_at_first[None], pivot_inv[0], second_ok)
     row_after = eliminate(
-        row_before,
-        lax.dynamic_slice_in_dim(lower_first, a2, 1, 0),
+        second_row[None],
+        lower_first_at_second,
         upper_first,
         first,
-        lax.dynamic_slice_in_dim(rows_first, a2, 1, 0),
+        second_ok,
         cols_first,
-        local_row,
+        pattern[second][front_cols][None],
         front_cols,
     )
-    upper_second = row_bcast(row_after[0], second % nrow)
-    b2 = second // ncol
-    local_col = lax.dynamic_slice_in_dim(local, b2, 1, 1)
-    col_before = masked(lax.dynamic_slice_in_dim(front, b2, 1, 1), local_col)
+    upper_second = row_after[0]
     col_after = eliminate(
-        col_before,
+        second_col[:, None],
         lower_first,
-        lax.dynamic_slice_in_dim(upper_first, b2, 1, 0),
+        first_at_second[None],
         first,
         rows_first,
-        lax.dynamic_slice_in_dim(cols_first, b2, 1, 0),
-        local_col,
-        lax.dynamic_slice_in_dim(front_cols, b2, 1, 0),
-    )
-    lower_second = col_bcast(lower_local(col_after[:, 0], pivot_inv[1], rows_second), second % ncol)
+        second_ok,
+        pattern[front_rows, second][:, None],
+        second[None],
+    )
+    lower_second = lower_local(col_after[:, 0], pivot_inv[1], rows_second)
 
     keep = local > 0
     update_first = rows_first[:, None] & cols_first[None, :] & keep

time: 232 us -> 312 us (1.34)
  waiting for transfers between devices: 98.4 us -> 164 us
  between operations: 6.91 us -> 25.6 us
  starting transfers between devices: 46.4 us -> 28.9 us
  other arithmetic: 41.1 us -> 53.7 us
    psum x0 -> x1, waiting for transfers between devices: none -> 63 us  [body(): lax.psum(jnp.stack([one_block(a1, b2, r1, c2), one_block(a2, b1, r2, c1)]...]
    ppermute x8 -> x4, waiting for transfers between devices: 46.7 us -> 25.8 us  [ring_bcast(): got_minus = lax.ppermute(second, axis, minus)]
    ppermute x8 -> x4, waiting for transfers between devices: 20.6 us -> 40.8 us  [ring_bcast(): got_plus = lax.ppermute(first, axis, plus)]
    select_n x28 -> x15, other arithmetic: 28.5 us -> 38.7 us  [the longest x12 37.4 us: per_part(): return jnp.where(cond.reshape((-1,) + (1,) * (a.ndim - 1)), a, b)]
    ppermute x8 -> x4, waiting for transfers between devices: 20.2 us -> 30 us  [ring_bcast(): got_plus2 = lax.ppermute(send_plus, axis, plus)]
    ppermute x8 -> x4, starting transfers between devices: 11 us -> 3.66 us  [ring_bcast(): got_plus2 = lax.ppermute(send_plus, axis, plus)]
    ppermute x8 -> x4, waiting for transfers between devices: 10.9 us -> 4.88 us  [ring_bcast(): got_minus2 = lax.ppermute(send_minus, axis, minus)]
    ppermute x8 -> x4, starting transfers between devices: 8.29 us -> 4.31 us  [ring_bcast(): got_plus = lax.ppermute(first, axis, plus)]
  transfers between devices with their start and end apart: 42 -> 22, of which waited for: 22 -> 12; matrix products, arithmetic and copies ran while one was open for 20% -> 18% of each run, Pallas kernels for 0% -> 0%
where the time goes in v3:
time: 312 us; the launch traced here: 308 us
  waiting for transfers between devices  164 us (53%)
  other arithmetic  53.7 us (17%)
  starting transfers between devices  28.9 us (9%)
  between operations  25.6 us (8%)
  Pallas kernels  16.7 us (5%)
  local copies, waits for them, and re-layouts  9.59 us (3%)
  matrix products  9.07 us (3%)
    psum x1, waiting for transfers between devices, body(): lax.psum(jnp.stack([one_block(a1, b2, r1, c2), one_block(a2, b1, r2, c1)]...  63 us
    ppermute x4, waiting for transfers between devices, ring_bcast(): got_plus = lax.ppermute(first, axis, plus)  40.8 us
    select_n x12, other arithmetic, per_part(): return jnp.where(cond.reshape((-1,) + (1,) * (a.ndim - 1)), a, b)  37.4 us
    ppermute x4, waiting for transfers between devices, ring_bcast(): got_plus2 = lax.ppermute(send_plus, axis, plus)  30 us
    ppermute x4, waiting for transfers between devices, ring_bcast(): got_minus = lax.ppermute(second, axis, minus)  25.8 us
    pallas_call x1, Pallas kernels, both_updates(): pl.pallas_call(update_kernel, grid_spec=pltpu.PrefetchScalarGridSpec(num_...  16.7 us
    ppermute x4, starting transfers between devices, ring_bcast(): got_minus = lax.ppermute(second, axis, minus)  8.91 us
    ppermute x4, starting transfers between devices, ring_bcast(): got_minus2 = lax.ppermute(send_minus, axis, minus)  7.96 us
  transfers between devices with their start and end apart: 22, of which 12 were waited for; matrix products, arithmetic and copies ran while one was open for 18% of the time, Pallas kernels for 0%

profile of v3, /device:TPU:6, one launch (start us, length us, event | category | flops | bytes accessed | tf_op | source)
XLA Modules:
  0.0 308.0 jit_solution(9485332715735135968)
XLA Ops:
  14.7 2.2 dynamic-slice_select_fusion.1
  25.7 12.9 %collective-permute-done.7 = bf16[2,3,256,256]{3,2,1,0:T(8,128)(2,1)} collective-permute-done((bf16[2,3,256,256]{3,2,1,0:T(8,128)(2,1)}, bf16[2,3,256,256]{3,2,1,0:T(8,128)(2,1)}, u32[]{:S(2)}, u32[]{:S(2)}) %collective-permute-start.7) | collective-permute-done | bytes 786464 | tf_op jit(solution)/shard_map/ppermute | solution.py:27
  38.6 2.5 broadcast_select_fusion.4
  42.7 2.0 collective-permute-start.8
  44.7 14.9 %collective-permute-done.5 = bf16[2,3,256,256]{3,2,1,0:T(8,128)(2,1)S(1)} collective-permute-done((bf16[2,3,256,256]{3,2,1,0:T(8,128)(2,1)S(1)}, bf16[2,3,256,256]{3,2,1,0:T(8,128)(2,1)S(1)}, u32[]{:S(2)}, u32[]{:S(2)}) %collective-permute-start.5) | collective-permute-done | bytes 786464 | tf_op jit(solution)/shard_map/ppermute | solution.py:26
  62.2 4.0 %collective-permute-start.15 = (bf16[2,3,256,256]{3,2,1,0:T(8,128)(2,1)}, bf16[2,3,256,256]{3,2,1,0:T(8,128)(2,1)}, u32[]{:S(2)}, u32[]{:S(2)}) collective-permute-start(bf16[2,3,256,256]{3,2,1,0:T(8,128)(2,1)} %get-tuple-element.34), channel_id=1, source_target_pairs={{0,96},{8,104},{16,112},{24,120},{32,0},{40,8},{48,16},{56,24},{64... | collective-permute-start | bytes 2359304 | tf_op jit(solution)/shard_map/ppermute | solution.py:27
  66.3 12.4 %collective-permute-done.6 = bf16[2,3,256,256]{3,2,1,0:T(8,128)(2,1)} collective-permute-done((bf16[2,3,256,256]{3,2,1,0:T(8,128)(2,1)}, bf16[2,3,256,256]{3,2,1,0:T(8,128)(2,1)}, u32[]{:S(2)}, u32[]{:S(2)}) %collective-permute-start.6) | collective-permute-done | bytes 786464 | tf_op jit(solution)/shard_map/ppermute | solution.py:32
  78.7 2.8 select_select_fusion.6
  81.4 4.0 %collective-permute-start.11 = (bf16[2,3,256,256]{3,2,1,0:T(8,128)(2,1)}, bf16[2,3,256,256]{3,2,1,0:T(8,128)(2,1)}, u32[]{:S(2)}, u32[]{:S(2)}) collective-permute-start(bf16[2,3,256,256]{3,2,1,0:T(8,128)(2,1)} %select_select_fusion.6), channel_id=1, source_target_pairs={{0,96},{8,104},{16,112},{24,120},{32,0},{40,8},{48,16},{56,24},{64... | collective-permute-start | bytes 2359304 | tf_op jit(solution)/shard_map/ppermute | solution.py:27
  85.6 3.9 %broadcast_select_fusion = bf16[2,8,256,256]{3,2,1,0:T(8,128)(2,1)} fusion(bf16[2,8,256,256]{3,2,1,0:T(8,128)(2,1)} %collective-permute-done, pred[2]{0:T(512)(128)(4,1)S(1)} %broadcast_compare_fusion.2, bf16[1,8,256,256]{3,2,1,0:T(8,128)(2,1)} %copy-done, bf16[1,8,256,256]{3,2,1,0:T(8,128)(2,1)} %copy-done.2), kind=kLoop, calls=%fused_computation.21 | loop fusion | flops 2097152 | bytes 6291458 | tf_op jit(solution)/shard_map/jit(_where)/select_n | solution.py:13
  92.3 7.7 %collective-permute-done.11 = bf16[2,3,256,256]{3,2,1,0:T(8,128)(2,1)} collective-permute-done((bf16[2,3,256,256]{3,2,1,0:T(8,128)(2,1)}, bf16[2,3,256,256]{3,2,1,0:T(8,128)(2,1)}, u32[]{:S(2)}, u32[]{:S(2)}) %collective-permute-start.11) | collective-permute-done | bytes 786464 | tf_op jit(solution)/shard_map/ppermute | solution.py:27
  100.0 3.8 %broadcast_select_fusion.8 = (bf16[2,3,256,256]{3,2,1,0:T(8,128)(2,1)}, bf16[2,3,256,256]{3,2,1,0:T(8,128)(2,1)}, bf16[2,3,256,256]{3,2,1,0:T(8,128)(2,1)}, bf16[2,3,256,256]{3,2,1,0:T(8,128)(2,1)}) fusion(bf16[2,3,256,256]{3,2,1,0:T(8,128)(2,1)} %collective-permute-done.11, pred[2]{0:T(512)(128)(4,1)S(1)} %get-tuple-element.50, ...), kind=kLoop, calls=%fused_computation.62 | loop fusion | flops 2359296 | bytes 11010056 | tf_op jit(solution)/shard_map/jit(_where)/select_n | solution.py:13
  113.1 13.2 %collective-permute-done.9 = bf16[2,3,256,256]{3,2,1,0:T(8,128)(2,1)} collective-permute-done((bf16[2,3,256,256]{3,2,1,0:T(8,128)(2,1)}, bf16[2,3,256,256]{3,2,1,0:T(8,128)(2,1)}, u32[]{:S(2)}, u32[]{:S(2)}) %collective-permute-start.9) | collective-permute-done | bytes 786464 | tf_op jit(solution)/shard_map/ppermute | solution.py:26
  126.3 12.8 %collective-permute-done.13 = bf16[2,3,256,256]{3,2,1,0:T(8,128)(2,1)} collective-permute-done((bf16[2,3,256,256]{3,2,1,0:T(8,128)(2,1)}, bf16[2,3,256,256]{3,2,1,0:T(8,128)(2,1)}, u32[]{:S(2)}, u32[]{:S(2)}) %collective-permute-start.13) | collective-permute-done | bytes 786464 | tf_op jit(solution)/shard_map/ppermute | solution.py:26
  139.1 3.1 %broadcast_select_fusion.9 = (bf16[2,3,256,256]{3,2,1,0:T(8,128)(2,1)}, bf16[2,3,256,256]{3,2,1,0:T(8,128)(2,1)}) fusion(bf16[2,3,256,256]{3,2,1,0:T(8,128)(2,1)} %select_select_fusion.6, bf16[2,3,256,256]{3,2,1,0:T(8,128)(2,1)} %collective-permute-done.9, pred[2]{0:T(512)(128)(4,1)S(1)} %get-tuple-element.50, bf16[2,3,256,256]{3,2,1,0:T(8,128)(2,1)S(1)} %copy-done.6, ...), kind=kLoop, calls=%fused_computation.63 | loop fusion | flops 786432 | bytes 4718594 | tf_op jit(solution)/shard_map/jit(_where)/select_n | solution.py:13
  145.4 3.3 %collective-permute-start.12 = (bf16[2,3,256,256]{3,2,1,0:T(8,128)(2,1)}, bf16[2,3,256,256]{3,2,1,0:T(8,128)(2,1)}, u32[]{:S(2)}, u32[]{:S(2)}) collective-permute-start(bf16[2,3,256,256]{3,2,1,0:T(8,128)(2,1)} %get-tuple-element.13), channel_id=1, source_target_pairs={{0,96},{8,104},{16,112},{24,120},{32,0},{40,8},{48,16},{56,24},{64... | collective-permute-start | bytes 2359304 | tf_op jit(solution)/shard_map/ppermute | solution.py:33
  148.7 2.6 broadcast_select_fusion.1
  154.2 10.2 %collective-permute-done.14 = bf16[2,3,256,256]{3,2,1,0:T(8,128)(2,1)} collective-permute-done((bf16[2,3,256,256]{3,2,1,0:T(8,128)(2,1)}, bf16[2,3,256,256]{3,2,1,0:T(8,128)(2,1)}, u32[]{:S(2)}, u32[]{:S(2)}) %collective-permute-start.14) | collective-permute-done | bytes 786464 | tf_op jit(solution)/shard_map/ppermute | solution.py:32
  164.4 2.8 select_select_fusion.2
  170.5 5.3 %collective-permute-done.10 = bf16[2,3,256,256]{3,2,1,0:T(8,128)(2,1)} collective-permute-done((bf16[2,3,256,256]{3,2,1,0:T(8,128)(2,1)}, bf16[2,3,256,256]{3,2,1,0:T(8,128)(2,1)}, u32[]{:S(2)}, u32[]{:S(2)}) %collective-permute-start.10) | collective-permute-done | bytes 786464 | tf_op jit(solution)/shard_map/ppermute | solution.py:32
  175.8 5.2 %collective-permute-done.19 = bf16[2,3,256,256]{3,2,1,0:T(8,128)(2,1)} collective-permute-done((bf16[2,3,256,256]{3,2,1,0:T(8,128)(2,1)}, bf16[2,3,256,256]{3,2,1,0:T(8,128)(2,1)}, u32[]{:S(2)}, u32[]{:S(2)}) %collective-permute-start.19) | collective-permute-done | bytes 786464 | tf_op jit(solution)/shard_map/ppermute | solution.py:27
  181.0 5.3 %select_select_fusion.5 = (bf16[2,3,256,256]{3,2,1,0:T(8,128)(2,1)S(1)}, bf16[2,3,256,256]{3,2,1,0:T(8,128)(2,1)}, bf16[2,3,256,256]{3,2,1,0:T(8,128)(2,1)}, bf16[2,3,256,256]{3,2,1,0:T(8,128)(2,1)}) fusion(bf16[2,3,256,256]{3,2,1,0:T(8,128)(2,1)} %get-tuple-element.14, bf16[2,3,256,256]{3,2,1,0:T(8,128)(2,1)} %collective-permute-done.9, ...), kind=kLoop, calls=%fused_computation.53 | loop fusion | flops 3932160 | bytes 11796488 | tf_op jit(solution)/shard_map/jit(_where)/select_n | solution.py:13
  186.2 2.0 collective-permute-start.17
  190.3 63.0 %all-reduce.3.cloned.1.call-done = bf16[2,256,256]{1,2,0:T(8,128)(2,1)} async-done(((bf16[2,256,256]{1,2,0:T(8,128)(2,1)}), bf16[2,256,256]{1,2,0:T(8,128)(2,1)}) %all-reduce.3.cloned.1.call-update) | async-done | bytes 262160 | tf_op jit(solution)/shard_map/psum | solution.py:196
  256.2 2.4 broadcast_select_fusion.3
  258.6 2.2 collective-permute-start.18
  260.8 4.4 %fusion.4 = bf16[2,8,256,256]{3,2,1,0:T(8,128)(2,1)S(1)} fusion(bf16[2,8,256,256]{3,2,1,0:T(8,128)(2,1)} %collective-permute-done.2, bf16[2,8,256,256]{3,2,1,0:T(8,128)(2,1)} %collective-permute-done.1, bf16[2,4,256,256]{3,2,1,0:T(8,128)(2,1)} %collective-permute-done.4, bf16[2,4,256,256]{3,2,1,0:T(8,128)(2,1)} %collective-permute-done.3, ...), kind=kLoop, calls=%fused_computation.16 | loop fusion | flops 8388608 | bytes 12582921 | tf_op jit(solution)/shard_map/jit(_where)/select_n | solution.py:13
  267.6 3.7 %select_convert_fusion.l2_ref = bf16[8,256,256]{2,1,0:T(8,128)(2,1)} fusion(bf16[2,8,256,256]{3,2,1,0:T(8,128)(2,1)} %copy-done.7, pred[8]{0:T(512)(128)(4,1)S(1)} %get-tuple-element.51, pred[8]{0:T(512)(128)(4,1)S(1)} %copy-done.21, pred[8]{0:T(512)(128)(4,1)S(1)} %get-tuple-element.52, bf16[2,256,256]{1,2,0:T(8,128)(2,1)S(1)} %copy-done.23, ...), kind=kOutput, calls=%fused_computation.19 | convolution fusion | flops 540540928 | bytes 4457984 | tf_op jit(solution)/shard_map/iab,bc->iac/dot_general | solution.py:94
  271.3 4.9 %collective-permute-done.20 = bf16[2,3,256,256]{3,2,1,0:T(8,128)(2,1)} collective-permute-done((bf16[2,3,256,256]{3,2,1,0:T(8,128)(2,1)}, bf16[2,3,256,256]{3,2,1,0:T(8,128)(2,1)}, u32[]{:S(2)}, u32[]{:S(2)}) %collective-permute-start.20) | collective-permute-done | bytes 786464 | tf_op jit(solution)/shard_map/ppermute | solution.py:33
  276.1 2.1 collective-permute-done.18
  278.2 2.6 select_select_fusion.1
  284.4 16.7 %shard_map.46 = bf16[8,12,256,256]{3,2,1,0:T(8,128)(2,1)} custom-call(s32[8,12]{1,0:T(8,128)} %select_add_fusion.codes, bf16[8,12,256,256]{3,2,1,0:T(8,128)(2,1)} %front_ref.1, bf16[8,256,256]{2,1,0:T(8,128)(2,1)} %slice_bitcast_fusion.2.l1_ref, bf16[8,256,256]{2,1,0:T(8,128)(2,1)} %select_convert_fusion.l2_ref, ...), custom_call_target="tpu_custom_call" | custom-call | tf_op jit(solution)/shard_map/pallas_call | solution.py:131
  (119 shorter events, 41.7 us)
Async XLA Ops:
  6.5 246.7 %all-reduce.3.cloned.1.call-start = ((), (), s32[]{:S(2)}) async-start(), calls=%async_computation | async-start | bytes 524288 | tf_op jit(solution)/shard_map/psum | solution.py:196
  17.8 20.8 %collective-permute-start.7 = (bf16[2,3,256,256]{3,2,1,0:T(8,128)(2,1)}, bf16[2,3,256,256]{3,2,1,0:T(8,128)(2,1)}, u32[]{:S(2)}, u32[]{:S(2)}) collective-permute-start(bf16[2,3,256,256]{3,2,1,0:T(8,128)(2,1)} %fusion.20), channel_id=1, source_target_pairs={{0,24},{8,0},{16,8},{24,16},{32,56},{40,32},{48,40},{56,48},{64,88... | collective-permute-start | bytes 2359304 | tf_op jit(solution)/shard_map/ppermute | solution.py:27
  23.9 17.2 %copy-start.2 = (bf16[1,8,256,256]{3,2,1,0:T(8,128)(2,1)}, bf16[1,8,256,256]{3,2,1,0:T(8,128)(2,1)S(1)}, u32[]{:S(2)}) copy-start(bf16[1,8,256,256]{3,2,1,0:T(8,128)(2,1)S(1)} %fusion.9) | copy-start | bytes 3145732
  24.0 54.7 %copy-start.13 = (pred[2]{0:T(512)(128)(4,1)}, pred[2]{0:T(512)(128)(4,1)S(1)}, u32[]{:S(2)}) copy-start(pred[2]{0:T(512)(128)(4,1)S(1)} %get-tuple-element.47) | copy-start | bytes 10
  25.7 15.4 %copy-start = (bf16[1,8,256,256]{3,2,1,0:T(8,128)(2,1)}, bf16[1,8,256,256]{3,2,1,0:T(8,128)(2,1)S(1)}, u32[]{:S(2)}) copy-start(bf16[1,8,256,256]{3,2,1,0:T(8,128)(2,1)S(1)} %bitcast_select_fusion.2) | copy-start | bytes 3145732
  41.1 18.4 %collective-permute-start.5 = (bf16[2,3,256,256]{3,2,1,0:T(8,128)(2,1)S(1)}, bf16[2,3,256,256]{3,2,1,0:T(8,128)(2,1)S(1)}, u32[]{:S(2)}, u32[]{:S(2)}) collective-permute-start(bf16[2,3,256,256]{3,2,1,0:T(8,128)(2,1)S(1)} %get-tuple-element.16), channel_id=1, source_target_pairs={{0,8},{8,16},{16,24},{24,0},{32,40},{40,48},{48,56},{56,32},{64,72... | collective-permute-start | bytes 2359304 | tf_op jit(solution)/shard_map/ppermute | solution.py:26
  42.7 42.9 %collective-permute-start = (bf16[2,8,256,256]{3,2,1,0:T(8,128)(2,1)}, bf16[2,8,256,256]{3,2,1,0:T(8,128)(2,1)}, u32[]{:S(2)}, u32[]{:S(2)}) collective-permute-start(bf16[2,8,256,256]{3,2,1,0:T(8,128)(2,1)} %pad_maximum_fusion.1), channel_id=1, source_target_pairs={{0,1},{1,0},{2,3},{3,2},{4,5},{5,4},{6,7},{7,6},{8,9},{9,8},{10,11... | collective-permute-start | bytes 6291464 | tf_op jit(solution)/shard_map/ppermute | solution.py:71
  42.7 23.6 %collective-permute-start.8 = (bf16[2,3,256,256]{3,2,1,0:T(8,128)(2,1)}, bf16[2,3,256,256]{3,2,1,0:T(8,128)(2,1)}, u32[]{:S(2)}, u32[]{:S(2)}) collective-permute-start(bf16[2,3,256,256]{3,2,1,0:T(8,128)(2,1)} %get-tuple-element.15), channel_id=1, source_target_pairs={{0,24},{8,0},{16,8},{24,16},{32,56},{40,32},{48,40},{56,48},{64,88... | collective-permute-start | bytes 2359304 | tf_op jit(solution)/shard_map/ppermute | solution.py:33
  60.8 17.9 %collective-permute-start.6 = (bf16[2,3,256,256]{3,2,1,0:T(8,128)(2,1)}, bf16[2,3,256,256]{3,2,1,0:T(8,128)(2,1)}, u32[]{:S(2)}, u32[]{:S(2)}) collective-permute-start(bf16[2,3,256,256]{3,2,1,0:T(8,128)(2,1)} %broadcast_select_fusion.5), channel_id=1, source_target_pairs={{0,8},{8,16},{16,24},{24,0},{32,40},{40,48},{48,56},{56,32},{64,72... | collective-permute-start | bytes 2359304 | tf_op jit(solution)/shard_map/ppermute | solution.py:32
  62.2 30.1 %collective-permute-start.15 = (bf16[2,3,256,256]{3,2,1,0:T(8,128)(2,1)}, bf16[2,3,256,256]{3,2,1,0:T(8,128)(2,1)}, u32[]{:S(2)}, u32[]{:S(2)}) collective-permute-start(bf16[2,3,256,256]{3,2,1,0:T(8,128)(2,1)} %get-tuple-element.34), channel_id=1, source_target_pairs={{0,96},{8,104},{16,112},{24,120},{32,0},{40,8},{48,16},{56,24},{64... | collective-permute-start | bytes 2359304 | tf_op jit(solution)/shard_map/ppermute | solution.py:27
  81.4 18.5 %collective-permute-start.11 = (bf16[2,3,256,256]{3,2,1,0:T(8,128)(2,1)}, bf16[2,3,256,256]{3,2,1,0:T(8,128)(2,1)}, u32[]{:S(2)}, u32[]{:S(2)}) collective-permute-start(bf16[2,3,256,256]{3,2,1,0:T(8,128)(2,1)} %select_select_fusion.6), channel_id=1, source_target_pairs={{0,96},{8,104},{16,112},{24,120},{32,0},{40,8},{48,16},{56,24},{64... | collective-permute-start | bytes 2359304 | tf_op jit(solution)/shard_map/ppermute | solution.py:27
  89.5 59.2 %collective-permute-start.1 = (bf16[2,8,256,256]{3,2,1,0:T(8,128)(2,1)}, bf16[2,8,256,256]{3,2,1,0:T(8,128)(2,1)}, u32[]{:S(2)}, u32[]{:S(2)}) collective-permute-start(bf16[2,8,256,256]{3,2,1,0:T(8,128)(2,1)} %broadcast_select_fusion), channel_id=1, source_target_pairs={{0,2},{2,4},{4,6},{6,0},{1,7},{3,1},{5,3},{7,5},{8,10},{10,12},{12... | collective-permute-start | bytes 6291464 | tf_op jit(solution)/shard_map/ppermute | solution.py:73
  103.8 35.3 %copy-start.6 = (bf16[2,3,256,256]{3,2,1,0:T(8,128)(2,1)S(1)}, bf16[2,3,256,256]{3,2,1,0:T(8,128)(2,1)}, u32[]{:S(2)}) copy-start(bf16[2,3,256,256]{3,2,1,0:T(8,128)(2,1)} %get-tuple-element.34) | copy-start | bytes 2359300
  103.8 22.5 %collective-permute-start.9 = (bf16[2,3,256,256]{3,2,1,0:T(8,128)(2,1)}, bf16[2,3,256,256]{3,2,1,0:T(8,128)(2,1)}, u32[]{:S(2)}, u32[]{:S(2)}) collective-permute-start(bf16[2,3,256,256]{3,2,1,0:T(8,128)(2,1)} %get-tuple-element.14), channel_id=1, source_target_pairs={{0,32},{8,40},{16,48},{24,56},{32,64},{40,72},{48,80},{56,88},{64,... | collective-permute-start | bytes 2359304 | tf_op jit(solution)/shard_map/ppermute | solution.py:26
  104.3 34.7 %collective-permute-start.13 = (bf16[2,3,256,256]{3,2,1,0:T(8,128)(2,1)}, bf16[2,3,256,256]{3,2,1,0:T(8,128)(2,1)}, u32[]{:S(2)}, u32[]{:S(2)}) collective-permute-start(bf16[2,3,256,256]{3,2,1,0:T(8,128)(2,1)} %get-tuple-element.46), channel_id=1, source_target_pairs={{0,32},{8,40},{16,48},{24,56},{32,64},{40,72},{48,80},{56,88},{64,... | collective-permute-start | bytes 2359304 | tf_op jit(solution)/shard_map/ppermute | solution.py:26
  111.5 33.3 %copy-start.5 = (s32[128,96]{0,1:T(8,128)S(1)}, s32[128,96]{0,1:T(8,128)}, u32[]{:S(2)}) copy-start(s32[128,96]{0,1:T(8,128)} %param.5) | copy-start | bytes 147460
  111.5 37.2 %copy-start.1 = (bf16[1,8,256,256]{3,2,1,0:T(8,128)(2,1)S(1)}, bf16[1,8,256,256]{3,2,1,0:T(8,128)(2,1)}, u32[]{:S(2)}) copy-start(bf16[1,8,256,256]{3,2,1,0:T(8,128)(2,1)} %copy-done) | copy-start | bytes 3145732
  111.5 37.2 %copy-start.3 = (bf16[1,8,256,256]{3,2,1,0:T(8,128)(2,1)S(1)}, bf16[1,8,256,256]{3,2,1,0:T(8,128)(2,1)}, u32[]{:S(2)}) copy-start(bf16[1,8,256,256]{3,2,1,0:T(8,128)(2,1)} %copy-done.2) | copy-start | bytes 3145732
  111.5 42.7 %collective-permute-start.16 = (bf16[2,3,256,256]{3,2,1,0:T(8,128)(2,1)}, bf16[2,3,256,256]{3,2,1,0:T(8,128)(2,1)}, u32[]{:S(2)}, u32[]{:S(2)}) collective-permute-start(bf16[2,3,256,256]{3,2,1,0:T(8,128)(2,1)} %get-tuple-element.45), channel_id=1, source_target_pairs={{0,96},{8,104},{16,112},{24,120},{32,0},{40,8},{48,16},{56,24},{64... | collective-permute-start | bytes 2359304 | tf_op jit(solution)/shard_map/ppermute | solution.py:33
  142.2 22.2 %collective-permute-start.14 = (bf16[2,3,256,256]{3,2,1,0:T(8,128)(2,1)}, bf16[2,3,256,256]{3,2,1,0:T(8,128)(2,1)}, u32[]{:S(2)}, u32[]{:S(2)}) collective-permute-start(bf16[2,3,256,256]{3,2,1,0:T(8,128)(2,1)} %get-tuple-element.44), channel_id=1, source_target_pairs={{0,32},{8,40},{16,48},{24,56},{32,64},{40,72},{48,80},{56,88},{64,... | collective-permute-start | bytes 2359304 | tf_op jit(solution)/shard_map/ppermute | solution.py:32
  145.4 25.1 %collective-permute-start.12 = (bf16[2,3,256,256]{3,2,1,0:T(8,128)(2,1)}, bf16[2,3,256,256]{3,2,1,0:T(8,128)(2,1)}, u32[]{:S(2)}, u32[]{:S(2)}) collective-permute-start(bf16[2,3,256,256]{3,2,1,0:T(8,128)(2,1)} %get-tuple-element.13), channel_id=1, source_target_pairs={{0,96},{8,104},{16,112},{24,120},{32,0},{40,8},{48,16},{56,24},{64... | collective-permute-start | bytes 2359304 | tf_op jit(solution)/shard_map/ppermute | solution.py:33
  148.7 27.1 %collective-permute-start.10 = (bf16[2,3,256,256]{3,2,1,0:T(8,128)(2,1)}, bf16[2,3,256,256]{3,2,1,0:T(8,128)(2,1)}, u32[]{:S(2)}, u32[]{:S(2)}) collective-permute-start(bf16[2,3,256,256]{3,2,1,0:T(8,128)(2,1)} %get-tuple-element.43), channel_id=1, source_target_pairs={{0,32},{8,40},{16,48},{24,56},{32,64},{40,72},{48,80},{56,88},{64,... | collective-permute-start | bytes 2359304 | tf_op jit(solution)/shard_map/ppermute | solution.py:32
  151.3 15.9 %copy-start.4 = (bf16[2,8,256,256]{3,2,1,0:T(8,128)(2,1)}, bf16[2,8,256,256]{3,2,1,0:T(8,128)(2,1)S(1)}, u32[]{:S(2)}) copy-start(bf16[2,8,256,256]{3,2,1,0:T(8,128)(2,1)S(1)} %broadcast_select_fusion.1) | copy-start | bytes 6291460
  152.6 17.1 %collective-permute-start.3 = (bf16[2,4,256,256]{3,2,1,0:T(8,128)(2,1)}, bf16[2,4,256,256]{3,2,1,0:T(8,128)(2,1)}, u32[]{:S(2)}, u32[]{:S(2)}) collective-permute-start(bf16[2,4,256,256]{3,2,1,0:T(8,128)(2,1)} %slice_select_fusion), channel_id=1, source_target_pairs={{0,2},{2,4},{4,6},{6,0},{1,7},{3,1},{5,3},{7,5},{8,10},{10,12},{12... | collective-permute-start | bytes 3145736 | tf_op jit(solution)/shard_map/ppermute | solution.py:79
  167.2 13.8 %collective-permute-start.19 = (bf16[2,3,256,256]{3,2,1,0:T(8,128)(2,1)}, bf16[2,3,256,256]{3,2,1,0:T(8,128)(2,1)}, u32[]{:S(2)}, u32[]{:S(2)}) collective-permute-start(bf16[2,3,256,256]{3,2,1,0:T(8,128)(2,1)} %select_select_fusion.2), channel_id=1, source_target_pairs={{0,24},{8,0},{16,8},{24,16},{32,56},{40,32},{48,40},{56,48},{64,88... | collective-permute-start | bytes 2359304 | tf_op jit(solution)/shard_map/ppermute | solution.py:27
  168.3 92.5 %collective-permute-start.2 = (bf16[2,8,256,256]{3,2,1,0:T(8,128)(2,1)}, bf16[2,8,256,256]{3,2,1,0:T(8,128)(2,1)}, u32[]{:S(2)}, u32[]{:S(2)}) collective-permute-start(bf16[2,8,256,256]{3,2,1,0:T(8,128)(2,1)} %copy-done.4), channel_id=1, source_target_pairs={{0,1},{1,0},{2,3},{3,2},{4,5},{5,4},{6,7},{7,6},{8,9},{9,8},{10,11... | collective-permute-start | bytes 6291464 | tf_op jit(solution)/shard_map/ppermute | solution.py:76
  169.7 19.3 %copy-start.18 = (pred[8]{0:T(512)(128)(4,1)S(1)}, pred[8]{0:T(512)(128)(4,1)}, u32[]{:S(2)}) copy-start(pred[8]{0:T(512)(128)(4,1)} %copy-done.17) | copy-start | bytes 28
  169.7 83.6 %copy-start.22 = (bf16[2,256,256]{2,1,0:T(8,128)(2,1)S(1)}, bf16[2,256,256]{2,1,0:T(8,128)(2,1)}, u32[]{:S(2)}) copy-start(bf16[2,256,256]{2,1,0:T(8,128)(2,1)} %param.7) | copy-start | bytes 786436
  169.7 91.0 %collective-permute-start.4 = (bf16[2,4,256,256]{3,2,1,0:T(8,128)(2,1)}, bf16[2,4,256,256]{3,2,1,0:T(8,128)(2,1)}, u32[]{:S(2)}, u32[]{:S(2)}) collective-permute-start(bf16[2,4,256,256]{3,2,1,0:T(8,128)(2,1)} %collective-permute-done.3), channel_id=1, source_target_pairs={{0,1},{1,0},{2,3},{3,2},{4,5},{5,4},{6,7},{7,6},{8,9},{9,8},{10,11... | collective-permute-start | bytes 3145736 | tf_op jit(solution)/shard_map/ppermute | solution.py:80
  186.2 69.9 %collective-permute-start.17 = (bf16[2,3,256,256]{3,2,1,0:T(8,128)(2,1)}, bf16[2,3,256,256]{3,2,1,0:T(8,128)(2,1)}, u32[]{:S(2)}, u32[]{:S(2)}) collective-permute-start(bf16[2,3,256,256]{3,2,1,0:T(8,128)(2,1)} %get-tuple-element.42), channel_id=1, source_target_pairs={{0,8},{8,16},{16,24},{24,0},{32,40},{40,48},{48,56},{56,32},{64,72... | collective-permute-start | bytes 2359304 | tf_op jit(solution)/shard_map/ppermute | solution.py:26
  255.1 21.1 %collective-permute-start.20 = (bf16[2,3,256,256]{3,2,1,0:T(8,128)(2,1)}, bf16[2,3,256,256]{3,2,1,0:T(8,128)(2,1)}, u32[]{:S(2)}, u32[]{:S(2)}) collective-permute-start(bf16[2,3,256,256]{3,2,1,0:T(8,128)(2,1)} %get-tuple-element.41), channel_id=1, source_target_pairs={{0,24},{8,0},{16,8},{24,16},{32,56},{40,32},{48,40},{56,48},{64,88... | collective-permute-start | bytes 2359304 | tf_op jit(solution)/shard_map/ppermute | solution.py:33
  258.6 19.6 %collective-permute-start.18 = (bf16[2,3,256,256]{3,2,1,0:T(8,128)(2,1)}, bf16[2,3,256,256]{3,2,1,0:T(8,128)(2,1)}, u32[]{:S(2)}, u32[]{:S(2)}) collective-permute-start(bf16[2,3,256,256]{3,2,1,0:T(8,128)(2,1)} %broadcast_select_fusion.3), channel_id=1, source_target_pairs={{0,8},{8,16},{16,24},{24,0},{32,40},{40,48},{48,56},{56,32},{64,72... | collective-permute-start | bytes 2359304 | tf_op jit(solution)/shard_map/ppermute | solution.py:32
  (15 other events, 104.4 us)
Sparse Core Ops, SparseCore 0:
  110.2 143.0 all-reduce.2

commit v4 on v2

--- a/solution.py
+++ b/solution.py
@@ -86,6 +86,11 @@
     return jnp.where(dist == 0, on_root_chip, out)
 
 
+def from_root(value, axis, source):
+    kept = jnp.where(lax.axis_index(axis) == source, value, 0).astype(value.dtype)
+    return lax.psum(kept, axis)
+
+
 def lower_local(column, inverse, rows_ok):
     lower = jnp.einsum("iab,bc->iac", column, inverse, preferred_element_type=jnp.float32)
     return jnp.where(rows_ok[:, None, None], lower, 0.0).astype(jnp.bfloat16)
@@ -166,7 +171,7 @@
         lax.dynamic_index_in_dim(front, b1, 1, keepdims=False),
         lax.dynamic_index_in_dim(local, b1, 1, keepdims=False),
     )
-    lower_first = col_bcast(lower_local(column_first, pivot_inv[0], rows_first), first % ncol)
+    lower_first = from_root(lower_local(column_first, pivot_inv[0], rows_first), "col", first % ncol)
     a1 = first // nrow
     first_row = masked(
         lax.dynamic_index_in_dim(front, a1, 0, keepdims=False),
@@ -201,7 +206,9 @@
         local_col,
         lax.dynamic_slice_in_dim(front_cols, b2, 1, 0),
     )
-    lower_second = col_bcast(lower_local(col_after[:, 0], pivot_inv[1], rows_second), second % ncol)
+    lower_second = from_root(
+        lower_local(col_after[:, 0], pivot_inv[1], rows_second), "col", second % ncol
+    )
 
     keep = local > 0
     update_first = rows_first[:, None] & cols_first[None, :] & keep

time: 232 us -> 327 us (1.41)
  waiting for transfers between devices: 98.4 us -> 188 us
  between operations: 6.91 us -> 20.3 us
  other arithmetic: 41.1 us -> 33.3 us
    psum x0 -> x2, waiting for transfers between devices: none -> 108 us  [from_root(): return lax.psum(kept, axis)]
    select_n x8 -> x0, other arithmetic: 10.6 us -> none  [the longest x2 4.25 us: col_bcast(): return jnp.where(dist == 0, on_root_chip, out)]
    ppermute x8, waiting for transfers between devices: 20.2 us -> 12 us  [ring_bcast(): got_plus2 = lax.ppermute(send_plus, axis, plus)]
    ppermute x8, waiting for transfers between devices: 46.7 us -> 39.6 us  [ring_bcast(): got_minus = lax.ppermute(second, axis, minus)]
    ppermute x8, starting transfers between devices: 10.6 us -> 15.7 us  [ring_bcast(): got_minus = lax.ppermute(second, axis, minus)]
    ppermute x10 -> x0, starting transfers between devices: 4.83 us -> none  [the longest x2 2.61 us: col_bcast(): got_hop = lax.ppermute(on_root_chip, 'col', hop)]
    ppermute x8, waiting for transfers between devices: 10.9 us -> 7.16 us  [ring_bcast(): got_minus2 = lax.ppermute(send_minus, axis, minus)]
  transfers between devices with their start and end apart: 42 -> 34, of which waited for: 22 -> 19; matrix products, arithmetic and copies ran while one was open for 20% -> 10% of each run, Pallas kernels for 0% -> 0%
where the time goes in v4:
time: 327 us; the launch traced here: 326 us
  waiting for transfers between devices  188 us (57%)
  starting transfers between devices  48.5 us (15%)
  other arithmetic  33.3 us (10%)
  between operations  20.3 us (6%)
  Pallas kernels  16.7 us (5%)
  local copies, waits for them, and re-layouts  10.5 us (3%)
  matrix products  8.88 us (3%)
    psum x2, waiting for transfers between devices, from_root(): return lax.psum(kept, axis)  108 us
    ppermute x8, waiting for transfers between devices, ring_bcast(): got_minus = lax.ppermute(second, axis, minus)  39.6 us
    ppermute x8, waiting for transfers between devices, ring_bcast(): got_plus = lax.ppermute(first, axis, plus)  21.3 us
    pallas_call x1, Pallas kernels, both_updates(): pl.pallas_call(update_kernel, grid_spec=pltpu.PrefetchScalarGridSpec(num_...  16.7 us
    ppermute x8, starting transfers between devices, ring_bcast(): got_minus = lax.ppermute(second, axis, minus)  15.7 us
    ppermute x8, starting transfers between devices, ring_bcast(): got_plus2 = lax.ppermute(send_plus, axis, plus)  13.7 us
    ppermute x8, waiting for transfers between devices, ring_bcast(): got_plus2 = lax.ppermute(send_plus, axis, plus)  12 us
    ppermute x8, starting transfers between devices, ring_bcast(): got_minus2 = lax.ppermute(send_minus, axis, minus)  11 us
  transfers between devices with their start and end apart: 34, of which 19 were waited for; matrix products, arithmetic and copies ran while one was open for 10% of the time, Pallas kernels for 0%

profile of v4, /device:TPU:6, one launch (start us, length us, event | category | flops | bytes accessed | tf_op | source)
XLA Modules:
  0.0 325.8 jit_solution(4628711618590542474)
XLA Ops:
  17.2 11.2 %collective-permute-done.2 = bf16[3,256,256]{2,1,0:T(8,128)(2,1)S(1)} collective-permute-done((bf16[3,256,256]{2,1,0:T(8,128)(2,1)S(1)}, bf16[3,256,256]{2,1,0:T(8,128)(2,1)S(1)}, u32[]{:S(2)}, u32[]{:S(2)}) %collective-permute-start.2) | collective-permute-done | bytes 393248 | tf_op jit(solution)/shard_map/ppermute | solution.py:23
  30.6 8.0 %collective-permute-done = bf16[3,256,256]{2,1,0:T(8,128)(2,1)S(1)} collective-permute-done((bf16[3,256,256]{2,1,0:T(8,128)(2,1)S(1)}, bf16[3,256,256]{2,1,0:T(8,128)(2,1)S(1)}, u32[]{:S(2)}, u32[]{:S(2)}) %collective-permute-start) | collective-permute-done | bytes 393248 | tf_op jit(solution)/shard_map/ppermute | solution.py:22
  40.9 7.8 %collective-permute-done.1 = bf16[3,256,256]{2,1,0:T(8,128)(2,1)S(1)} collective-permute-done((bf16[3,256,256]{2,1,0:T(8,128)(2,1)}, bf16[3,256,256]{2,1,0:T(8,128)(2,1)S(1)}, u32[]{:S(2)}, u32[]{:S(2)}) %collective-permute-start.1) | collective-permute-done | bytes 393248 | tf_op jit(solution)/shard_map/ppermute | solution.py:28
  48.7 4.1 %collective-permute-start.6 = (bf16[3,256,256]{2,1,0:T(8,128)(2,1)S(1)}, bf16[3,256,256]{2,1,0:T(8,128)(2,1)S(1)}, u32[]{:S(2)}, u32[]{:S(2)}) collective-permute-start(bf16[3,256,256]{2,1,0:T(8,128)(2,1)S(1)} %select_select_fusion.14), channel_id=1, source_target_pairs={{0,96},{8,104},{16,112},{24,120},{32,0},{40,8},{48,16},{56,24},{64... | collective-permute-start | bytes 1179656 | tf_op jit(solution)/shard_map/ppermute | solution.py:23
  52.8 5.7 %collective-permute-done.6 = bf16[3,256,256]{2,1,0:T(8,128)(2,1)S(1)} collective-permute-done((bf16[3,256,256]{2,1,0:T(8,128)(2,1)S(1)}, bf16[3,256,256]{2,1,0:T(8,128)(2,1)S(1)}, u32[]{:S(2)}, u32[]{:S(2)}) %collective-permute-start.6) | collective-permute-done | bytes 393248 | tf_op jit(solution)/shard_map/ppermute | solution.py:23
  59.5 3.7 %collective-permute-start.10 = (bf16[3,256,256]{2,1,0:T(8,128)(2,1)S(1)}, bf16[3,256,256]{2,1,0:T(8,128)(2,1)S(1)}, u32[]{:S(2)}, u32[]{:S(2)}) collective-permute-start(bf16[3,256,256]{2,1,0:T(8,128)(2,1)S(1)} %get-tuple-element.31), channel_id=1, source_target_pairs={{0,96},{8,104},{16,112},{24,120},{32,0},{40,8},{48,16},{56,24},{64... | collective-permute-start | bytes 1179656 | tf_op jit(solution)/shard_map/ppermute | solution.py:23
  63.2 5.3 %collective-permute-done.10 = bf16[3,256,256]{2,1,0:T(8,128)(2,1)S(1)} collective-permute-done((bf16[3,256,256]{2,1,0:T(8,128)(2,1)S(1)}, bf16[3,256,256]{2,1,0:T(8,128)(2,1)S(1)}, u32[]{:S(2)}, u32[]{:S(2)}) %collective-permute-start.10) | collective-permute-done | bytes 393248 | tf_op jit(solution)/shard_map/ppermute | solution.py:23
  68.5 4.2 %collective-permute-done.8 = bf16[3,256,256]{2,1,0:T(8,128)(2,1)S(1)} collective-permute-done((bf16[3,256,256]{2,1,0:T(8,128)(2,1)S(1)}, bf16[3,256,256]{2,1,0:T(8,128)(2,1)S(1)}, u32[]{:S(2)}, u32[]{:S(2)}) %collective-permute-start.8) | collective-permute-done | bytes 393248 | tf_op jit(solution)/shard_map/ppermute | solution.py:22
  73.5 2.0 collective-permute-start.9
  77.5 4.0 %collective-permute-done.11 = bf16[3,256,256]{2,1,0:T(8,128)(2,1)S(1)} collective-permute-done((bf16[3,256,256]{2,1,0:T(8,128)(2,1)}, bf16[3,256,256]{2,1,0:T(8,128)(2,1)S(1)}, u32[]{:S(2)}, u32[]{:S(2)}) %collective-permute-start.11) | collective-permute-done | bytes 393248 | tf_op jit(solution)/shard_map/ppermute | solution.py:29
  87.2 2.7 fusion.4
  94.6 2.9 collective-permute-start.12
  101.9 3.8 %collective-permute-done.12 = bf16[3,256,256]{2,1,0:T(8,128)(2,1)S(1)} collective-permute-done((bf16[3,256,256]{2,1,0:T(8,128)(2,1)S(1)}, bf16[3,256,256]{2,1,0:T(8,128)(2,1)S(1)}, u32[]{:S(2)}, u32[]{:S(2)}) %collective-permute-start.12) | collective-permute-done | bytes 393248 | tf_op jit(solution)/shard_map/ppermute | solution.py:22
  106.6 3.4 %collective-permute-start.13 = (bf16[3,256,256]{2,1,0:T(8,128)(2,1)}, bf16[3,256,256]{2,1,0:T(8,128)(2,1)}, u32[]{:S(2)}, u32[]{:S(2)}) collective-permute-start(bf16[3,256,256]{2,1,0:T(8,128)(2,1)} %broadcast_select_fusion.10), channel_id=1, source_target_pairs={{0,8},{8,16},{16,24},{24,0},{32,40},{40,48},{48,56},{56,32},{64,72... | collective-permute-start | bytes 1179656 | tf_op jit(solution)/shard_map/ppermute | solution.py:28
  110.0 44.2 %all-reduce.3.cloned.1.call-done.l1_ref = bf16[8,256,256]{2,1,0:T(8,128)(2,1)} async-done(((bf16[8,256,256]{2,1,0:T(8,128)(2,1)}), bf16[8,256,256]{2,1,0:T(8,128)(2,1)}) %all-reduce.3.cloned.1.call-update) | async-done | bytes 1048592 | tf_op jit(solution)/shard_map/psum | solution.py:91
  157.7 2.2 broadcast_select_fusion
  162.0 2.4 collective-permute-start.16
  164.4 7.0 %collective-permute-done.18 = bf16[3,256,256]{2,1,0:T(8,128)(2,1)S(1)} collective-permute-done((bf16[3,256,256]{2,1,0:T(8,128)(2,1)}, bf16[3,256,256]{2,1,0:T(8,128)(2,1)S(1)}, u32[]{:S(2)}, u32[]{:S(2)}) %collective-permute-start.18) | collective-permute-done | bytes 393248 | tf_op jit(solution)/shard_map/ppermute | solution.py:23
  172.5 3.2 collective-permute-start.17
  175.7 2.9 collective-permute-start.26
  178.7 3.1 collective-permute-done.19
  183.7 3.0 collective-permute-start.22
  189.7 2.9 collective-permute-done.22
  192.6 2.3 broadcast_select_fusion.7
  196.2 2.3 collective-permute-start.27
  201.8 2.4 collective-permute-done.25
  207.2 7.2 %collective-permute-done.30 = bf16[3,256,256]{2,1,0:T(8,128)(2,1)S(1)} collective-permute-done((bf16[3,256,256]{2,1,0:T(8,128)(2,1)S(1)}, bf16[3,256,256]{2,1,0:T(8,128)(2,1)S(1)}, u32[]{:S(2)}, u32[]{:S(2)}) %collective-permute-start.30) | collective-permute-done | bytes 393248 | tf_op jit(solution)/shard_map/ppermute | solution.py:23
  217.6 2.2 collective-permute-start.23
  221.9 5.3 %collective-permute-done.28 = bf16[3,256,256]{2,1,0:T(8,128)(2,1)S(1)} collective-permute-done((bf16[3,256,256]{2,1,0:T(8,128)(2,1)S(1)}, bf16[3,256,256]{2,1,0:T(8,128)(2,1)S(1)}, u32[]{:S(2)}, u32[]{:S(2)}) %collective-permute-start.28) | collective-permute-done | bytes 393248 | tf_op jit(solution)/shard_map/ppermute | solution.py:22
  229.2 4.0 %fusion.5 = bf16[8,256,256]{2,1,0:T(8,128)(2,1)} fusion(pred[8]{0:T(512)(128)(4,1)S(1)} %compare_and_fusion.1, pred[]{:T(512)S(6)} %eq.132, bf16[8,256,256]{2,1,0:T(8,128)(2,1)} %all-reduce.3.cloned.1.call-done.l1_ref, bf16[8,12,256,256]{3,2,1,0:T(8,128)(2,1)} %front_ref.1, s32[]{:T(128)S(6)} %select_n.476, pred[8]{0:T(512)(128)(4,1)S(1)} %copy-done.28, ...), kind=kOutput, calls=%fused_computation.13 | convolution fusion | flops 541589504 | bytes 4460032 | tf_op jit(solution)/shard_map/iab,bc->iac/dot_general | solution.py:95
  238.9 63.3 %all-reduce.5.cloned.1.call-done.l2_ref = bf16[8,256,256]{2,1,0:T(8,128)(2,1)} async-done(((bf16[8,256,256]{2,1,0:T(8,128)(2,1)}), bf16[8,256,256]{2,1,0:T(8,128)(2,1)}) %all-reduce.5.cloned.1.call-update) | async-done | bytes 1048592 | tf_op jit(solution)/shard_map/psum | solution.py:91
  302.2 16.7 %shard_map.46 = bf16[8,12,256,256]{3,2,1,0:T(8,128)(2,1)} custom-call(s32[8,12]{1,0:T(8,128)} %select_add_fusion.codes, bf16[8,12,256,256]{3,2,1,0:T(8,128)(2,1)} %front_ref.1, bf16[8,256,256]{2,1,0:T(8,128)(2,1)} %all-reduce.3.cloned.1.call-done.l1_ref, bf16[8,256,256]{2,1,0:T(8,128)(2,1)} %all-reduce.5.cloned.1.call-done.l2_ref, ...), custom_call_target="tpu_custom_call" | custom-call | tf_op jit(solution)/shard_map/pallas_call | solution.py:132
  (147 shorter events, 59.8 us)
Async XLA Ops:
  6.5 147.7 %all-reduce.3.cloned.1.call-start = ((), (), s32[]{:S(2)}) async-start(), calls=%async_computation | async-start | bytes 2097152 | tf_op jit(solution)/shard_map/psum | solution.py:91
  16.3 12.1 %collective-permute-start.2 = (bf16[3,256,256]{2,1,0:T(8,128)(2,1)S(1)}, bf16[3,256,256]{2,1,0:T(8,128)(2,1)S(1)}, u32[]{:S(2)}, u32[]{:S(2)}) collective-permute-start(bf16[3,256,256]{2,1,0:T(8,128)(2,1)S(1)} %slice.79), channel_id=1, source_target_pairs={{0,24},{8,0},{16,8},{24,16},{32,56},{40,32},{48,40},{56,48},{64,88... | collective-permute-start | bytes 1179656 | tf_op jit(solution)/shard_map/ppermute | solution.py:23
  28.5 10.1 %collective-permute-start = (bf16[3,256,256]{2,1,0:T(8,128)(2,1)S(1)}, bf16[3,256,256]{2,1,0:T(8,128)(2,1)S(1)}, u32[]{:S(2)}, u32[]{:S(2)}) collective-permute-start(bf16[3,256,256]{2,1,0:T(8,128)(2,1)S(1)} %get-tuple-element.34), channel_id=1, source_target_pairs={{0,8},{8,16},{16,24},{24,0},{32,40},{40,48},{48,56},{56,32},{64,72... | collective-permute-start | bytes 1179656 | tf_op jit(solution)/shard_map/ppermute | solution.py:22
  28.6 12.3 %collective-permute-start.3 = (bf16[3,256,256]{2,1,0:T(8,128)(2,1)S(1)}, bf16[3,256,256]{2,1,0:T(8,128)(2,1)S(1)}, u32[]{:S(2)}, u32[]{:S(2)}) collective-permute-start(bf16[3,256,256]{2,1,0:T(8,128)(2,1)S(1)} %get-tuple-element.33), channel_id=1, source_target_pairs={{0,24},{8,0},{16,8},{24,16},{32,56},{40,32},{48,40},{56,48},{64,88... | collective-permute-start | bytes 1179656 | tf_op jit(solution)/shard_map/ppermute | solution.py:29
  39.4 9.3 %collective-permute-start.1 = (bf16[3,256,256]{2,1,0:T(8,128)(2,1)}, bf16[3,256,256]{2,1,0:T(8,128)(2,1)S(1)}, u32[]{:S(2)}, u32[]{:S(2)}) collective-permute-start(bf16[3,256,256]{2,1,0:T(8,128)(2,1)} %broadcast_select_fusion.12), channel_id=1, source_target_pairs={{0,8},{8,16},{16,24},{24,0},{32,40},{40,48},{48,56},{56,32},{64,72... | collective-permute-start | bytes 1179656 | tf_op jit(solution)/shard_map/ppermute | solution.py:28
  48.7 9.8 %collective-permute-start.6 = (bf16[3,256,256]{2,1,0:T(8,128)(2,1)S(1)}, bf16[3,256,256]{2,1,0:T(8,128)(2,1)S(1)}, u32[]{:S(2)}, u32[]{:S(2)}) collective-permute-start(bf16[3,256,256]{2,1,0:T(8,128)(2,1)S(1)} %select_select_fusion.14), channel_id=1, source_target_pairs={{0,96},{8,104},{16,112},{24,120},{32,0},{40,8},{48,16},{56,24},{64... | collective-permute-start | bytes 1179656 | tf_op jit(solution)/shard_map/ppermute | solution.py:23
  59.5 9.0 %collective-permute-start.10 = (bf16[3,256,256]{2,1,0:T(8,128)(2,1)S(1)}, bf16[3,256,256]{2,1,0:T(8,128)(2,1)S(1)}, u32[]{:S(2)}, u32[]{:S(2)}) collective-permute-start(bf16[3,256,256]{2,1,0:T(8,128)(2,1)S(1)} %get-tuple-element.31), channel_id=1, source_target_pairs={{0,96},{8,104},{16,112},{24,120},{32,0},{40,8},{48,16},{56,24},{64... | collective-permute-start | bytes 1179656 | tf_op jit(solution)/shard_map/ppermute | solution.py:23
  63.2 9.5 %collective-permute-start.8 = (bf16[3,256,256]{2,1,0:T(8,128)(2,1)S(1)}, bf16[3,256,256]{2,1,0:T(8,128)(2,1)S(1)}, u32[]{:S(2)}, u32[]{:S(2)}) collective-permute-start(bf16[3,256,256]{2,1,0:T(8,128)(2,1)S(1)} %get-tuple-element.32), channel_id=1, source_target_pairs={{0,32},{8,40},{16,48},{24,56},{32,64},{40,72},{48,80},{56,88},{64,... | collective-permute-start | bytes 1179656 | tf_op jit(solution)/shard_map/ppermute | solution.py:22
  73.5 9.0 %collective-permute-start.9 = (bf16[3,256,256]{2,1,0:T(8,128)(2,1)S(1)}, bf16[3,256,256]{2,1,0:T(8,128)(2,1)S(1)}, u32[]{:S(2)}, u32[]{:S(2)}) collective-permute-start(bf16[3,256,256]{2,1,0:T(8,128)(2,1)S(1)} %get-tuple-element.36), channel_id=1, source_target_pairs={{0,32},{8,40},{16,48},{24,56},{32,64},{40,72},{48,80},{56,88},{64,... | collective-permute-start | bytes 1179656 | tf_op jit(solution)/shard_map/ppermute | solution.py:28
  83.7 9.1 %collective-permute-start.14 = (bf16[3,256,256]{2,1,0:T(8,128)(2,1)S(1)}, bf16[3,256,256]{2,1,0:T(8,128)(2,1)S(1)}, u32[]{:S(2)}, u32[]{:S(2)}) collective-permute-start(bf16[3,256,256]{2,1,0:T(8,128)(2,1)S(1)} %select_select_fusion.10), channel_id=1, source_target_pairs={{0,24},{8,0},{16,8},{24,16},{32,56},{40,32},{48,40},{56,48},{64,88... | collective-permute-start | bytes 1179656 | tf_op jit(solution)/shard_map/ppermute | solution.py:23
  85.8 11.7 %collective-permute-start.4 = (bf16[3,256,256]{2,1,0:T(8,128)(2,1)}, bf16[3,256,256]{2,1,0:T(8,128)(2,1)}, u32[]{:S(2)}, u32[]{:S(2)}) collective-permute-start(bf16[3,256,256]{2,1,0:T(8,128)(2,1)} %get-tuple-element.18), channel_id=1, source_target_pairs={{0,32},{8,40},{16,48},{24,56},{32,64},{40,72},{48,80},{56,88},{64,... | collective-permute-start | bytes 1179656 | tf_op jit(solution)/shard_map/ppermute | solution.py:22
  89.9 212.3 %all-reduce.5.cloned.1.call-start = ((), (), s32[]{:S(2)}) async-start(), calls=%async_computation.1 | async-start | bytes 2097152 | tf_op jit(solution)/shard_map/psum | solution.py:91
  90.6 64.6 %collective-permute-start.7 = (bf16[3,256,256]{2,1,0:T(8,128)(2,1)}, bf16[3,256,256]{2,1,0:T(8,128)(2,1)}, u32[]{:S(2)}, u32[]{:S(2)}) collective-permute-start(bf16[3,256,256]{2,1,0:T(8,128)(2,1)} %get-tuple-element.17), channel_id=1, source_target_pairs={{0,96},{8,104},{16,112},{24,120},{32,0},{40,8},{48,16},{56,24},{64... | collective-permute-start | bytes 1179656 | tf_op jit(solution)/shard_map/ppermute | solution.py:29
  94.6 11.1 %collective-permute-start.12 = (bf16[3,256,256]{2,1,0:T(8,128)(2,1)S(1)}, bf16[3,256,256]{2,1,0:T(8,128)(2,1)S(1)}, u32[]{:S(2)}, u32[]{:S(2)}) collective-permute-start(bf16[3,256,256]{2,1,0:T(8,128)(2,1)S(1)} %get-tuple-element.20), channel_id=1, source_target_pairs={{0,8},{8,16},{16,24},{24,0},{32,40},{40,48},{48,56},{56,32},{64,72... | collective-permute-start | bytes 1179656 | tf_op jit(solution)/shard_map/ppermute | solution.py:22
  97.6 57.5 %collective-permute-start.5 = (bf16[3,256,256]{2,1,0:T(8,128)(2,1)S(1)}, bf16[3,256,256]{2,1,0:T(8,128)(2,1)}, u32[]{:S(2)}, u32[]{:S(2)}) collective-permute-start(bf16[3,256,256]{2,1,0:T(8,128)(2,1)S(1)} %broadcast_select_fusion.16), channel_id=1, source_target_pairs={{0,32},{8,40},{16,48},{24,56},{32,64},{40,72},{48,80},{56,88},{64,... | collective-permute-start | bytes 1179656 | tf_op jit(solution)/shard_map/ppermute | solution.py:28
  100.6 55.8 %collective-permute-start.15 = (bf16[3,256,256]{2,1,0:T(8,128)(2,1)}, bf16[3,256,256]{2,1,0:T(8,128)(2,1)}, u32[]{:S(2)}, u32[]{:S(2)}) collective-permute-start(bf16[3,256,256]{2,1,0:T(8,128)(2,1)} %get-tuple-element.19), channel_id=1, source_target_pairs={{0,24},{8,0},{16,8},{24,16},{32,56},{40,32},{48,40},{56,48},{64,88... | collective-permute-start | bytes 1179656 | tf_op jit(solution)/shard_map/ppermute | solution.py:29
  106.6 49.9 %collective-permute-start.13 = (bf16[3,256,256]{2,1,0:T(8,128)(2,1)}, bf16[3,256,256]{2,1,0:T(8,128)(2,1)}, u32[]{:S(2)}, u32[]{:S(2)}) collective-permute-start(bf16[3,256,256]{2,1,0:T(8,128)(2,1)} %broadcast_select_fusion.10), channel_id=1, source_target_pairs={{0,8},{8,16},{16,24},{24,0},{32,40},{40,48},{48,56},{56,32},{64,72... | collective-permute-start | bytes 1179656 | tf_op jit(solution)/shard_map/ppermute | solution.py:28
  161.1 10.3 %collective-permute-start.18 = (bf16[3,256,256]{2,1,0:T(8,128)(2,1)}, bf16[3,256,256]{2,1,0:T(8,128)(2,1)S(1)}, u32[]{:S(2)}, u32[]{:S(2)}) collective-permute-start(bf16[3,256,256]{2,1,0:T(8,128)(2,1)} %get-tuple-element.27), channel_id=1, source_target_pairs={{0,24},{8,0},{16,8},{24,16},{32,56},{40,32},{48,40},{56,48},{64,88... | collective-permute-start | bytes 1179656 | tf_op jit(solution)/shard_map/ppermute | solution.py:23
  162.0 9.4 %collective-permute-start.16 = (bf16[3,256,256]{2,1,0:T(8,128)(2,1)}, bf16[3,256,256]{2,1,0:T(8,128)(2,1)S(1)}, u32[]{:S(2)}, u32[]{:S(2)}) collective-permute-start(bf16[3,256,256]{2,1,0:T(8,128)(2,1)} %get-tuple-element.30), channel_id=1, source_target_pairs={{0,8},{8,16},{16,24},{24,0},{32,40},{40,48},{48,56},{56,32},{64,72... | collective-permute-start | bytes 1179656 | tf_op jit(solution)/shard_map/ppermute | solution.py:22
  172.5 9.3 %collective-permute-start.19 = (bf16[3,256,256]{2,1,0:T(8,128)(2,1)}, bf16[3,256,256]{2,1,0:T(8,128)(2,1)S(1)}, u32[]{:S(2)}, u32[]{:S(2)}) collective-permute-start(bf16[3,256,256]{2,1,0:T(8,128)(2,1)} %get-tuple-element.25), channel_id=1, source_target_pairs={{0,24},{8,0},{16,8},{24,16},{32,56},{40,32},{48,40},{56,48},{64,88... | collective-permute-start | bytes 1179656 | tf_op jit(solution)/shard_map/ppermute | solution.py:29
  172.5 9.3 %collective-permute-start.17 = (bf16[3,256,256]{2,1,0:T(8,128)(2,1)}, bf16[3,256,256]{2,1,0:T(8,128)(2,1)}, u32[]{:S(2)}, u32[]{:S(2)}) collective-permute-start(bf16[3,256,256]{2,1,0:T(8,128)(2,1)} %get-tuple-element.26), channel_id=1, source_target_pairs={{0,8},{8,16},{16,24},{24,0},{32,40},{40,48},{48,56},{56,32},{64,72... | collective-permute-start | bytes 1179656 | tf_op jit(solution)/shard_map/ppermute | solution.py:28
  175.7 14.0 %collective-permute-start.26 = (bf16[3,256,256]{2,1,0:T(8,128)(2,1)}, bf16[3,256,256]{2,1,0:T(8,128)(2,1)}, u32[]{:S(2)}, u32[]{:S(2)}) collective-permute-start(bf16[3,256,256]{2,1,0:T(8,128)(2,1)} %get-tuple-element.28), channel_id=1, source_target_pairs={{0,96},{8,104},{16,112},{24,120},{32,0},{40,8},{48,16},{56,24},{64... | collective-permute-start | bytes 1179656 | tf_op jit(solution)/shard_map/ppermute | solution.py:23
  178.7 11.1 %collective-permute-start.24 = (bf16[3,256,256]{2,1,0:T(8,128)(2,1)}, bf16[3,256,256]{2,1,0:T(8,128)(2,1)}, u32[]{:S(2)}, u32[]{:S(2)}) collective-permute-start(bf16[3,256,256]{2,1,0:T(8,128)(2,1)} %get-tuple-element.29), channel_id=1, source_target_pairs={{0,32},{8,40},{16,48},{24,56},{32,64},{40,72},{48,80},{56,88},{64,... | collective-permute-start | bytes 1179656 | tf_op jit(solution)/shard_map/ppermute | solution.py:22
  183.7 8.9 %collective-permute-start.22 = (bf16[3,256,256]{2,1,0:T(8,128)(2,1)S(1)}, bf16[3,256,256]{2,1,0:T(8,128)(2,1)S(1)}, u32[]{:S(2)}, u32[]{:S(2)}) collective-permute-start(bf16[3,256,256]{2,1,0:T(8,128)(2,1)S(1)} %select_select_fusion.6), channel_id=1, source_target_pairs={{0,96},{8,104},{16,112},{24,120},{32,0},{40,8},{48,16},{56,24},{64... | collective-permute-start | bytes 1179656 | tf_op jit(solution)/shard_map/ppermute | solution.py:23
  194.9 9.3 %collective-permute-start.25 = (bf16[3,256,256]{2,1,0:T(8,128)(2,1)S(1)}, bf16[3,256,256]{2,1,0:T(8,128)(2,1)S(1)}, u32[]{:S(2)}, u32[]{:S(2)}) collective-permute-start(bf16[3,256,256]{2,1,0:T(8,128)(2,1)S(1)} %get-tuple-element.23), channel_id=1, source_target_pairs={{0,32},{8,40},{16,48},{24,56},{32,64},{40,72},{48,80},{56,88},{64,... | collective-permute-start | bytes 1179656 | tf_op jit(solution)/shard_map/ppermute | solution.py:28
  205.3 9.1 %collective-permute-start.30 = (bf16[3,256,256]{2,1,0:T(8,128)(2,1)S(1)}, bf16[3,256,256]{2,1,0:T(8,128)(2,1)S(1)}, u32[]{:S(2)}, u32[]{:S(2)}) collective-permute-start(bf16[3,256,256]{2,1,0:T(8,128)(2,1)S(1)} %select_select_fusion.2), channel_id=1, source_target_pairs={{0,24},{8,0},{16,8},{24,16},{32,56},{40,32},{48,40},{56,48},{64,88... | collective-permute-start | bytes 1179656 | tf_op jit(solution)/shard_map/ppermute | solution.py:23
  206.8 13.0 %collective-permute-start.20 = (bf16[3,256,256]{2,1,0:T(8,128)(2,1)S(1)}, bf16[3,256,256]{2,1,0:T(8,128)(2,1)S(1)}, u32[]{:S(2)}, u32[]{:S(2)}) collective-permute-start(bf16[3,256,256]{2,1,0:T(8,128)(2,1)S(1)} %get-tuple-element.10), channel_id=1, source_target_pairs={{0,32},{8,40},{16,48},{24,56},{32,64},{40,72},{48,80},{56,88},{64,... | collective-permute-start | bytes 1179656 | tf_op jit(solution)/shard_map/ppermute | solution.py:22
  216.4 10.8 %collective-permute-start.28 = (bf16[3,256,256]{2,1,0:T(8,128)(2,1)S(1)}, bf16[3,256,256]{2,1,0:T(8,128)(2,1)S(1)}, u32[]{:S(2)}, u32[]{:S(2)}) collective-permute-start(bf16[3,256,256]{2,1,0:T(8,128)(2,1)S(1)} %get-tuple-element.12), channel_id=1, source_target_pairs={{0,8},{8,16},{16,24},{24,0},{32,40},{40,48},{48,56},{56,32},{64,72... | collective-permute-start | bytes 1179656 | tf_op jit(solution)/shard_map/ppermute | solution.py:22
  217.6 15.7 %collective-permute-start.23 = (bf16[3,256,256]{2,1,0:T(8,128)(2,1)}, bf16[3,256,256]{2,1,0:T(8,128)(2,1)S(1)}, u32[]{:S(2)}, u32[]{:S(2)}) collective-permute-start(bf16[3,256,256]{2,1,0:T(8,128)(2,1)} %get-tuple-element.9), channel_id=1, source_target_pairs={{0,96},{8,104},{16,112},{24,120},{32,0},{40,8},{48,16},{56,24},{64... | collective-permute-start | bytes 1179656 | tf_op jit(solution)/shard_map/ppermute | solution.py:29
  220.7 13.3 %collective-permute-start.21 = (bf16[3,256,256]{2,1,0:T(8,128)(2,1)}, bf16[3,256,256]{2,1,0:T(8,128)(2,1)}, u32[]{:S(2)}, u32[]{:S(2)}) collective-permute-start(bf16[3,256,256]{2,1,0:T(8,128)(2,1)} %broadcast_select_fusion.8), channel_id=1, source_target_pairs={{0,32},{8,40},{16,48},{24,56},{32,64},{40,72},{48,80},{56,88},{64,... | collective-permute-start | bytes 1179656 | tf_op jit(solution)/shard_map/ppermute | solution.py:28
  220.7 14.7 %collective-permute-start.31 = (bf16[3,256,256]{2,1,0:T(8,128)(2,1)}, bf16[3,256,256]{2,1,0:T(8,128)(2,1)}, u32[]{:S(2)}, u32[]{:S(2)}) collective-permute-start(bf16[3,256,256]{2,1,0:T(8,128)(2,1)} %get-tuple-element.11), channel_id=1, source_target_pairs={{0,24},{8,0},{16,8},{24,16},{32,56},{40,32},{48,40},{56,48},{64,88... | collective-permute-start | bytes 1179656 | tf_op jit(solution)/shard_map/ppermute | solution.py:29
  228.1 8.1 %collective-permute-start.29 = (bf16[3,256,256]{2,1,0:T(8,128)(2,1)}, bf16[3,256,256]{2,1,0:T(8,128)(2,1)}, u32[]{:S(2)}, u32[]{:S(2)}) collective-permute-start(bf16[3,256,256]{2,1,0:T(8,128)(2,1)} %broadcast_select_fusion.2), channel_id=1, source_target_pairs={{0,8},{8,16},{16,24},{24,0},{32,40},{40,48},{48,56},{56,32},{64,72... | collective-permute-start | bytes 1179656 | tf_op jit(solution)/shard_map/ppermute | solution.py:28
  (33 other events, 300.8 us)
Sparse Core Ops, SparseCore 0:
  90.1 64.1 all-reduce.2
  233.4 68.8 all-reduce.4

commit v5 on v2

--- a/solution.py
+++ b/solution.py
@@ -86,6 +86,51 @@
     return jnp.where(dist == 0, on_root_chip, out)
 
 
+ROW_ORDERS = ((3, 2, 1, 0), (1, 0, 3, 2))
+COL_ORDER = (0, 1, 2)
+
+
+def xor_pairs(nrow, ncol, on_row, step):
+    pairs = []
+    for r in range(nrow):
+        for c in range(ncol):
+            if on_row:
+                pairs.append((r * ncol + c, (r ^ (1 << ROW_ORDERS[c % CORES][step])) * ncol + c))
+            else:
+                pairs.append((r * ncol + c, r * ncol + (c ^ (1 << COL_ORDER[step]))))
+    return pairs
+
+
+def xor_bcast(value, root, on_row):
+    nrow = lax.axis_size("row")
+    ncol = lax.axis_size("col")
+    me = lax.axis_index("row") if on_row else lax.axis_index("col")
+    parity = lax.axis_index("col") % CORES
+    steps = (nrow if on_row else ncol).bit_length() - 1
+    relative = me ^ root
+
+    def bit(step):
+        if on_row:
+            b = jnp.where(parity == 0, ROW_ORDERS[0][step], ROW_ORDERS[1][step])
+        else:
+            b = COL_ORDER[step]
+        return (relative >> b) & 1
+
+    shape = value.shape
+    pieces = 1 << steps
+    buf = value.reshape(pieces, -1, shape[-1])
+    axes = ("row", "col")
+    for step in range(steps):
+        half = buf.shape[0] // 2
+        got = lax.ppermute(buf[half:], axes, xor_pairs(nrow, ncol, on_row, step))
+        buf = jnp.where(bit(step) == 1, got, buf[:half])
+    for step in reversed(range(steps)):
+        got = lax.ppermute(buf, axes, xor_pairs(nrow, ncol, on_row, step))
+        low = bit(step) == 0
+        buf = jnp.where(low, jnp.concatenate([buf, got]), jnp.concatenate([got, buf]))
+    return buf.reshape(shape)
+
+
 def lower_local(column, inverse, rows_ok):
     lower = jnp.einsum("iab,bc->iac", column, inverse, preferred_element_type=jnp.float32)
     return jnp.where(rows_ok[:, None, None], lower, 0.0).astype(jnp.bfloat16)
@@ -166,13 +211,13 @@
         lax.dynamic_index_in_dim(front, b1, 1, keepdims=False),
         lax.dynamic_index_in_dim(local, b1, 1, keepdims=False),
     )
-    lower_first = col_bcast(lower_local(column_first, pivot_inv[0], rows_first), first % ncol)
+    lower_first = xor_bcast(lower_local(column_first, pivot_inv[0], rows_first), first % ncol, False)
     a1 = first // nrow
     first_row = masked(
         lax.dynamic_index_in_dim(front, a1, 0, keepdims=False),
         lax.dynamic_index_in_dim(local, a1, 0, keepdims=False),
     )
-    upper_first = row_bcast(first_row, first % nrow)
+    upper_first = xor_bcast(first_row, first % nrow, True)
 
     a2 = second // nrow
     local_row = lax.dynamic_slice_in_dim(local, a2, 1, 0)
@@ -187,7 +232,7 @@
         local_row,
         front_cols,
     )
-    upper_second = row_bcast(row_after[0], second % nrow)
+    upper_second = xor_bcast(row_after[0], second % nrow, True)
     b2 = second // ncol
     local_col = lax.dynamic_slice_in_dim(local, b2, 1, 1)
     col_before = masked(lax.dynamic_slice_in_dim(front, b2, 1, 1), local_col)
@@ -201,7 +246,9 @@
         local_col,
         lax.dynamic_slice_in_dim(front_cols, b2, 1, 0),
     )
-    lower_second = col_bcast(lower_local(col_after[:, 0], pivot_inv[1], rows_second), second % ncol)
+    lower_second = xor_bcast(
+        lower_local(col_after[:, 0], pivot_inv[1], rows_second), second % ncol, False
+    )
 
     keep = local > 0
     update_first = rows_first[:, None] & cols_first[None, :] & keep

time: 232 us -> 180 us (0.78)
  other arithmetic: 41.1 us -> 15.7 us
  waiting for transfers between devices: 98.4 us -> 73.2 us
    ppermute x42 -> x28, waiting for transfers between devices: 98.4 us -> 73.2 us  [the longest x14 38.7 us: xor_bcast(): got = lax.ppermute(buf, axes, xor_pairs(nrow, ncol, on_row, step))]
    select_n x28, other arithmetic: 28.5 us -> 6.18 us  [the longest x14 3.53 us: xor_bcast(): jnp.where(low, jnp.concatenate([buf, got]), jnp.concatenate([got, buf]))]
    slice x2 -> x14, local copies, waits for them, and re-layouts: 1.02 us -> 4.8 us  [the longest x12 3.69 us: xor_bcast(): got = lax.ppermute(buf[half:], axes, xor_pairs(nrow, ncol, on_row, step))]
    concatenate x2 -> x0, other arithmetic: 2.72 us -> none  [row_bcast(): return jnp.concatenate([along_x, along_z], axis=0)]
    ppermute x42 -> x28, starting transfers between devices: 46.4 us -> 46.6 us  [the longest x14 23.7 us: xor_bcast(): got = lax.ppermute(buf, axes, xor_pairs(nrow, ncol, on_row, step))]
  transfers between devices with their start and end apart: 42 -> 28, of which waited for: 22 -> 18; matrix products, arithmetic and copies ran while one was open for 20% -> 12% of each run, Pallas kernels for 0% -> 0%
where the time goes in v5:
time: 180 us; the launch traced here: 179 us
  waiting for transfers between devices  73.2 us (41%)
  starting transfers between devices  46.6 us (26%)
  Pallas kernels  16.7 us (9%)
  other arithmetic  15.7 us (9%)
  local copies, waits for them, and re-layouts  10.6 us (6%)
  matrix products  9.22 us (5%)
  between operations  6.42 us (4%)
    ppermute x14, waiting for transfers between devices, xor_bcast(): got = lax.ppermute(buf, axes, xor_pairs(nrow, ncol, on_row, step))  38.7 us
    ppermute x14, waiting for transfers between devices, xor_bcast(): got = lax.ppermute(buf[half:], axes, xor_pairs(nrow, ncol, on_row, step))  34.5 us
    ppermute x14, starting transfers between devices, xor_bcast(): got = lax.ppermute(buf, axes, xor_pairs(nrow, ncol, on_row, step))  23.7 us
    ppermute x14, starting transfers between devices, xor_bcast(): got = lax.ppermute(buf[half:], axes, xor_pairs(nrow, ncol, on_row, step))  22.9 us
    pallas_call x1, Pallas kernels, both_updates(): pl.pallas_call(update_kernel, grid_spec=pltpu.PrefetchScalarGridSpec(num_...  16.7 us
    dot_general x2, matrix products, lower_local(): jnp.einsum('iab,bc->iac', column, inverse, preferred_element_type=jnp.flo...  6.63 us
    slice x12, local copies, waits for them, and re-layouts, xor_bcast(): got = lax.ppermute(buf[half:], axes, xor_pairs(nrow, ncol, on_row, step))  3.69 us
  transfers between devices with their start and end apart: 28, of which 18 were waited for; matrix products, arithmetic and copies ran while one was open for 12% of the time, Pallas kernels for 0%

profile of v5, /device:TPU:6, one launch (start us, length us, event | category | flops | bytes accessed | tf_op | source)
XLA Modules:
  0.0 178.6 jit_solution(1195607827174782785)
XLA Ops:
  9.4 4.0 %collective-permute-start.6 = (bf16[8,192,256]{2,1,0:T(8,128)(2,1)S(1)}, bf16[8,192,256]{2,1,0:T(8,128)(2,1)S(1)}, u32[]{:S(2)}, u32[]{:S(2)}) collective-permute-start(bf16[8,192,256]{2,1,0:T(8,128)(2,1)S(1)} %bitcast.95), channel_id=1, source_target_pairs={{0,64},{1,17},{2,66},{3,19},{4,68},{5,21},{6,70},{7,23},{8,72},{9,... | collective-permute-start | bytes 2359304 | tf_op jit(solution)/shard_map/ppermute | solution.py:125
  15.2 8.1 %collective-permute-done.6 = bf16[8,192,256]{2,1,0:T(8,128)(2,1)S(1)} collective-permute-done((bf16[8,192,256]{2,1,0:T(8,128)(2,1)S(1)}, bf16[8,192,256]{2,1,0:T(8,128)(2,1)S(1)}, u32[]{:S(2)}, u32[]{:S(2)}) %collective-permute-start.6) | collective-permute-done | bytes 786464 | tf_op jit(solution)/shard_map/ppermute | solution.py:125
  28.9 2.5 %collective-permute-done.7 = bf16[4,192,256]{2,1,0:T(8,128)(2,1)} collective-permute-done((bf16[4,192,256]{2,1,0:T(8,128)(2,1)S(1)}, bf16[4,192,256]{2,1,0:T(8,128)(2,1)}, u32[]{:S(2)}, u32[]{:S(2)}) %collective-permute-start.7) | collective-permute-done | bytes 393248 | tf_op jit(solution)/shard_map/ppermute | solution.py:125
  34.0 5.8 %collective-permute-done.8 = bf16[2,192,256]{2,1,0:T(8,128)(2,1)S(1)} collective-permute-done((bf16[2,192,256]{2,1,0:T(8,128)(2,1)S(1)}, bf16[2,192,256]{2,1,0:T(8,128)(2,1)S(1)}, u32[]{:S(2)}, u32[]{:S(2)}) %collective-permute-start.8) | collective-permute-done | bytes 196640 | tf_op jit(solution)/shard_map/ppermute | solution.py:125
  42.5 2.0 %collective-permute-done.9 = bf16[1,192,256]{2,1,0:T(8,128)(2,1)S(1)} collective-permute-done((bf16[1,192,256]{2,1,0:T(8,128)(2,1)S(1)}, bf16[1,192,256]{2,1,0:T(8,128)(2,1)S(1)}, u32[]{:S(2)}, u32[]{:S(2)}) %collective-permute-start.9) | collective-permute-done | bytes 98336 | tf_op jit(solution)/shard_map/ppermute | solution.py:125
  45.4 3.8 %collective-permute-done.10 = bf16[1,192,256]{2,1,0:T(8,128)(2,1)S(1)} collective-permute-done((bf16[1,192,256]{2,1,0:T(8,128)(2,1)S(1)}, bf16[1,192,256]{2,1,0:T(8,128)(2,1)S(1)}, u32[]{:S(2)}, u32[]{:S(2)}) %collective-permute-start.10) | collective-permute-done | bytes 98336 | tf_op jit(solution)/shard_map/ppermute | solution.py:128
  50.8 3.3 %collective-permute-start.2 = (bf16[1,256,256]{2,1,0:T(8,128)(2,1)S(1)}, bf16[1,256,256]{2,1,0:T(8,128)(2,1)S(1)}, u32[]{:S(2)}, u32[]{:S(2)}) collective-permute-start(bf16[1,256,256]{2,1,0:T(8,128)(2,1)S(1)} %slice.148), channel_id=1, source_target_pairs={{0,4},{1,5},{2,6},{3,7},{4,0},{5,1},{6,2},{7,3},{8,12},{9,13},{10,... | collective-permute-start | bytes 393224 | tf_op jit(solution)/shard_map/ppermute | solution.py:125
  54.1 4.5 %collective-permute-done.11 = bf16[2,192,256]{2,1,0:T(8,128)(2,1)S(1)} collective-permute-done((bf16[2,192,256]{2,1,0:T(8,128)(2,1)S(1)}, bf16[2,192,256]{2,1,0:T(8,128)(2,1)S(1)}, u32[]{:S(2)}, u32[]{:S(2)}) %collective-permute-start.11) | collective-permute-done | bytes 196640 | tf_op jit(solution)/shard_map/ppermute | solution.py:128
  59.2 3.3 %collective-permute-start.3 = (bf16[1,256,256]{2,1,0:T(8,128)(2,1)S(1)}, bf16[1,256,256]{2,1,0:T(8,128)(2,1)S(1)}, u32[]{:S(2)}, u32[]{:S(2)}) collective-permute-start(bf16[1,256,256]{2,1,0:T(8,128)(2,1)S(1)} %slice_select_fusion.9), channel_id=1, source_target_pairs={{0,4},{1,5},{2,6},{3,7},{4,0},{5,1},{6,2},{7,3},{8,12},{9,13},{10,... | collective-permute-start | bytes 393224 | tf_op jit(solution)/shard_map/ppermute | solution.py:128
  62.5 4.6 %collective-permute-done.3 = bf16[1,256,256]{2,1,0:T(8,128)(2,1)S(1)} collective-permute-done((bf16[1,256,256]{2,1,0:T(8,128)(2,1)S(1)}, bf16[1,256,256]{2,1,0:T(8,128)(2,1)S(1)}, u32[]{:S(2)}, u32[]{:S(2)}) %collective-permute-start.3) | collective-permute-done | bytes 131104 | tf_op jit(solution)/shard_map/ppermute | solution.py:128
  68.5 3.2 %collective-permute-start.13 = (bf16[8,192,256]{2,1,0:T(8,128)(2,1)S(1)}, bf16[8,192,256]{2,1,0:T(8,128)(2,1)S(1)}, u32[]{:S(2)}, u32[]{:S(2)}) collective-permute-start(bf16[8,192,256]{2,1,0:T(8,128)(2,1)S(1)} %maximum_select_fusion.5), channel_id=1, source_target_pairs={{0,64},{1,17},{2,66},{3,19},{4,68},{5,21},{6,70},{7,23},{8,72},{9,... | collective-permute-start | bytes 2359304 | tf_op jit(solution)/shard_map/ppermute | solution.py:128
  71.7 1.9 %collective-permute-done.4 = bf16[2,256,256]{2,1,0:T(8,128)(2,1)S(1)} collective-permute-done((bf16[2,256,256]{2,1,0:T(8,128)(2,1)S(1)}, bf16[2,256,256]{2,1,0:T(8,128)(2,1)S(1)}, u32[]{:S(2)}, u32[]{:S(2)}) %collective-permute-start.4) | collective-permute-done | bytes 262176 | tf_op jit(solution)/shard_map/ppermute | solution.py:128
  74.4 1.7 and_and_fusion
  76.9 5.1 %collective-permute-done.13 = bf16[8,192,256]{2,1,0:T(8,128)(2,1)S(1)} collective-permute-done((bf16[8,192,256]{2,1,0:T(8,128)(2,1)S(1)}, bf16[8,192,256]{2,1,0:T(8,128)(2,1)S(1)}, u32[]{:S(2)}, u32[]{:S(2)}) %collective-permute-start.13) | collective-permute-done | bytes 786464 | tf_op jit(solution)/shard_map/ppermute | solution.py:128
  82.3 2.6 %broadcast_select_fusion = bf16[1,12,256,256]{3,2,1,0:T(8,128)(2,1)S(1)} fusion(pred[12]{0:T(512)(128)(4,1)S(1)} %get-tuple-element.23, bf16[256,256]{1,0:T(8,128)(2,1)S(1)} %dynamic-slice_bitcast_fusion, bf16[12,256,256]{2,1,0:T(8,128)(2,1)S(1)} %bitcast.88, bf16[8,12,256,256]{3,2,1,0:T(8,128)(2,1)} %front_ref.1, s32[]{:T(128)S(6)} %select_n.443, ...), kind=kOutput, calls=%fused_computation.10 | convolution fusion | flops 407371776 | bytes 4983296 | tf_op jit(solution)/shard_map/iab,jbc->ijac/dot_general | solution.py:140
  85.9 3.2 %collective-permute-start.20 = (bf16[8,192,256]{2,1,0:T(8,128)(2,1)}, bf16[8,192,256]{2,1,0:T(8,128)(2,1)S(1)}, u32[]{:S(2)}, u32[]{:S(2)}) collective-permute-start(bf16[8,192,256]{2,1,0:T(8,128)(2,1)} %bitcast.26), channel_id=1, source_target_pairs={{0,64},{1,17},{2,66},{3,19},{4,68},{5,21},{6,70},{7,23},{8,72},{9,... | collective-permute-start | bytes 2359304 | tf_op jit(solution)/shard_map/ppermute | solution.py:125
  89.7 1.9 %fusion.35 = (pred[8]{0:T(512)(128)(4,1)}, pred[8]{0:T(512)(128)(4,1)}) fusion(pred[8,1,1,1]{1,0,3,2:T(8,128)(4,1)S(1)} %get-tuple-element.19, s32[]{:T(128)} %bitcast.1, s32[]{:T(128)S(6)} %axis_index.15, pred[]{:T(512)} %bitcast.9), kind=kLoop, calls=%fused_computation.75 | loop fusion | flops 40 | bytes 33 | tf_op jit(solution)/shard_map/and | solution.py:141
  92.2 7.4 %collective-permute-done.20 = bf16[8,192,256]{2,1,0:T(8,128)(2,1)S(1)} collective-permute-done((bf16[8,192,256]{2,1,0:T(8,128)(2,1)}, bf16[8,192,256]{2,1,0:T(8,128)(2,1)S(1)}, u32[]{:S(2)}, u32[]{:S(2)}) %collective-permute-start.20) | collective-permute-done | bytes 786464 | tf_op jit(solution)/shard_map/ppermute | solution.py:125
  103.1 4.9 %select_convert_fusion = bf16[8,256,256]{2,1,0:T(8,128)(2,1)} fusion(bf16[4,1,256,256]{3,2,0,1:T(8,128)(2,1)} %bitcast.96, bf16[4,1,256,256]{3,2,0,1:T(8,128)(2,1)} %bitcast.94, pred[8]{0:T(512)(128)(4,1)S(1)} %copy-done.7, pred[8]{0:T(512)(128)(4,1)S(1)} %compare_and_fusion.1, pred[]{:T(512)S(6)} %eq.137, bf16[8,12,256,256]{3,2,1,0:T(8,128)(2,1)} %front_ref.1, ...), kind=kOutput, calls=%fused_computation.5 | convolution fusion | flops 547356672 | bytes 4460544 | tf_op jit(solution)/shard_map/iab,bc->iac/dot_general | solution.py:135
  108.1 2.0 %slice.158 = bf16[4,256,256]{2,1,0:T(8,128)(2,1)} slice(bf16[8,256,256]{2,1,0:T(8,128)(2,1)} %select_convert_fusion), slice={[4:8], [0:256], [0:256]} | slice | bytes 1048576 | tf_op jit(solution)/shard_map/slice | solution.py:125
  112.3 5.5 %collective-permute-done.22 = bf16[2,192,256]{2,1,0:T(8,128)(2,1)S(1)} collective-permute-done((bf16[2,192,256]{2,1,0:T(8,128)(2,1)S(1)}, bf16[2,192,256]{2,1,0:T(8,128)(2,1)S(1)}, u32[]{:S(2)}, u32[]{:S(2)}) %collective-permute-start.22) | collective-permute-done | bytes 196640 | tf_op jit(solution)/shard_map/ppermute | solution.py:125
  120.1 2.5 %collective-permute-done.23 = bf16[1,192,256]{2,1,0:T(8,128)(2,1)S(1)} collective-permute-done((bf16[1,192,256]{2,1,0:T(8,128)(2,1)S(1)}, bf16[1,192,256]{2,1,0:T(8,128)(2,1)S(1)}, u32[]{:S(2)}, u32[]{:S(2)}) %collective-permute-start.23) | collective-permute-done | bytes 98336 | tf_op jit(solution)/shard_map/ppermute | solution.py:125
  123.6 3.8 %collective-permute-done.24 = bf16[1,192,256]{2,1,0:T(8,128)(2,1)S(1)} collective-permute-done((bf16[1,192,256]{2,1,0:T(8,128)(2,1)S(1)}, bf16[1,192,256]{2,1,0:T(8,128)(2,1)S(1)}, u32[]{:S(2)}, u32[]{:S(2)}) %collective-permute-start.24) | collective-permute-done | bytes 98336 | tf_op jit(solution)/shard_map/ppermute | solution.py:128
  129.1 2.3 %collective-permute-start.16 = (bf16[1,256,256]{2,1,0:T(8,128)(2,1)S(1)}, bf16[1,256,256]{2,1,0:T(8,128)(2,1)S(1)}, u32[]{:S(2)}, u32[]{:S(2)}) collective-permute-start(bf16[1,256,256]{2,1,0:T(8,128)(2,1)S(1)} %slice.162), channel_id=1, source_target_pairs={{0,4},{1,5},{2,6},{3,7},{4,0},{5,1},{6,2},{7,3},{8,12},{9,13},{10,... | collective-permute-start | bytes 393224 | tf_op jit(solution)/shard_map/ppermute | solution.py:125
  131.5 3.1 %collective-permute-done.25 = bf16[2,192,256]{2,1,0:T(8,128)(2,1)S(1)} collective-permute-done((bf16[2,192,256]{2,1,0:T(8,128)(2,1)S(1)}, bf16[2,192,256]{2,1,0:T(8,128)(2,1)S(1)}, u32[]{:S(2)}, u32[]{:S(2)}) %collective-permute-start.25) | collective-permute-done | bytes 196640 | tf_op jit(solution)/shard_map/ppermute | solution.py:128
  134.7 2.1 %collective-permute-start.26 = (bf16[4,192,256]{2,1,0:T(8,128)(2,1)S(1)}, bf16[4,192,256]{2,1,0:T(8,128)(2,1)S(1)}, u32[]{:S(2)}, u32[]{:S(2)}) collective-permute-start(bf16[4,192,256]{2,1,0:T(8,128)(2,1)S(1)} %maximum_select_fusion.10), channel_id=1, source_target_pairs={{0,32},{1,9},{2,34},{3,11},{4,36},{5,13},{6,38},{7,15},{8,40},{9,1... | collective-permute-start | bytes 1179656 | tf_op jit(solution)/shard_map/ppermute | solution.py:128
  136.8 3.2 %collective-permute-start.17 = (bf16[1,256,256]{2,1,0:T(8,128)(2,1)S(1)}, bf16[1,256,256]{2,1,0:T(8,128)(2,1)S(1)}, u32[]{:S(2)}, u32[]{:S(2)}) collective-permute-start(bf16[1,256,256]{2,1,0:T(8,128)(2,1)S(1)} %slice_select_fusion.8), channel_id=1, source_target_pairs={{0,4},{1,5},{2,6},{3,7},{4,0},{5,1},{6,2},{7,3},{8,12},{9,13},{10,... | collective-permute-start | bytes 393224 | tf_op jit(solution)/shard_map/ppermute | solution.py:128
  140.0 4.4 %collective-permute-done.17 = bf16[1,256,256]{2,1,0:T(8,128)(2,1)S(1)} collective-permute-done((bf16[1,256,256]{2,1,0:T(8,128)(2,1)S(1)}, bf16[1,256,256]{2,1,0:T(8,128)(2,1)S(1)}, u32[]{:S(2)}, u32[]{:S(2)}) %collective-permute-start.17) | collective-permute-done | bytes 131104 | tf_op jit(solution)/shard_map/ppermute | solution.py:128
  144.4 2.2 %collective-permute-start.18 = (bf16[2,256,256]{2,1,0:T(8,128)(2,1)S(1)}, bf16[2,256,256]{2,1,0:T(8,128)(2,1)S(1)}, u32[]{:S(2)}, u32[]{:S(2)}) collective-permute-start(bf16[2,256,256]{2,1,0:T(8,128)(2,1)S(1)} %maximum_select_fusion.12), channel_id=1, source_target_pairs={{0,2},{1,3},{2,0},{3,1},{4,6},{5,7},{6,4},{7,5},{8,10},{9,11},{10,... | collective-permute-start | bytes 786440 | tf_op jit(solution)/shard_map/ppermute | solution.py:128
  146.9 2.8 %collective-permute-start.27 = (bf16[8,192,256]{2,1,0:T(8,128)(2,1)S(1)}, bf16[8,192,256]{2,1,0:T(8,128)(2,1)S(1)}, u32[]{:S(2)}, u32[]{:S(2)}) collective-permute-start(bf16[8,192,256]{2,1,0:T(8,128)(2,1)S(1)} %maximum_select_fusion.6), channel_id=1, source_target_pairs={{0,64},{1,17},{2,66},{3,19},{4,68},{5,21},{6,70},{7,23},{8,72},{9,... | collective-permute-start | bytes 2359304 | tf_op jit(solution)/shard_map/ppermute | solution.py:128
  154.2 6.3 %collective-permute-done.27 = bf16[8,192,256]{2,1,0:T(8,128)(2,1)S(1)} collective-permute-done((bf16[8,192,256]{2,1,0:T(8,128)(2,1)S(1)}, bf16[8,192,256]{2,1,0:T(8,128)(2,1)S(1)}, u32[]{:S(2)}, u32[]{:S(2)}) %collective-permute-start.27) | collective-permute-done | bytes 786464 | tf_op jit(solution)/shard_map/ppermute | solution.py:128
  161.9 16.7 %shard_map.46 = bf16[8,12,256,256]{3,2,1,0:T(8,128)(2,1)} custom-call(s32[8,12]{1,0:T(8,128)} %select_add_fusion.codes, bf16[8,12,256,256]{3,2,1,0:T(8,128)(2,1)} %front_ref.1, bf16[8,256,256]{2,1,0:T(8,128)(2,1)} %copy-done.1, bf16[8,256,256]{2,1,0:T(8,128)(2,1)} %maximum_select_fusion.4.l2_ref, bf16[12,256,256]{2,1,0:T(8,128)(2,1)} %bitcast.90, ...), custom_call_target="tpu_custom_call" | custom-call | tf_op jit(solution)/shard_map/pallas_call | solution.py:172
  (107 shorter events, 41.4 us)
Async XLA Ops:
  9.4 13.9 %collective-permute-start.6 = (bf16[8,192,256]{2,1,0:T(8,128)(2,1)S(1)}, bf16[8,192,256]{2,1,0:T(8,128)(2,1)S(1)}, u32[]{:S(2)}, u32[]{:S(2)}) collective-permute-start(bf16[8,192,256]{2,1,0:T(8,128)(2,1)S(1)} %bitcast.95), channel_id=1, source_target_pairs={{0,64},{1,17},{2,66},{3,19},{4,68},{5,21},{6,70},{7,23},{8,72},{9,... | collective-permute-start | bytes 2359304 | tf_op jit(solution)/shard_map/ppermute | solution.py:125
  23.5 8.0 %collective-permute-start.7 = (bf16[4,192,256]{2,1,0:T(8,128)(2,1)S(1)}, bf16[4,192,256]{2,1,0:T(8,128)(2,1)}, u32[]{:S(2)}, u32[]{:S(2)}) collective-permute-start(bf16[4,192,256]{2,1,0:T(8,128)(2,1)S(1)} %slice.152), channel_id=1, source_target_pairs={{0,32},{1,9},{2,34},{3,11},{4,36},{5,13},{6,38},{7,15},{8,40},{9,1... | collective-permute-start | bytes 1179656 | tf_op jit(solution)/shard_map/ppermute | solution.py:125
  28.9 11.8 %collective-permute-start = (bf16[4,256,256]{2,1,0:T(8,128)(2,1)}, bf16[4,256,256]{2,1,0:T(8,128)(2,1)S(1)}, u32[]{:S(2)}, u32[]{:S(2)}) collective-permute-start(bf16[4,256,256]{2,1,0:T(8,128)(2,1)} %slice.144), channel_id=1, source_target_pairs={{0,1},{1,0},{2,3},{3,2},{4,5},{5,4},{6,7},{7,6},{8,9},{9,8},{10,11... | collective-permute-start | bytes 1572872 | tf_op jit(solution)/shard_map/ppermute | solution.py:125
  32.5 7.3 %collective-permute-start.8 = (bf16[2,192,256]{2,1,0:T(8,128)(2,1)S(1)}, bf16[2,192,256]{2,1,0:T(8,128)(2,1)S(1)}, u32[]{:S(2)}, u32[]{:S(2)}) collective-permute-start(bf16[2,192,256]{2,1,0:T(8,128)(2,1)S(1)} %slice.154), channel_id=1, source_target_pairs={{0,16},{1,65},{2,18},{3,67},{4,20},{5,69},{6,22},{7,71},{8,24},{9,... | collective-permute-start | bytes 589832 | tf_op jit(solution)/shard_map/ppermute | solution.py:125
  39.8 4.7 %collective-permute-start.9 = (bf16[1,192,256]{2,1,0:T(8,128)(2,1)S(1)}, bf16[1,192,256]{2,1,0:T(8,128)(2,1)S(1)}, u32[]{:S(2)}, u32[]{:S(2)}) collective-permute-start(bf16[1,192,256]{2,1,0:T(8,128)(2,1)S(1)} %slice.156), channel_id=1, source_target_pairs={{0,8},{1,33},{2,10},{3,35},{4,12},{5,37},{6,14},{7,39},{8,0},{9,41... | collective-permute-start | bytes 294920 | tf_op jit(solution)/shard_map/ppermute | solution.py:125
  40.8 9.9 %collective-permute-start.1 = (bf16[2,256,256]{2,1,0:T(8,128)(2,1)S(1)}, bf16[2,256,256]{2,1,0:T(8,128)(2,1)S(1)}, u32[]{:S(2)}, u32[]{:S(2)}) collective-permute-start(bf16[2,256,256]{2,1,0:T(8,128)(2,1)S(1)} %slice.146), channel_id=1, source_target_pairs={{0,2},{1,3},{2,0},{3,1},{4,6},{5,7},{6,4},{7,5},{8,10},{9,11},{10,... | collective-permute-start | bytes 786440 | tf_op jit(solution)/shard_map/ppermute | solution.py:125
  44.5 4.7 %collective-permute-start.10 = (bf16[1,192,256]{2,1,0:T(8,128)(2,1)S(1)}, bf16[1,192,256]{2,1,0:T(8,128)(2,1)S(1)}, u32[]{:S(2)}, u32[]{:S(2)}) collective-permute-start(bf16[1,192,256]{2,1,0:T(8,128)(2,1)S(1)} %slice_select_fusion.11), channel_id=1, source_target_pairs={{0,8},{1,33},{2,10},{3,35},{4,12},{5,37},{6,14},{7,39},{8,0},{9,41... | collective-permute-start | bytes 294920 | tf_op jit(solution)/shard_map/ppermute | solution.py:128
  49.2 9.4 %collective-permute-start.11 = (bf16[2,192,256]{2,1,0:T(8,128)(2,1)S(1)}, bf16[2,192,256]{2,1,0:T(8,128)(2,1)S(1)}, u32[]{:S(2)}, u32[]{:S(2)}) collective-permute-start(bf16[2,192,256]{2,1,0:T(8,128)(2,1)S(1)} %maximum_select_fusion.13), channel_id=1, source_target_pairs={{0,16},{1,65},{2,18},{3,67},{4,20},{5,69},{6,22},{7,71},{8,24},{9,... | collective-permute-start | bytes 589832 | tf_op jit(solution)/shard_map/ppermute | solution.py:128
  50.8 8.4 %collective-permute-start.2 = (bf16[1,256,256]{2,1,0:T(8,128)(2,1)S(1)}, bf16[1,256,256]{2,1,0:T(8,128)(2,1)S(1)}, u32[]{:S(2)}, u32[]{:S(2)}) collective-permute-start(bf16[1,256,256]{2,1,0:T(8,128)(2,1)S(1)} %slice.148), channel_id=1, source_target_pairs={{0,4},{1,5},{2,6},{3,7},{4,0},{5,1},{6,2},{7,3},{8,12},{9,13},{10,... | collective-permute-start | bytes 393224 | tf_op jit(solution)/shard_map/ppermute | solution.py:125
  58.6 9.7 %collective-permute-start.12 = (bf16[4,192,256]{2,1,0:T(8,128)(2,1)S(1)}, bf16[4,192,256]{2,1,0:T(8,128)(2,1)S(1)}, u32[]{:S(2)}, u32[]{:S(2)}) collective-permute-start(bf16[4,192,256]{2,1,0:T(8,128)(2,1)S(1)} %maximum_select_fusion.9), channel_id=1, source_target_pairs={{0,32},{1,9},{2,34},{3,11},{4,36},{5,13},{6,38},{7,15},{8,40},{9,1... | collective-permute-start | bytes 1179656 | tf_op jit(solution)/shard_map/ppermute | solution.py:128
  59.2 7.9 %collective-permute-start.3 = (bf16[1,256,256]{2,1,0:T(8,128)(2,1)S(1)}, bf16[1,256,256]{2,1,0:T(8,128)(2,1)S(1)}, u32[]{:S(2)}, u32[]{:S(2)}) collective-permute-start(bf16[1,256,256]{2,1,0:T(8,128)(2,1)S(1)} %slice_select_fusion.9), channel_id=1, source_target_pairs={{0,4},{1,5},{2,6},{3,7},{4,0},{5,1},{6,2},{7,3},{8,12},{9,13},{10,... | collective-permute-start | bytes 393224 | tf_op jit(solution)/shard_map/ppermute | solution.py:128
  67.1 6.5 %collective-permute-start.4 = (bf16[2,256,256]{2,1,0:T(8,128)(2,1)S(1)}, bf16[2,256,256]{2,1,0:T(8,128)(2,1)S(1)}, u32[]{:S(2)}, u32[]{:S(2)}) collective-permute-start(bf16[2,256,256]{2,1,0:T(8,128)(2,1)S(1)} %maximum_select_fusion.11), channel_id=1, source_target_pairs={{0,2},{1,3},{2,0},{3,1},{4,6},{5,7},{6,4},{7,5},{8,10},{9,11},{10,... | collective-permute-start | bytes 786440 | tf_op jit(solution)/shard_map/ppermute | solution.py:128
  68.5 13.6 %collective-permute-start.13 = (bf16[8,192,256]{2,1,0:T(8,128)(2,1)S(1)}, bf16[8,192,256]{2,1,0:T(8,128)(2,1)S(1)}, u32[]{:S(2)}, u32[]{:S(2)}) collective-permute-start(bf16[8,192,256]{2,1,0:T(8,128)(2,1)S(1)} %maximum_select_fusion.5), channel_id=1, source_target_pairs={{0,64},{1,17},{2,66},{3,19},{4,68},{5,21},{6,70},{7,23},{8,72},{9,... | collective-permute-start | bytes 2359304 | tf_op jit(solution)/shard_map/ppermute | solution.py:128
  73.7 2.4 %collective-permute-start.5 = (bf16[4,256,256]{2,1,0:T(8,128)(2,1)S(1)}, bf16[4,256,256]{2,1,0:T(8,128)(2,1)S(1)}, u32[]{:S(2)}, u32[]{:S(2)}) collective-permute-start(bf16[4,256,256]{2,1,0:T(8,128)(2,1)S(1)} %maximum_select_fusion.7), channel_id=1, source_target_pairs={{0,1},{1,0},{2,3},{3,2},{4,5},{5,4},{6,7},{7,6},{8,9},{9,8},{10,11... | collective-permute-start | bytes 1572872 | tf_op jit(solution)/shard_map/ppermute | solution.py:128
  76.3 6.0 %copy-start.1 = (bf16[8,256,256]{2,1,0:T(8,128)(2,1)}, bf16[8,256,256]{2,1,0:T(8,128)(2,1)S(1)}, u32[]{:S(2)}) copy-start(bf16[8,256,256]{2,1,0:T(8,128)(2,1)S(1)} %maximum_select_fusion.2.l1_ref) | copy-start | bytes 3145732
  82.3 20.9 %copy-start = (bf16[16,192,256]{2,1,0:T(8,128)(2,1)}, bf16[16,192,256]{2,1,0:T(8,128)(2,1)S(1)}, u32[]{:S(2)}) copy-start(bf16[16,192,256]{2,1,0:T(8,128)(2,1)S(1)} %maximum_select_fusion) | copy-start | bytes 4718596
  85.9 13.7 %collective-permute-start.20 = (bf16[8,192,256]{2,1,0:T(8,128)(2,1)}, bf16[8,192,256]{2,1,0:T(8,128)(2,1)S(1)}, u32[]{:S(2)}, u32[]{:S(2)}) collective-permute-start(bf16[8,192,256]{2,1,0:T(8,128)(2,1)} %bitcast.26), channel_id=1, source_target_pairs={{0,64},{1,17},{2,66},{3,19},{4,68},{5,21},{6,70},{7,23},{8,72},{9,... | collective-permute-start | bytes 2359304 | tf_op jit(solution)/shard_map/ppermute | solution.py:125
  102.5 8.1 %collective-permute-start.21 = (bf16[4,192,256]{2,1,0:T(8,128)(2,1)}, bf16[4,192,256]{2,1,0:T(8,128)(2,1)}, u32[]{:S(2)}, u32[]{:S(2)}) collective-permute-start(bf16[4,192,256]{2,1,0:T(8,128)(2,1)} %slice.166), channel_id=1, source_target_pairs={{0,32},{1,9},{2,34},{3,11},{4,36},{5,13},{6,38},{7,15},{8,40},{9,1... | collective-permute-start | bytes 1179656 | tf_op jit(solution)/shard_map/ppermute | solution.py:125
  108.1 10.8 %copy-start.3 = (bf16[8,256,256]{2,1,0:T(8,128)(2,1)S(1)}, bf16[8,256,256]{2,1,0:T(8,128)(2,1)}, u32[]{:S(2)}) copy-start(bf16[8,256,256]{2,1,0:T(8,128)(2,1)} %select_convert_fusion) | copy-start | bytes 3145732
  110.0 8.8 %collective-permute-start.14 = (bf16[4,256,256]{2,1,0:T(8,128)(2,1)}, bf16[4,256,256]{2,1,0:T(8,128)(2,1)S(1)}, u32[]{:S(2)}, u32[]{:S(2)}) collective-permute-start(bf16[4,256,256]{2,1,0:T(8,128)(2,1)} %slice.158), channel_id=1, source_target_pairs={{0,1},{1,0},{2,3},{3,2},{4,5},{5,4},{6,7},{7,6},{8,9},{9,8},{10,11... | collective-permute-start | bytes 1572872 | tf_op jit(solution)/shard_map/ppermute | solution.py:125
  110.6 7.3 %collective-permute-start.22 = (bf16[2,192,256]{2,1,0:T(8,128)(2,1)S(1)}, bf16[2,192,256]{2,1,0:T(8,128)(2,1)S(1)}, u32[]{:S(2)}, u32[]{:S(2)}) collective-permute-start(bf16[2,192,256]{2,1,0:T(8,128)(2,1)S(1)} %slice.168), channel_id=1, source_target_pairs={{0,16},{1,65},{2,18},{3,67},{4,20},{5,69},{6,22},{7,71},{8,24},{9,... | collective-permute-start | bytes 589832 | tf_op jit(solution)/shard_map/ppermute | solution.py:125
  117.9 4.7 %collective-permute-start.23 = (bf16[1,192,256]{2,1,0:T(8,128)(2,1)S(1)}, bf16[1,192,256]{2,1,0:T(8,128)(2,1)S(1)}, u32[]{:S(2)}, u32[]{:S(2)}) collective-permute-start(bf16[1,192,256]{2,1,0:T(8,128)(2,1)S(1)} %slice.170), channel_id=1, source_target_pairs={{0,8},{1,33},{2,10},{3,35},{4,12},{5,37},{6,14},{7,39},{8,0},{9,41... | collective-permute-start | bytes 294920 | tf_op jit(solution)/shard_map/ppermute | solution.py:125
  118.9 10.1 %collective-permute-start.15 = (bf16[2,256,256]{2,1,0:T(8,128)(2,1)S(1)}, bf16[2,256,256]{2,1,0:T(8,128)(2,1)S(1)}, u32[]{:S(2)}, u32[]{:S(2)}) collective-permute-start(bf16[2,256,256]{2,1,0:T(8,128)(2,1)S(1)} %slice.160), channel_id=1, source_target_pairs={{0,2},{1,3},{2,0},{3,1},{4,6},{5,7},{6,4},{7,5},{8,10},{9,11},{10,... | collective-permute-start | bytes 786440 | tf_op jit(solution)/shard_map/ppermute | solution.py:125
  122.6 4.7 %collective-permute-start.24 = (bf16[1,192,256]{2,1,0:T(8,128)(2,1)S(1)}, bf16[1,192,256]{2,1,0:T(8,128)(2,1)S(1)}, u32[]{:S(2)}, u32[]{:S(2)}) collective-permute-start(bf16[1,192,256]{2,1,0:T(8,128)(2,1)S(1)} %slice_select_fusion.10), channel_id=1, source_target_pairs={{0,8},{1,33},{2,10},{3,35},{4,12},{5,37},{6,14},{7,39},{8,0},{9,41... | collective-permute-start | bytes 294920 | tf_op jit(solution)/shard_map/ppermute | solution.py:128
  127.4 7.3 %collective-permute-start.25 = (bf16[2,192,256]{2,1,0:T(8,128)(2,1)S(1)}, bf16[2,192,256]{2,1,0:T(8,128)(2,1)S(1)}, u32[]{:S(2)}, u32[]{:S(2)}) collective-permute-start(bf16[2,192,256]{2,1,0:T(8,128)(2,1)S(1)} %maximum_select_fusion.14), channel_id=1, source_target_pairs={{0,16},{1,65},{2,18},{3,67},{4,20},{5,69},{6,22},{7,71},{8,24},{9,... | collective-permute-start | bytes 589832 | tf_op jit(solution)/shard_map/ppermute | solution.py:128
  129.1 7.6 %collective-permute-start.16 = (bf16[1,256,256]{2,1,0:T(8,128)(2,1)S(1)}, bf16[1,256,256]{2,1,0:T(8,128)(2,1)S(1)}, u32[]{:S(2)}, u32[]{:S(2)}) collective-permute-start(bf16[1,256,256]{2,1,0:T(8,128)(2,1)S(1)} %slice.162), channel_id=1, source_target_pairs={{0,4},{1,5},{2,6},{3,7},{4,0},{5,1},{6,2},{7,3},{8,12},{9,13},{10,... | collective-permute-start | bytes 393224 | tf_op jit(solution)/shard_map/ppermute | solution.py:125
  134.7 12.1 %collective-permute-start.26 = (bf16[4,192,256]{2,1,0:T(8,128)(2,1)S(1)}, bf16[4,192,256]{2,1,0:T(8,128)(2,1)S(1)}, u32[]{:S(2)}, u32[]{:S(2)}) collective-permute-start(bf16[4,192,256]{2,1,0:T(8,128)(2,1)S(1)} %maximum_select_fusion.10), channel_id=1, source_target_pairs={{0,32},{1,9},{2,34},{3,11},{4,36},{5,13},{6,38},{7,15},{8,40},{9,1... | collective-permute-start | bytes 1179656 | tf_op jit(solution)/shard_map/ppermute | solution.py:128
  136.8 7.6 %collective-permute-start.17 = (bf16[1,256,256]{2,1,0:T(8,128)(2,1)S(1)}, bf16[1,256,256]{2,1,0:T(8,128)(2,1)S(1)}, u32[]{:S(2)}, u32[]{:S(2)}) collective-permute-start(bf16[1,256,256]{2,1,0:T(8,128)(2,1)S(1)} %slice_select_fusion.8), channel_id=1, source_target_pairs={{0,4},{1,5},{2,6},{3,7},{4,0},{5,1},{6,2},{7,3},{8,12},{9,13},{10,... | collective-permute-start | bytes 393224 | tf_op jit(solution)/shard_map/ppermute | solution.py:128
  140.0 12.4 %copy-start.6 = (pred[12]{0:T(512)(128)(4,1)S(1)}, pred[12]{0:T(512)(128)(4,1)}, u32[]{:S(2)}) copy-start(pred[12]{0:T(512)(128)(4,1)} %get-tuple-element.24) | copy-start | bytes 40
  144.4 6.5 %collective-permute-start.18 = (bf16[2,256,256]{2,1,0:T(8,128)(2,1)S(1)}, bf16[2,256,256]{2,1,0:T(8,128)(2,1)S(1)}, u32[]{:S(2)}, u32[]{:S(2)}) collective-permute-start(bf16[2,256,256]{2,1,0:T(8,128)(2,1)S(1)} %maximum_select_fusion.12), channel_id=1, source_target_pairs={{0,2},{1,3},{2,0},{3,1},{4,6},{5,7},{6,4},{7,5},{8,10},{9,11},{10,... | collective-permute-start | bytes 786440 | tf_op jit(solution)/shard_map/ppermute | solution.py:128
  146.9 13.6 %collective-permute-start.27 = (bf16[8,192,256]{2,1,0:T(8,128)(2,1)S(1)}, bf16[8,192,256]{2,1,0:T(8,128)(2,1)S(1)}, u32[]{:S(2)}, u32[]{:S(2)}) collective-permute-start(bf16[8,192,256]{2,1,0:T(8,128)(2,1)S(1)} %maximum_select_fusion.6), channel_id=1, source_target_pairs={{0,64},{1,17},{2,66},{3,19},{4,68},{5,21},{6,70},{7,23},{8,72},{9,... | collective-permute-start | bytes 2359304 | tf_op jit(solution)/shard_map/ppermute | solution.py:128
  151.0 2.0 %collective-permute-start.19 = (bf16[4,256,256]{2,1,0:T(8,128)(2,1)S(1)}, bf16[4,256,256]{2,1,0:T(8,128)(2,1)S(1)}, u32[]{:S(2)}, u32[]{:S(2)}) collective-permute-start(bf16[4,256,256]{2,1,0:T(8,128)(2,1)S(1)} %maximum_select_fusion.8), channel_id=1, source_target_pairs={{0,1},{1,0},{2,3},{3,2},{4,5},{5,4},{6,7},{7,6},{8,9},{9,8},{10,11... | collective-permute-start | bytes 1572872 | tf_op jit(solution)/shard_map/ppermute | solution.py:128
  (5 other events, 10.0 us)

commit v6 on v5

--- a/solution.py
+++ b/solution.py
@@ -7,6 +7,10 @@
 
 RING = 4
 CORES = 2
+
+
+def per_part(cond, a, b):
+    return jnp.where(cond.reshape((-1,) + (1,) * (a.ndim - 1)), a, b)
 
 
 def pick(index, options):
@@ -118,17 +122,28 @@
 
     shape = value.shape
     pieces = 1 << steps
-    buf = value.reshape(pieces, -1, shape[-1])
+    buf = value.reshape(shape[0], pieces, -1, shape[-1])
     axes = ("row", "col")
     for step in range(steps):
-        half = buf.shape[0] // 2
-        got = lax.ppermute(buf[half:], axes, xor_pairs(nrow, ncol, on_row, step))
-        buf = jnp.where(bit(step) == 1, got, buf[:half])
+        half = buf.shape[1] // 2
+        got = lax.ppermute(buf[:, half:], axes, xor_pairs(nrow, ncol, on_row, step))
+        buf = per_part(bit(step) == 1, got, buf[:, :half])
     for step in reversed(range(steps)):
         got = lax.ppermute(buf, axes, xor_pairs(nrow, ncol, on_row, step))
         low = bit(step) == 0
-        buf = jnp.where(low, jnp.concatenate([buf, got]), jnp.concatenate([got, buf]))
+        buf = per_part(low, jnp.concatenate([buf, got], 1), jnp.concatenate([got, buf], 1))
     return buf.reshape(shape)
+
+
+def all_bcast(value, root):
+    nrow = lax.axis_size("row")
+    ncol = lax.axis_size("col")
+    n = nrow * ncol
+    relative = (lax.axis_index("row") * ncol + lax.axis_index("col")) ^ root
+    for b in range(n.bit_length() - 1):
+        got = lax.ppermute(value, ("row", "col"), [(d, d ^ (1 << b)) for d in range(n)])
+        value = per_part((relative >> b) == 1, got, value)
+    return value
 
 
 def lower_local(column, inverse, rows_ok):
@@ -206,49 +221,59 @@
     rows_second = rows_first & (front_rows != second)
     cols_second = cols_first & (front_cols != second)
 
-    b1 = first // ncol
-    column_first = masked(
-        lax.dynamic_index_in_dim(front, b1, 1, keepdims=False),
-        lax.dynamic_index_in_dim(local, b1, 1, keepdims=False),
-    )
-    lower_first = xor_bcast(lower_local(column_first, pivot_inv[0], rows_first), first % ncol, False)
-    a1 = first // nrow
-    first_row = masked(
-        lax.dynamic_index_in_dim(front, a1, 0, keepdims=False),
-        lax.dynamic_index_in_dim(local, a1, 0, keepdims=False),
-    )
-    upper_first = xor_bcast(first_row, first % nrow, True)
-
-    a2 = second // nrow
-    local_row = lax.dynamic_slice_in_dim(local, a2, 1, 0)
-    row_before = masked(lax.dynamic_slice_in_dim(front, a2, 1, 0), local_row)
+    a1, b1 = first // nrow, first // ncol
+    a2, b2 = second // nrow, second // ncol
+    r1, c1 = first % nrow, first % ncol
+    r2, c2 = second % nrow, second % ncol
+
+    def local_row(a):
+        return masked(
+            lax.dynamic_index_in_dim(front, a, 0, keepdims=False),
+            lax.dynamic_index_in_dim(local, a, 0, keepdims=False),
+        )
+
+    def local_col(b):
+        return masked(
+            lax.dynamic_index_in_dim(front, b, 1, keepdims=False),
+            lax.dynamic_index_in_dim(local, b, 1, keepdims=False),
+        )
+
+    lower_first = lower_local(local_col(b1), pivot_inv[0], rows_first)
+    cols_sent = xor_bcast(jnp.stack([lower_first, local_col(b2)]), jnp.stack([c1, c2]), False)
+    rows_sent = xor_bcast(jnp.stack([local_row(a1), local_row(a2)]), jnp.stack([r1, r2]), True)
+    lower_first, second_col = cols_sent[0], cols_sent[1]
+    upper_first, second_row = rows_sent[0], rows_sent[1]
+
+    cross = all_bcast(
+        jnp.stack([masked(front[a1, b2], local[a1, b2]), masked(front[a2, b1], local[a2, b1])]),
+        jnp.stack([r1 * ncol + c2, r2 * ncol + c1]),
+    )
+    first_at_second, second_at_first = cross[0], cross[1]
+
+    second_ok = (second != first)[None]
+    lower_first_at_second = lower_local(second_at_first[None], pivot_inv[0], second_ok)
     row_after = eliminate(
-        row_before,
-        lax.dynamic_slice_in_dim(lower_first, a2, 1, 0),
+        second_row[None],
+        lower_first_at_second,
         upper_first,
         first,
-        lax.dynamic_slice_in_dim(rows_first, a2, 1, 0),
+        second_ok,
         cols_first,
-        local_row,
+        pattern[second][front_cols][None],
         front_cols,
     )
-    upper_second = xor_bcast(row_after[0], second % nrow, True)
-    b2 = second // ncol
-    local_col = lax.dynamic_slice_in_dim(local, b2, 1, 1)
-    col_before = masked(lax.dynamic_slice_in_dim(front, b2, 1, 1), local_col)
+    upper_second = row_after[0]
     col_after = eliminate(
-        col_before,
+        second_col[:, None],
         lower_first,
-        lax.dynamic_slice_in_dim(upper_first, b2, 1, 0),
+        first_at_second[None],
         first,
         rows_first,
-        lax.dynamic_slice_in_dim(cols_first, b2, 1, 0),
-        local_col,
-        lax.dynamic_slice_in_dim(front_cols, b2, 1, 0),
-    )
-    lower_second = xor_bcast(
-        lower_local(col_after[:, 0], pivot_inv[1], rows_second), second % ncol, False
-    )
+        second_ok,
+        pattern[front_rows, second][:, None],
+        second[None],
+    )
+    lower_second = lower_local(col_after[:, 0], pivot_inv[1], rows_second)
 
     keep = local > 0
     update_first = rows_first[:, None] & cols_first[None, :] & keep

time: 180 us -> 170 us (0.944)
  starting transfers between devices: 46.6 us -> 36.4 us
  waiting for transfers between devices: 73.2 us -> 63.4 us
  other arithmetic: 15.7 us -> 25 us
  between operations: 6.42 us -> 11 us
  matrix products: 9.22 us -> 6.64 us
    ppermute x14 -> x7, starting transfers between devices: 23.7 us -> 4.45 us  [xor_bcast(): got = lax.ppermute(buf, axes, xor_pairs(nrow, ncol, on_row, step))]
    ppermute x14 -> x7, waiting for transfers between devices: 38.7 us -> 25.2 us  [xor_bcast(): got = lax.ppermute(buf, axes, xor_pairs(nrow, ncol, on_row, step))]
    ppermute x14, starting transfers between devices: 22.9 us -> 32 us  [the longest x7 18.3 us: all_bcast(): lax.ppermute(value, ('row', 'col'), [(d, d ^ 1 << b) for d in range(n)])]
    slice x14 -> x6, local copies, waits for them, and re-layouts: 4.8 us -> 0.42 us  [the longest x1 0.27 us: body(): upper_first, second_row = (rows_sent[0], rows_sent[1])]
    ppermute x14, waiting for transfers between devices: 34.5 us -> 38.2 us  [the longest x7 20.1 us: xor_bcast(): got = lax.ppermute(buf[:, half:], axes, xor_pairs(nrow, ncol, on_row, step))]
    select_n x28 -> x22, other arithmetic: 6.18 us -> 9.46 us  [the longest x21 9.45 us: per_part(): return jnp.where(cond.reshape((-1,) + (1,) * (a.ndim - 1)), a, b)]
    another operation x0 -> x3, other arithmetic: none -> 3.25 us  [the longest x1 1.28 us: body(): jnp.stack([local_row(a1), local_row(a2)])]
    dot_general x1, matrix products: 2.6 us -> 0.58 us  [eliminate(): jnp.einsum('iab,jbc->ijac', lower, upper, preferred_element_type=jnp.floa...]
  transfers between devices with their start and end apart: 28 -> 21, of which waited for: 18 -> 11; matrix products, arithmetic and copies ran while one was open for 12% -> 19% of each run, Pallas kernels for 0% -> 0%
where the time goes in v6:
time: 170 us; the launch traced here: 169 us
  waiting for transfers between devices  63.4 us (37%)
  starting transfers between devices  36.4 us (21%)
  other arithmetic  25 us (15%)
  Pallas kernels  16.7 us (10%)
  between operations  11 us (6%)
  local copies, waits for them, and re-layouts  10.2 us (6%)
  matrix products  6.64 us (4%)
    ppermute x7, waiting for transfers between devices, xor_bcast(): got = lax.ppermute(buf, axes, xor_pairs(nrow, ncol, on_row, step))  25.2 us
    ppermute x7, waiting for transfers between devices, xor_bcast(): got = lax.ppermute(buf[:, half:], axes, xor_pairs(nrow, ncol, on_row, step))  20.1 us
    ppermute x7, starting transfers between devices, all_bcast(): lax.ppermute(value, ('row', 'col'), [(d, d ^ 1 << b) for d in range(n)])  18.3 us
    ppermute x7, waiting for transfers between devices, all_bcast(): lax.ppermute(value, ('row', 'col'), [(d, d ^ 1 << b) for d in range(n)])  18.1 us
    pallas_call x1, Pallas kernels, both_updates(): pl.pallas_call(update_kernel, grid_spec=pltpu.PrefetchScalarGridSpec(num_...  16.7 us
    ppermute x7, starting transfers between devices, xor_bcast(): got = lax.ppermute(buf[:, half:], axes, xor_pairs(nrow, ncol, on_row, step))  13.7 us
    select_n x21, other arithmetic, per_part(): return jnp.where(cond.reshape((-1,) + (1,) * (a.ndim - 1)), a, b)  9.45 us
    dot_general x3, matrix products, lower_local(): jnp.einsum('iab,bc->iac', column, inverse, preferred_element_type=jnp.flo...  6.06 us
  transfers between devices with their start and end apart: 21, of which 11 were waited for; matrix products, arithmetic and copies ran while one was open for 19% of the time, Pallas kernels for 0%

profile of v6, /device:TPU:6, one launch (start us, length us, event | category | flops | bytes accessed | tf_op | source)
XLA Modules:
  0.0 169.3 jit_solution(14146756184904920081)
XLA Ops:
  0.0 1.3 fusion.41
  13.3 1.4 bitcast_select_fusion.2
  14.7 2.1 %fusion.8 = bf16[1,8,256,256]{3,2,1,0:T(8,128)(2,1)S(1)} fusion(bf16[8,12,256,256]{3,2,1,0:T(8,128)(2,1)} %front_ref.1, s32[]{:T(128)S(6)} %select_n.287, pred[8]{0:T(512)(128)(4,1)S(1)} %get-tuple-element.8, pred[8]{0:T(512)(128)(4,1)S(1)} %get-tuple-element.18, bf16[2,256,256]{2,1,0:T(8,128)(2,1)S(1)} %copy-done.12), kind=kOutput, calls=%fused_computation.24 | convolution fusion | flops 270008320 | bytes 2229252 | tf_op jit(solution)/shard_map/iab,bc->iac/dot_general | solution.py:150
  19.3 2.2 %dynamic-slice_select_fusion = (bf16[1,12,256,256]{3,2,1,0:T(8,128)(2,1)S(1)}, bf16[1,12,256,256]{3,2,1,0:T(8,128)(2,1)S(1)}) fusion(bf16[8,12,256,256]{3,2,1,0:T(8,128)(2,1)} %front_ref.1, s32[]{:T(128)S(6)} %select_n.312, pred[12]{0:T(512)(128)(4,1)S(1)} %get-tuple-element.5, s32[]{:T(128)S(6)} %select_n.307, pred[12]{0:T(512)(128)(4,1)S(1)} %get-tuple-element.6), kind=kLoop, calls=%fused_computation.21 | loop fusion | flops 1572864 | bytes 6291488 | tf_op jit(solution)/shard_map/jit(_where)/select_n | solution.py:202
  21.5 1.3 fusion.5
  22.7 3.9 %collective-permute-start.13 = (bf16[2,8,192,256]{3,2,1,0:T(8,128)(2,1)}, bf16[2,8,192,256]{3,2,1,0:T(8,128)(2,1)}, u32[]{:S(2)}, u32[]{:S(2)}) collective-permute-start(bf16[2,8,192,256]{3,2,1,0:T(8,128)(2,1)} %fusion.5), channel_id=1, source_target_pairs={{0,64},{1,17},{2,66},{3,19},{4,68},{5,21},{6,70},{7,23},{8,72},{9,... | collective-permute-start | bytes 4718600 | tf_op jit(solution)/shard_map/ppermute | solution.py:129
  34.7 10.6 %collective-permute-done.13 = bf16[2,8,192,256]{3,2,1,0:T(8,128)(2,1)} collective-permute-done((bf16[2,8,192,256]{3,2,1,0:T(8,128)(2,1)}, bf16[2,8,192,256]{3,2,1,0:T(8,128)(2,1)}, u32[]{:S(2)}, u32[]{:S(2)}) %collective-permute-start.13) | collective-permute-done | bytes 1572896 | tf_op jit(solution)/shard_map/ppermute | solution.py:129
  45.3 1.7 fusion.6
  47.1 1.6 collective-permute-start.14
  50.7 1.7 collective-permute-start.7
  52.3 1.4 fusion.11
  54.3 4.8 %collective-permute-done.14 = bf16[2,4,192,256]{3,2,1,0:T(8,128)(2,1)S(1)} collective-permute-done((bf16[2,4,192,256]{3,2,1,0:T(8,128)(2,1)S(1)}, bf16[2,4,192,256]{3,2,1,0:T(8,128)(2,1)S(1)}, u32[]{:S(2)}, u32[]{:S(2)}) %collective-permute-start.14) | collective-permute-done | bytes 786464 | tf_op jit(solution)/shard_map/ppermute | solution.py:129
  59.3 1.5 collective-permute-start.15
  61.9 3.3 %collective-permute-start.8 = (bf16[2,256,256]{1,2,0:T(8,128)(2,1)S(1)}, bf16[2,256,256]{1,2,0:T(8,128)(2,1)S(1)}, u32[]{:S(2)}, u32[]{:S(2)}) collective-permute-start(bf16[2,256,256]{1,2,0:T(8,128)(2,1)S(1)} %broadcast_select_fusion.1), channel_id=1, source_target_pairs={{0,4},{1,5},{2,6},{3,7},{4,0},{5,1},{6,2},{7,3},{8,12},{9,13},{10,... | collective-permute-start | bytes 786440 | tf_op jit(solution)/shard_map/ppermute | solution.py:144
  65.2 4.6 %collective-permute-done.1 = bf16[2,2,256,256]{3,2,1,0:T(8,128)(2,1)S(1)} collective-permute-done((bf16[2,2,256,256]{3,2,1,0:T(8,128)(2,1)S(1)}, bf16[2,2,256,256]{3,2,1,0:T(8,128)(2,1)S(1)}, u32[]{:S(2)}, u32[]{:S(2)}) %collective-permute-start.1) | collective-permute-done | bytes 524320 | tf_op jit(solution)/shard_map/ppermute | solution.py:129
  69.9 4.5 %collective-permute-start.2 = (bf16[2,1,256,256]{3,2,1,0:T(8,128)(2,1)S(1)}, bf16[2,1,256,256]{3,2,1,0:T(8,128)(2,1)S(1)}, u32[]{:S(2)}, u32[]{:S(2)}) collective-permute-start(bf16[2,1,256,256]{3,2,1,0:T(8,128)(2,1)S(1)} %slice.110), channel_id=1, source_target_pairs={{0,4},{1,5},{2,6},{3,7},{4,0},{5,1},{6,2},{7,3},{8,12},{9,13},{10,... | collective-permute-start | bytes 786440 | tf_op jit(solution)/shard_map/ppermute | solution.py:129
  75.7 3.1 %collective-permute-done.8 = bf16[2,256,256]{1,2,0:T(8,128)(2,1)S(1)} collective-permute-done((bf16[2,256,256]{1,2,0:T(8,128)(2,1)S(1)}, bf16[2,256,256]{1,2,0:T(8,128)(2,1)S(1)}, u32[]{:S(2)}, u32[]{:S(2)}) %collective-permute-start.8) | collective-permute-done | bytes 262176 | tf_op jit(solution)/shard_map/ppermute | solution.py:144
  80.4 1.6 collective-permute-start.17
  82.1 1.7 collective-permute-start.3
  83.8 4.5 %collective-permute-done.17 = bf16[2,1,192,256]{3,2,1,0:T(8,128)(2,1)S(1)} collective-permute-done((bf16[2,1,192,256]{3,2,1,0:T(8,128)(2,1)S(1)}, bf16[2,1,192,256]{3,2,1,0:T(8,128)(2,1)S(1)}, u32[]{:S(2)}, u32[]{:S(2)}) %collective-permute-start.17) | collective-permute-done | bytes 196640 | tf_op jit(solution)/shard_map/ppermute | solution.py:132
  89.1 3.0 %collective-permute-start.10 = (bf16[2,256,256]{1,2,0:T(8,128)(2,1)S(1)}, bf16[2,256,256]{1,2,0:T(8,128)(2,1)S(1)}, u32[]{:S(2)}, u32[]{:S(2)}) collective-permute-start(bf16[2,256,256]{1,2,0:T(8,128)(2,1)S(1)} %broadcast_select_fusion.3), channel_id=1, source_target_pairs={{0,16},{1,17},{2,18},{3,19},{4,20},{5,21},{6,22},{7,23},{8,24},{9,... | collective-permute-start | bytes 786440 | tf_op jit(solution)/shard_map/ppermute | solution.py:144
  92.4 9.5 %collective-permute-done.18 = bf16[2,2,192,256]{3,2,1,0:T(8,128)(2,1)S(1)} collective-permute-done((bf16[2,2,192,256]{3,2,1,0:T(8,128)(2,1)S(1)}, bf16[2,2,192,256]{3,2,1,0:T(8,128)(2,1)S(1)}, u32[]{:S(2)}, u32[]{:S(2)}) %collective-permute-start.18) | collective-permute-done | bytes 393248 | tf_op jit(solution)/shard_map/ppermute | solution.py:132
  102.2 5.3 %collective-permute-done.10 = bf16[2,256,256]{1,2,0:T(8,128)(2,1)S(1)} collective-permute-done((bf16[2,256,256]{1,2,0:T(8,128)(2,1)S(1)}, bf16[2,256,256]{1,2,0:T(8,128)(2,1)S(1)}, u32[]{:S(2)}, u32[]{:S(2)}) %collective-permute-start.10) | collective-permute-done | bytes 262176 | tf_op jit(solution)/shard_map/ppermute | solution.py:144
  108.9 1.5 maximum_select_fusion.3
  110.5 6.5 %collective-permute-done.11 = bf16[2,256,256]{1,2,0:T(8,128)(2,1)S(1)} collective-permute-done((bf16[2,256,256]{1,2,0:T(8,128)(2,1)S(1)}, bf16[2,256,256]{1,2,0:T(8,128)(2,1)S(1)}, u32[]{:S(2)}, u32[]{:S(2)}) %collective-permute-start.11) | collective-permute-done | bytes 262176 | tf_op jit(solution)/shard_map/ppermute | solution.py:144
  117.1 8.9 %collective-permute-start.12 = (bf16[2,256,256]{1,2,0:T(8,128)(2,1)S(1)}, bf16[2,256,256]{1,2,0:T(8,128)(2,1)S(1)}, u32[]{:S(2)}, u32[]{:S(2)}) collective-permute-start(bf16[2,256,256]{1,2,0:T(8,128)(2,1)S(1)} %broadcast_select_fusion.5), channel_id=1, source_target_pairs={{0,64},{1,65},{2,66},{3,67},{4,68},{5,69},{6,70},{7,71},{8,72},{9,... | collective-permute-start | bytes 786440 | tf_op jit(solution)/shard_map/ppermute | solution.py:144
  127.3 3.1 %collective-permute-done.12 = bf16[2,256,256]{1,2,0:T(8,128)(2,1)S(1)} collective-permute-done((bf16[2,256,256]{1,2,0:T(8,128)(2,1)S(1)}, bf16[2,256,256]{1,2,0:T(8,128)(2,1)S(1)}, u32[]{:S(2)}, u32[]{:S(2)}) %collective-permute-start.12) | collective-permute-done | bytes 262176 | tf_op jit(solution)/shard_map/ppermute | solution.py:144
  131.1 1.3 copy-done.4
  133.5 3.7 %select_convert_fusion.l2_ref = bf16[8,256,256]{2,1,0:T(8,128)(2,1)} fusion(bf16[2,8,256,256]{3,2,1,0:T(8,128)(2,1)} %copy-done.4, pred[8]{0:T(512)(128)(4,1)S(1)} %copy-done.11, pred[8]{0:T(512)(128)(4,1)S(1)} %copy-done.10, pred[8]{0:T(512)(128)(4,1)S(1)} %get-tuple-element.43, bf16[2,256,256]{1,2,0:T(8,128)(2,1)S(1)} %broadcast_select_fusion.6, ...), kind=kOutput, calls=%fused_computation.13 | convolution fusion | flops 540540928 | bytes 4457984 | tf_op jit(solution)/shard_map/iab,bc->iac/dot_general | solution.py:150
  137.2 11.3 %collective-permute-done.20 = bf16[2,8,192,256]{3,2,1,0:T(8,128)(2,1)S(1)} collective-permute-done((bf16[2,8,192,256]{3,2,1,0:T(8,128)(2,1)S(1)}, bf16[2,8,192,256]{3,2,1,0:T(8,128)(2,1)S(1)}, u32[]{:S(2)}, u32[]{:S(2)}) %collective-permute-start.20) | collective-permute-done | bytes 1572896 | tf_op jit(solution)/shard_map/ppermute | solution.py:132
  150.6 2.0 %fusion.4.u2_ref = bf16[12,256,256]{2,1,0:T(8,128)(2,1)} fusion(bf16[1,12,256,256]{3,2,1,0:T(8,128)(2,1)S(1)} %bitcast.114, f32[12,256,256]{1,2,0:T(8,128)S(1)} %fusion.20, pred[12]{0:T(512)(128)(4,1)S(1)} %copy-done.9, pred[12]{0:T(512)(128)(4,1)S(1)} %copy-done.8, bf16[256,256]{1,0:T(8,128)(2,1)S(1)} %fusion.9), kind=kLoop, calls=%fused_computation.16 | loop fusion | flops 3932160 | bytes 6422552 | tf_op jit(solution)/shard_map/squeeze | solution.py:265
  152.6 16.7 %shard_map.46 = bf16[8,12,256,256]{3,2,1,0:T(8,128)(2,1)} custom-call(s32[8,12]{1,0:T(8,128)} %select_add_fusion.codes, bf16[8,12,256,256]{3,2,1,0:T(8,128)(2,1)} %front_ref.1, bf16[8,256,256]{2,1,0:T(8,128)(2,1)} %slice_bitcast_fusion.1.l1_ref, bf16[8,256,256]{2,1,0:T(8,128)(2,1)} %select_convert_fusion.l2_ref, bf16[12,256,256]{2,1,0:T(8,128)(2,1)} %bitcast.109, ...), custom_call_target="tpu_custom_call" | custom-call | tf_op jit(solution)/shard_map/pallas_call | solution.py:187
  (105 shorter events, 26.9 us)
Async XLA Ops:
  8.1 10.6 %copy-start.7 = (s32[8,16,12,8]{1,0,3,2:T(8,128)}, s32[8,16,12,8]{1,0,3,2:T(8,128)S(1)}, u32[]{:S(2)}) copy-start(s32[8,16,12,8]{1,0,3,2:T(8,128)S(1)} %reshape.620) | copy-start | bytes 147460
  10.0 4.7 %copy-start.12 = (bf16[2,256,256]{2,1,0:T(8,128)(2,1)S(1)}, bf16[2,256,256]{2,1,0:T(8,128)(2,1)}, u32[]{:S(2)}) copy-start(bf16[2,256,256]{2,1,0:T(8,128)(2,1)} %param.7) | copy-start | bytes 786436
  10.8 38.8 %collective-permute-start.6 = (bf16[2,256,256]{1,2,0:T(8,128)(2,1)}, bf16[2,256,256]{1,2,0:T(8,128)(2,1)}, u32[]{:S(2)}, u32[]{:S(2)}) collective-permute-start(bf16[2,256,256]{1,2,0:T(8,128)(2,1)} %pad_maximum_fusion.2), channel_id=1, source_target_pairs={{0,1},{1,0},{2,3},{3,2},{4,5},{5,4},{6,7},{7,6},{8,9},{9,8},{10,11... | collective-permute-start | bytes 786440 | tf_op jit(solution)/shard_map/ppermute | solution.py:144
  14.7 2.1 %copy-start.1 = (bf16[1,8,256,256]{3,2,1,0:T(8,128)(2,1)}, bf16[1,8,256,256]{3,2,1,0:T(8,128)(2,1)S(1)}, u32[]{:S(2)}) copy-start(bf16[1,8,256,256]{3,2,1,0:T(8,128)(2,1)S(1)} %bitcast_select_fusion.2) | copy-start | bytes 3145732
  16.8 1.4 copy-start.5
  18.2 34.2 %collective-permute-start = (bf16[2,4,256,256]{3,2,1,0:T(8,128)(2,1)}, bf16[2,4,256,256]{3,2,1,0:T(8,128)(2,1)}, u32[]{:S(2)}, u32[]{:S(2)}) collective-permute-start(bf16[2,4,256,256]{3,2,1,0:T(8,128)(2,1)} %fusion.10), channel_id=1, source_target_pairs={{0,1},{1,0},{2,3},{3,2},{4,5},{5,4},{6,7},{7,6},{8,9},{9,8},{10,11... | collective-permute-start | bytes 3145736 | tf_op jit(solution)/shard_map/ppermute | solution.py:129
  21.5 8.7 %copy-start.3 = (s32[128,96]{0,1:T(8,128)S(1)}, s32[128,96]{0,1:T(8,128)}, u32[]{:S(2)}) copy-start(s32[128,96]{0,1:T(8,128)} %param.5) | copy-start | bytes 147460
  22.7 22.6 %collective-permute-start.13 = (bf16[2,8,192,256]{3,2,1,0:T(8,128)(2,1)}, bf16[2,8,192,256]{3,2,1,0:T(8,128)(2,1)}, u32[]{:S(2)}, u32[]{:S(2)}) collective-permute-start(bf16[2,8,192,256]{3,2,1,0:T(8,128)(2,1)} %fusion.5), channel_id=1, source_target_pairs={{0,64},{1,17},{2,66},{3,19},{4,68},{5,21},{6,70},{7,23},{8,72},{9,... | collective-permute-start | bytes 4718600 | tf_op jit(solution)/shard_map/ppermute | solution.py:129
  47.0 5.3 %copy-start.2 = (bf16[1,8,256,256]{3,2,1,0:T(8,128)(2,1)S(1)}, bf16[1,8,256,256]{3,2,1,0:T(8,128)(2,1)}, u32[]{:S(2)}) copy-start(bf16[1,8,256,256]{3,2,1,0:T(8,128)(2,1)} %copy-done.1) | copy-start | bytes 3145732
  47.0 5.3 %copy-start.6 = (bf16[1,8,256,256]{3,2,1,0:T(8,128)(2,1)S(1)}, bf16[1,8,256,256]{3,2,1,0:T(8,128)(2,1)}, u32[]{:S(2)}) copy-start(bf16[1,8,256,256]{3,2,1,0:T(8,128)(2,1)} %copy-done.5) | copy-start | bytes 3145732
  47.1 12.1 %collective-permute-start.14 = (bf16[2,4,192,256]{3,2,1,0:T(8,128)(2,1)S(1)}, bf16[2,4,192,256]{3,2,1,0:T(8,128)(2,1)S(1)}, u32[]{:S(2)}, u32[]{:S(2)}) collective-permute-start(bf16[2,4,192,256]{3,2,1,0:T(8,128)(2,1)S(1)} %slice.117), channel_id=1, source_target_pairs={{0,32},{1,9},{2,34},{3,11},{4,36},{5,13},{6,38},{7,15},{8,40},{9,1... | collective-permute-start | bytes 2359304 | tf_op jit(solution)/shard_map/ppermute | solution.py:129
  50.7 10.1 %collective-permute-start.7 = (bf16[2,256,256]{1,2,0:T(8,128)(2,1)S(1)}, bf16[2,256,256]{1,2,0:T(8,128)(2,1)S(1)}, u32[]{:S(2)}, u32[]{:S(2)}) collective-permute-start(bf16[2,256,256]{1,2,0:T(8,128)(2,1)S(1)} %broadcast_select_fusion), channel_id=1, source_target_pairs={{0,2},{1,3},{2,0},{3,1},{4,6},{5,7},{6,4},{7,5},{8,10},{9,11},{10,... | collective-permute-start | bytes 786440 | tf_op jit(solution)/shard_map/ppermute | solution.py:144
  53.8 15.9 %collective-permute-start.1 = (bf16[2,2,256,256]{3,2,1,0:T(8,128)(2,1)S(1)}, bf16[2,2,256,256]{3,2,1,0:T(8,128)(2,1)S(1)}, u32[]{:S(2)}, u32[]{:S(2)}) collective-permute-start(bf16[2,2,256,256]{3,2,1,0:T(8,128)(2,1)S(1)} %slice.108), channel_id=1, source_target_pairs={{0,2},{1,3},{2,0},{3,1},{4,6},{5,7},{6,4},{7,5},{8,10},{9,11},{10,... | collective-permute-start | bytes 1572872 | tf_op jit(solution)/shard_map/ppermute | solution.py:129
  59.3 15.1 %collective-permute-start.15 = (bf16[2,2,192,256]{3,2,1,0:T(8,128)(2,1)S(1)}, bf16[2,2,192,256]{3,2,1,0:T(8,128)(2,1)S(1)}, u32[]{:S(2)}, u32[]{:S(2)}) collective-permute-start(bf16[2,2,192,256]{3,2,1,0:T(8,128)(2,1)S(1)} %slice.119), channel_id=1, source_target_pairs={{0,16},{1,65},{2,18},{3,67},{4,20},{5,69},{6,22},{7,71},{8,24},{9,... | collective-permute-start | bytes 1179656 | tf_op jit(solution)/shard_map/ppermute | solution.py:129
  61.9 17.0 %collective-permute-start.8 = (bf16[2,256,256]{1,2,0:T(8,128)(2,1)S(1)}, bf16[2,256,256]{1,2,0:T(8,128)(2,1)S(1)}, u32[]{:S(2)}, u32[]{:S(2)}) collective-permute-start(bf16[2,256,256]{1,2,0:T(8,128)(2,1)S(1)} %broadcast_select_fusion.1), channel_id=1, source_target_pairs={{0,4},{1,5},{2,6},{3,7},{4,0},{5,1},{6,2},{7,3},{8,12},{9,13},{10,... | collective-permute-start | bytes 786440 | tf_op jit(solution)/shard_map/ppermute | solution.py:144
  69.9 12.1 %collective-permute-start.2 = (bf16[2,1,256,256]{3,2,1,0:T(8,128)(2,1)S(1)}, bf16[2,1,256,256]{3,2,1,0:T(8,128)(2,1)S(1)}, u32[]{:S(2)}, u32[]{:S(2)}) collective-permute-start(bf16[2,1,256,256]{3,2,1,0:T(8,128)(2,1)S(1)} %slice.110), channel_id=1, source_target_pairs={{0,4},{1,5},{2,6},{3,7},{4,0},{5,1},{6,2},{7,3},{8,12},{9,13},{10,... | collective-permute-start | bytes 786440 | tf_op jit(solution)/shard_map/ppermute | solution.py:129
  74.6 5.7 %collective-permute-start.16 = (bf16[2,1,192,256]{3,2,1,0:T(8,128)(2,1)S(1)}, bf16[2,1,192,256]{3,2,1,0:T(8,128)(2,1)S(1)}, u32[]{:S(2)}, u32[]{:S(2)}) collective-permute-start(bf16[2,1,192,256]{3,2,1,0:T(8,128)(2,1)S(1)} %slice.121), channel_id=1, source_target_pairs={{0,8},{1,33},{2,10},{3,35},{4,12},{5,37},{6,14},{7,39},{8,0},{9,41... | collective-permute-start | bytes 589832 | tf_op jit(solution)/shard_map/ppermute | solution.py:129
  79.0 10.1 %collective-permute-start.9 = (bf16[2,256,256]{1,2,0:T(8,128)(2,1)S(1)}, bf16[2,256,256]{1,2,0:T(8,128)(2,1)S(1)}, u32[]{:S(2)}, u32[]{:S(2)}) collective-permute-start(bf16[2,256,256]{1,2,0:T(8,128)(2,1)S(1)} %broadcast_select_fusion.2), channel_id=1, source_target_pairs={{0,8},{1,9},{2,10},{3,11},{4,12},{5,13},{6,14},{7,15},{8,0},{9,1},... | collective-permute-start | bytes 786440 | tf_op jit(solution)/shard_map/ppermute | solution.py:144
  80.4 7.8 %collective-permute-start.17 = (bf16[2,1,192,256]{3,2,1,0:T(8,128)(2,1)S(1)}, bf16[2,1,192,256]{3,2,1,0:T(8,128)(2,1)S(1)}, u32[]{:S(2)}, u32[]{:S(2)}) collective-permute-start(bf16[2,1,192,256]{3,2,1,0:T(8,128)(2,1)S(1)} %slice_select_fusion.4), channel_id=1, source_target_pairs={{0,8},{1,33},{2,10},{3,35},{4,12},{5,37},{6,14},{7,39},{8,0},{9,41... | collective-permute-start | bytes 589832 | tf_op jit(solution)/shard_map/ppermute | solution.py:132
  82.1 10.0 %collective-permute-start.3 = (bf16[2,1,256,256]{3,2,1,0:T(8,128)(2,1)S(1)}, bf16[2,1,256,256]{3,2,1,0:T(8,128)(2,1)S(1)}, u32[]{:S(2)}, u32[]{:S(2)}) collective-permute-start(bf16[2,1,256,256]{3,2,1,0:T(8,128)(2,1)S(1)} %slice_select_fusion.3), channel_id=1, source_target_pairs={{0,4},{1,5},{2,6},{3,7},{4,0},{5,1},{6,2},{7,3},{8,12},{9,13},{10,... | collective-permute-start | bytes 786440 | tf_op jit(solution)/shard_map/ppermute | solution.py:132
  88.4 13.5 %collective-permute-start.18 = (bf16[2,2,192,256]{3,2,1,0:T(8,128)(2,1)S(1)}, bf16[2,2,192,256]{3,2,1,0:T(8,128)(2,1)S(1)}, u32[]{:S(2)}, u32[]{:S(2)}) collective-permute-start(bf16[2,2,192,256]{3,2,1,0:T(8,128)(2,1)S(1)} %maximum_select_fusion.6), channel_id=1, source_target_pairs={{0,16},{1,65},{2,18},{3,67},{4,20},{5,69},{6,22},{7,71},{8,24},{9,... | collective-permute-start | bytes 1179656 | tf_op jit(solution)/shard_map/ppermute | solution.py:132
  89.1 18.4 %collective-permute-start.10 = (bf16[2,256,256]{1,2,0:T(8,128)(2,1)S(1)}, bf16[2,256,256]{1,2,0:T(8,128)(2,1)S(1)}, u32[]{:S(2)}, u32[]{:S(2)}) collective-permute-start(bf16[2,256,256]{1,2,0:T(8,128)(2,1)S(1)} %broadcast_select_fusion.3), channel_id=1, source_target_pairs={{0,16},{1,17},{2,18},{3,19},{4,20},{5,21},{6,22},{7,23},{8,24},{9,... | collective-permute-start | bytes 786440 | tf_op jit(solution)/shard_map/ppermute | solution.py:144
  92.3 16.6 %collective-permute-start.4 = (bf16[2,2,256,256]{3,2,1,0:T(8,128)(2,1)S(1)}, bf16[2,2,256,256]{3,2,1,0:T(8,128)(2,1)}, u32[]{:S(2)}, u32[]{:S(2)}) collective-permute-start(bf16[2,2,256,256]{3,2,1,0:T(8,128)(2,1)S(1)} %maximum_select_fusion.5), channel_id=1, source_target_pairs={{0,2},{1,3},{2,0},{3,1},{4,6},{5,7},{6,4},{7,5},{8,10},{9,11},{10,... | collective-permute-start | bytes 1572872 | tf_op jit(solution)/shard_map/ppermute | solution.py:132
  102.1 23.9 %collective-permute-start.19 = (bf16[2,4,192,256]{3,2,1,0:T(8,128)(2,1)S(1)}, bf16[2,4,192,256]{3,2,1,0:T(8,128)(2,1)S(1)}, u32[]{:S(2)}, u32[]{:S(2)}) collective-permute-start(bf16[2,4,192,256]{3,2,1,0:T(8,128)(2,1)S(1)} %maximum_select_fusion.4), channel_id=1, source_target_pairs={{0,32},{1,9},{2,34},{3,11},{4,36},{5,13},{6,38},{7,15},{8,40},{9,1... | collective-permute-start | bytes 2359304 | tf_op jit(solution)/shard_map/ppermute | solution.py:132
  107.6 9.3 %collective-permute-start.11 = (bf16[2,256,256]{1,2,0:T(8,128)(2,1)S(1)}, bf16[2,256,256]{1,2,0:T(8,128)(2,1)S(1)}, u32[]{:S(2)}, u32[]{:S(2)}) collective-permute-start(bf16[2,256,256]{1,2,0:T(8,128)(2,1)S(1)} %broadcast_select_fusion.4), channel_id=1, source_target_pairs={{0,32},{1,33},{2,34},{3,35},{4,36},{5,37},{6,38},{7,39},{8,40},{9,... | collective-permute-start | bytes 786440 | tf_op jit(solution)/shard_map/ppermute | solution.py:144
  110.4 20.3 %collective-permute-start.5 = (bf16[2,4,256,256]{3,2,1,0:T(8,128)(2,1)S(1)}, bf16[2,4,256,256]{3,2,1,0:T(8,128)(2,1)S(1)}, u32[]{:S(2)}, u32[]{:S(2)}) collective-permute-start(bf16[2,4,256,256]{3,2,1,0:T(8,128)(2,1)S(1)} %maximum_select_fusion.3), channel_id=1, source_target_pairs={{0,1},{1,0},{2,3},{3,2},{4,5},{5,4},{6,7},{7,6},{8,9},{9,8},{10,11... | collective-permute-start | bytes 3145736 | tf_op jit(solution)/shard_map/ppermute | solution.py:132
  117.1 13.3 %collective-permute-start.12 = (bf16[2,256,256]{1,2,0:T(8,128)(2,1)S(1)}, bf16[2,256,256]{1,2,0:T(8,128)(2,1)S(1)}, u32[]{:S(2)}, u32[]{:S(2)}) collective-permute-start(bf16[2,256,256]{1,2,0:T(8,128)(2,1)S(1)} %broadcast_select_fusion.5), channel_id=1, source_target_pairs={{0,64},{1,65},{2,66},{3,67},{4,68},{5,69},{6,70},{7,71},{8,72},{9,... | collective-permute-start | bytes 786440 | tf_op jit(solution)/shard_map/ppermute | solution.py:144
  126.0 4.4 %copy-start.13 = (bf16[2,256,256]{2,1,0:T(8,128)(2,1)S(1)}, bf16[2,256,256]{2,1,0:T(8,128)(2,1)}, u32[]{:S(2)}) copy-start(bf16[2,256,256]{2,1,0:T(8,128)(2,1)} %param.7) | copy-start | bytes 786436
  126.3 22.2 %collective-permute-start.20 = (bf16[2,8,192,256]{3,2,1,0:T(8,128)(2,1)S(1)}, bf16[2,8,192,256]{3,2,1,0:T(8,128)(2,1)S(1)}, u32[]{:S(2)}, u32[]{:S(2)}) collective-permute-start(bf16[2,8,192,256]{3,2,1,0:T(8,128)(2,1)S(1)} %maximum_select_fusion.2), channel_id=1, source_target_pairs={{0,64},{1,17},{2,66},{3,19},{4,68},{5,21},{6,70},{7,23},{8,72},{9,... | collective-permute-start | bytes 4718600 | tf_op jit(solution)/shard_map/ppermute | solution.py:132
  131.1 1.3 copy-start.4
  149.4 1.2 copy-start
  149.4 1.2 copy-start.8
  (3 other events, 3.3 us)

commit v7 on v6

--- a/solution.py
+++ b/solution.py
@@ -162,21 +162,23 @@
 
 def update_kernel(codes, front_ref, l1_ref, l2_ref, u1_ref, u2_ref, out_ref):
     i = pl.program_id(0)
-    lower1 = l1_ref[0]
-    lower2 = l2_ref[0]
     for j in range(front_ref.shape[1]):
         code = codes[i, j]
         block = front_ref[0, j]
-        block = jnp.where((code & 1) != 0, block, jnp.zeros_like(block))
-        product = jnp.dot(lower1, u1_ref[j], preferred_element_type=jnp.float32)
-        changed = (block.astype(jnp.float32) - product).astype(jnp.bfloat16)
-        block = jnp.where((code & 2) != 0, changed, block)
-        block = jnp.where((code & 4) != 0, lower1, block)
-        product = jnp.dot(lower2, u2_ref[j], preferred_element_type=jnp.float32)
-        changed = (block.astype(jnp.float32) - product).astype(jnp.bfloat16)
-        block = jnp.where((code & 8) != 0, changed, block)
-        block = jnp.where((code & 16) != 0, lower2, block)
-        out_ref[0, j] = block
+        out_ref[0, j] = jnp.where((code & 1) != 0, block, jnp.zeros_like(block))
+
+        def step(lower_ref, upper_ref, update_bit, place_bit, j=j, code=code):
+            @pl.when((code & update_bit) != 0)
+            def _():
+                product = jnp.dot(lower_ref[0], upper_ref[j], preferred_element_type=jnp.float32)
+                out_ref[0, j] = (out_ref[0, j].astype(jnp.float32) - product).astype(jnp.bfloat16)
+
+            @pl.when((code & place_bit) != 0)
+            def _():
+                out_ref[0, j] = lower_ref[0]
+
+        step(l1_ref, u1_ref, 2, 4)
+        step(l2_ref, u2_ref, 8, 16)
 
 
 def both_updates(front, codes, lower1, lower2, upper1, upper2):

time: 170 us -> 188 us (1.11)
  the two profiles are of different devices: /device:TPU:6 before, /device:TPU:108 now
where the time goes in v7:
time: 188 us; the launch traced here: 187 us
  waiting for transfers between devices  68.6 us (36%)
  Pallas kernels  38.7 us (21%)
  starting transfers between devices  26.6 us (14%)
  other arithmetic  25 us (13%)
  between operations  11 us (6%)
  local copies, waits for them, and re-layouts  10.2 us (5%)
  matrix products  6.64 us (4%)
    pallas_call x1, Pallas kernels, both_updates(): pl.pallas_call(update_kernel, grid_spec=pltpu.PrefetchScalarGridSpec(num_...  38.7 us
    ppermute x7, waiting for transfers between devices, xor_bcast(): got = lax.ppermute(buf[:, half:], axes, xor_pairs(nrow, ncol, on_row, step))  28.3 us
    ppermute x7, waiting for transfers between devices, xor_bcast(): got = lax.ppermute(buf, axes, xor_pairs(nrow, ncol, on_row, step))  22.3 us
    ppermute x7, waiting for transfers between devices, all_bcast(): lax.ppermute(value, ('row', 'col'), [(d, d ^ 1 << b) for d in range(n)])  18 us
    ppermute x7, starting transfers between devices, xor_bcast(): got = lax.ppermute(buf, axes, xor_pairs(nrow, ncol, on_row, step))  10.5 us
    select_n x21, other arithmetic, per_part(): return jnp.where(cond.reshape((-1,) + (1,) * (a.ndim - 1)), a, b)  9.46 us
    ppermute x7, starting transfers between devices, all_bcast(): lax.ppermute(value, ('row', 'col'), [(d, d ^ 1 << b) for d in range(n)])  8.41 us
    ppermute x7, starting transfers between devices, xor_bcast(): got = lax.ppermute(buf[:, half:], axes, xor_pairs(nrow, ncol, on_row, step))  7.7 us
  transfers between devices with their start and end apart: 21, of which 11 were waited for; matrix products, arithmetic and copies ran while one was open for 17% of the time, Pallas kernels for 0%

profile of v7, /device:TPU:108, one launch (start us, length us, event | category | flops | bytes accessed | tf_op | source)
XLA Modules:
  0.0 186.6 jit_solution(4152728044976237530)
XLA Ops:
  0.0 1.3 fusion.41
  13.3 1.4 bitcast_select_fusion.2
  14.7 2.1 %fusion.8 = bf16[1,8,256,256]{3,2,1,0:T(8,128)(2,1)S(1)} fusion(bf16[8,12,256,256]{3,2,1,0:T(8,128)(2,1)} %front_ref.1, s32[]{:T(128)S(6)} %select_n.287, pred[8]{0:T(512)(128)(4,1)S(1)} %get-tuple-element.8, pred[8]{0:T(512)(128)(4,1)S(1)} %get-tuple-element.18, bf16[2,256,256]{2,1,0:T(8,128)(2,1)S(1)} %copy-done.12), kind=kOutput, calls=%fused_computation.24 | convolution fusion | flops 270008320 | bytes 2229252 | tf_op jit(solution)/shard_map/iab,bc->iac/dot_general | solution.py:150
  19.3 2.2 %dynamic-slice_select_fusion = (bf16[1,12,256,256]{3,2,1,0:T(8,128)(2,1)S(1)}, bf16[1,12,256,256]{3,2,1,0:T(8,128)(2,1)S(1)}) fusion(bf16[8,12,256,256]{3,2,1,0:T(8,128)(2,1)} %front_ref.1, s32[]{:T(128)S(6)} %select_n.312, pred[12]{0:T(512)(128)(4,1)S(1)} %get-tuple-element.5, s32[]{:T(128)S(6)} %select_n.307, pred[12]{0:T(512)(128)(4,1)S(1)} %get-tuple-element.6), kind=kLoop, calls=%fused_computation.21 | loop fusion | flops 1572864 | bytes 6291488 | tf_op jit(solution)/shard_map/jit(_where)/select_n | solution.py:204
  31.4 13.6 %collective-permute-done.13 = bf16[2,8,192,256]{3,2,1,0:T(8,128)(2,1)} collective-permute-done((bf16[2,8,192,256]{3,2,1,0:T(8,128)(2,1)}, bf16[2,8,192,256]{3,2,1,0:T(8,128)(2,1)}, u32[]{:S(2)}, u32[]{:S(2)}) %collective-permute-start.13) | collective-permute-done | bytes 1572896 | tf_op jit(solution)/shard_map/ppermute | solution.py:129
  45.0 1.7 fusion.6
  49.8 1.4 fusion.11
  51.2 1.7 collective-permute-start.1
  52.9 6.0 %collective-permute-done.14 = bf16[2,4,192,256]{3,2,1,0:T(8,128)(2,1)S(1)} collective-permute-done((bf16[2,4,192,256]{3,2,1,0:T(8,128)(2,1)S(1)}, bf16[2,4,192,256]{3,2,1,0:T(8,128)(2,1)S(1)}, u32[]{:S(2)}, u32[]{:S(2)}) %collective-permute-start.14) | collective-permute-done | bytes 786464 | tf_op jit(solution)/shard_map/ppermute | solution.py:129
  61.0 2.4 %collective-permute-start.8 = (bf16[2,256,256]{1,2,0:T(8,128)(2,1)S(1)}, bf16[2,256,256]{1,2,0:T(8,128)(2,1)S(1)}, u32[]{:S(2)}, u32[]{:S(2)}) collective-permute-start(bf16[2,256,256]{1,2,0:T(8,128)(2,1)S(1)} %broadcast_select_fusion.1), channel_id=1, source_target_pairs={{0,4},{1,5},{2,6},{3,7},{4,0},{5,1},{6,2},{7,3},{8,12},{9,13},{10,... | collective-permute-start | bytes 786440 | tf_op jit(solution)/shard_map/ppermute | solution.py:144
  63.4 6.4 %collective-permute-done.1 = bf16[2,2,256,256]{3,2,1,0:T(8,128)(2,1)S(1)} collective-permute-done((bf16[2,2,256,256]{3,2,1,0:T(8,128)(2,1)S(1)}, bf16[2,2,256,256]{3,2,1,0:T(8,128)(2,1)S(1)}, u32[]{:S(2)}, u32[]{:S(2)}) %collective-permute-start.1) | collective-permute-done | bytes 524320 | tf_op jit(solution)/shard_map/ppermute | solution.py:129
  69.9 2.4 %collective-permute-start.2 = (bf16[2,1,256,256]{3,2,1,0:T(8,128)(2,1)S(1)}, bf16[2,1,256,256]{3,2,1,0:T(8,128)(2,1)S(1)}, u32[]{:S(2)}, u32[]{:S(2)}) collective-permute-start(bf16[2,1,256,256]{3,2,1,0:T(8,128)(2,1)S(1)} %slice.110), channel_id=1, source_target_pairs={{0,4},{1,5},{2,6},{3,7},{4,0},{5,1},{6,2},{7,3},{8,12},{9,13},{10,... | collective-permute-start | bytes 786440 | tf_op jit(solution)/shard_map/ppermute | solution.py:129
  72.4 1.3 collective-permute-start.16
  73.7 2.7 %collective-permute-done.8 = bf16[2,256,256]{1,2,0:T(8,128)(2,1)S(1)} collective-permute-done((bf16[2,256,256]{1,2,0:T(8,128)(2,1)S(1)}, bf16[2,256,256]{1,2,0:T(8,128)(2,1)S(1)}, u32[]{:S(2)}, u32[]{:S(2)}) %collective-permute-start.8) | collective-permute-done | bytes 262176 | tf_op jit(solution)/shard_map/ppermute | solution.py:144
  77.8 2.3 %collective-permute-done.16 = bf16[2,1,192,256]{3,2,1,0:T(8,128)(2,1)S(1)} collective-permute-done((bf16[2,1,192,256]{3,2,1,0:T(8,128)(2,1)S(1)}, bf16[2,1,192,256]{3,2,1,0:T(8,128)(2,1)S(1)}, u32[]{:S(2)}, u32[]{:S(2)}) %collective-permute-start.16) | collective-permute-done | bytes 196640 | tf_op jit(solution)/shard_map/ppermute | solution.py:129
  80.1 1.5 collective-permute-start.17
  81.7 1.3 collective-permute-start.3
  83.1 4.0 %collective-permute-done.17 = bf16[2,1,192,256]{3,2,1,0:T(8,128)(2,1)S(1)} collective-permute-done((bf16[2,1,192,256]{3,2,1,0:T(8,128)(2,1)S(1)}, bf16[2,1,192,256]{3,2,1,0:T(8,128)(2,1)S(1)}, u32[]{:S(2)}, u32[]{:S(2)}) %collective-permute-start.17) | collective-permute-done | bytes 196640 | tf_op jit(solution)/shard_map/ppermute | solution.py:132
  87.4 3.6 %collective-permute-start.10 = (bf16[2,256,256]{1,2,0:T(8,128)(2,1)S(1)}, bf16[2,256,256]{1,2,0:T(8,128)(2,1)S(1)}, u32[]{:S(2)}, u32[]{:S(2)}) collective-permute-start(bf16[2,256,256]{1,2,0:T(8,128)(2,1)S(1)} %broadcast_select_fusion.3), channel_id=1, source_target_pairs={{0,16},{1,17},{2,18},{3,19},{4,20},{5,21},{6,22},{7,23},{8,24},{9,... | collective-permute-start | bytes 786440 | tf_op jit(solution)/shard_map/ppermute | solution.py:144
  91.2 1.4 collective-permute-start.4
  92.5 8.3 %collective-permute-done.18 = bf16[2,2,192,256]{3,2,1,0:T(8,128)(2,1)S(1)} collective-permute-done((bf16[2,2,192,256]{3,2,1,0:T(8,128)(2,1)S(1)}, bf16[2,2,192,256]{3,2,1,0:T(8,128)(2,1)S(1)}, u32[]{:S(2)}, u32[]{:S(2)}) %collective-permute-start.18) | collective-permute-done | bytes 393248 | tf_op jit(solution)/shard_map/ppermute | solution.py:132
  101.0 2.4 %collective-permute-start.19 = (bf16[2,4,192,256]{3,2,1,0:T(8,128)(2,1)S(1)}, bf16[2,4,192,256]{3,2,1,0:T(8,128)(2,1)S(1)}, u32[]{:S(2)}, u32[]{:S(2)}) collective-permute-start(bf16[2,4,192,256]{3,2,1,0:T(8,128)(2,1)S(1)} %maximum_select_fusion.4), channel_id=1, source_target_pairs={{0,32},{1,9},{2,34},{3,11},{4,36},{5,13},{6,38},{7,15},{8,40},{9,1... | collective-permute-start | bytes 2359304 | tf_op jit(solution)/shard_map/ppermute | solution.py:132
  103.4 3.1 %collective-permute-done.10 = bf16[2,256,256]{1,2,0:T(8,128)(2,1)S(1)} collective-permute-done((bf16[2,256,256]{1,2,0:T(8,128)(2,1)S(1)}, bf16[2,256,256]{1,2,0:T(8,128)(2,1)S(1)}, u32[]{:S(2)}, u32[]{:S(2)}) %collective-permute-start.10) | collective-permute-done | bytes 262176 | tf_op jit(solution)/shard_map/ppermute | solution.py:144
  108.3 1.5 maximum_select_fusion.3
  109.9 9.1 %collective-permute-done.11 = bf16[2,256,256]{1,2,0:T(8,128)(2,1)S(1)} collective-permute-done((bf16[2,256,256]{1,2,0:T(8,128)(2,1)S(1)}, bf16[2,256,256]{1,2,0:T(8,128)(2,1)S(1)}, u32[]{:S(2)}, u32[]{:S(2)}) %collective-permute-start.11) | collective-permute-done | bytes 262176 | tf_op jit(solution)/shard_map/ppermute | solution.py:144
  119.5 3.8 %collective-permute-start.20 = (bf16[2,8,192,256]{3,2,1,0:T(8,128)(2,1)S(1)}, bf16[2,8,192,256]{3,2,1,0:T(8,128)(2,1)S(1)}, u32[]{:S(2)}, u32[]{:S(2)}) collective-permute-start(bf16[2,8,192,256]{3,2,1,0:T(8,128)(2,1)S(1)} %maximum_select_fusion.2), channel_id=1, source_target_pairs={{0,64},{1,17},{2,66},{3,19},{4,68},{5,21},{6,70},{7,23},{8,72},{9,... | collective-permute-start | bytes 4718600 | tf_op jit(solution)/shard_map/ppermute | solution.py:132
  123.9 3.1 %collective-permute-done.12 = bf16[2,256,256]{1,2,0:T(8,128)(2,1)S(1)} collective-permute-done((bf16[2,256,256]{1,2,0:T(8,128)(2,1)S(1)}, bf16[2,256,256]{1,2,0:T(8,128)(2,1)S(1)}, u32[]{:S(2)}, u32[]{:S(2)}) %collective-permute-start.12) | collective-permute-done | bytes 262176 | tf_op jit(solution)/shard_map/ppermute | solution.py:144
  127.8 1.3 copy-done.4
  130.2 3.7 %select_convert_fusion.l2_ref = bf16[8,256,256]{2,1,0:T(8,128)(2,1)} fusion(bf16[2,8,256,256]{3,2,1,0:T(8,128)(2,1)} %copy-done.4, pred[8]{0:T(512)(128)(4,1)S(1)} %copy-done.11, pred[8]{0:T(512)(128)(4,1)S(1)} %copy-done.10, pred[8]{0:T(512)(128)(4,1)S(1)} %get-tuple-element.43, bf16[2,256,256]{1,2,0:T(8,128)(2,1)S(1)} %broadcast_select_fusion.6, ...), kind=kOutput, calls=%fused_computation.13 | convolution fusion | flops 540540928 | bytes 4457984 | tf_op jit(solution)/shard_map/iab,bc->iac/dot_general | solution.py:150
  133.9 10.0 %collective-permute-done.20 = bf16[2,8,192,256]{3,2,1,0:T(8,128)(2,1)S(1)} collective-permute-done((bf16[2,8,192,256]{3,2,1,0:T(8,128)(2,1)S(1)}, bf16[2,8,192,256]{3,2,1,0:T(8,128)(2,1)S(1)}, u32[]{:S(2)}, u32[]{:S(2)}) %collective-permute-start.20) | collective-permute-done | bytes 1572896 | tf_op jit(solution)/shard_map/ppermute | solution.py:132
  146.0 2.0 %fusion.4.u2_ref = bf16[12,256,256]{2,1,0:T(8,128)(2,1)} fusion(bf16[1,12,256,256]{3,2,1,0:T(8,128)(2,1)S(1)} %bitcast.114, f32[12,256,256]{1,2,0:T(8,128)S(1)} %fusion.20, pred[12]{0:T(512)(128)(4,1)S(1)} %copy-done.9, pred[12]{0:T(512)(128)(4,1)S(1)} %copy-done.8, bf16[256,256]{1,0:T(8,128)(2,1)S(1)} %fusion.9), kind=kLoop, calls=%fused_computation.16 | loop fusion | flops 3932160 | bytes 6422552 | tf_op jit(solution)/shard_map/squeeze | solution.py:267
  148.0 38.7 %shard_map.46 = bf16[8,12,256,256]{3,2,1,0:T(8,128)(2,1)} custom-call(s32[8,12]{1,0:T(8,128)} %select_add_fusion.codes, bf16[8,12,256,256]{3,2,1,0:T(8,128)(2,1)} %front_ref.1, bf16[8,256,256]{2,1,0:T(8,128)(2,1)} %slice_bitcast_fusion.1.l1_ref, bf16[8,256,256]{2,1,0:T(8,128)(2,1)} %select_convert_fusion.l2_ref, bf16[12,256,256]{2,1,0:T(8,128)(2,1)} %bitcast.109, ...), custom_call_target="tpu_custom_call" | custom-call | tf_op jit(solution)/shard_map/pallas_call | solution.py:189
  (105 shorter events, 28.4 us)
Async XLA Ops:
  8.1 10.6 %copy-start.7 = (s32[8,16,12,8]{1,0,3,2:T(8,128)}, s32[8,16,12,8]{1,0,3,2:T(8,128)S(1)}, u32[]{:S(2)}) copy-start(s32[8,16,12,8]{1,0,3,2:T(8,128)S(1)} %reshape.620) | copy-start | bytes 147460
  10.0 4.7 %copy-start.12 = (bf16[2,256,256]{2,1,0:T(8,128)(2,1)S(1)}, bf16[2,256,256]{2,1,0:T(8,128)(2,1)}, u32[]{:S(2)}) copy-start(bf16[2,256,256]{2,1,0:T(8,128)(2,1)} %param.7) | copy-start | bytes 786436
  10.8 37.4 %collective-permute-start.6 = (bf16[2,256,256]{1,2,0:T(8,128)(2,1)}, bf16[2,256,256]{1,2,0:T(8,128)(2,1)}, u32[]{:S(2)}, u32[]{:S(2)}) collective-permute-start(bf16[2,256,256]{1,2,0:T(8,128)(2,1)} %pad_maximum_fusion.2), channel_id=1, source_target_pairs={{0,1},{1,0},{2,3},{3,2},{4,5},{5,4},{6,7},{7,6},{8,9},{9,8},{10,11... | collective-permute-start | bytes 786440 | tf_op jit(solution)/shard_map/ppermute | solution.py:144
  14.7 2.1 %copy-start.1 = (bf16[1,8,256,256]{3,2,1,0:T(8,128)(2,1)}, bf16[1,8,256,256]{3,2,1,0:T(8,128)(2,1)S(1)}, u32[]{:S(2)}) copy-start(bf16[1,8,256,256]{3,2,1,0:T(8,128)(2,1)S(1)} %bitcast_select_fusion.2) | copy-start | bytes 3145732
  16.8 1.4 copy-start.5
  18.2 31.6 %collective-permute-start = (bf16[2,4,256,256]{3,2,1,0:T(8,128)(2,1)}, bf16[2,4,256,256]{3,2,1,0:T(8,128)(2,1)}, u32[]{:S(2)}, u32[]{:S(2)}) collective-permute-start(bf16[2,4,256,256]{3,2,1,0:T(8,128)(2,1)} %fusion.10), channel_id=1, source_target_pairs={{0,1},{1,0},{2,3},{3,2},{4,5},{5,4},{6,7},{7,6},{8,9},{9,8},{10,11... | collective-permute-start | bytes 3145736 | tf_op jit(solution)/shard_map/ppermute | solution.py:129
  21.5 5.4 %copy-start.3 = (s32[128,96]{0,1:T(8,128)S(1)}, s32[128,96]{0,1:T(8,128)}, u32[]{:S(2)}) copy-start(s32[128,96]{0,1:T(8,128)} %param.5) | copy-start | bytes 147460
  22.7 22.2 %collective-permute-start.13 = (bf16[2,8,192,256]{3,2,1,0:T(8,128)(2,1)}, bf16[2,8,192,256]{3,2,1,0:T(8,128)(2,1)}, u32[]{:S(2)}, u32[]{:S(2)}) collective-permute-start(bf16[2,8,192,256]{3,2,1,0:T(8,128)(2,1)} %fusion.5), channel_id=1, source_target_pairs={{0,64},{1,17},{2,66},{3,19},{4,68},{5,21},{6,70},{7,23},{8,72},{9,... | collective-permute-start | bytes 4718600 | tf_op jit(solution)/shard_map/ppermute | solution.py:129
  46.7 3.1 %copy-start.2 = (bf16[1,8,256,256]{3,2,1,0:T(8,128)(2,1)S(1)}, bf16[1,8,256,256]{3,2,1,0:T(8,128)(2,1)}, u32[]{:S(2)}) copy-start(bf16[1,8,256,256]{3,2,1,0:T(8,128)(2,1)} %copy-done.1) | copy-start | bytes 3145732
  46.7 3.1 %copy-start.6 = (bf16[1,8,256,256]{3,2,1,0:T(8,128)(2,1)S(1)}, bf16[1,8,256,256]{3,2,1,0:T(8,128)(2,1)}, u32[]{:S(2)}) copy-start(bf16[1,8,256,256]{3,2,1,0:T(8,128)(2,1)} %copy-done.5) | copy-start | bytes 3145732
  46.7 12.2 %collective-permute-start.14 = (bf16[2,4,192,256]{3,2,1,0:T(8,128)(2,1)S(1)}, bf16[2,4,192,256]{3,2,1,0:T(8,128)(2,1)S(1)}, u32[]{:S(2)}, u32[]{:S(2)}) collective-permute-start(bf16[2,4,192,256]{3,2,1,0:T(8,128)(2,1)S(1)} %slice.117), channel_id=1, source_target_pairs={{0,32},{1,9},{2,34},{3,11},{4,36},{5,13},{6,38},{7,15},{8,40},{9,1... | collective-permute-start | bytes 2359304 | tf_op jit(solution)/shard_map/ppermute | solution.py:129
  49.2 10.7 %collective-permute-start.7 = (bf16[2,256,256]{1,2,0:T(8,128)(2,1)S(1)}, bf16[2,256,256]{1,2,0:T(8,128)(2,1)S(1)}, u32[]{:S(2)}, u32[]{:S(2)}) collective-permute-start(bf16[2,256,256]{1,2,0:T(8,128)(2,1)S(1)} %broadcast_select_fusion), channel_id=1, source_target_pairs={{0,2},{1,3},{2,0},{3,1},{4,6},{5,7},{6,4},{7,5},{8,10},{9,11},{10,... | collective-permute-start | bytes 786440 | tf_op jit(solution)/shard_map/ppermute | solution.py:144
  51.2 18.5 %collective-permute-start.1 = (bf16[2,2,256,256]{3,2,1,0:T(8,128)(2,1)S(1)}, bf16[2,2,256,256]{3,2,1,0:T(8,128)(2,1)S(1)}, u32[]{:S(2)}, u32[]{:S(2)}) collective-permute-start(bf16[2,2,256,256]{3,2,1,0:T(8,128)(2,1)S(1)} %slice.108), channel_id=1, source_target_pairs={{0,2},{1,3},{2,0},{3,1},{4,6},{5,7},{6,4},{7,5},{8,10},{9,11},{10,... | collective-permute-start | bytes 1572872 | tf_op jit(solution)/shard_map/ppermute | solution.py:129
  59.1 13.2 %collective-permute-start.15 = (bf16[2,2,192,256]{3,2,1,0:T(8,128)(2,1)S(1)}, bf16[2,2,192,256]{3,2,1,0:T(8,128)(2,1)S(1)}, u32[]{:S(2)}, u32[]{:S(2)}) collective-permute-start(bf16[2,2,192,256]{3,2,1,0:T(8,128)(2,1)S(1)} %slice.119), channel_id=1, source_target_pairs={{0,16},{1,65},{2,18},{3,67},{4,20},{5,69},{6,22},{7,71},{8,24},{9,... | collective-permute-start | bytes 1179656 | tf_op jit(solution)/shard_map/ppermute | solution.py:129
  61.0 15.4 %collective-permute-start.8 = (bf16[2,256,256]{1,2,0:T(8,128)(2,1)S(1)}, bf16[2,256,256]{1,2,0:T(8,128)(2,1)S(1)}, u32[]{:S(2)}, u32[]{:S(2)}) collective-permute-start(bf16[2,256,256]{1,2,0:T(8,128)(2,1)S(1)} %broadcast_select_fusion.1), channel_id=1, source_target_pairs={{0,4},{1,5},{2,6},{3,7},{4,0},{5,1},{6,2},{7,3},{8,12},{9,13},{10,... | collective-permute-start | bytes 786440 | tf_op jit(solution)/shard_map/ppermute | solution.py:144
  69.9 11.7 %collective-permute-start.2 = (bf16[2,1,256,256]{3,2,1,0:T(8,128)(2,1)S(1)}, bf16[2,1,256,256]{3,2,1,0:T(8,128)(2,1)S(1)}, u32[]{:S(2)}, u32[]{:S(2)}) collective-permute-start(bf16[2,1,256,256]{3,2,1,0:T(8,128)(2,1)S(1)} %slice.110), channel_id=1, source_target_pairs={{0,4},{1,5},{2,6},{3,7},{4,0},{5,1},{6,2},{7,3},{8,12},{9,13},{10,... | collective-permute-start | bytes 786440 | tf_op jit(solution)/shard_map/ppermute | solution.py:129
  72.4 7.6 %collective-permute-start.16 = (bf16[2,1,192,256]{3,2,1,0:T(8,128)(2,1)S(1)}, bf16[2,1,192,256]{3,2,1,0:T(8,128)(2,1)S(1)}, u32[]{:S(2)}, u32[]{:S(2)}) collective-permute-start(bf16[2,1,192,256]{3,2,1,0:T(8,128)(2,1)S(1)} %slice.121), channel_id=1, source_target_pairs={{0,8},{1,33},{2,10},{3,35},{4,12},{5,37},{6,14},{7,39},{8,0},{9,41... | collective-permute-start | bytes 589832 | tf_op jit(solution)/shard_map/ppermute | solution.py:129
  76.5 10.8 %collective-permute-start.9 = (bf16[2,256,256]{1,2,0:T(8,128)(2,1)S(1)}, bf16[2,256,256]{1,2,0:T(8,128)(2,1)S(1)}, u32[]{:S(2)}, u32[]{:S(2)}) collective-permute-start(bf16[2,256,256]{1,2,0:T(8,128)(2,1)S(1)} %broadcast_select_fusion.2), channel_id=1, source_target_pairs={{0,8},{1,9},{2,10},{3,11},{4,12},{5,13},{6,14},{7,15},{8,0},{9,1},... | collective-permute-start | bytes 786440 | tf_op jit(solution)/shard_map/ppermute | solution.py:144
  80.1 7.0 %collective-permute-start.17 = (bf16[2,1,192,256]{3,2,1,0:T(8,128)(2,1)S(1)}, bf16[2,1,192,256]{3,2,1,0:T(8,128)(2,1)S(1)}, u32[]{:S(2)}, u32[]{:S(2)}) collective-permute-start(bf16[2,1,192,256]{3,2,1,0:T(8,128)(2,1)S(1)} %slice_select_fusion.4), channel_id=1, source_target_pairs={{0,8},{1,33},{2,10},{3,35},{4,12},{5,37},{6,14},{7,39},{8,0},{9,41... | collective-permute-start | bytes 589832 | tf_op jit(solution)/shard_map/ppermute | solution.py:132
  81.7 9.3 %collective-permute-start.3 = (bf16[2,1,256,256]{3,2,1,0:T(8,128)(2,1)S(1)}, bf16[2,1,256,256]{3,2,1,0:T(8,128)(2,1)S(1)}, u32[]{:S(2)}, u32[]{:S(2)}) collective-permute-start(bf16[2,1,256,256]{3,2,1,0:T(8,128)(2,1)S(1)} %slice_select_fusion.3), channel_id=1, source_target_pairs={{0,4},{1,5},{2,6},{3,7},{4,0},{5,1},{6,2},{7,3},{8,12},{9,13},{10,... | collective-permute-start | bytes 786440 | tf_op jit(solution)/shard_map/ppermute | solution.py:132
  87.2 13.6 %collective-permute-start.18 = (bf16[2,2,192,256]{3,2,1,0:T(8,128)(2,1)S(1)}, bf16[2,2,192,256]{3,2,1,0:T(8,128)(2,1)S(1)}, u32[]{:S(2)}, u32[]{:S(2)}) collective-permute-start(bf16[2,2,192,256]{3,2,1,0:T(8,128)(2,1)S(1)} %maximum_select_fusion.6), channel_id=1, source_target_pairs={{0,16},{1,65},{2,18},{3,67},{4,20},{5,69},{6,22},{7,71},{8,24},{9,... | collective-permute-start | bytes 1179656 | tf_op jit(solution)/shard_map/ppermute | solution.py:132
  87.4 19.0 %collective-permute-start.10 = (bf16[2,256,256]{1,2,0:T(8,128)(2,1)S(1)}, bf16[2,256,256]{1,2,0:T(8,128)(2,1)S(1)}, u32[]{:S(2)}, u32[]{:S(2)}) collective-permute-start(bf16[2,256,256]{1,2,0:T(8,128)(2,1)S(1)} %broadcast_select_fusion.3), channel_id=1, source_target_pairs={{0,16},{1,17},{2,18},{3,19},{4,20},{5,21},{6,22},{7,23},{8,24},{9,... | collective-permute-start | bytes 786440 | tf_op jit(solution)/shard_map/ppermute | solution.py:144
  91.2 17.1 %collective-permute-start.4 = (bf16[2,2,256,256]{3,2,1,0:T(8,128)(2,1)S(1)}, bf16[2,2,256,256]{3,2,1,0:T(8,128)(2,1)}, u32[]{:S(2)}, u32[]{:S(2)}) collective-permute-start(bf16[2,2,256,256]{3,2,1,0:T(8,128)(2,1)S(1)} %maximum_select_fusion.5), channel_id=1, source_target_pairs={{0,2},{1,3},{2,0},{3,1},{4,6},{5,7},{6,4},{7,5},{8,10},{9,11},{10,... | collective-permute-start | bytes 1572872 | tf_op jit(solution)/shard_map/ppermute | solution.py:132
  101.0 18.2 %collective-permute-start.19 = (bf16[2,4,192,256]{3,2,1,0:T(8,128)(2,1)S(1)}, bf16[2,4,192,256]{3,2,1,0:T(8,128)(2,1)S(1)}, u32[]{:S(2)}, u32[]{:S(2)}) collective-permute-start(bf16[2,4,192,256]{3,2,1,0:T(8,128)(2,1)S(1)} %maximum_select_fusion.4), channel_id=1, source_target_pairs={{0,32},{1,9},{2,34},{3,11},{4,36},{5,13},{6,38},{7,15},{8,40},{9,1... | collective-permute-start | bytes 2359304 | tf_op jit(solution)/shard_map/ppermute | solution.py:132
  106.6 12.4 %collective-permute-start.11 = (bf16[2,256,256]{1,2,0:T(8,128)(2,1)S(1)}, bf16[2,256,256]{1,2,0:T(8,128)(2,1)S(1)}, u32[]{:S(2)}, u32[]{:S(2)}) collective-permute-start(bf16[2,256,256]{1,2,0:T(8,128)(2,1)S(1)} %broadcast_select_fusion.4), channel_id=1, source_target_pairs={{0,32},{1,33},{2,34},{3,35},{4,36},{5,37},{6,38},{7,39},{8,40},{9,... | collective-permute-start | bytes 786440 | tf_op jit(solution)/shard_map/ppermute | solution.py:144
  109.8 17.6 %collective-permute-start.5 = (bf16[2,4,256,256]{3,2,1,0:T(8,128)(2,1)S(1)}, bf16[2,4,256,256]{3,2,1,0:T(8,128)(2,1)S(1)}, u32[]{:S(2)}, u32[]{:S(2)}) collective-permute-start(bf16[2,4,256,256]{3,2,1,0:T(8,128)(2,1)S(1)} %maximum_select_fusion.3), channel_id=1, source_target_pairs={{0,1},{1,0},{2,3},{3,2},{4,5},{5,4},{6,7},{7,6},{8,9},{9,8},{10,11... | collective-permute-start | bytes 3145736 | tf_op jit(solution)/shard_map/ppermute | solution.py:132
  119.1 8.0 %collective-permute-start.12 = (bf16[2,256,256]{1,2,0:T(8,128)(2,1)S(1)}, bf16[2,256,256]{1,2,0:T(8,128)(2,1)S(1)}, u32[]{:S(2)}, u32[]{:S(2)}) collective-permute-start(bf16[2,256,256]{1,2,0:T(8,128)(2,1)S(1)} %broadcast_select_fusion.5), channel_id=1, source_target_pairs={{0,64},{1,65},{2,66},{3,67},{4,68},{5,69},{6,70},{7,71},{8,72},{9,... | collective-permute-start | bytes 786440 | tf_op jit(solution)/shard_map/ppermute | solution.py:144
  119.2 8.0 %copy-start.13 = (bf16[2,256,256]{2,1,0:T(8,128)(2,1)S(1)}, bf16[2,256,256]{2,1,0:T(8,128)(2,1)}, u32[]{:S(2)}) copy-start(bf16[2,256,256]{2,1,0:T(8,128)(2,1)} %param.7) | copy-start | bytes 786436
  119.5 24.4 %collective-permute-start.20 = (bf16[2,8,192,256]{3,2,1,0:T(8,128)(2,1)S(1)}, bf16[2,8,192,256]{3,2,1,0:T(8,128)(2,1)S(1)}, u32[]{:S(2)}, u32[]{:S(2)}) collective-permute-start(bf16[2,8,192,256]{3,2,1,0:T(8,128)(2,1)S(1)} %maximum_select_fusion.2), channel_id=1, source_target_pairs={{0,64},{1,17},{2,66},{3,19},{4,68},{5,21},{6,70},{7,23},{8,72},{9,... | collective-permute-start | bytes 4718600 | tf_op jit(solution)/shard_map/ppermute | solution.py:132
  127.8 1.3 copy-start.4
  144.8 1.2 copy-start
  144.8 1.2 copy-start.8
  (3 other events, 3.3 us)

commit v8 on v6

--- a/solution.py
+++ b/solution.py
@@ -16,7 +16,7 @@
 def pick(index, options):
     out = options[-1]
     for k in range(len(options) - 2, -1, -1):
-        out = jnp.where(index == k, options[k], out)
+        out = per_part(index == k, options[k], out)
     return out
 
 
@@ -105,33 +105,60 @@
     return pairs
 
 
+def dims_of(on_row, parity, step):
+    if on_row:
+        z_first = (parity == 0) == (step == 0)
+        return (2 if z_first else 0), RING
+    return ((0, CORES), (1, RING))[step]
+
+
+def digit_pairs(nrow, ncol, on_row, step, mask):
+    pairs = []
+    for r in range(nrow):
+        for c in range(ncol):
+            shift, _ = dims_of(on_row, c % CORES, step)
+            if on_row:
+                pairs.append((r * ncol + c, (r ^ (mask << shift)) * ncol + c))
+            else:
+                pairs.append((r * ncol + c, r * ncol + (c ^ (mask << shift))))
+    return pairs
+
+
 def xor_bcast(value, root, on_row):
     nrow = lax.axis_size("row")
     ncol = lax.axis_size("col")
     me = lax.axis_index("row") if on_row else lax.axis_index("col")
     parity = lax.axis_index("col") % CORES
-    steps = (nrow if on_row else ncol).bit_length() - 1
     relative = me ^ root
-
-    def bit(step):
+    axes = ("row", "col")
+
+    def digit(step):
         if on_row:
-            b = jnp.where(parity == 0, ROW_ORDERS[0][step], ROW_ORDERS[1][step])
+            shift = jnp.where(parity == 0, 2 if step == 0 else 0, 0 if step == 0 else 2)
         else:
-            b = COL_ORDER[step]
-        return (relative >> b) & 1
-
+            shift = dims_of(False, 0, step)[0]
+        return (relative >> shift) & (RING - 1 if on_row or step == 1 else CORES - 1)
+
+    sizes = [dims_of(on_row, 0, step)[1] for step in range(2)]
     shape = value.shape
-    pieces = 1 << steps
-    buf = value.reshape(shape[0], pieces, -1, shape[-1])
-    axes = ("row", "col")
-    for step in range(steps):
-        half = buf.shape[1] // 2
-        got = lax.ppermute(buf[:, half:], axes, xor_pairs(nrow, ncol, on_row, step))
-        buf = per_part(bit(step) == 1, got, buf[:, :half])
-    for step in reversed(range(steps)):
-        got = lax.ppermute(buf, axes, xor_pairs(nrow, ncol, on_row, step))
-        low = bit(step) == 0
-        buf = per_part(low, jnp.concatenate([buf, got], 1), jnp.concatenate([got, buf], 1))
+    buf = value.reshape(shape[0], sizes[0], sizes[1], -1, shape[-1])
+    for step in range(2):
+        d = digit(step)
+        groups = [buf[:, m] for m in range(sizes[step])]
+        got = [None] + [
+            lax.ppermute(groups[m], axes, digit_pairs(nrow, ncol, on_row, step, m))
+            for m in range(1, sizes[step])
+        ]
+        buf = pick(d, [groups[0]] + got[1:])
+    for step in reversed(range(2)):
+        d = digit(step)
+        got = [buf] + [
+            lax.ppermute(buf, axes, digit_pairs(nrow, ncol, on_row, step, m))
+            for m in range(1, sizes[step])
+        ]
+        buf = jnp.stack(
+            [pick(d, [got[dd ^ t] for dd in range(sizes[step])]) for t in range(sizes[step])], axis=1
+        )
     return buf.reshape(shape)
 
 

time: 170 us -> 157 us (0.924)
  waiting for transfers between devices: 63.4 us -> 43.8 us
  starting transfers between devices: 36.4 us -> 45 us
  other arithmetic: 25 us -> 23.1 us
    ppermute x14 -> x20, waiting for transfers between devices: 45.3 us -> 15.2 us  [the longest x10 12.3 us: xor_bcast(): lax.ppermute(groups[m], axes, digit_pairs(nrow, ncol, on_row, step, m))]
    ppermute x14 -> x20, starting transfers between devices: 18.2 us -> 34.3 us  [the longest x10 18.4 us: xor_bcast(): lax.ppermute(groups[m], axes, digit_pairs(nrow, ncol, on_row, step, m))]
    ppermute x7, waiting for transfers between devices: 18.1 us -> 28.6 us  [all_bcast(): lax.ppermute(value, ('row', 'col'), [(d, d ^ 1 << b) for d in range(n)])]
    ppermute x7, starting transfers between devices: 18.3 us -> 10.7 us  [all_bcast(): lax.ppermute(value, ('row', 'col'), [(d, d ^ 1 << b) for d in range(n)])]
    squeeze x0 -> x2, other arithmetic: none -> 2.65 us  [xor_bcast(): groups = [buf[:, m] for m in range(sizes[step])]]
    select_n x21 -> x11, other arithmetic: 9.45 us -> 8.5 us  [per_part(): return jnp.where(cond.reshape((-1,) + (1,) * (a.ndim - 1)), a, b)]
  transfers between devices with their start and end apart: 21 -> 27, of which waited for: 11 -> 8; matrix products, arithmetic and copies ran while one was open for 19% -> 19% of each run, Pallas kernels for 0% -> 0%
where the time goes in v8:
time: 157 us; the launch traced here: 156 us
  starting transfers between devices  45 us (29%)
  waiting for transfers between devices  43.8 us (28%)
  other arithmetic  23.1 us (15%)
  Pallas kernels  16.7 us (11%)
  between operations  11.3 us (7%)
  local copies, waits for them, and re-layouts  10.1 us (6%)
  matrix products  5.71 us (4%)
    ppermute x7, waiting for transfers between devices, all_bcast(): lax.ppermute(value, ('row', 'col'), [(d, d ^ 1 << b) for d in range(n)])  28.6 us
    ppermute x10, starting transfers between devices, xor_bcast(): lax.ppermute(groups[m], axes, digit_pairs(nrow, ncol, on_row, step, m))  18.4 us
    pallas_call x1, Pallas kernels, both_updates(): pl.pallas_call(update_kernel, grid_spec=pltpu.PrefetchScalarGridSpec(num_...  16.7 us
    ppermute x10, starting transfers between devices, xor_bcast(): lax.ppermute(buf, axes, digit_pairs(nrow, ncol, on_row, step, m))  15.9 us
    ppermute x10, waiting for transfers between devices, xor_bcast(): lax.ppermute(groups[m], axes, digit_pairs(nrow, ncol, on_row, step, m))  12.3 us
    ppermute x7, starting transfers between devices, all_bcast(): lax.ppermute(value, ('row', 'col'), [(d, d ^ 1 << b) for d in range(n)])  10.7 us
    select_n x11, other arithmetic, per_part(): return jnp.where(cond.reshape((-1,) + (1,) * (a.ndim - 1)), a, b)  8.5 us
    dot_general x3, matrix products, lower_local(): jnp.einsum('iab,bc->iac', column, inverse, preferred_element_type=jnp.flo...  5.13 us
  transfers between devices with their start and end apart: 27, of which 8 were waited for; matrix products, arithmetic and copies ran while one was open for 19% of the time, Pallas kernels for 0%

profile of v8, /device:TPU:6, one launch (start us, length us, event | category | flops | bytes accessed | tf_op | source)
XLA Modules:
  0.0 155.7 jit_solution(14507978358226181474)
XLA Ops:
  14.7 2.1 %select_convert_fusion.1 = bf16[8,256,256]{2,1,0:T(8,128)(2,1)S(1)} fusion(bf16[8,12,256,256]{3,2,1,0:T(8,128)(2,1)} %front_ref.1, s32[]{:T(128)S(6)} %select_n.376, pred[8]{0:T(512)(128)(4,1)S(1)} %get-tuple-element.7, pred[8]{0:T(512)(128)(4,1)S(1)} %get-tuple-element.18, bf16[2,256,256]{2,1,0:T(8,128)(2,1)S(1)} %copy-done.8), kind=kOutput, calls=%fused_computation.19 | convolution fusion | flops 270008320 | bytes 2229252 | tf_op jit(solution)/shard_map/iab,bc->iac/dot_general | solution.py:177
  19.1 2.2 %dynamic-slice_select_fusion = (bf16[1,12,256,256]{3,2,1,0:T(8,128)(2,1)S(1)}, bf16[1,12,256,256]{3,2,1,0:T(8,128)(2,1)S(1)}) fusion(bf16[8,12,256,256]{3,2,1,0:T(8,128)(2,1)} %front_ref.1, s32[]{:T(128)S(6)} %select_n.413, pred[12]{0:T(512)(128)(4,1)S(1)} %get-tuple-element.5, s32[]{:T(128)S(6)} %select_n.408, pred[12]{0:T(512)(128)(4,1)S(1)} %get-tuple-element.6), kind=kLoop, calls=%fused_computation.22 | loop fusion | flops 1572864 | bytes 6291488 | tf_op jit(solution)/shard_map/jit(_where)/select_n | solution.py:229
  21.3 1.5 fusion.25
  22.8 4.0 %collective-permute-start.17 = (bf16[2,4,192,256]{3,2,1,0:T(8,128)(2,1)}, bf16[2,4,192,256]{3,2,1,0:T(8,128)(2,1)}, u32[]{:S(2)}, u32[]{:S(2)}) collective-permute-start(bf16[2,4,192,256]{3,2,1,0:T(8,128)(2,1)} %get-tuple-element.30), channel_id=1, source_target_pairs={{0,96},{1,25},{2,98},{3,27},{4,100},{5,29},{6,102},{7,31},{8,104},... | collective-permute-start | bytes 2359304 | tf_op jit(solution)/shard_map/ppermute | solution.py:149
  26.8 1.5 collective-permute-start.16
  36.7 1.7 %broadcast_select_fusion.1 = bf16[2,256,256]{1,2,0:T(8,128)(2,1)} fusion(bf16[2,256,256]{1,2,0:T(8,128)(2,1)} %collective-permute-done.8, pred[2]{0:T(512)(128)(4,1)S(1)} %get-tuple-element.63, bf16[1,256,256]{1,2,0:T(8,128)(2,1)S(1)} %get-tuple-element.73, bf16[1,256,256]{1,2,0:T(8,128)(2,1)S(1)} %get-tuple-element.74), kind=kLoop, calls=%fused_computation.69 | loop fusion | flops 262144 | bytes 786434 | tf_op jit(solution)/shard_map/jit(_where)/select_n | solution.py:13
  38.5 1.6 %collective-permute-start.9 = (bf16[2,256,256]{1,2,0:T(8,128)(2,1)}, bf16[2,256,256]{1,2,0:T(8,128)(2,1)}, u32[]{:S(2)}, u32[]{:S(2)}) collective-permute-start(bf16[2,256,256]{1,2,0:T(8,128)(2,1)} %broadcast_select_fusion.1), channel_id=1, source_target_pairs={{0,2},{1,3},{2,0},{3,1},{4,6},{5,7},{6,4},{7,5},{8,10},{9,11},{10,... | collective-permute-start | bytes 786440 | tf_op jit(solution)/shard_map/ppermute | solution.py:171
  40.1 5.2 %collective-permute-done.9 = bf16[2,256,256]{1,2,0:T(8,128)(2,1)} collective-permute-done((bf16[2,256,256]{1,2,0:T(8,128)(2,1)}, bf16[2,256,256]{1,2,0:T(8,128)(2,1)}, u32[]{:S(2)}, u32[]{:S(2)}) %collective-permute-start.9) | collective-permute-done | bytes 262176 | tf_op jit(solution)/shard_map/ppermute | solution.py:171
  45.4 1.8 %broadcast_select_fusion.2 = bf16[2,256,256]{1,2,0:T(8,128)(2,1)} fusion(bf16[2,256,256]{1,2,0:T(8,128)(2,1)} %collective-permute-done.9, pred[2]{0:T(512)(128)(4,1)S(1)} %get-tuple-element.59, bf16[2,256,256]{1,2,0:T(8,128)(2,1)} %collective-permute-done.8, bf16[1,256,256]{1,2,0:T(8,128)(2,1)S(1)} %get-tuple-element.73, ...), kind=kLoop, calls=%fused_computation.70 | loop fusion | flops 393216 | bytes 1048580 | tf_op jit(solution)/shard_map/jit(_where)/select_n | solution.py:13
  47.2 3.2 %collective-permute-start.10 = (bf16[2,256,256]{1,2,0:T(8,128)(2,1)}, bf16[2,256,256]{1,2,0:T(8,128)(2,1)S(1)}, u32[]{:S(2)}, u32[]{:S(2)}) collective-permute-start(bf16[2,256,256]{1,2,0:T(8,128)(2,1)} %broadcast_select_fusion.2), channel_id=1, source_target_pairs={{0,4},{1,5},{2,6},{3,7},{4,0},{5,1},{6,2},{7,3},{8,12},{9,13},{10,... | collective-permute-start | bytes 786440 | tf_op jit(solution)/shard_map/ppermute | solution.py:171
  51.3 4.0 %collective-permute-done.10 = bf16[2,256,256]{1,2,0:T(8,128)(2,1)S(1)} collective-permute-done((bf16[2,256,256]{1,2,0:T(8,128)(2,1)}, bf16[2,256,256]{1,2,0:T(8,128)(2,1)S(1)}, u32[]{:S(2)}, u32[]{:S(2)}) %collective-permute-start.10) | collective-permute-done | bytes 262176 | tf_op jit(solution)/shard_map/ppermute | solution.py:171
  57.1 1.8 %fusion.22 = bf16[2,4,192,256]{3,2,1,0:T(8,128)(2,1)S(1)} fusion(bf16[1,4,4,192,256]{4,3,2,0,1:T(8,128)(2,1)S(1)} %bitcast.197, bf16[1,4,4,192,256]{4,3,2,0,1:T(8,128)(2,1)S(1)} %bitcast.195, bf16[2,4,192,256]{3,2,1,0:T(8,128)(2,1)} %collective-permute-done.15, bf16[2,4,192,256]{3,2,1,0:T(8,128)(2,1)} %collective-permute-done.16, ...), kind=kLoop, calls=%fused_computation.48 | loop fusion | flops 1572864 | bytes 6291462 | tf_op jit(solution)/shard_map/jit(_where)/select_n | solution.py:13
  60.5 3.2 %collective-permute-start.19 = (bf16[2,192,256]{2,1,0:T(8,128)(2,1)S(1)}, bf16[2,192,256]{2,1,0:T(8,128)(2,1)S(1)}, u32[]{:S(2)}, u32[]{:S(2)}) collective-permute-start(bf16[2,192,256]{2,1,0:T(8,128)(2,1)S(1)} %get-tuple-element.50), channel_id=1, source_target_pairs={{0,16},{1,65},{2,18},{3,67},{4,20},{5,69},{6,22},{7,71},{8,24},{9,... | collective-permute-start | bytes 589832 | tf_op jit(solution)/shard_map/ppermute | solution.py:149
  63.7 2.2 %collective-permute-done.20 = bf16[2,192,256]{2,1,0:T(8,128)(2,1)S(1)} collective-permute-done((bf16[2,192,256]{2,1,0:T(8,128)(2,1)S(1)}, bf16[2,192,256]{2,1,0:T(8,128)(2,1)S(1)}, u32[]{:S(2)}, u32[]{:S(2)}) %collective-permute-start.20) | collective-permute-done | bytes 196640 | tf_op jit(solution)/shard_map/ppermute | solution.py:149
  65.9 3.6 %collective-permute-done.19 = bf16[2,192,256]{2,1,0:T(8,128)(2,1)S(1)} collective-permute-done((bf16[2,192,256]{2,1,0:T(8,128)(2,1)S(1)}, bf16[2,192,256]{2,1,0:T(8,128)(2,1)S(1)}, u32[]{:S(2)}, u32[]{:S(2)}) %collective-permute-start.19) | collective-permute-done | bytes 196640 | tf_op jit(solution)/shard_map/ppermute | solution.py:149
  71.9 1.8 %collective-permute-start.21 = (bf16[2,192,256]{2,1,0:T(8,128)(2,1)S(1)}, bf16[2,192,256]{2,1,0:T(8,128)(2,1)S(1)}, u32[]{:S(2)}, u32[]{:S(2)}) collective-permute-start(bf16[2,192,256]{2,1,0:T(8,128)(2,1)S(1)} %fusion.28), channel_id=1, source_target_pairs={{0,8},{1,33},{2,10},{3,35},{4,12},{5,37},{6,14},{7,39},{8,0},{9,41... | collective-permute-start | bytes 589832 | tf_op jit(solution)/shard_map/ppermute | solution.py:156
  73.9 1.5 collective-permute-start.12
  76.9 3.1 %collective-permute-start.3 = (bf16[2,256,256]{2,1,0:T(8,128)(2,1)S(1)}, bf16[2,256,256]{2,1,0:T(8,128)(2,1)S(1)}, u32[]{:S(2)}, u32[]{:S(2)}) collective-permute-start(bf16[2,256,256]{2,1,0:T(8,128)(2,1)S(1)} %get-tuple-element.41), channel_id=1, source_target_pairs={{0,6},{1,7},{2,4},{3,5},{4,2},{5,3},{6,0},{7,1},{8,14},{9,15},{10,... | collective-permute-start | bytes 786440 | tf_op jit(solution)/shard_map/ppermute | solution.py:149
  80.0 1.5 collective-permute-done.23
  81.5 1.6 %collective-permute-start.1 = (bf16[2,256,256]{2,1,0:T(8,128)(2,1)S(1)}, bf16[2,256,256]{2,1,0:T(8,128)(2,1)S(1)}, u32[]{:S(2)}, u32[]{:S(2)}) collective-permute-start(bf16[2,256,256]{2,1,0:T(8,128)(2,1)S(1)} %get-tuple-element.42), channel_id=1, source_target_pairs={{0,2},{1,3},{2,0},{3,1},{4,6},{5,7},{6,4},{7,5},{8,10},{9,11},{10,... | collective-permute-start | bytes 786440 | tf_op jit(solution)/shard_map/ppermute | solution.py:149
  83.0 2.9 %collective-permute-start.2 = (bf16[2,256,256]{2,1,0:T(8,128)(2,1)S(1)}, bf16[2,256,256]{2,1,0:T(8,128)(2,1)S(1)}, u32[]{:S(2)}, u32[]{:S(2)}) collective-permute-start(bf16[2,256,256]{2,1,0:T(8,128)(2,1)S(1)} %get-tuple-element.43), channel_id=1, source_target_pairs={{0,4},{1,5},{2,6},{3,7},{4,0},{5,1},{6,2},{7,3},{8,12},{9,13},{10,... | collective-permute-start | bytes 786440 | tf_op jit(solution)/shard_map/ppermute | solution.py:149
  86.2 1.7 %collective-permute-start.13 = (bf16[2,256,256]{1,2,0:T(8,128)(2,1)S(1)}, bf16[2,256,256]{1,2,0:T(8,128)(2,1)S(1)}, u32[]{:S(2)}, u32[]{:S(2)}) collective-permute-start(bf16[2,256,256]{1,2,0:T(8,128)(2,1)S(1)} %broadcast_select_fusion.5), channel_id=1, source_target_pairs={{0,32},{1,33},{2,34},{3,35},{4,36},{5,37},{6,38},{7,39},{8,40},{9,... | collective-permute-start | bytes 786440 | tf_op jit(solution)/shard_map/ppermute | solution.py:171
  87.9 6.6 %collective-permute-done.2 = bf16[2,256,256]{2,1,0:T(8,128)(2,1)S(1)} collective-permute-done((bf16[2,256,256]{2,1,0:T(8,128)(2,1)S(1)}, bf16[2,256,256]{2,1,0:T(8,128)(2,1)S(1)}, u32[]{:S(2)}, u32[]{:S(2)}) %collective-permute-start.2) | collective-permute-done | bytes 262176 | tf_op jit(solution)/shard_map/ppermute | solution.py:149
  94.7 2.7 %collective-permute-start.5 = (bf16[2,256,256]{2,1,0:T(8,128)(2,1)S(1)}, bf16[2,256,256]{2,1,0:T(8,128)(2,1)S(1)}, u32[]{:S(2)}, u32[]{:S(2)}) collective-permute-start(bf16[2,256,256]{2,1,0:T(8,128)(2,1)S(1)} %fusion.27), channel_id=1, source_target_pairs={{0,4},{1,5},{2,6},{3,7},{4,0},{5,1},{6,2},{7,3},{8,12},{9,13},{10,... | collective-permute-start | bytes 786440 | tf_op jit(solution)/shard_map/ppermute | solution.py:156
  98.9 3.2 %collective-permute-start.26 = (bf16[2,4,192,256]{3,2,1,0:T(8,128)(2,1)S(1)}, bf16[2,4,192,256]{3,2,1,0:T(8,128)(2,1)S(1)}, u32[]{:S(2)}, u32[]{:S(2)}) collective-permute-start(bf16[2,4,192,256]{3,2,1,0:T(8,128)(2,1)S(1)} %pad_maximum_fusion.5), channel_id=1, source_target_pairs={{0,96},{1,25},{2,98},{3,27},{4,100},{5,29},{6,102},{7,31},{8,104},... | collective-permute-start | bytes 2359304 | tf_op jit(solution)/shard_map/ppermute | solution.py:156
  102.1 1.5 collective-permute-start.25
  105.1 2.6 %collective-permute-start.24 = (bf16[2,4,192,256]{3,2,1,0:T(8,128)(2,1)S(1)}, bf16[2,4,192,256]{3,2,1,0:T(8,128)(2,1)S(1)}, u32[]{:S(2)}, u32[]{:S(2)}) collective-permute-start(bf16[2,4,192,256]{3,2,1,0:T(8,128)(2,1)S(1)} %pad_maximum_fusion.5), channel_id=1, source_target_pairs={{0,32},{1,9},{2,34},{3,11},{4,36},{5,13},{6,38},{7,15},{8,40},{9,1... | collective-permute-start | bytes 2359304 | tf_op jit(solution)/shard_map/ppermute | solution.py:156
  107.7 2.0 %collective-permute-start.14 = (bf16[2,256,256]{1,2,0:T(8,128)(2,1)S(1)}, bf16[2,256,256]{1,2,0:T(8,128)(2,1)S(1)}, u32[]{:S(2)}, u32[]{:S(2)}) collective-permute-start(bf16[2,256,256]{1,2,0:T(8,128)(2,1)S(1)} %broadcast_select_fusion.6), channel_id=1, source_target_pairs={{0,64},{1,65},{2,66},{3,67},{4,68},{5,69},{6,70},{7,71},{8,72},{9,... | collective-permute-start | bytes 786440 | tf_op jit(solution)/shard_map/ppermute | solution.py:171
  110.3 19.4 %collective-permute-done.14 = bf16[2,256,256]{1,2,0:T(8,128)(2,1)S(1)} collective-permute-done((bf16[2,256,256]{1,2,0:T(8,128)(2,1)S(1)}, bf16[2,256,256]{1,2,0:T(8,128)(2,1)S(1)}, u32[]{:S(2)}, u32[]{:S(2)}) %collective-permute-start.14) | collective-permute-done | bytes 262176 | tf_op jit(solution)/shard_map/ppermute | solution.py:171
  132.6 2.0 %fusion.4.u2_ref = bf16[12,256,256]{2,1,0:T(8,128)(2,1)} fusion(bf16[1,12,256,256]{3,2,1,0:T(8,128)(2,1)S(1)} %bitcast.200, f32[12,256,256]{1,2,0:T(8,128)S(1)} %fusion.29, pred[12]{0:T(512)(128)(4,1)S(1)} %get-tuple-element.11, pred[12]{0:T(512)(128)(4,1)S(1)} %get-tuple-element.9, bf16[256,256]{1,0:T(8,128)(2,1)S(1)} %fusion.8), kind=kLoop, calls=%fused_computation.21 | loop fusion | flops 3932160 | bytes 6422552 | tf_op jit(solution)/shard_map/squeeze | solution.py:292
  136.1 2.8 %select_convert_fusion.l2_ref = bf16[8,256,256]{2,1,0:T(8,128)(2,1)} fusion(pred[8]{0:T(512)(128)(4,1)S(1)} %get-tuple-element.65, bf16[8,1,256,256]{2,3,0,1:T(8,128)(2,1)S(1)} %bitcast.205, bf16[8,1,256,256]{2,3,0,1:T(8,128)(2,1)S(1)} %bitcast.204, bf16[8,256,256]{2,1,0:T(8,128)(2,1)S(1)} %bitcast.198, pred[8]{0:T(512)(128)(4,1)S(1)} %get-tuple-element.64, ...), kind=kOutput, calls=%fused_computation.18 | convolution fusion | flops 540540928 | bytes 4457984 | tf_op jit(solution)/shard_map/iab,bc->iac/dot_general | solution.py:177
  138.9 16.7 %shard_map.46 = bf16[8,12,256,256]{3,2,1,0:T(8,128)(2,1)} custom-call(s32[8,12]{1,0:T(8,128)} %select_add_fusion.codes, bf16[8,12,256,256]{3,2,1,0:T(8,128)(2,1)} %front_ref.1, bf16[8,256,256]{2,1,0:T(8,128)(2,1)} %bitcast.199, bf16[8,256,256]{2,1,0:T(8,128)(2,1)} %select_convert_fusion.l2_ref, bf16[12,256,256]{2,1,0:T(8,128)(2,1)} %bitcast.193, ...), custom_call_target="tpu_custom_call" | custom-call | tf_op jit(solution)/shard_map/pallas_call | solution.py:214
  (109 shorter events, 31.3 us)
Async XLA Ops:
  8.3 10.2 %copy-start.7 = (s32[8,16,12,8]{1,0,3,2:T(8,128)}, s32[8,16,12,8]{1,0,3,2:T(8,128)S(1)}, u32[]{:S(2)}) copy-start(s32[8,16,12,8]{1,0,3,2:T(8,128)S(1)} %reshape.615) | copy-start | bytes 147460
  11.1 25.7 %collective-permute-start.8 = (bf16[2,256,256]{1,2,0:T(8,128)(2,1)}, bf16[2,256,256]{1,2,0:T(8,128)(2,1)}, u32[]{:S(2)}, u32[]{:S(2)}) collective-permute-start(bf16[2,256,256]{1,2,0:T(8,128)(2,1)} %pad_maximum_fusion.6), channel_id=1, source_target_pairs={{0,1},{1,0},{2,3},{3,2},{4,5},{5,4},{6,7},{7,6},{8,9},{9,8},{10,11... | collective-permute-start | bytes 786440 | tf_op jit(solution)/shard_map/ppermute | solution.py:171
  18.0 57.4 %collective-permute-start = (bf16[2,4,256,256]{3,2,1,0:T(8,128)(2,1)}, bf16[2,4,256,256]{3,2,1,0:T(8,128)(2,1)}, u32[]{:S(2)}, u32[]{:S(2)}) collective-permute-start(bf16[2,4,256,256]{3,2,1,0:T(8,128)(2,1)} %fusion.13), channel_id=1, source_target_pairs={{0,1},{1,0},{2,3},{3,2},{4,5},{5,4},{6,7},{7,6},{8,9},{9,8},{10,11... | collective-permute-start | bytes 3145736 | tf_op jit(solution)/shard_map/ppermute | solution.py:149
  21.3 11.4 %copy-start.4 = (s32[128,96]{0,1:T(8,128)S(1)}, s32[128,96]{0,1:T(8,128)}, u32[]{:S(2)}) copy-start(s32[128,96]{0,1:T(8,128)} %param.5) | copy-start | bytes 147460
  22.8 34.3 %collective-permute-start.17 = (bf16[2,4,192,256]{3,2,1,0:T(8,128)(2,1)}, bf16[2,4,192,256]{3,2,1,0:T(8,128)(2,1)}, u32[]{:S(2)}, u32[]{:S(2)}) collective-permute-start(bf16[2,4,192,256]{3,2,1,0:T(8,128)(2,1)} %get-tuple-element.30), channel_id=1, source_target_pairs={{0,96},{1,25},{2,98},{3,27},{4,100},{5,29},{6,102},{7,31},{8,104},... | collective-permute-start | bytes 2359304 | tf_op jit(solution)/shard_map/ppermute | solution.py:149
  26.8 30.2 %collective-permute-start.15 = (bf16[2,4,192,256]{3,2,1,0:T(8,128)(2,1)}, bf16[2,4,192,256]{3,2,1,0:T(8,128)(2,1)}, u32[]{:S(2)}, u32[]{:S(2)}) collective-permute-start(bf16[2,4,192,256]{3,2,1,0:T(8,128)(2,1)} %get-tuple-element.31), channel_id=1, source_target_pairs={{0,32},{1,9},{2,34},{3,11},{4,36},{5,13},{6,38},{7,15},{8,40},{9,1... | collective-permute-start | bytes 2359304 | tf_op jit(solution)/shard_map/ppermute | solution.py:149
  26.8 30.2 %collective-permute-start.16 = (bf16[2,4,192,256]{3,2,1,0:T(8,128)(2,1)}, bf16[2,4,192,256]{3,2,1,0:T(8,128)(2,1)}, u32[]{:S(2)}, u32[]{:S(2)}) collective-permute-start(bf16[2,4,192,256]{3,2,1,0:T(8,128)(2,1)} %get-tuple-element.32), channel_id=1, source_target_pairs={{0,64},{1,17},{2,66},{3,19},{4,68},{5,21},{6,70},{7,23},{8,72},{9,... | collective-permute-start | bytes 2359304 | tf_op jit(solution)/shard_map/ppermute | solution.py:149
  38.5 6.9 %collective-permute-start.9 = (bf16[2,256,256]{1,2,0:T(8,128)(2,1)}, bf16[2,256,256]{1,2,0:T(8,128)(2,1)}, u32[]{:S(2)}, u32[]{:S(2)}) collective-permute-start(bf16[2,256,256]{1,2,0:T(8,128)(2,1)} %broadcast_select_fusion.1), channel_id=1, source_target_pairs={{0,2},{1,3},{2,0},{3,1},{4,6},{5,7},{6,4},{7,5},{8,10},{9,11},{10,... | collective-permute-start | bytes 786440 | tf_op jit(solution)/shard_map/ppermute | solution.py:171
  47.2 8.1 %collective-permute-start.10 = (bf16[2,256,256]{1,2,0:T(8,128)(2,1)}, bf16[2,256,256]{1,2,0:T(8,128)(2,1)S(1)}, u32[]{:S(2)}, u32[]{:S(2)}) collective-permute-start(bf16[2,256,256]{1,2,0:T(8,128)(2,1)} %broadcast_select_fusion.2), channel_id=1, source_target_pairs={{0,4},{1,5},{2,6},{3,7},{4,0},{5,1},{6,2},{7,3},{8,12},{9,13},{10,... | collective-permute-start | bytes 786440 | tf_op jit(solution)/shard_map/ppermute | solution.py:171
  56.3 17.4 %collective-permute-start.11 = (bf16[2,256,256]{1,2,0:T(8,128)(2,1)S(1)}, bf16[2,256,256]{1,2,0:T(8,128)(2,1)S(1)}, u32[]{:S(2)}, u32[]{:S(2)}) collective-permute-start(bf16[2,256,256]{1,2,0:T(8,128)(2,1)S(1)} %broadcast_select_fusion.3), channel_id=1, source_target_pairs={{0,8},{1,9},{2,10},{3,11},{4,12},{5,13},{6,14},{7,15},{8,0},{9,1},... | collective-permute-start | bytes 786440 | tf_op jit(solution)/shard_map/ppermute | solution.py:171
  58.9 16.5 %copy-start.2 = (bf16[1,2,4,256,256]{4,3,2,1,0:T(8,128)(2,1)S(1)}, bf16[1,2,4,256,256]{4,3,2,1,0:T(8,128)(2,1)}, u32[]{:S(2)}) copy-start(bf16[1,2,4,256,256]{4,3,2,1,0:T(8,128)(2,1)} %copy-done.1) | copy-start | bytes 3145732
  58.9 16.5 %copy-start.6 = (bf16[8,256,256]{2,1,0:T(8,128)(2,1)S(1)}, bf16[8,256,256]{2,1,0:T(8,128)(2,1)}, u32[]{:S(2)}) copy-start(bf16[8,256,256]{2,1,0:T(8,128)(2,1)} %copy-done.5) | copy-start | bytes 3145732
  58.9 7.0 %collective-permute-start.20 = (bf16[2,192,256]{2,1,0:T(8,128)(2,1)S(1)}, bf16[2,192,256]{2,1,0:T(8,128)(2,1)S(1)}, u32[]{:S(2)}, u32[]{:S(2)}) collective-permute-start(bf16[2,192,256]{2,1,0:T(8,128)(2,1)S(1)} %get-tuple-element.48), channel_id=1, source_target_pairs={{0,24},{1,97},{2,26},{3,99},{4,28},{5,101},{6,30},{7,103},{8,16},{... | collective-permute-start | bytes 589832 | tf_op jit(solution)/shard_map/ppermute | solution.py:149
  60.2 5.7 %collective-permute-start.18 = (bf16[2,192,256]{2,1,0:T(8,128)(2,1)S(1)}, bf16[2,192,256]{2,1,0:T(8,128)(2,1)S(1)}, u32[]{:S(2)}, u32[]{:S(2)}) collective-permute-start(bf16[2,192,256]{2,1,0:T(8,128)(2,1)S(1)} %get-tuple-element.49), channel_id=1, source_target_pairs={{0,8},{1,33},{2,10},{3,35},{4,12},{5,37},{6,14},{7,39},{8,0},{9,41... | collective-permute-start | bytes 589832 | tf_op jit(solution)/shard_map/ppermute | solution.py:149
  60.5 9.0 %collective-permute-start.19 = (bf16[2,192,256]{2,1,0:T(8,128)(2,1)S(1)}, bf16[2,192,256]{2,1,0:T(8,128)(2,1)S(1)}, u32[]{:S(2)}, u32[]{:S(2)}) collective-permute-start(bf16[2,192,256]{2,1,0:T(8,128)(2,1)S(1)} %get-tuple-element.50), channel_id=1, source_target_pairs={{0,16},{1,65},{2,18},{3,67},{4,20},{5,69},{6,22},{7,71},{8,24},{9,... | collective-permute-start | bytes 589832 | tf_op jit(solution)/shard_map/ppermute | solution.py:149
  69.6 11.9 %collective-permute-start.23 = (bf16[2,192,256]{2,1,0:T(8,128)(2,1)S(1)}, bf16[2,192,256]{2,1,0:T(8,128)(2,1)S(1)}, u32[]{:S(2)}, u32[]{:S(2)}) collective-permute-start(bf16[2,192,256]{2,1,0:T(8,128)(2,1)S(1)} %fusion.28), channel_id=1, source_target_pairs={{0,24},{1,97},{2,26},{3,99},{4,28},{5,101},{6,30},{7,103},{8,16},{... | collective-permute-start | bytes 589832 | tf_op jit(solution)/shard_map/ppermute | solution.py:156
  70.8 12.2 %collective-permute-start.22 = (bf16[2,192,256]{2,1,0:T(8,128)(2,1)S(1)}, bf16[2,192,256]{2,1,0:T(8,128)(2,1)S(1)}, u32[]{:S(2)}, u32[]{:S(2)}) collective-permute-start(bf16[2,192,256]{2,1,0:T(8,128)(2,1)S(1)} %fusion.28), channel_id=1, source_target_pairs={{0,16},{1,65},{2,18},{3,67},{4,20},{5,69},{6,22},{7,71},{8,24},{9,... | collective-permute-start | bytes 589832 | tf_op jit(solution)/shard_map/ppermute | solution.py:156
  71.9 14.0 %collective-permute-start.21 = (bf16[2,192,256]{2,1,0:T(8,128)(2,1)S(1)}, bf16[2,192,256]{2,1,0:T(8,128)(2,1)S(1)}, u32[]{:S(2)}, u32[]{:S(2)}) collective-permute-start(bf16[2,192,256]{2,1,0:T(8,128)(2,1)S(1)} %fusion.28), channel_id=1, source_target_pairs={{0,8},{1,33},{2,10},{3,35},{4,12},{5,37},{6,14},{7,39},{8,0},{9,41... | collective-permute-start | bytes 589832 | tf_op jit(solution)/shard_map/ppermute | solution.py:156
  73.9 12.3 %collective-permute-start.12 = (bf16[2,256,256]{1,2,0:T(8,128)(2,1)S(1)}, bf16[2,256,256]{1,2,0:T(8,128)(2,1)S(1)}, u32[]{:S(2)}, u32[]{:S(2)}) collective-permute-start(bf16[2,256,256]{1,2,0:T(8,128)(2,1)S(1)} %broadcast_select_fusion.4), channel_id=1, source_target_pairs={{0,16},{1,17},{2,18},{3,19},{4,20},{5,21},{6,22},{7,23},{8,24},{9,... | collective-permute-start | bytes 786440 | tf_op jit(solution)/shard_map/ppermute | solution.py:171
  76.9 11.1 %collective-permute-start.3 = (bf16[2,256,256]{2,1,0:T(8,128)(2,1)S(1)}, bf16[2,256,256]{2,1,0:T(8,128)(2,1)S(1)}, u32[]{:S(2)}, u32[]{:S(2)}) collective-permute-start(bf16[2,256,256]{2,1,0:T(8,128)(2,1)S(1)} %get-tuple-element.41), channel_id=1, source_target_pairs={{0,6},{1,7},{2,4},{3,5},{4,2},{5,3},{6,0},{7,1},{8,14},{9,15},{10,... | collective-permute-start | bytes 786440 | tf_op jit(solution)/shard_map/ppermute | solution.py:149
  81.5 6.5 %collective-permute-start.1 = (bf16[2,256,256]{2,1,0:T(8,128)(2,1)S(1)}, bf16[2,256,256]{2,1,0:T(8,128)(2,1)S(1)}, u32[]{:S(2)}, u32[]{:S(2)}) collective-permute-start(bf16[2,256,256]{2,1,0:T(8,128)(2,1)S(1)} %get-tuple-element.42), channel_id=1, source_target_pairs={{0,2},{1,3},{2,0},{3,1},{4,6},{5,7},{6,4},{7,5},{8,10},{9,11},{10,... | collective-permute-start | bytes 786440 | tf_op jit(solution)/shard_map/ppermute | solution.py:149
  83.0 11.4 %collective-permute-start.2 = (bf16[2,256,256]{2,1,0:T(8,128)(2,1)S(1)}, bf16[2,256,256]{2,1,0:T(8,128)(2,1)S(1)}, u32[]{:S(2)}, u32[]{:S(2)}) collective-permute-start(bf16[2,256,256]{2,1,0:T(8,128)(2,1)S(1)} %get-tuple-element.43), channel_id=1, source_target_pairs={{0,4},{1,5},{2,6},{3,7},{4,0},{5,1},{6,2},{7,3},{8,12},{9,13},{10,... | collective-permute-start | bytes 786440 | tf_op jit(solution)/shard_map/ppermute | solution.py:149
  86.2 15.9 %collective-permute-start.13 = (bf16[2,256,256]{1,2,0:T(8,128)(2,1)S(1)}, bf16[2,256,256]{1,2,0:T(8,128)(2,1)S(1)}, u32[]{:S(2)}, u32[]{:S(2)}) collective-permute-start(bf16[2,256,256]{1,2,0:T(8,128)(2,1)S(1)} %broadcast_select_fusion.5), channel_id=1, source_target_pairs={{0,32},{1,33},{2,34},{3,35},{4,36},{5,37},{6,38},{7,39},{8,40},{9,... | collective-permute-start | bytes 786440 | tf_op jit(solution)/shard_map/ppermute | solution.py:171
  94.6 10.5 %collective-permute-start.6 = (bf16[2,256,256]{2,1,0:T(8,128)(2,1)S(1)}, bf16[2,256,256]{2,1,0:T(8,128)(2,1)S(1)}, u32[]{:S(2)}, u32[]{:S(2)}) collective-permute-start(bf16[2,256,256]{2,1,0:T(8,128)(2,1)S(1)} %fusion.27), channel_id=1, source_target_pairs={{0,6},{1,7},{2,4},{3,5},{4,2},{5,3},{6,0},{7,1},{8,14},{9,15},{10,... | collective-permute-start | bytes 786440 | tf_op jit(solution)/shard_map/ppermute | solution.py:156
  94.7 13.0 %collective-permute-start.5 = (bf16[2,256,256]{2,1,0:T(8,128)(2,1)S(1)}, bf16[2,256,256]{2,1,0:T(8,128)(2,1)S(1)}, u32[]{:S(2)}, u32[]{:S(2)}) collective-permute-start(bf16[2,256,256]{2,1,0:T(8,128)(2,1)S(1)} %fusion.27), channel_id=1, source_target_pairs={{0,4},{1,5},{2,6},{3,7},{4,0},{5,1},{6,2},{7,3},{8,12},{9,13},{10,... | collective-permute-start | bytes 786440 | tf_op jit(solution)/shard_map/ppermute | solution.py:156
  97.4 12.3 %collective-permute-start.4 = (bf16[2,256,256]{2,1,0:T(8,128)(2,1)S(1)}, bf16[2,256,256]{2,1,0:T(8,128)(2,1)S(1)}, u32[]{:S(2)}, u32[]{:S(2)}) collective-permute-start(bf16[2,256,256]{2,1,0:T(8,128)(2,1)S(1)} %fusion.27), channel_id=1, source_target_pairs={{0,2},{1,3},{2,0},{3,1},{4,6},{5,7},{6,4},{7,5},{8,10},{9,11},{10,... | collective-permute-start | bytes 786440 | tf_op jit(solution)/shard_map/ppermute | solution.py:156
  98.9 31.1 %collective-permute-start.26 = (bf16[2,4,192,256]{3,2,1,0:T(8,128)(2,1)S(1)}, bf16[2,4,192,256]{3,2,1,0:T(8,128)(2,1)S(1)}, u32[]{:S(2)}, u32[]{:S(2)}) collective-permute-start(bf16[2,4,192,256]{3,2,1,0:T(8,128)(2,1)S(1)} %pad_maximum_fusion.5), channel_id=1, source_target_pairs={{0,96},{1,25},{2,98},{3,27},{4,100},{5,29},{6,102},{7,31},{8,104},... | collective-permute-start | bytes 2359304 | tf_op jit(solution)/shard_map/ppermute | solution.py:156
  102.1 27.9 %collective-permute-start.25 = (bf16[2,4,192,256]{3,2,1,0:T(8,128)(2,1)S(1)}, bf16[2,4,192,256]{3,2,1,0:T(8,128)(2,1)S(1)}, u32[]{:S(2)}, u32[]{:S(2)}) collective-permute-start(bf16[2,4,192,256]{3,2,1,0:T(8,128)(2,1)S(1)} %pad_maximum_fusion.5), channel_id=1, source_target_pairs={{0,64},{1,17},{2,66},{3,19},{4,68},{5,21},{6,70},{7,23},{8,72},{9,... | collective-permute-start | bytes 2359304 | tf_op jit(solution)/shard_map/ppermute | solution.py:156
  103.7 26.0 %copy-start.9 = (bf16[2,256,256]{2,1,0:T(8,128)(2,1)S(1)}, bf16[2,256,256]{2,1,0:T(8,128)(2,1)}, u32[]{:S(2)}) copy-start(bf16[2,256,256]{2,1,0:T(8,128)(2,1)} %param.7) | copy-start | bytes 786436
  105.1 25.0 %collective-permute-start.24 = (bf16[2,4,192,256]{3,2,1,0:T(8,128)(2,1)S(1)}, bf16[2,4,192,256]{3,2,1,0:T(8,128)(2,1)S(1)}, u32[]{:S(2)}, u32[]{:S(2)}) collective-permute-start(bf16[2,4,192,256]{3,2,1,0:T(8,128)(2,1)S(1)} %pad_maximum_fusion.5), channel_id=1, source_target_pairs={{0,32},{1,9},{2,34},{3,11},{4,36},{5,13},{6,38},{7,15},{8,40},{9,1... | collective-permute-start | bytes 2359304 | tf_op jit(solution)/shard_map/ppermute | solution.py:156
  107.7 22.0 %collective-permute-start.14 = (bf16[2,256,256]{1,2,0:T(8,128)(2,1)S(1)}, bf16[2,256,256]{1,2,0:T(8,128)(2,1)S(1)}, u32[]{:S(2)}, u32[]{:S(2)}) collective-permute-start(bf16[2,256,256]{1,2,0:T(8,128)(2,1)S(1)} %broadcast_select_fusion.6), channel_id=1, source_target_pairs={{0,64},{1,65},{2,66},{3,67},{4,68},{5,69},{6,70},{7,71},{8,72},{9,... | collective-permute-start | bytes 786440 | tf_op jit(solution)/shard_map/ppermute | solution.py:171
  110.0 24.6 %collective-permute-start.7 = (bf16[2,4,256,256]{3,2,0,1:T(8,128)(2,1)S(1)}, bf16[2,4,256,256]{3,2,0,1:T(8,128)(2,1)S(1)}, u32[]{:S(2)}, u32[]{:S(2)}) collective-permute-start(bf16[2,4,256,256]{3,2,0,1:T(8,128)(2,1)S(1)} %pad_maximum_fusion.3), channel_id=1, source_target_pairs={{0,1},{1,0},{2,3},{3,2},{4,5},{5,4},{6,7},{7,6},{8,9},{9,8},{10,11... | collective-permute-start | bytes 3145736 | tf_op jit(solution)/shard_map/ppermute | solution.py:156
  (5 other events, 10.1 us)

commit v9 on v8

--- a/solution.py
+++ b/solution.py
@@ -167,9 +167,15 @@
     ncol = lax.axis_size("col")
     n = nrow * ncol
     relative = (lax.axis_index("row") * ncol + lax.axis_index("col")) ^ root
-    for b in range(n.bit_length() - 1):
-        got = lax.ppermute(value, ("row", "col"), [(d, d ^ (1 << b)) for d in range(n)])
-        value = per_part((relative >> b) == 1, got, value)
+    shift = 0
+    for size in (CORES, RING, RING, RING):
+        mask = size - 1
+        got = [value] + [
+            lax.ppermute(value, ("row", "col"), [(d, d ^ (m << shift)) for d in range(n)])
+            for m in range(1, size)
+        ]
+        value = pick((relative >> shift) & mask, got)
+        shift += mask.bit_length()
     return value
 
 

time: 157 us -> 158 us (level); the launches traced: 156 us -> 155 us
  waiting for transfers between devices: 43.8 us -> 36.9 us
  other arithmetic: 23.1 us -> 25.8 us
  local copies, waits for them, and re-layouts: 10.1 us -> 12.2 us
    ppermute x10, waiting for transfers between devices: 2.87 us -> 14.9 us  [xor_bcast(): lax.ppermute(buf, axes, digit_pairs(nrow, ncol, on_row, step, m))]
    ppermute x10, waiting for transfers between devices: 12.3 us -> 0.98 us  [xor_bcast(): lax.ppermute(groups[m], axes, digit_pairs(nrow, ncol, on_row, step, m))]
    ppermute x7 -> x10, waiting for transfers between devices: 28.6 us -> 21 us  [all_bcast(): lax.ppermute(value, ('row', 'col'), [(d, d ^ m << shift) for d in range(n)])]
    ppermute x10, starting transfers between devices: 18.4 us -> 11.3 us  [xor_bcast(): lax.ppermute(groups[m], axes, digit_pairs(nrow, ncol, on_row, step, m))]
    ppermute x7 -> x10, starting transfers between devices: 10.7 us -> 15 us  [all_bcast(): lax.ppermute(value, ('row', 'col'), [(d, d ^ m << shift) for d in range(n)])]
    ppermute x10, starting transfers between devices: 15.9 us -> 19.6 us  [xor_bcast(): lax.ppermute(buf, axes, digit_pairs(nrow, ncol, on_row, step, m))]
    select_n x11 -> x8, other arithmetic: 8.5 us -> 6.92 us  [per_part(): return jnp.where(cond.reshape((-1,) + (1,) * (a.ndim - 1)), a, b)]
  transfers between devices with their start and end apart: 27 -> 30, of which waited for: 8 -> 9; matrix products, arithmetic and copies ran while one was open for 19% -> 21% of each run, Pallas kernels for 0% -> 0%
where the time goes in v9:
time: 158 us; the launch traced here: 155 us
  starting transfers between devices  45.8 us (29%)
  waiting for transfers between devices  36.9 us (23%)
  other arithmetic  25.8 us (16%)
  Pallas kernels  16.7 us (11%)
  local copies, waits for them, and re-layouts  12.2 us (8%)
  between operations  12 us (8%)
  matrix products  5.34 us (3%)
    ppermute x10, waiting for transfers between devices, all_bcast(): lax.ppermute(value, ('row', 'col'), [(d, d ^ m << shift) for d in range(n)])  21 us
    ppermute x10, starting transfers between devices, xor_bcast(): lax.ppermute(buf, axes, digit_pairs(nrow, ncol, on_row, step, m))  19.6 us
    pallas_call x1, Pallas kernels, both_updates(): pl.pallas_call(update_kernel, grid_spec=pltpu.PrefetchScalarGridSpec(num_...  16.7 us
    ppermute x10, starting transfers between devices, all_bcast(): lax.ppermute(value, ('row', 'col'), [(d, d ^ m << shift) for d in range(n)])  15 us
    ppermute x10, waiting for transfers between devices, xor_bcast(): lax.ppermute(buf, axes, digit_pairs(nrow, ncol, on_row, step, m))  14.9 us
    ppermute x10, starting transfers between devices, xor_bcast(): lax.ppermute(groups[m], axes, digit_pairs(nrow, ncol, on_row, step, m))  11.3 us
    select_n x8, other arithmetic, per_part(): return jnp.where(cond.reshape((-1,) + (1,) * (a.ndim - 1)), a, b)  6.92 us
    dot_general x3, matrix products, lower_local(): jnp.einsum('iab,bc->iac', column, inverse, preferred_element_type=jnp.flo...  4.76 us
  transfers between devices with their start and end apart: 30, of which 9 were waited for; matrix products, arithmetic and copies ran while one was open for 21% of the time, Pallas kernels for 0%

profile of v9, /device:TPU:6, one launch (start us, length us, event | category | flops | bytes accessed | tf_op | source)
XLA Modules:
  0.0 154.7 jit_solution(4487146132153599436)
XLA Ops:
  12.1 2.2 %dynamic-slice_select_fusion = (bf16[1,12,256,256]{3,2,1,0:T(8,128)(2,1)S(1)}, bf16[1,12,256,256]{3,2,1,0:T(8,128)(2,1)S(1)}) fusion(bf16[8,12,256,256]{3,2,1,0:T(8,128)(2,1)} %front_ref.1, s32[]{:T(128)S(6)} %select_n.422, pred[12]{0:T(512)(128)(4,1)S(1)} %get-tuple-element.5, s32[]{:T(128)S(6)} %select_n.417, pred[12]{0:T(512)(128)(4,1)S(1)} %get-tuple-element.6), kind=kLoop, calls=%fused_computation.22 | loop fusion | flops 1572864 | bytes 6291488 | tf_op jit(solution)/shard_map/jit(_where)/select_n | solution.py:235
  14.2 1.5 fusion.25
  15.7 4.0 %collective-permute-start.20 = (bf16[2,4,192,256]{3,2,1,0:T(8,128)(2,1)}, bf16[2,4,192,256]{3,2,1,0:T(8,128)(2,1)}, u32[]{:S(2)}, u32[]{:S(2)}) collective-permute-start(bf16[2,4,192,256]{3,2,1,0:T(8,128)(2,1)} %get-tuple-element.30), channel_id=1, source_target_pairs={{0,96},{1,25},{2,98},{3,27},{4,100},{5,29},{6,102},{7,31},{8,104},... | collective-permute-start | bytes 2359304 | tf_op jit(solution)/shard_map/ppermute | solution.py:149
  19.8 1.5 collective-permute-start.19
  24.7 2.3 %constant_dynamic-slice_fusion.2 = bf16[8,1,256,256]{3,2,1,0:T(8,128)(2,1)} fusion(bf16[8,12,256,256]{3,2,1,0:T(8,128)(2,1)} %front_ref.1, s32[]{:T(128)S(6)} %select_n.391), kind=kLoop, calls=%fused_computation.107 | loop fusion | bytes 2097156 | tf_op jit(solution)/shard_map/jit(dynamic_index_in_dim)/dynamic_slice | solution.py:270
  34.9 1.7 %select_convert_fusion.1 = bf16[8,256,256]{2,1,0:T(8,128)(2,1)S(1)} fusion(bf16[8,12,256,256]{3,2,1,0:T(8,128)(2,1)} %front_ref.1, s32[]{:T(128)S(6)} %select_n.385, pred[8]{0:T(512)(128)(4,1)S(1)} %get-tuple-element.7, pred[8]{0:T(512)(128)(4,1)S(1)} %get-tuple-element.18, bf16[2,256,256]{2,1,0:T(8,128)(2,1)} %param.7), kind=kOutput, calls=%fused_computation.19 | convolution fusion | flops 270008320 | bytes 2228244 | tf_op jit(solution)/shard_map/iab,bc->iac/dot_general | solution.py:183
  39.1 1.7 %broadcast_select_fusion.1 = bf16[2,256,256]{1,2,0:T(8,128)(2,1)} fusion(bf16[2,256,256]{1,2,0:T(8,128)(2,1)} %collective-permute-done.8, pred[2]{0:T(512)(128)(4,1)S(1)} %get-tuple-element.63, bf16[1,256,256]{1,2,0:T(8,128)(2,1)S(1)} %get-tuple-element.76, bf16[1,256,256]{1,2,0:T(8,128)(2,1)S(1)} %get-tuple-element.77), kind=kLoop, calls=%fused_computation.72 | loop fusion | flops 262144 | bytes 786434 | tf_op jit(solution)/shard_map/jit(_where)/select_n | solution.py:13
  40.8 3.0 %collective-permute-start.11 = (bf16[2,256,256]{1,2,0:T(8,128)(2,1)}, bf16[2,256,256]{1,2,0:T(8,128)(2,1)}, u32[]{:S(2)}, u32[]{:S(2)}) collective-permute-start(bf16[2,256,256]{1,2,0:T(8,128)(2,1)} %broadcast_select_fusion.1), channel_id=1, source_target_pairs={{0,6},{1,7},{2,4},{3,5},{4,2},{5,3},{6,0},{7,1},{8,14},{9,15},{10,... | collective-permute-start | bytes 786440 | tf_op jit(solution)/shard_map/ppermute | solution.py:174
  46.6 8.5 %collective-permute-done.11 = bf16[2,256,256]{1,2,0:T(8,128)(2,1)} collective-permute-done((bf16[2,256,256]{1,2,0:T(8,128)(2,1)}, bf16[2,256,256]{1,2,0:T(8,128)(2,1)}, u32[]{:S(2)}, u32[]{:S(2)}) %collective-permute-start.11) | collective-permute-done | bytes 262176 | tf_op jit(solution)/shard_map/ppermute | solution.py:174
  58.1 6.0 %collective-permute-done.9 = bf16[2,256,256]{1,2,0:T(8,128)(2,1)} collective-permute-done((bf16[2,256,256]{1,2,0:T(8,128)(2,1)}, bf16[2,256,256]{1,2,0:T(8,128)(2,1)}, u32[]{:S(2)}, u32[]{:S(2)}) %collective-permute-start.9) | collective-permute-done | bytes 262176 | tf_op jit(solution)/shard_map/ppermute | solution.py:174
  66.0 1.4 collective-permute-start.13
  67.5 2.2 %collective-permute-start.12 = (bf16[2,256,256]{1,2,0:T(8,128)(2,1)S(1)}, bf16[2,256,256]{1,2,0:T(8,128)(2,1)S(1)}, u32[]{:S(2)}, u32[]{:S(2)}) collective-permute-start(bf16[2,256,256]{1,2,0:T(8,128)(2,1)S(1)} %select_select_fusion.2), channel_id=1, source_target_pairs={{0,8},{1,9},{2,10},{3,11},{4,12},{5,13},{6,14},{7,15},{8,0},{9,1},... | collective-permute-start | bytes 786440 | tf_op jit(solution)/shard_map/ppermute | solution.py:174
  69.7 2.0 %fusion.22 = bf16[2,4,192,256]{3,2,1,0:T(8,128)(2,1)S(1)} fusion(bf16[1,4,4,192,256]{4,3,2,0,1:T(8,128)(2,1)S(1)} %bitcast.197, bf16[1,4,4,192,256]{4,3,2,0,1:T(8,128)(2,1)S(1)} %bitcast.195, bf16[2,4,192,256]{3,2,1,0:T(8,128)(2,1)} %collective-permute-done.18, bf16[2,4,192,256]{3,2,1,0:T(8,128)(2,1)} %collective-permute-done.19, ...), kind=kLoop, calls=%fused_computation.48 | loop fusion | flops 1572864 | bytes 6291462 | tf_op jit(solution)/shard_map/jit(_where)/select_n | solution.py:13
  72.4 1.4 fusion.12
  73.9 6.4 %collective-permute-done.14 = bf16[2,256,256]{1,2,0:T(8,128)(2,1)S(1)} collective-permute-done((bf16[2,256,256]{1,2,0:T(8,128)(2,1)S(1)}, bf16[2,256,256]{1,2,0:T(8,128)(2,1)S(1)}, u32[]{:S(2)}, u32[]{:S(2)}) %collective-permute-start.14) | collective-permute-done | bytes 262176 | tf_op jit(solution)/shard_map/ppermute | solution.py:174
  80.3 3.0 %collective-permute-start.3 = (bf16[2,256,256]{2,1,0:T(8,128)(2,1)S(1)}, bf16[2,256,256]{2,1,0:T(8,128)(2,1)S(1)}, u32[]{:S(2)}, u32[]{:S(2)}) collective-permute-start(bf16[2,256,256]{2,1,0:T(8,128)(2,1)S(1)} %get-tuple-element.41), channel_id=1, source_target_pairs={{0,6},{1,7},{2,4},{3,5},{4,2},{5,3},{6,0},{7,1},{8,14},{9,15},{10,... | collective-permute-start | bytes 786440 | tf_op jit(solution)/shard_map/ppermute | solution.py:149
  83.3 2.1 %collective-permute-start.2 = (bf16[2,256,256]{2,1,0:T(8,128)(2,1)S(1)}, bf16[2,256,256]{2,1,0:T(8,128)(2,1)S(1)}, u32[]{:S(2)}, u32[]{:S(2)}) collective-permute-start(bf16[2,256,256]{2,1,0:T(8,128)(2,1)S(1)} %get-tuple-element.43), channel_id=1, source_target_pairs={{0,4},{1,5},{2,6},{3,7},{4,0},{5,1},{6,2},{7,3},{8,12},{9,13},{10,... | collective-permute-start | bytes 786440 | tf_op jit(solution)/shard_map/ppermute | solution.py:149
  85.5 4.1 %collective-permute-start.17 = (bf16[2,256,256]{1,2,0:T(8,128)(2,1)S(1)}, bf16[2,256,256]{1,2,0:T(8,128)(2,1)S(1)}, u32[]{:S(2)}, u32[]{:S(2)}) collective-permute-start(bf16[2,256,256]{1,2,0:T(8,128)(2,1)S(1)} %select_select_fusion.1), channel_id=1, source_target_pairs={{0,96},{1,97},{2,98},{3,99},{4,100},{5,101},{6,102},{7,103},{8,104... | collective-permute-start | bytes 786440 | tf_op jit(solution)/shard_map/ppermute | solution.py:174
  89.6 1.7 %collective-permute-start.16 = (bf16[2,256,256]{1,2,0:T(8,128)(2,1)S(1)}, bf16[2,256,256]{1,2,0:T(8,128)(2,1)S(1)}, u32[]{:S(2)}, u32[]{:S(2)}) collective-permute-start(bf16[2,256,256]{1,2,0:T(8,128)(2,1)S(1)} %select_select_fusion.1), channel_id=1, source_target_pairs={{0,64},{1,65},{2,66},{3,67},{4,68},{5,69},{6,70},{7,71},{8,72},{9,... | collective-permute-start | bytes 786440 | tf_op jit(solution)/shard_map/ppermute | solution.py:174
  92.1 3.5 %collective-permute-start.25 = (bf16[2,192,256]{2,1,0:T(8,128)(2,1)S(1)}, bf16[2,192,256]{2,1,0:T(8,128)(2,1)S(1)}, u32[]{:S(2)}, u32[]{:S(2)}) collective-permute-start(bf16[2,192,256]{2,1,0:T(8,128)(2,1)S(1)} %fusion.28), channel_id=1, source_target_pairs={{0,16},{1,65},{2,18},{3,67},{4,20},{5,69},{6,22},{7,71},{8,24},{9,... | collective-permute-start | bytes 589832 | tf_op jit(solution)/shard_map/ppermute | solution.py:156
  97.7 2.9 %collective-permute-done.26 = bf16[2,192,256]{2,1,0:T(8,128)(2,1)S(1)} collective-permute-done((bf16[2,192,256]{2,1,0:T(8,128)(2,1)S(1)}, bf16[2,192,256]{2,1,0:T(8,128)(2,1)S(1)}, u32[]{:S(2)}, u32[]{:S(2)}) %collective-permute-start.26) | collective-permute-done | bytes 196640 | tf_op jit(solution)/shard_map/ppermute | solution.py:156
  101.6 3.0 %collective-permute-start.6 = (bf16[2,256,256]{2,1,0:T(8,128)(2,1)S(1)}, bf16[2,256,256]{2,1,0:T(8,128)(2,1)S(1)}, u32[]{:S(2)}, u32[]{:S(2)}) collective-permute-start(bf16[2,256,256]{2,1,0:T(8,128)(2,1)S(1)} %fusion.27), channel_id=1, source_target_pairs={{0,6},{1,7},{2,4},{3,5},{4,2},{5,3},{6,0},{7,1},{8,14},{9,15},{10,... | collective-permute-start | bytes 786440 | tf_op jit(solution)/shard_map/ppermute | solution.py:156
  104.8 1.8 %collective-permute-start.29 = (bf16[2,4,192,256]{3,2,1,0:T(8,128)(2,1)S(1)}, bf16[2,4,192,256]{3,2,1,0:T(8,128)(2,1)S(1)}, u32[]{:S(2)}, u32[]{:S(2)}) collective-permute-start(bf16[2,4,192,256]{3,2,1,0:T(8,128)(2,1)S(1)} %pad_maximum_fusion.5), channel_id=1, source_target_pairs={{0,96},{1,25},{2,98},{3,27},{4,100},{5,29},{6,102},{7,31},{8,104},... | collective-permute-start | bytes 2359304 | tf_op jit(solution)/shard_map/ppermute | solution.py:156
  106.6 1.4 collective-permute-start.28
  110.2 1.9 %collective-permute-start.4 = (bf16[2,256,256]{2,1,0:T(8,128)(2,1)S(1)}, bf16[2,256,256]{2,1,0:T(8,128)(2,1)S(1)}, u32[]{:S(2)}, u32[]{:S(2)}) collective-permute-start(bf16[2,256,256]{2,1,0:T(8,128)(2,1)S(1)} %fusion.27), channel_id=1, source_target_pairs={{0,2},{1,3},{2,0},{3,1},{4,6},{5,7},{6,4},{7,5},{8,10},{9,11},{10,... | collective-permute-start | bytes 786440 | tf_op jit(solution)/shard_map/ppermute | solution.py:156
  112.5 4.4 %collective-permute-done.5 = bf16[2,256,256]{2,1,0:T(8,128)(2,1)S(1)} collective-permute-done((bf16[2,256,256]{2,1,0:T(8,128)(2,1)S(1)}, bf16[2,256,256]{2,1,0:T(8,128)(2,1)S(1)}, u32[]{:S(2)}, u32[]{:S(2)}) %collective-permute-start.5) | collective-permute-done | bytes 262176 | tf_op jit(solution)/shard_map/ppermute | solution.py:156
  116.9 4.0 %collective-permute-done.4 = bf16[2,256,256]{2,1,0:T(8,128)(2,1)S(1)} collective-permute-done((bf16[2,256,256]{2,1,0:T(8,128)(2,1)S(1)}, bf16[2,256,256]{2,1,0:T(8,128)(2,1)S(1)}, u32[]{:S(2)}, u32[]{:S(2)}) %collective-permute-start.4) | collective-permute-done | bytes 262176 | tf_op jit(solution)/shard_map/ppermute | solution.py:156
  121.2 4.2 %collective-permute-start.7 = (bf16[2,4,256,256]{3,2,0,1:T(8,128)(2,1)S(1)}, bf16[2,4,256,256]{3,2,0,1:T(8,128)(2,1)S(1)}, u32[]{:S(2)}, u32[]{:S(2)}) collective-permute-start(bf16[2,4,256,256]{3,2,0,1:T(8,128)(2,1)S(1)} %pad_maximum_fusion.3), channel_id=1, source_target_pairs={{0,1},{1,0},{2,3},{3,2},{4,5},{5,4},{6,7},{7,6},{8,9},{9,8},{10,11... | collective-permute-start | bytes 3145736 | tf_op jit(solution)/shard_map/ppermute | solution.py:156
  126.5 2.5 %collective-permute-done.27 = bf16[2,4,192,256]{3,2,1,0:T(8,128)(2,1)S(1)} collective-permute-done((bf16[2,4,192,256]{3,2,1,0:T(8,128)(2,1)S(1)}, bf16[2,4,192,256]{3,2,1,0:T(8,128)(2,1)S(1)}, u32[]{:S(2)}, u32[]{:S(2)}) %collective-permute-start.27) | collective-permute-done | bytes 786464 | tf_op jit(solution)/shard_map/ppermute | solution.py:156
  131.6 2.0 %fusion.4.u2_ref = bf16[12,256,256]{2,1,0:T(8,128)(2,1)} fusion(bf16[1,12,256,256]{3,2,1,0:T(8,128)(2,1)S(1)} %bitcast.200, f32[12,256,256]{1,2,0:T(8,128)S(1)} %fusion.29, pred[12]{0:T(512)(128)(4,1)S(1)} %copy-done.10, pred[12]{0:T(512)(128)(4,1)S(1)} %copy-done.9, bf16[256,256]{1,0:T(8,128)(2,1)S(1)} %fusion.8), kind=kLoop, calls=%fused_computation.21 | loop fusion | flops 3932160 | bytes 6422552 | tf_op jit(solution)/shard_map/squeeze | solution.py:298
  135.2 2.8 %select_convert_fusion.l2_ref = bf16[8,256,256]{2,1,0:T(8,128)(2,1)} fusion(pred[8]{0:T(512)(128)(4,1)S(1)} %get-tuple-element.68, bf16[8,1,256,256]{2,3,0,1:T(8,128)(2,1)S(1)} %bitcast.205, bf16[8,1,256,256]{2,3,0,1:T(8,128)(2,1)S(1)} %bitcast.204, bf16[8,256,256]{2,1,0:T(8,128)(2,1)S(1)} %bitcast.198, pred[8]{0:T(512)(128)(4,1)S(1)} %copy-done.12, ...), kind=kOutput, calls=%fused_computation.18 | convolution fusion | flops 540540928 | bytes 4457984 | tf_op jit(solution)/shard_map/iab,bc->iac/dot_general | solution.py:183
  138.0 16.7 %shard_map.46 = bf16[8,12,256,256]{3,2,1,0:T(8,128)(2,1)} custom-call(s32[8,12]{1,0:T(8,128)} %select_add_fusion.codes, bf16[8,12,256,256]{3,2,1,0:T(8,128)(2,1)} %front_ref.1, bf16[8,256,256]{2,1,0:T(8,128)(2,1)} %bitcast.199, bf16[8,256,256]{2,1,0:T(8,128)(2,1)} %select_convert_fusion.l2_ref, bf16[12,256,256]{2,1,0:T(8,128)(2,1)} %bitcast.193, ...), custom_call_target="tpu_custom_call" | custom-call | tf_op jit(solution)/shard_map/pallas_call | solution.py:220
  (120 shorter events, 35.0 us)
Async XLA Ops:
  11.5 27.6 %collective-permute-start.8 = (bf16[2,256,256]{1,2,0:T(8,128)(2,1)}, bf16[2,256,256]{1,2,0:T(8,128)(2,1)}, u32[]{:S(2)}, u32[]{:S(2)}) collective-permute-start(bf16[2,256,256]{1,2,0:T(8,128)(2,1)} %pad_maximum_fusion.6), channel_id=1, source_target_pairs={{0,1},{1,0},{2,3},{3,2},{4,5},{5,4},{6,7},{7,6},{8,9},{9,8},{10,11... | collective-permute-start | bytes 786440 | tf_op jit(solution)/shard_map/ppermute | solution.py:174
  15.7 13.8 %copy-start.4 = (s32[128,96]{0,1:T(8,128)S(1)}, s32[128,96]{0,1:T(8,128)}, u32[]{:S(2)}) copy-start(s32[128,96]{0,1:T(8,128)} %param.5) | copy-start | bytes 147460
  15.7 50.3 %collective-permute-start.20 = (bf16[2,4,192,256]{3,2,1,0:T(8,128)(2,1)}, bf16[2,4,192,256]{3,2,1,0:T(8,128)(2,1)}, u32[]{:S(2)}, u32[]{:S(2)}) collective-permute-start(bf16[2,4,192,256]{3,2,1,0:T(8,128)(2,1)} %get-tuple-element.30), channel_id=1, source_target_pairs={{0,96},{1,25},{2,98},{3,27},{4,100},{5,29},{6,102},{7,31},{8,104},... | collective-permute-start | bytes 2359304 | tf_op jit(solution)/shard_map/ppermute | solution.py:149
  19.8 47.7 %collective-permute-start.18 = (bf16[2,4,192,256]{3,2,1,0:T(8,128)(2,1)}, bf16[2,4,192,256]{3,2,1,0:T(8,128)(2,1)}, u32[]{:S(2)}, u32[]{:S(2)}) collective-permute-start(bf16[2,4,192,256]{3,2,1,0:T(8,128)(2,1)} %get-tuple-element.31), channel_id=1, source_target_pairs={{0,32},{1,9},{2,34},{3,11},{4,36},{5,13},{6,38},{7,15},{8,40},{9,1... | collective-permute-start | bytes 2359304 | tf_op jit(solution)/shard_map/ppermute | solution.py:149
  19.8 49.9 %collective-permute-start.19 = (bf16[2,4,192,256]{3,2,1,0:T(8,128)(2,1)}, bf16[2,4,192,256]{3,2,1,0:T(8,128)(2,1)}, u32[]{:S(2)}, u32[]{:S(2)}) collective-permute-start(bf16[2,4,192,256]{3,2,1,0:T(8,128)(2,1)} %get-tuple-element.32), channel_id=1, source_target_pairs={{0,64},{1,17},{2,66},{3,19},{4,68},{5,21},{6,70},{7,23},{8,72},{9,... | collective-permute-start | bytes 2359304 | tf_op jit(solution)/shard_map/ppermute | solution.py:149
  40.8 14.3 %collective-permute-start.11 = (bf16[2,256,256]{1,2,0:T(8,128)(2,1)}, bf16[2,256,256]{1,2,0:T(8,128)(2,1)}, u32[]{:S(2)}, u32[]{:S(2)}) collective-permute-start(bf16[2,256,256]{1,2,0:T(8,128)(2,1)} %broadcast_select_fusion.1), channel_id=1, source_target_pairs={{0,6},{1,7},{2,4},{3,5},{4,2},{5,3},{6,0},{7,1},{8,14},{9,15},{10,... | collective-permute-start | bytes 786440 | tf_op jit(solution)/shard_map/ppermute | solution.py:174
  43.9 11.3 %collective-permute-start.10 = (bf16[2,256,256]{1,2,0:T(8,128)(2,1)}, bf16[2,256,256]{1,2,0:T(8,128)(2,1)}, u32[]{:S(2)}, u32[]{:S(2)}) collective-permute-start(bf16[2,256,256]{1,2,0:T(8,128)(2,1)} %broadcast_select_fusion.1), channel_id=1, source_target_pairs={{0,4},{1,5},{2,6},{3,7},{4,0},{5,1},{6,2},{7,3},{8,12},{9,13},{10,... | collective-permute-start | bytes 786440 | tf_op jit(solution)/shard_map/ppermute | solution.py:174
  55.1 17.1 %collective-permute-start = (bf16[2,4,256,256]{3,2,1,0:T(8,128)(2,1)}, bf16[2,4,256,256]{3,2,1,0:T(8,128)(2,1)}, u32[]{:S(2)}, u32[]{:S(2)}) collective-permute-start(bf16[2,4,256,256]{3,2,1,0:T(8,128)(2,1)} %fusion.13), channel_id=1, source_target_pairs={{0,1},{1,0},{2,3},{3,2},{4,5},{5,4},{6,7},{7,6},{8,9},{9,8},{10,11... | collective-permute-start | bytes 3145736 | tf_op jit(solution)/shard_map/ppermute | solution.py:149
  55.1 9.0 %collective-permute-start.9 = (bf16[2,256,256]{1,2,0:T(8,128)(2,1)}, bf16[2,256,256]{1,2,0:T(8,128)(2,1)}, u32[]{:S(2)}, u32[]{:S(2)}) collective-permute-start(bf16[2,256,256]{1,2,0:T(8,128)(2,1)} %broadcast_select_fusion.1), channel_id=1, source_target_pairs={{0,2},{1,3},{2,0},{3,1},{4,6},{5,7},{6,4},{7,5},{8,10},{9,11},{10,... | collective-permute-start | bytes 786440 | tf_op jit(solution)/shard_map/ppermute | solution.py:174
  65.5 14.8 %collective-permute-start.14 = (bf16[2,256,256]{1,2,0:T(8,128)(2,1)S(1)}, bf16[2,256,256]{1,2,0:T(8,128)(2,1)S(1)}, u32[]{:S(2)}, u32[]{:S(2)}) collective-permute-start(bf16[2,256,256]{1,2,0:T(8,128)(2,1)S(1)} %select_select_fusion.2), channel_id=1, source_target_pairs={{0,24},{1,25},{2,26},{3,27},{4,28},{5,29},{6,30},{7,31},{8,16},{9,... | collective-permute-start | bytes 786440 | tf_op jit(solution)/shard_map/ppermute | solution.py:174
  66.0 14.3 %collective-permute-start.13 = (bf16[2,256,256]{1,2,0:T(8,128)(2,1)S(1)}, bf16[2,256,256]{1,2,0:T(8,128)(2,1)S(1)}, u32[]{:S(2)}, u32[]{:S(2)}) collective-permute-start(bf16[2,256,256]{1,2,0:T(8,128)(2,1)S(1)} %select_select_fusion.2), channel_id=1, source_target_pairs={{0,16},{1,17},{2,18},{3,19},{4,20},{5,21},{6,22},{7,23},{8,24},{9,... | collective-permute-start | bytes 786440 | tf_op jit(solution)/shard_map/ppermute | solution.py:174
  67.5 15.8 %collective-permute-start.12 = (bf16[2,256,256]{1,2,0:T(8,128)(2,1)S(1)}, bf16[2,256,256]{1,2,0:T(8,128)(2,1)S(1)}, u32[]{:S(2)}, u32[]{:S(2)}) collective-permute-start(bf16[2,256,256]{1,2,0:T(8,128)(2,1)S(1)} %select_select_fusion.2), channel_id=1, source_target_pairs={{0,8},{1,9},{2,10},{3,11},{4,12},{5,13},{6,14},{7,15},{8,0},{9,1},... | collective-permute-start | bytes 786440 | tf_op jit(solution)/shard_map/ppermute | solution.py:174
  71.7 11.6 %collective-permute-start.23 = (bf16[2,192,256]{2,1,0:T(8,128)(2,1)S(1)}, bf16[2,192,256]{2,1,0:T(8,128)(2,1)S(1)}, u32[]{:S(2)}, u32[]{:S(2)}) collective-permute-start(bf16[2,192,256]{2,1,0:T(8,128)(2,1)S(1)} %get-tuple-element.48), channel_id=1, source_target_pairs={{0,24},{1,97},{2,26},{3,99},{4,28},{5,101},{6,30},{7,103},{8,16},{... | collective-permute-start | bytes 589832 | tf_op jit(solution)/shard_map/ppermute | solution.py:149
  72.2 13.3 %collective-permute-start.21 = (bf16[2,192,256]{2,1,0:T(8,128)(2,1)S(1)}, bf16[2,192,256]{2,1,0:T(8,128)(2,1)S(1)}, u32[]{:S(2)}, u32[]{:S(2)}) collective-permute-start(bf16[2,192,256]{2,1,0:T(8,128)(2,1)S(1)} %get-tuple-element.49), channel_id=1, source_target_pairs={{0,8},{1,33},{2,10},{3,35},{4,12},{5,37},{6,14},{7,39},{8,0},{9,41... | collective-permute-start | bytes 589832 | tf_op jit(solution)/shard_map/ppermute | solution.py:149
  80.3 9.3 %collective-permute-start.22 = (bf16[2,192,256]{2,1,0:T(8,128)(2,1)S(1)}, bf16[2,192,256]{2,1,0:T(8,128)(2,1)S(1)}, u32[]{:S(2)}, u32[]{:S(2)}) collective-permute-start(bf16[2,192,256]{2,1,0:T(8,128)(2,1)S(1)} %get-tuple-element.50), channel_id=1, source_target_pairs={{0,16},{1,65},{2,18},{3,67},{4,20},{5,69},{6,22},{7,71},{8,24},{9,... | collective-permute-start | bytes 589832 | tf_op jit(solution)/shard_map/ppermute | solution.py:149
  80.3 11.2 %collective-permute-start.3 = (bf16[2,256,256]{2,1,0:T(8,128)(2,1)S(1)}, bf16[2,256,256]{2,1,0:T(8,128)(2,1)S(1)}, u32[]{:S(2)}, u32[]{:S(2)}) collective-permute-start(bf16[2,256,256]{2,1,0:T(8,128)(2,1)S(1)} %get-tuple-element.41), channel_id=1, source_target_pairs={{0,6},{1,7},{2,4},{3,5},{4,2},{5,3},{6,0},{7,1},{8,14},{9,15},{10,... | collective-permute-start | bytes 786440 | tf_op jit(solution)/shard_map/ppermute | solution.py:149
  83.3 8.8 %collective-permute-start.1 = (bf16[2,256,256]{2,1,0:T(8,128)(2,1)S(1)}, bf16[2,256,256]{2,1,0:T(8,128)(2,1)S(1)}, u32[]{:S(2)}, u32[]{:S(2)}) collective-permute-start(bf16[2,256,256]{2,1,0:T(8,128)(2,1)S(1)} %get-tuple-element.42), channel_id=1, source_target_pairs={{0,2},{1,3},{2,0},{3,1},{4,6},{5,7},{6,4},{7,5},{8,10},{9,11},{10,... | collective-permute-start | bytes 786440 | tf_op jit(solution)/shard_map/ppermute | solution.py:149
  83.3 13.2 %collective-permute-start.2 = (bf16[2,256,256]{2,1,0:T(8,128)(2,1)S(1)}, bf16[2,256,256]{2,1,0:T(8,128)(2,1)S(1)}, u32[]{:S(2)}, u32[]{:S(2)}) collective-permute-start(bf16[2,256,256]{2,1,0:T(8,128)(2,1)S(1)} %get-tuple-element.43), channel_id=1, source_target_pairs={{0,4},{1,5},{2,6},{3,7},{4,0},{5,1},{6,2},{7,3},{8,12},{9,13},{10,... | collective-permute-start | bytes 786440 | tf_op jit(solution)/shard_map/ppermute | solution.py:149
  85.5 21.1 %collective-permute-start.17 = (bf16[2,256,256]{1,2,0:T(8,128)(2,1)S(1)}, bf16[2,256,256]{1,2,0:T(8,128)(2,1)S(1)}, u32[]{:S(2)}, u32[]{:S(2)}) collective-permute-start(bf16[2,256,256]{1,2,0:T(8,128)(2,1)S(1)} %select_select_fusion.1), channel_id=1, source_target_pairs={{0,96},{1,97},{2,98},{3,99},{4,100},{5,101},{6,102},{7,103},{8,104... | collective-permute-start | bytes 786440 | tf_op jit(solution)/shard_map/ppermute | solution.py:174
  89.6 18.4 %collective-permute-start.16 = (bf16[2,256,256]{1,2,0:T(8,128)(2,1)S(1)}, bf16[2,256,256]{1,2,0:T(8,128)(2,1)S(1)}, u32[]{:S(2)}, u32[]{:S(2)}) collective-permute-start(bf16[2,256,256]{1,2,0:T(8,128)(2,1)S(1)} %select_select_fusion.1), channel_id=1, source_target_pairs={{0,64},{1,65},{2,66},{3,67},{4,68},{5,69},{6,70},{7,71},{8,72},{9,... | collective-permute-start | bytes 786440 | tf_op jit(solution)/shard_map/ppermute | solution.py:174
  91.5 9.1 %collective-permute-start.26 = (bf16[2,192,256]{2,1,0:T(8,128)(2,1)S(1)}, bf16[2,192,256]{2,1,0:T(8,128)(2,1)S(1)}, u32[]{:S(2)}, u32[]{:S(2)}) collective-permute-start(bf16[2,192,256]{2,1,0:T(8,128)(2,1)S(1)} %fusion.28), channel_id=1, source_target_pairs={{0,24},{1,97},{2,26},{3,99},{4,28},{5,101},{6,30},{7,103},{8,16},{... | collective-permute-start | bytes 589832 | tf_op jit(solution)/shard_map/ppermute | solution.py:156
  92.1 9.5 %collective-permute-start.25 = (bf16[2,192,256]{2,1,0:T(8,128)(2,1)S(1)}, bf16[2,192,256]{2,1,0:T(8,128)(2,1)S(1)}, u32[]{:S(2)}, u32[]{:S(2)}) collective-permute-start(bf16[2,192,256]{2,1,0:T(8,128)(2,1)S(1)} %fusion.28), channel_id=1, source_target_pairs={{0,16},{1,65},{2,18},{3,67},{4,20},{5,69},{6,22},{7,71},{8,24},{9,... | collective-permute-start | bytes 589832 | tf_op jit(solution)/shard_map/ppermute | solution.py:156
  96.5 8.1 %collective-permute-start.24 = (bf16[2,192,256]{2,1,0:T(8,128)(2,1)S(1)}, bf16[2,192,256]{2,1,0:T(8,128)(2,1)S(1)}, u32[]{:S(2)}, u32[]{:S(2)}) collective-permute-start(bf16[2,192,256]{2,1,0:T(8,128)(2,1)S(1)} %fusion.28), channel_id=1, source_target_pairs={{0,8},{1,33},{2,10},{3,35},{4,12},{5,37},{6,14},{7,39},{8,0},{9,41... | collective-permute-start | bytes 589832 | tf_op jit(solution)/shard_map/ppermute | solution.py:156
  97.7 14.6 %copy-start.13 = (bf16[2,256,256]{2,1,0:T(8,128)(2,1)S(1)}, bf16[2,256,256]{2,1,0:T(8,128)(2,1)}, u32[]{:S(2)}) copy-start(bf16[2,256,256]{2,1,0:T(8,128)(2,1)} %param.7) | copy-start | bytes 786436
  100.6 8.4 %collective-permute-start.15 = (bf16[2,256,256]{1,2,0:T(8,128)(2,1)S(1)}, bf16[2,256,256]{1,2,0:T(8,128)(2,1)S(1)}, u32[]{:S(2)}, u32[]{:S(2)}) collective-permute-start(bf16[2,256,256]{1,2,0:T(8,128)(2,1)S(1)} %select_select_fusion.1), channel_id=1, source_target_pairs={{0,32},{1,33},{2,34},{3,35},{4,36},{5,37},{6,38},{7,39},{8,40},{9,... | collective-permute-start | bytes 786440 | tf_op jit(solution)/shard_map/ppermute | solution.py:174
  101.6 8.6 %collective-permute-start.6 = (bf16[2,256,256]{2,1,0:T(8,128)(2,1)S(1)}, bf16[2,256,256]{2,1,0:T(8,128)(2,1)S(1)}, u32[]{:S(2)}, u32[]{:S(2)}) collective-permute-start(bf16[2,256,256]{2,1,0:T(8,128)(2,1)S(1)} %fusion.27), channel_id=1, source_target_pairs={{0,6},{1,7},{2,4},{3,5},{4,2},{5,3},{6,0},{7,1},{8,14},{9,15},{10,... | collective-permute-start | bytes 786440 | tf_op jit(solution)/shard_map/ppermute | solution.py:156
  104.8 21.7 %collective-permute-start.29 = (bf16[2,4,192,256]{3,2,1,0:T(8,128)(2,1)S(1)}, bf16[2,4,192,256]{3,2,1,0:T(8,128)(2,1)S(1)}, u32[]{:S(2)}, u32[]{:S(2)}) collective-permute-start(bf16[2,4,192,256]{3,2,1,0:T(8,128)(2,1)S(1)} %pad_maximum_fusion.5), channel_id=1, source_target_pairs={{0,96},{1,25},{2,98},{3,27},{4,100},{5,29},{6,102},{7,31},{8,104},... | collective-permute-start | bytes 2359304 | tf_op jit(solution)/shard_map/ppermute | solution.py:156
  106.6 19.9 %collective-permute-start.28 = (bf16[2,4,192,256]{3,2,1,0:T(8,128)(2,1)S(1)}, bf16[2,4,192,256]{3,2,1,0:T(8,128)(2,1)S(1)}, u32[]{:S(2)}, u32[]{:S(2)}) collective-permute-start(bf16[2,4,192,256]{3,2,1,0:T(8,128)(2,1)S(1)} %pad_maximum_fusion.5), channel_id=1, source_target_pairs={{0,64},{1,17},{2,66},{3,19},{4,68},{5,21},{6,70},{7,23},{8,72},{9,... | collective-permute-start | bytes 2359304 | tf_op jit(solution)/shard_map/ppermute | solution.py:156
  108.0 21.1 %collective-permute-start.27 = (bf16[2,4,192,256]{3,2,1,0:T(8,128)(2,1)S(1)}, bf16[2,4,192,256]{3,2,1,0:T(8,128)(2,1)S(1)}, u32[]{:S(2)}, u32[]{:S(2)}) collective-permute-start(bf16[2,4,192,256]{3,2,1,0:T(8,128)(2,1)S(1)} %pad_maximum_fusion.5), channel_id=1, source_target_pairs={{0,32},{1,9},{2,34},{3,11},{4,36},{5,13},{6,38},{7,15},{8,40},{9,1... | collective-permute-start | bytes 2359304 | tf_op jit(solution)/shard_map/ppermute | solution.py:156
  109.0 7.9 %collective-permute-start.5 = (bf16[2,256,256]{2,1,0:T(8,128)(2,1)S(1)}, bf16[2,256,256]{2,1,0:T(8,128)(2,1)S(1)}, u32[]{:S(2)}, u32[]{:S(2)}) collective-permute-start(bf16[2,256,256]{2,1,0:T(8,128)(2,1)S(1)} %fusion.27), channel_id=1, source_target_pairs={{0,4},{1,5},{2,6},{3,7},{4,0},{5,1},{6,2},{7,3},{8,12},{9,13},{10,... | collective-permute-start | bytes 786440 | tf_op jit(solution)/shard_map/ppermute | solution.py:156
  110.2 10.7 %collective-permute-start.4 = (bf16[2,256,256]{2,1,0:T(8,128)(2,1)S(1)}, bf16[2,256,256]{2,1,0:T(8,128)(2,1)S(1)}, u32[]{:S(2)}, u32[]{:S(2)}) collective-permute-start(bf16[2,256,256]{2,1,0:T(8,128)(2,1)S(1)} %fusion.27), channel_id=1, source_target_pairs={{0,2},{1,3},{2,0},{3,1},{4,6},{5,7},{6,4},{7,5},{8,10},{9,11},{10,... | collective-permute-start | bytes 786440 | tf_op jit(solution)/shard_map/ppermute | solution.py:156
  121.2 12.4 %collective-permute-start.7 = (bf16[2,4,256,256]{3,2,0,1:T(8,128)(2,1)S(1)}, bf16[2,4,256,256]{3,2,0,1:T(8,128)(2,1)S(1)}, u32[]{:S(2)}, u32[]{:S(2)}) collective-permute-start(bf16[2,4,256,256]{3,2,0,1:T(8,128)(2,1)S(1)} %pad_maximum_fusion.3), channel_id=1, source_target_pairs={{0,1},{1,0},{2,3},{3,2},{4,5},{5,4},{6,7},{7,6},{8,9},{9,8},{10,11... | collective-permute-start | bytes 3145736 | tf_op jit(solution)/shard_map/ppermute | solution.py:156
  (12 other events, 23.6 us)

commit v10 on v9

--- a/solution.py
+++ b/solution.py
@@ -124,42 +124,61 @@
     return pairs
 
 
-def xor_bcast(value, root, on_row):
+def xor_bcast(value, root, on_row, rider, rider_root):
     nrow = lax.axis_size("row")
     ncol = lax.axis_size("col")
     me = lax.axis_index("row") if on_row else lax.axis_index("col")
     parity = lax.axis_index("col") % CORES
-    relative = me ^ root
     axes = ("row", "col")
 
-    def digit(step):
+    def digit(step, relative):
         if on_row:
             shift = jnp.where(parity == 0, 2 if step == 0 else 0, 0 if step == 0 else 2)
         else:
             shift = dims_of(False, 0, step)[0]
         return (relative >> shift) & (RING - 1 if on_row or step == 1 else CORES - 1)
 
+    def send(main, extra, step, mask):
+        pairs = digit_pairs(nrow, ncol, on_row, step, mask)
+        flat = main.reshape(main.shape[0], -1, main.shape[-1])
+        both = jnp.concatenate([flat, extra.reshape(extra.shape[0], -1, extra.shape[-1])], axis=1)
+        got = lax.ppermute(both, axes, pairs)
+        return got[:, : flat.shape[1]].reshape(main.shape), got[:, flat.shape[1] :].reshape(extra.shape)
+
+    def ride(step, gots):
+        return pick(digit(step, me ^ rider_root), [rider] + gots)
+
+    relative = me ^ root
     sizes = [dims_of(on_row, 0, step)[1] for step in range(2)]
     shape = value.shape
     buf = value.reshape(shape[0], sizes[0], sizes[1], -1, shape[-1])
     for step in range(2):
-        d = digit(step)
         groups = [buf[:, m] for m in range(sizes[step])]
-        got = [None] + [
-            lax.ppermute(groups[m], axes, digit_pairs(nrow, ncol, on_row, step, m))
-            for m in range(1, sizes[step])
-        ]
-        buf = pick(d, [groups[0]] + got[1:])
+        if on_row:
+            got = [
+                lax.ppermute(groups[m], axes, digit_pairs(nrow, ncol, on_row, step, m))
+                for m in range(1, sizes[step])
+            ]
+        else:
+            pairs = [send(groups[m], rider, step, m) for m in range(1, sizes[step])]
+            got = [g for g, _ in pairs]
+            rider = ride(step, [r for _, r in pairs])
+        buf = pick(digit(step, relative), [groups[0]] + got)
     for step in reversed(range(2)):
-        d = digit(step)
-        got = [buf] + [
-            lax.ppermute(buf, axes, digit_pairs(nrow, ncol, on_row, step, m))
-            for m in range(1, sizes[step])
-        ]
+        if on_row:
+            pairs = [send(buf, rider, step, m) for m in range(1, sizes[step])]
+            got = [buf] + [g for g, _ in pairs]
+            rider = ride(step, [r for _, r in pairs])
+        else:
+            got = [buf] + [
+                lax.ppermute(buf, axes, digit_pairs(nrow, ncol, on_row, step, m))
+                for m in range(1, sizes[step])
+            ]
+        d = digit(step, relative)
         buf = jnp.stack(
             [pick(d, [got[dd ^ t] for dd in range(sizes[step])]) for t in range(sizes[step])], axis=1
         )
-    return buf.reshape(shape)
+    return buf.reshape(shape), rider
 
 
 def all_bcast(value, root):
@@ -272,15 +291,15 @@
         )
 
     lower_first = lower_local(local_col(b1), pivot_inv[0], rows_first)
-    cols_sent = xor_bcast(jnp.stack([lower_first, local_col(b2)]), jnp.stack([c1, c2]), False)
-    rows_sent = xor_bcast(jnp.stack([local_row(a1), local_row(a2)]), jnp.stack([r1, r2]), True)
+    cross = jnp.stack([masked(front[a1, b2], local[a1, b2]), masked(front[a2, b1], local[a2, b1])])
+    cols_sent, cross = xor_bcast(
+        jnp.stack([lower_first, local_col(b2)]), jnp.stack([c1, c2]), False, cross, jnp.stack([c2, c1])
+    )
+    rows_sent, cross = xor_bcast(
+        jnp.stack([local_row(a1), local_row(a2)]), jnp.stack([r1, r2]), True, cross, jnp.stack([r1, r2])
+    )
     lower_first, second_col = cols_sent[0], cols_sent[1]
     upper_first, second_row = rows_sent[0], rows_sent[1]
-
-    cross = all_bcast(
-        jnp.stack([masked(front[a1, b2], local[a1, b2]), masked(front[a2, b1], local[a2, b1])]),
-        jnp.stack([r1 * ncol + c2, r2 * ncol + c1]),
-    )
     first_at_second, second_at_first = cross[0], cross[1]
 
     second_ok = (second != first)[None]

time: 158 us -> 208 us (1.32)
  local copies, waits for them, and re-layouts: 12.2 us -> 53.9 us
  starting transfers between devices: 45.8 us -> 25.5 us
  waiting for transfers between devices: 36.9 us -> 55 us
  other arithmetic: 25.8 us -> 33.4 us
  matrix products: 5.34 us -> 10 us
    ppermute x10, waiting for transfers between devices: 21 us -> 46 us  [send(): got = lax.ppermute(both, axes, pairs)]
    ppermute x10 -> x4, starting transfers between devices: 19.6 us -> 4.18 us  [xor_bcast(): lax.ppermute(buf, axes, digit_pairs(nrow, ncol, on_row, step, m))]
    ppermute x10 -> x4, waiting for transfers between devices: 14.9 us -> 2.96 us  [xor_bcast(): lax.ppermute(buf, axes, digit_pairs(nrow, ncol, on_row, step, m))]
    another operation x0 -> x5, local copies, waits for them, and re-layouts: none -> 9.56 us  [the longest x2 6.68 us: body(): jnp.stack([local_row(a1), local_row(a2)])]
    slice x0 -> x8, local copies, waits for them, and re-layouts: none -> 8.42 us  [the longest x7 6.63 us: send(): got[:, :flat.shape[1]].reshape(main.shape)]
    slice x1 -> x3, local copies, waits for them, and re-layouts: 0.27 us -> 7.96 us  [body(): upper_first, second_row = (rows_sent[0], rows_sent[1])]
    squeeze x2 -> x5, local copies, waits for them, and re-layouts: 0.09 us -> 6.82 us  [xor_bcast(): groups = [buf[:, m] for m in range(sizes[step])]]
    ppermute x0 -> x3, local copies, waits for them, and re-layouts: none -> 6.73 us  [xor_bcast(): lax.ppermute(groups[m], axes, digit_pairs(nrow, ncol, on_row, step, m))]
  transfers between devices with their start and end apart: 30 -> 20, of which waited for: 9 -> 8; matrix products, arithmetic and copies ran while one was open for 21% -> 25% of each run, Pallas kernels for 0% -> 0%
where the time goes in v10:
time: 208 us; the launch traced here: 207 us
  waiting for transfers between devices  55 us (26%)
  local copies, waits for them, and re-layouts  53.9 us (26%)
  other arithmetic  33.4 us (16%)
  starting transfers between devices  25.5 us (12%)
  Pallas kernels  16.7 us (8%)
  between operations  12.2 us (6%)
  matrix products  10 us (5%)
    ppermute x10, waiting for transfers between devices, send(): got = lax.ppermute(both, axes, pairs)  46 us
    pallas_call x1, Pallas kernels, both_updates(): pl.pallas_call(update_kernel, grid_spec=pltpu.PrefetchScalarGridSpec(num_...  16.7 us
    ppermute x10, starting transfers between devices, send(): got = lax.ppermute(both, axes, pairs)  12.7 us
    select_n x10, other arithmetic, per_part(): return jnp.where(cond.reshape((-1,) + (1,) * (a.ndim - 1)), a, b)  9.21 us
    ppermute x6, starting transfers between devices, xor_bcast(): lax.ppermute(groups[m], axes, digit_pairs(nrow, ncol, on_row, step, m))  8.71 us
    slice x3, local copies, waits for them, and re-layouts, body(): upper_first, second_row = (rows_sent[0], rows_sent[1])  7.96 us
    squeeze x5, local copies, waits for them, and re-layouts, xor_bcast(): groups = [buf[:, m] for m in range(sizes[step])]  6.82 us
    ppermute x3, local copies, waits for them, and re-layouts, xor_bcast(): lax.ppermute(groups[m], axes, digit_pairs(nrow, ncol, on_row, step, m))  6.73 us
  transfers between devices with their start and end apart: 20, of which 8 were waited for; matrix products, arithmetic and copies ran while one was open for 25% of the time, Pallas kernels for 0%

profile of v10, /device:TPU:6, one launch (start us, length us, event | category | flops | bytes accessed | tf_op | source)
XLA Modules:
  0.0 206.7 jit_solution(8372285130753864622)
XLA Ops:
  15.2 1.7 select_convert_fusion.1
  20.3 1.8 copy.134
  22.0 1.8 reshape_squeeze.3
  26.6 3.8 %dynamic-slice_select_fusion = (bf16[1,12,256,256]{3,2,1,0:T(8,128)(2,1)}, bf16[1,12,256,256]{3,2,1,0:T(8,128)(2,1)}) fusion(bf16[8,12,256,256]{3,2,1,0:T(8,128)(2,1)} %front_ref.1, s32[]{:T(128)S(6)} %select_n.486, pred[12]{0:T(512)(128)(4,1)S(1)} %get-tuple-element.5, s32[]{:T(128)S(6)} %select_n.481, pred[12]{0:T(512)(128)(4,1)S(1)} %get-tuple-element.6), kind=kLoop, calls=%fused_computation.21 | loop fusion | flops 1572864 | bytes 6291488 | tf_op jit(solution)/shard_map/jit(_where)/select_n | solution.py:254
  30.4 2.7 %copy.139 = bf16[1,4,4,192,256]{3,4,0,2,1:T(8,128)(2,1)S(1)} copy(bf16[1,4,4,192,256]{4,3,2,1,0:T(8,128)(2,1)} %bitcast.156) | data formatting | bytes 3145728 | tf_op jit(solution)/shard_map/stack | solution.py:299
  33.1 4.0 %copy.140 = bf16[1,4,4,192,256]{3,4,0,2,1:T(8,128)(2,1)} copy(bf16[1,4,4,192,256]{4,3,2,1,0:T(8,128)(2,1)} %bitcast.155) | data formatting | bytes 3145728 | tf_op jit(solution)/shard_map/stack | solution.py:299
  37.1 3.3 %fusion.16 = (bf16[2,4,192,256]{2,3,0,1:T(8,128)(2,1)}, bf16[2,4,192,256]{2,3,0,1:T(8,128)(2,1)}, bf16[2,4,192,256]{2,3,0,1:T(8,128)(2,1)}) fusion(bf16[1,4,4,192,256]{3,4,0,2,1:T(8,128)(2,1)} %copy.140, bf16[1,4,4,192,256]{3,4,0,2,1:T(8,128)(2,1)S(1)} %copy.139), kind=kLoop, calls=%fused_computation.39 | loop fusion | flops 1179648 | bytes 5505024 | tf_op jit(solution)/shard_map/squeeze | solution.py:156
  40.3 2.2 %copy.142 = bf16[2,4,192,256]{3,2,1,0:T(8,128)(2,1)} copy(bf16[2,4,192,256]{2,3,0,1:T(8,128)(2,1)} %get-tuple-element.32) | data formatting | bytes 1572864 | tf_op jit(solution)/shard_map/squeeze | solution.py:156
  42.6 3.9 %collective-permute-start.9 = (bf16[2,4,192,256]{3,2,1,0:T(8,128)(2,1)}, bf16[2,4,192,256]{3,2,1,0:T(8,128)(2,1)}, u32[]{:S(2)}, u32[]{:S(2)}) collective-permute-start(bf16[2,4,192,256]{3,2,1,0:T(8,128)(2,1)} %copy.142), channel_id=1, source_target_pairs={{0,64},{1,17},{2,66},{3,19},{4,68},{5,21},{6,70},{7,23},{8,72},{9,... | collective-permute-start | bytes 2359304 | tf_op jit(solution)/shard_map/ppermute | solution.py:159
  46.4 2.2 %copy.141 = bf16[2,4,192,256]{3,2,1,0:T(8,128)(2,1)} copy(bf16[2,4,192,256]{2,3,0,1:T(8,128)(2,1)} %get-tuple-element.31) | data formatting | bytes 1572864 | tf_op jit(solution)/shard_map/squeeze | solution.py:156
  49.7 2.3 %copy.143 = bf16[2,4,192,256]{3,2,1,0:T(8,128)(2,1)} copy(bf16[2,4,192,256]{2,3,0,1:T(8,128)(2,1)} %get-tuple-element.30) | data formatting | bytes 1572864 | tf_op jit(solution)/shard_map/squeeze | solution.py:156
  58.0 2.2 %copy.144 = bf16[2,4,192,256]{2,3,0,1:T(8,128)(2,1)} copy(bf16[2,4,192,256]{3,2,1,0:T(8,128)(2,1)} %collective-permute-done.9) | data formatting | bytes 1572864 | tf_op jit(solution)/shard_map/ppermute | solution.py:159
  60.2 6.0 %collective-permute-done.8 = bf16[2,4,192,256]{3,2,1,0:T(8,128)(2,1)} collective-permute-done((bf16[2,4,192,256]{3,2,1,0:T(8,128)(2,1)}, bf16[2,4,192,256]{3,2,1,0:T(8,128)(2,1)}, u32[]{:S(2)}, u32[]{:S(2)}) %collective-permute-start.8) | collective-permute-done | bytes 786464 | tf_op jit(solution)/shard_map/ppermute | solution.py:159
  66.2 2.2 %copy.146 = bf16[2,4,192,256]{2,3,0,1:T(8,128)(2,1)} copy(bf16[2,4,192,256]{3,2,1,0:T(8,128)(2,1)} %collective-permute-done.8) | data formatting | bytes 1572864 | tf_op jit(solution)/shard_map/ppermute | solution.py:159
  68.4 2.3 %copy.145 = bf16[2,4,192,256]{2,3,0,1:T(8,128)(2,1)} copy(bf16[2,4,192,256]{3,2,1,0:T(8,128)(2,1)} %collective-permute-done.10) | data formatting | bytes 1572864 | tf_op jit(solution)/shard_map/ppermute | solution.py:159
  75.6 2.9 %collective-permute-start.2 = (bf16[2,512,256]{1,2,0:T(8,128)(2,1)S(1)}, bf16[2,512,256]{1,2,0:T(8,128)(2,1)S(1)}, u32[]{:S(2)}, u32[]{:S(2)}) collective-permute-start(bf16[2,512,256]{1,2,0:T(8,128)(2,1)S(1)} %get-tuple-element.56), channel_id=1, source_target_pairs={{0,4},{1,5},{2,6},{3,7},{4,0},{5,1},{6,2},{7,3},{8,12},{9,13},{10,... | collective-permute-start | bytes 1572872 | tf_op jit(solution)/shard_map/ppermute | solution.py:145
  79.7 2.4 %collective-permute-start.12 = (bf16[2,192,256]{1,2,0:T(8,128)(2,1)S(1)}, bf16[2,192,256]{1,2,0:T(8,128)(2,1)S(1)}, u32[]{:S(2)}, u32[]{:S(2)}) collective-permute-start(bf16[2,192,256]{1,2,0:T(8,128)(2,1)S(1)} %get-tuple-element.48), channel_id=1, source_target_pairs={{0,16},{1,65},{2,18},{3,67},{4,20},{5,69},{6,22},{7,71},{8,24},{9,... | collective-permute-start | bytes 589832 | tf_op jit(solution)/shard_map/ppermute | solution.py:159
  82.1 6.8 %collective-permute-done.1 = bf16[2,512,256]{1,2,0:T(8,128)(2,1)S(1)} collective-permute-done((bf16[2,512,256]{1,2,0:T(8,128)(2,1)S(1)}, bf16[2,512,256]{1,2,0:T(8,128)(2,1)S(1)}, u32[]{:S(2)}, u32[]{:S(2)}) %collective-permute-start.1) | collective-permute-done | bytes 524320 | tf_op jit(solution)/shard_map/ppermute | solution.py:145
  89.7 8.0 %collective-permute-done.2 = bf16[2,512,256]{1,2,0:T(8,128)(2,1)S(1)} collective-permute-done((bf16[2,512,256]{1,2,0:T(8,128)(2,1)S(1)}, bf16[2,512,256]{1,2,0:T(8,128)(2,1)S(1)}, u32[]{:S(2)}, u32[]{:S(2)}) %collective-permute-start.2) | collective-permute-done | bytes 524320 | tf_op jit(solution)/shard_map/ppermute | solution.py:145
  97.6 7.8 %collective-permute-done.3 = bf16[2,512,256]{1,2,0:T(8,128)(2,1)S(1)} collective-permute-done((bf16[2,512,256]{1,2,0:T(8,128)(2,1)S(1)}, bf16[2,512,256]{1,2,0:T(8,128)(2,1)S(1)}, u32[]{:S(2)}, u32[]{:S(2)}) %collective-permute-start.3) | collective-permute-done | bytes 524320 | tf_op jit(solution)/shard_map/ppermute | solution.py:145
  107.0 3.8 %collective-permute-start.4 = (bf16[2,256,256]{1,2,0:T(8,128)(2,1)S(1)}, bf16[2,256,256]{1,2,0:T(8,128)(2,1)S(1)}, u32[]{:S(2)}, u32[]{:S(2)}) collective-permute-start(bf16[2,256,256]{1,2,0:T(8,128)(2,1)S(1)} %get-tuple-element.42), channel_id=1, source_target_pairs={{0,2},{1,3},{2,0},{3,1},{4,6},{5,7},{6,4},{7,5},{8,10},{9,11},{10,... | collective-permute-start | bytes 786440 | tf_op jit(solution)/shard_map/ppermute | solution.py:174
  111.2 2.9 %collective-permute-start.15 = (bf16[2,448,256]{1,2,0:T(8,128)(2,1)S(1)}, bf16[2,448,256]{1,2,0:T(8,128)(2,1)S(1)}, u32[]{:S(2)}, u32[]{:S(2)}) collective-permute-start(bf16[2,448,256]{1,2,0:T(8,128)(2,1)S(1)} %pad_maximum_fusion.11), channel_id=1, source_target_pairs={{0,16},{1,65},{2,18},{3,67},{4,20},{5,69},{6,22},{7,71},{8,24},{9,... | collective-permute-start | bytes 1376264 | tf_op jit(solution)/shard_map/ppermute | solution.py:145
  114.1 3.0 %collective-permute-done.6 = bf16[2,256,256]{1,2,0:T(8,128)(2,1)S(1)} collective-permute-done((bf16[2,256,256]{1,2,0:T(8,128)(2,1)S(1)}, bf16[2,256,256]{1,2,0:T(8,128)(2,1)S(1)}, u32[]{:S(2)}, u32[]{:S(2)}) %collective-permute-start.6) | collective-permute-done | bytes 262176 | tf_op jit(solution)/shard_map/ppermute | solution.py:174
  121.5 5.8 %collective-permute-done.16 = bf16[2,448,256]{1,2,0:T(8,128)(2,1)S(1)} collective-permute-done((bf16[2,448,256]{1,2,0:T(8,128)(2,1)S(1)}, bf16[2,448,256]{1,2,0:T(8,128)(2,1)S(1)}, u32[]{:S(2)}, u32[]{:S(2)}) %collective-permute-start.16) | collective-permute-done | bytes 458784 | tf_op jit(solution)/shard_map/ppermute | solution.py:145
  134.8 1.7 collective-permute-start.18
  144.2 16.7 %collective-permute-done.19 = bf16[2,1024,256]{1,2,0:T(8,128)(2,1)} collective-permute-done((bf16[2,1024,256]{1,2,0:T(8,128)(2,1)}, bf16[2,1024,256]{1,2,0:T(8,128)(2,1)}, u32[]{:S(2)}, u32[]{:S(2)}) %collective-permute-start.19) | collective-permute-done | bytes 1048608 | tf_op jit(solution)/shard_map/ppermute | solution.py:145
  174.5 1.7 fusion.52
  176.2 4.0 %copy.166 = bf16[1,4,4,192,256]{4,3,2,1,0:T(8,128)(2,1)} copy(bf16[1,4,4,192,256]{3,4,0,2,1:T(8,128)(2,1)} %get-tuple-element.28) | data formatting | bytes 3145728 | tf_op jit(solution)/shard_map/slice | solution.py:302
  180.3 2.3 %copy.165 = bf16[1,4,4,192,256]{4,3,2,1,0:T(8,128)(2,1)} copy(bf16[1,4,4,192,256]{3,4,0,2,1:T(8,128)(2,1)S(1)} %get-tuple-element.29) | data formatting | bytes 3145728 | tf_op jit(solution)/shard_map/slice | solution.py:302
  182.5 3.5 %select_convert_fusion.l2_ref = bf16[8,256,256]{2,1,0:T(8,128)(2,1)} fusion(bf16[8,1,256,256]{2,3,0,1:T(8,128)(2,1)S(1)} %bitcast.172, bf16[8,1,256,256]{2,3,0,1:T(8,128)(2,1)} %bitcast.180, bf16[8,256,256]{1,2,0:T(8,128)(2,1)S(1)} %bitcast.173, pred[8]{0:T(512)(128)(4,1)S(1)} %get-tuple-element.66, pred[8]{0:T(512)(128)(4,1)S(1)} %copy-done.31, ...), kind=kOutput, calls=%fused_computation.18 | convolution fusion | flops 540540928 | bytes 4457984 | tf_op jit(solution)/shard_map/iab,bc->iac/dot_general | solution.py:202
  186.1 3.9 %select_bitcast_fusion.u2_ref = bf16[12,256,256]{2,1,0:T(8,128)(2,1)} fusion(pred[12]{0:T(512)(128)(4,1)S(1)} %get-tuple-element.11, bf16[1,12,256,256]{3,2,1,0:T(8,128)(2,1)} %bitcast.178, bf16[12,256,256]{2,1,0:T(8,128)(2,1)S(1)} %bitcast.154, pred[12]{0:T(512)(128)(4,1)S(1)} %copy-done.32, bf16[256,256]{1,0:T(8,128)(2,1)S(1)} %copy-done.35), kind=kOutput, calls=%fused_computation.20 | convolution fusion | flops 406585344 | bytes 4849688 | tf_op jit(solution)/shard_map/iab,jbc->ijac/dot_general | solution.py:207
  190.0 16.7 %shard_map.46 = bf16[8,12,256,256]{3,2,1,0:T(8,128)(2,1)} custom-call(s32[8,12]{1,0:T(8,128)} %select_add_fusion.codes, bf16[8,12,256,256]{3,2,1,0:T(8,128)(2,1)} %front_ref.1, bf16[8,256,256]{2,1,0:T(8,128)(2,1)} %bitcast.157, bf16[8,256,256]{2,1,0:T(8,128)(2,1)} %select_convert_fusion.l2_ref, bf16[12,256,256]{2,1,0:T(8,128)(2,1)} %bitcast.153, ...), custom_call_target="tpu_custom_call" | custom-call | tf_op jit(solution)/shard_map/pallas_call | solution.py:239
  (169 shorter events, 58.3 us)
Async XLA Ops:
  0.0 12.8 %copy-start.3 = (s32[128,96]{0,1:T(8,128)S(1)}, s32[128,96]{0,1:T(8,128)}, u32[]{:S(2)}) copy-start(s32[128,96]{0,1:T(8,128)} %param.5) | copy-start | bytes 147460
  0.0 15.2 %copy-start.33 = (bf16[2,256,256]{2,1,0:T(8,128)(2,1)S(1)}, bf16[2,256,256]{2,1,0:T(8,128)(2,1)}, u32[]{:S(2)}) copy-start(bf16[2,256,256]{2,1,0:T(8,128)(2,1)} %param.7) | copy-start | bytes 786436
  25.1 45.6 %collective-permute-start = (bf16[2,1280,256]{1,2,0:T(8,128)(2,1)}, bf16[2,1280,256]{1,2,0:T(8,128)(2,1)}, u32[]{:S(2)}, u32[]{:S(2)}) collective-permute-start(bf16[2,1280,256]{1,2,0:T(8,128)(2,1)} %maximum_maximum_fusion), channel_id=1, source_target_pairs={{0,1},{1,0},{2,3},{3,2},{4,5},{5,4},{6,7},{7,6},{8,9},{9,8},{10,11... | collective-permute-start | bytes 3932168 | tf_op jit(solution)/shard_map/ppermute | solution.py:145
  42.6 15.4 %collective-permute-start.9 = (bf16[2,4,192,256]{3,2,1,0:T(8,128)(2,1)}, bf16[2,4,192,256]{3,2,1,0:T(8,128)(2,1)}, u32[]{:S(2)}, u32[]{:S(2)}) collective-permute-start(bf16[2,4,192,256]{3,2,1,0:T(8,128)(2,1)} %copy.142), channel_id=1, source_target_pairs={{0,64},{1,17},{2,66},{3,19},{4,68},{5,21},{6,70},{7,23},{8,72},{9,... | collective-permute-start | bytes 2359304 | tf_op jit(solution)/shard_map/ppermute | solution.py:159
  48.7 17.5 %collective-permute-start.8 = (bf16[2,4,192,256]{3,2,1,0:T(8,128)(2,1)}, bf16[2,4,192,256]{3,2,1,0:T(8,128)(2,1)}, u32[]{:S(2)}, u32[]{:S(2)}) collective-permute-start(bf16[2,4,192,256]{3,2,1,0:T(8,128)(2,1)} %copy.141), channel_id=1, source_target_pairs={{0,32},{1,9},{2,34},{3,11},{4,36},{5,13},{6,38},{7,15},{8,40},{9,1... | collective-permute-start | bytes 2359304 | tf_op jit(solution)/shard_map/ppermute | solution.py:159
  52.0 16.5 %collective-permute-start.10 = (bf16[2,4,192,256]{3,2,1,0:T(8,128)(2,1)}, bf16[2,4,192,256]{3,2,1,0:T(8,128)(2,1)}, u32[]{:S(2)}, u32[]{:S(2)}) collective-permute-start(bf16[2,4,192,256]{3,2,1,0:T(8,128)(2,1)} %copy.143), channel_id=1, source_target_pairs={{0,96},{1,25},{2,98},{3,27},{4,100},{5,29},{6,102},{7,31},{8,104},... | collective-permute-start | bytes 2359304 | tf_op jit(solution)/shard_map/ppermute | solution.py:159
  73.9 14.9 %collective-permute-start.1 = (bf16[2,512,256]{1,2,0:T(8,128)(2,1)S(1)}, bf16[2,512,256]{1,2,0:T(8,128)(2,1)S(1)}, u32[]{:S(2)}, u32[]{:S(2)}) collective-permute-start(bf16[2,512,256]{1,2,0:T(8,128)(2,1)S(1)} %get-tuple-element.55), channel_id=1, source_target_pairs={{0,2},{1,3},{2,0},{3,1},{4,6},{5,7},{6,4},{7,5},{8,10},{9,11},{10,... | collective-permute-start | bytes 1572872 | tf_op jit(solution)/shard_map/ppermute | solution.py:145
  75.6 22.1 %collective-permute-start.2 = (bf16[2,512,256]{1,2,0:T(8,128)(2,1)S(1)}, bf16[2,512,256]{1,2,0:T(8,128)(2,1)S(1)}, u32[]{:S(2)}, u32[]{:S(2)}) collective-permute-start(bf16[2,512,256]{1,2,0:T(8,128)(2,1)S(1)} %get-tuple-element.56), channel_id=1, source_target_pairs={{0,4},{1,5},{2,6},{3,7},{4,0},{5,1},{6,2},{7,3},{8,12},{9,13},{10,... | collective-permute-start | bytes 1572872 | tf_op jit(solution)/shard_map/ppermute | solution.py:145
  78.5 27.0 %collective-permute-start.3 = (bf16[2,512,256]{1,2,0:T(8,128)(2,1)S(1)}, bf16[2,512,256]{1,2,0:T(8,128)(2,1)S(1)}, u32[]{:S(2)}, u32[]{:S(2)}) collective-permute-start(bf16[2,512,256]{1,2,0:T(8,128)(2,1)S(1)} %get-tuple-element.57), channel_id=1, source_target_pairs={{0,6},{1,7},{2,4},{3,5},{4,2},{5,3},{6,0},{7,1},{8,14},{9,15},{10,... | collective-permute-start | bytes 1572872 | tf_op jit(solution)/shard_map/ppermute | solution.py:145
  79.1 27.9 %collective-permute-start.13 = (bf16[2,192,256]{1,2,0:T(8,128)(2,1)S(1)}, bf16[2,192,256]{1,2,0:T(8,128)(2,1)S(1)}, u32[]{:S(2)}, u32[]{:S(2)}) collective-permute-start(bf16[2,192,256]{1,2,0:T(8,128)(2,1)S(1)} %get-tuple-element.47), channel_id=1, source_target_pairs={{0,24},{1,97},{2,26},{3,99},{4,28},{5,101},{6,30},{7,103},{8,16},{... | collective-permute-start | bytes 589832 | tf_op jit(solution)/shard_map/ppermute | solution.py:159
  79.7 31.1 %collective-permute-start.12 = (bf16[2,192,256]{1,2,0:T(8,128)(2,1)S(1)}, bf16[2,192,256]{1,2,0:T(8,128)(2,1)S(1)}, u32[]{:S(2)}, u32[]{:S(2)}) collective-permute-start(bf16[2,192,256]{1,2,0:T(8,128)(2,1)S(1)} %get-tuple-element.48), channel_id=1, source_target_pairs={{0,16},{1,65},{2,18},{3,67},{4,20},{5,69},{6,22},{7,71},{8,24},{9,... | collective-permute-start | bytes 589832 | tf_op jit(solution)/shard_map/ppermute | solution.py:159
  88.8 21.9 %collective-permute-start.11 = (bf16[2,192,256]{1,2,0:T(8,128)(2,1)S(1)}, bf16[2,192,256]{1,2,0:T(8,128)(2,1)S(1)}, u32[]{:S(2)}, u32[]{:S(2)}) collective-permute-start(bf16[2,192,256]{1,2,0:T(8,128)(2,1)S(1)} %get-tuple-element.49), channel_id=1, source_target_pairs={{0,8},{1,33},{2,10},{3,35},{4,12},{5,37},{6,14},{7,39},{8,0},{9,41... | collective-permute-start | bytes 589832 | tf_op jit(solution)/shard_map/ppermute | solution.py:159
  106.6 10.5 %collective-permute-start.6 = (bf16[2,256,256]{1,2,0:T(8,128)(2,1)S(1)}, bf16[2,256,256]{1,2,0:T(8,128)(2,1)S(1)}, u32[]{:S(2)}, u32[]{:S(2)}) collective-permute-start(bf16[2,256,256]{1,2,0:T(8,128)(2,1)S(1)} %get-tuple-element.42), channel_id=1, source_target_pairs={{0,6},{1,7},{2,4},{3,5},{4,2},{5,3},{6,0},{7,1},{8,14},{9,15},{10,... | collective-permute-start | bytes 786440 | tf_op jit(solution)/shard_map/ppermute | solution.py:174
  106.9 13.1 %collective-permute-start.5 = (bf16[2,256,256]{1,2,0:T(8,128)(2,1)S(1)}, bf16[2,256,256]{1,2,0:T(8,128)(2,1)S(1)}, u32[]{:S(2)}, u32[]{:S(2)}) collective-permute-start(bf16[2,256,256]{1,2,0:T(8,128)(2,1)S(1)} %get-tuple-element.42), channel_id=1, source_target_pairs={{0,4},{1,5},{2,6},{3,7},{4,0},{5,1},{6,2},{7,3},{8,12},{9,13},{10,... | collective-permute-start | bytes 786440 | tf_op jit(solution)/shard_map/ppermute | solution.py:174
  107.0 13.1 %collective-permute-start.4 = (bf16[2,256,256]{1,2,0:T(8,128)(2,1)S(1)}, bf16[2,256,256]{1,2,0:T(8,128)(2,1)S(1)}, u32[]{:S(2)}, u32[]{:S(2)}) collective-permute-start(bf16[2,256,256]{1,2,0:T(8,128)(2,1)S(1)} %get-tuple-element.42), channel_id=1, source_target_pairs={{0,2},{1,3},{2,0},{3,1},{4,6},{5,7},{6,4},{7,5},{8,10},{9,11},{10,... | collective-permute-start | bytes 786440 | tf_op jit(solution)/shard_map/ppermute | solution.py:174
  111.1 16.1 %collective-permute-start.16 = (bf16[2,448,256]{1,2,0:T(8,128)(2,1)S(1)}, bf16[2,448,256]{1,2,0:T(8,128)(2,1)S(1)}, u32[]{:S(2)}, u32[]{:S(2)}) collective-permute-start(bf16[2,448,256]{1,2,0:T(8,128)(2,1)S(1)} %pad_maximum_fusion.11), channel_id=1, source_target_pairs={{0,24},{1,97},{2,26},{3,99},{4,28},{5,101},{6,30},{7,103},{8,16},{... | collective-permute-start | bytes 1376264 | tf_op jit(solution)/shard_map/ppermute | solution.py:145
  111.2 16.0 %collective-permute-start.15 = (bf16[2,448,256]{1,2,0:T(8,128)(2,1)S(1)}, bf16[2,448,256]{1,2,0:T(8,128)(2,1)S(1)}, u32[]{:S(2)}, u32[]{:S(2)}) collective-permute-start(bf16[2,448,256]{1,2,0:T(8,128)(2,1)S(1)} %pad_maximum_fusion.11), channel_id=1, source_target_pairs={{0,16},{1,65},{2,18},{3,67},{4,20},{5,69},{6,22},{7,71},{8,24},{9,... | collective-permute-start | bytes 1376264 | tf_op jit(solution)/shard_map/ppermute | solution.py:145
  117.1 11.2 %collective-permute-start.14 = (bf16[2,448,256]{1,2,0:T(8,128)(2,1)S(1)}, bf16[2,448,256]{1,2,0:T(8,128)(2,1)}, u32[]{:S(2)}, u32[]{:S(2)}) collective-permute-start(bf16[2,448,256]{1,2,0:T(8,128)(2,1)S(1)} %pad_maximum_fusion.11), channel_id=1, source_target_pairs={{0,8},{1,33},{2,10},{3,35},{4,12},{5,37},{6,14},{7,39},{8,0},{9,41... | collective-permute-start | bytes 1376264 | tf_op jit(solution)/shard_map/ppermute | solution.py:145
  120.2 9.1 %copy-start.16 = (bf16[2,1,256,256]{2,3,0,1:T(8,128)(2,1)}, bf16[2,1,256,256]{2,3,0,1:T(8,128)(2,1)S(1)}, u32[]{:S(2)}) copy-start(bf16[2,1,256,256]{2,3,0,1:T(8,128)(2,1)S(1)} %get-tuple-element.44) | copy-start | bytes 786436
  120.2 9.1 %copy-start.18 = (bf16[2,1,256,256]{2,3,0,1:T(8,128)(2,1)}, bf16[2,1,256,256]{2,3,0,1:T(8,128)(2,1)S(1)}, u32[]{:S(2)}) copy-start(bf16[2,1,256,256]{2,3,0,1:T(8,128)(2,1)S(1)} %get-tuple-element.45) | copy-start | bytes 786436
  120.2 9.1 %copy-start.20 = (bf16[2,1,256,256]{2,3,0,1:T(8,128)(2,1)}, bf16[2,1,256,256]{2,3,0,1:T(8,128)(2,1)S(1)}, u32[]{:S(2)}) copy-start(bf16[2,1,256,256]{2,3,0,1:T(8,128)(2,1)S(1)} %get-tuple-element.46) | copy-start | bytes 786436
  121.4 18.8 %collective-permute-start.7 = (bf16[2,4,256,256]{2,3,0,1:T(8,128)(2,1)}, bf16[2,4,256,256]{2,3,0,1:T(8,128)(2,1)}, u32[]{:S(2)}, u32[]{:S(2)}) collective-permute-start(bf16[2,4,256,256]{2,3,0,1:T(8,128)(2,1)} %pad_maximum_fusion.4), channel_id=1, source_target_pairs={{0,1},{1,0},{2,3},{3,2},{4,5},{5,4},{6,7},{7,6},{8,9},{9,8},{10,11... | collective-permute-start | bytes 3145736 | tf_op jit(solution)/shard_map/ppermute | solution.py:174
  130.5 9.0 %copy-start.29 = (pred[12]{0:T(512)(128)(4,1)S(1)}, pred[12]{0:T(512)(128)(4,1)}, u32[]{:S(2)}) copy-start(pred[12]{0:T(512)(128)(4,1)} %get-tuple-element.76) | copy-start | bytes 40
  130.5 9.0 %copy-start.30 = (pred[12]{0:T(512)(128)(4,1)S(1)}, pred[12]{0:T(512)(128)(4,1)}, u32[]{:S(2)}) copy-start(pred[12]{0:T(512)(128)(4,1)} %get-tuple-element.77) | copy-start | bytes 40
  130.6 9.7 %copy-start.17 = (bf16[2,1,256,256]{2,3,0,1:T(8,128)(2,1)S(1)}, bf16[2,1,256,256]{2,3,0,1:T(8,128)(2,1)}, u32[]{:S(2)}) copy-start(bf16[2,1,256,256]{2,3,0,1:T(8,128)(2,1)} %copy-done.16) | copy-start | bytes 786436
  130.6 9.7 %copy-start.19 = (bf16[2,1,256,256]{2,3,0,1:T(8,128)(2,1)S(1)}, bf16[2,1,256,256]{2,3,0,1:T(8,128)(2,1)}, u32[]{:S(2)}) copy-start(bf16[2,1,256,256]{2,3,0,1:T(8,128)(2,1)} %copy-done.18) | copy-start | bytes 786436
  130.6 9.7 %copy-start.21 = (bf16[2,1,256,256]{2,3,0,1:T(8,128)(2,1)S(1)}, bf16[2,1,256,256]{2,3,0,1:T(8,128)(2,1)}, u32[]{:S(2)}) copy-start(bf16[2,1,256,256]{2,3,0,1:T(8,128)(2,1)} %copy-done.20) | copy-start | bytes 786436
  132.2 9.6 %copy-start.22 = (bf16[2,256,256]{1,2,0:T(8,128)(2,1)}, bf16[2,256,256]{1,2,0:T(8,128)(2,1)S(1)}, u32[]{:S(2)}) copy-start(bf16[2,256,256]{1,2,0:T(8,128)(2,1)S(1)} %fusion.28) | copy-start | bytes 786436
  133.4 27.6 %collective-permute-start.19 = (bf16[2,1024,256]{1,2,0:T(8,128)(2,1)}, bf16[2,1024,256]{1,2,0:T(8,128)(2,1)}, u32[]{:S(2)}, u32[]{:S(2)}) collective-permute-start(bf16[2,1024,256]{1,2,0:T(8,128)(2,1)} %pad_maximum_fusion.6), channel_id=1, source_target_pairs={{0,96},{1,25},{2,98},{3,27},{4,100},{5,29},{6,102},{7,31},{8,104},... | collective-permute-start | bytes 3145736 | tf_op jit(solution)/shard_map/ppermute | solution.py:145
  134.8 28.2 %collective-permute-start.18 = (bf16[2,1024,256]{1,2,0:T(8,128)(2,1)}, bf16[2,1024,256]{1,2,0:T(8,128)(2,1)}, u32[]{:S(2)}, u32[]{:S(2)}) collective-permute-start(bf16[2,1024,256]{1,2,0:T(8,128)(2,1)} %pad_maximum_fusion.6), channel_id=1, source_target_pairs={{0,64},{1,17},{2,66},{3,19},{4,68},{5,21},{6,70},{7,23},{8,72},{9,... | collective-permute-start | bytes 3145736 | tf_op jit(solution)/shard_map/ppermute | solution.py:145
  136.5 28.5 %collective-permute-start.17 = (bf16[2,1024,256]{1,2,0:T(8,128)(2,1)}, bf16[2,1024,256]{1,2,0:T(8,128)(2,1)}, u32[]{:S(2)}, u32[]{:S(2)}) collective-permute-start(bf16[2,1024,256]{1,2,0:T(8,128)(2,1)} %pad_maximum_fusion.6), channel_id=1, source_target_pairs={{0,32},{1,9},{2,34},{3,11},{4,36},{5,13},{6,38},{7,15},{8,40},{9,1... | collective-permute-start | bytes 3145736 | tf_op jit(solution)/shard_map/ppermute | solution.py:145
  142.9 19.5 %copy-start.14 = (bf16[1,2,4,256,256]{3,4,0,2,1:T(8,128)(2,1)}, bf16[1,2,4,256,256]{3,4,0,2,1:T(8,128)(2,1)S(1)}, u32[]{:S(2)}) copy-start(bf16[1,2,4,256,256]{3,4,0,2,1:T(8,128)(2,1)S(1)} %get-tuple-element.36) | copy-start | bytes 3145732
  (24 other events, 67.6 us)

commit v11 on v8

--- a/solution.py
+++ b/solution.py
@@ -124,7 +124,7 @@
     return pairs
 
 
-def xor_bcast(value, root, on_row):
+def xor_bcast(value, root, on_row, hold=None):
     nrow = lax.axis_size("row")
     ncol = lax.axis_size("col")
     me = lax.axis_index("row") if on_row else lax.axis_index("col")
@@ -150,6 +150,8 @@
             for m in range(1, sizes[step])
         ]
         buf = pick(d, [groups[0]] + got[1:])
+    if hold is not None:
+        buf, hold = lax.optimization_barrier((buf, hold))
     for step in reversed(range(2)):
         d = digit(step)
         got = [buf] + [
@@ -159,7 +161,7 @@
         buf = jnp.stack(
             [pick(d, [got[dd ^ t] for dd in range(sizes[step])]) for t in range(sizes[step])], axis=1
         )
-    return buf.reshape(shape)
+    return buf.reshape(shape), hold
 
 
 def all_bcast(value, root):
@@ -266,15 +268,16 @@
         )
 
     lower_first = lower_local(local_col(b1), pivot_inv[0], rows_first)
-    cols_sent = xor_bcast(jnp.stack([lower_first, local_col(b2)]), jnp.stack([c1, c2]), False)
-    rows_sent = xor_bcast(jnp.stack([local_row(a1), local_row(a2)]), jnp.stack([r1, r2]), True)
-    lower_first, second_col = cols_sent[0], cols_sent[1]
-    upper_first, second_row = rows_sent[0], rows_sent[1]
-
     cross = all_bcast(
         jnp.stack([masked(front[a1, b2], local[a1, b2]), masked(front[a2, b1], local[a2, b1])]),
         jnp.stack([r1 * ncol + c2, r2 * ncol + c1]),
     )
+    cols_sent, _ = xor_bcast(jnp.stack([lower_first, local_col(b2)]), jnp.stack([c1, c2]), False)
+    rows_sent, cross = xor_bcast(
+        jnp.stack([local_row(a1), local_row(a2)]), jnp.stack([r1, r2]), True, cross
+    )
+    lower_first, second_col = cols_sent[0], cols_sent[1]
+    upper_first, second_row = rows_sent[0], rows_sent[1]
     first_at_second, second_at_first = cross[0], cross[1]
 
     second_ok = (second != first)[None]

time: 157 us -> 176 us (1.12)
  waiting for transfers between devices: 43.8 us -> 60.4 us
  starting transfers between devices: 45 us -> 40.7 us
  other arithmetic: 23.1 us -> 27.3 us
    ppermute x10, waiting for transfers between devices: 2.87 us -> 28.6 us  [xor_bcast(): lax.ppermute(buf, axes, digit_pairs(nrow, ncol, on_row, step, m))]
    ppermute x7, waiting for transfers between devices: 28.6 us -> 23 us  [all_bcast(): lax.ppermute(value, ('row', 'col'), [(d, d ^ 1 << b) for d in range(n)])]
    another operation x9, other arithmetic: 2.08 us -> 6.17 us  [xor_bcast(): jnp.stack([pick(d, [got[dd ^ t] for dd in range(sizes[step])]) for t in r...]
    ppermute x10, waiting for transfers between devices: 12.3 us -> 8.8 us  [xor_bcast(): lax.ppermute(groups[m], axes, digit_pairs(nrow, ncol, on_row, step, m))]
    ppermute x7, starting transfers between devices: 10.7 us -> 7.24 us  [all_bcast(): lax.ppermute(value, ('row', 'col'), [(d, d ^ 1 << b) for d in range(n)])]
  transfers between devices with their start and end apart: 27 -> 27, of which waited for: 8 -> 12; matrix products, arithmetic and copies ran while one was open for 19% -> 19% of each run, Pallas kernels for 0% -> 0%
where the time goes in v11:
time: 176 us; the launch traced here: 174 us
  waiting for transfers between devices  60.4 us (34%)
  starting transfers between devices  40.7 us (23%)
  other arithmetic  27.3 us (16%)
  Pallas kernels  16.7 us (9%)
  local copies, waits for them, and re-layouts  11.7 us (7%)
  between operations  11.2 us (6%)
  matrix products  6.01 us (3%)
    ppermute x10, waiting for transfers between devices, xor_bcast(): lax.ppermute(buf, axes, digit_pairs(nrow, ncol, on_row, step, m))  28.6 us
    ppermute x7, waiting for transfers between devices, all_bcast(): lax.ppermute(value, ('row', 'col'), [(d, d ^ 1 << b) for d in range(n)])  23 us
    ppermute x10, starting transfers between devices, xor_bcast(): lax.ppermute(groups[m], axes, digit_pairs(nrow, ncol, on_row, step, m))  18.5 us
    pallas_call x1, Pallas kernels, both_updates(): pl.pallas_call(update_kernel, grid_spec=pltpu.PrefetchScalarGridSpec(num_...  16.7 us
    ppermute x10, starting transfers between devices, xor_bcast(): lax.ppermute(buf, axes, digit_pairs(nrow, ncol, on_row, step, m))  15 us
    ppermute x10, waiting for transfers between devices, xor_bcast(): lax.ppermute(groups[m], axes, digit_pairs(nrow, ncol, on_row, step, m))  8.8 us
    select_n x11, other arithmetic, per_part(): return jnp.where(cond.reshape((-1,) + (1,) * (a.ndim - 1)), a, b)  8.59 us
    ppermute x7, starting transfers between devices, all_bcast(): lax.ppermute(value, ('row', 'col'), [(d, d ^ 1 << b) for d in range(n)])  7.24 us
  transfers between devices with their start and end apart: 27, of which 12 were waited for; matrix products, arithmetic and copies ran while one was open for 19% of the time, Pallas kernels for 0%

profile of v11, /device:TPU:6, one launch (start us, length us, event | category | flops | bytes accessed | tf_op | source)
XLA Modules:
  0.0 174.1 jit_solution(7774664325261610806)
XLA Ops:
  14.7 2.1 %select_convert_fusion.1 = bf16[8,256,256]{2,1,0:T(8,128)(2,1)S(1)} fusion(bf16[8,12,256,256]{3,2,1,0:T(8,128)(2,1)} %front_ref.1, s32[]{:T(128)S(6)} %select_n.376, pred[8]{0:T(512)(128)(4,1)S(1)} %get-tuple-element.11, pred[8]{0:T(512)(128)(4,1)S(1)} %get-tuple-element.22, bf16[2,256,256]{2,1,0:T(8,128)(2,1)S(1)} %copy-done.8), kind=kOutput, calls=%fused_computation.19 | convolution fusion | flops 270008320 | bytes 2229252 | tf_op jit(solution)/shard_map/iab,bc->iac/dot_general | solution.py:179
  19.1 2.2 %dynamic-slice_select_fusion = (bf16[1,12,256,256]{3,2,1,0:T(8,128)(2,1)S(1)}, bf16[1,12,256,256]{3,2,1,0:T(8,128)(2,1)S(1)}) fusion(bf16[8,12,256,256]{3,2,1,0:T(8,128)(2,1)} %front_ref.1, s32[]{:T(128)S(6)} %select_n.415, pred[12]{0:T(512)(128)(4,1)S(1)} %get-tuple-element.9, s32[]{:T(128)S(6)} %select_n.411, pred[12]{0:T(512)(128)(4,1)S(1)} %get-tuple-element.10), kind=kLoop, calls=%fused_computation.22 | loop fusion | flops 1572864 | bytes 6291488 | tf_op jit(solution)/shard_map/jit(_where)/select_n | solution.py:231
  22.8 4.0 %collective-permute-start.10 = (bf16[2,4,192,256]{3,2,1,0:T(8,128)(2,1)}, bf16[2,4,192,256]{3,2,1,0:T(8,128)(2,1)}, u32[]{:S(2)}, u32[]{:S(2)}) collective-permute-start(bf16[2,4,192,256]{3,2,1,0:T(8,128)(2,1)} %get-tuple-element.34), channel_id=1, source_target_pairs={{0,96},{1,25},{2,98},{3,27},{4,100},{5,29},{6,102},{7,31},{8,104},... | collective-permute-start | bytes 2359304 | tf_op jit(solution)/shard_map/ppermute | solution.py:149
  36.1 1.7 %broadcast_select_fusion.1 = bf16[2,256,256]{1,2,0:T(8,128)(2,1)} fusion(bf16[2,256,256]{1,2,0:T(8,128)(2,1)} %collective-permute-done.14, pred[2]{0:T(512)(128)(4,1)S(1)} %get-tuple-element.62, bf16[1,256,256]{1,2,0:T(8,128)(2,1)S(1)} %get-tuple-element.77, bf16[1,256,256]{1,2,0:T(8,128)(2,1)S(1)} %get-tuple-element.78), kind=kLoop, calls=%fused_computation.69 | loop fusion | flops 262144 | bytes 786434 | tf_op jit(solution)/shard_map/jit(_where)/select_n | solution.py:13
  37.8 1.6 collective-permute-start.15
  40.9 3.9 %collective-permute-done.15 = bf16[2,256,256]{1,2,0:T(8,128)(2,1)} collective-permute-done((bf16[2,256,256]{1,2,0:T(8,128)(2,1)}, bf16[2,256,256]{1,2,0:T(8,128)(2,1)}, u32[]{:S(2)}, u32[]{:S(2)}) %collective-permute-start.15) | collective-permute-done | bytes 262176 | tf_op jit(solution)/shard_map/ppermute | solution.py:173
  44.7 1.8 %broadcast_select_fusion.2 = bf16[2,256,256]{1,2,0:T(8,128)(2,1)} fusion(bf16[2,256,256]{1,2,0:T(8,128)(2,1)} %collective-permute-done.15, pred[2]{0:T(512)(128)(4,1)S(1)} %get-tuple-element.58, bf16[2,256,256]{1,2,0:T(8,128)(2,1)} %collective-permute-done.14, bf16[1,256,256]{1,2,0:T(8,128)(2,1)S(1)} %get-tuple-element.77, ...), kind=kLoop, calls=%fused_computation.70 | loop fusion | flops 393216 | bytes 1048580 | tf_op jit(solution)/shard_map/jit(_where)/select_n | solution.py:13
  46.6 3.2 %collective-permute-start.16 = (bf16[2,256,256]{1,2,0:T(8,128)(2,1)}, bf16[2,256,256]{1,2,0:T(8,128)(2,1)S(1)}, u32[]{:S(2)}, u32[]{:S(2)}) collective-permute-start(bf16[2,256,256]{1,2,0:T(8,128)(2,1)} %broadcast_select_fusion.2), channel_id=1, source_target_pairs={{0,4},{1,5},{2,6},{3,7},{4,0},{5,1},{6,2},{7,3},{8,12},{9,13},{10,... | collective-permute-start | bytes 786440 | tf_op jit(solution)/shard_map/ppermute | solution.py:173
  49.8 4.8 %collective-permute-done.16 = bf16[2,256,256]{1,2,0:T(8,128)(2,1)S(1)} collective-permute-done((bf16[2,256,256]{1,2,0:T(8,128)(2,1)}, bf16[2,256,256]{1,2,0:T(8,128)(2,1)S(1)}, u32[]{:S(2)}, u32[]{:S(2)}) %collective-permute-start.16) | collective-permute-done | bytes 262176 | tf_op jit(solution)/shard_map/ppermute | solution.py:173
  56.5 8.4 %collective-permute-done.17 = bf16[2,256,256]{1,2,0:T(8,128)(2,1)S(1)} collective-permute-done((bf16[2,256,256]{1,2,0:T(8,128)(2,1)S(1)}, bf16[2,256,256]{1,2,0:T(8,128)(2,1)S(1)}, u32[]{:S(2)}, u32[]{:S(2)}) %collective-permute-start.17) | collective-permute-done | bytes 262176 | tf_op jit(solution)/shard_map/ppermute | solution.py:173
  65.1 1.6 fusion.12
  66.8 3.1 %collective-permute-start.3 = (bf16[2,256,256]{2,1,0:T(8,128)(2,1)S(1)}, bf16[2,256,256]{2,1,0:T(8,128)(2,1)S(1)}, u32[]{:S(2)}, u32[]{:S(2)}) collective-permute-start(bf16[2,256,256]{2,1,0:T(8,128)(2,1)S(1)} %get-tuple-element.45), channel_id=1, source_target_pairs={{0,6},{1,7},{2,4},{3,5},{4,2},{5,3},{6,0},{7,1},{8,14},{9,15},{10,... | collective-permute-start | bytes 786440 | tf_op jit(solution)/shard_map/ppermute | solution.py:149
  70.0 1.6 collective-permute-start.2
  71.5 1.8 %fusion.22 = bf16[2,4,192,256]{3,2,1,0:T(8,128)(2,1)S(1)} fusion(bf16[1,4,4,192,256]{4,3,2,0,1:T(8,128)(2,1)S(1)} %bitcast.197, bf16[1,4,4,192,256]{4,3,2,0,1:T(8,128)(2,1)S(1)} %bitcast.195, bf16[2,4,192,256]{3,2,1,0:T(8,128)(2,1)} %collective-permute-done.8, bf16[2,4,192,256]{3,2,1,0:T(8,128)(2,1)} %collective-permute-done.9, ...), kind=kLoop, calls=%fused_computation.48 | loop fusion | flops 1572864 | bytes 6291462 | tf_op jit(solution)/shard_map/jit(_where)/select_n | solution.py:13
  75.0 3.0 %collective-permute-done.1 = bf16[2,256,256]{2,1,0:T(8,128)(2,1)S(1)} collective-permute-done((bf16[2,256,256]{2,1,0:T(8,128)(2,1)S(1)}, bf16[2,256,256]{2,1,0:T(8,128)(2,1)S(1)}, u32[]{:S(2)}, u32[]{:S(2)}) %collective-permute-start.1) | collective-permute-done | bytes 262176 | tf_op jit(solution)/shard_map/ppermute | solution.py:149
  78.1 2.7 %collective-permute-done.2 = bf16[2,256,256]{2,1,0:T(8,128)(2,1)S(1)} collective-permute-done((bf16[2,256,256]{2,1,0:T(8,128)(2,1)S(1)}, bf16[2,256,256]{2,1,0:T(8,128)(2,1)S(1)}, u32[]{:S(2)}, u32[]{:S(2)}) %collective-permute-start.2) | collective-permute-done | bytes 262176 | tf_op jit(solution)/shard_map/ppermute | solution.py:149
  80.9 5.7 %collective-permute-start.6 = (bf16[2,256,256]{2,1,0:T(8,128)(2,1)S(1)}, bf16[2,256,256]{2,1,0:T(8,128)(2,1)S(1)}, u32[]{:S(2)}, u32[]{:S(2)}) collective-permute-start(bf16[2,256,256]{2,1,0:T(8,128)(2,1)S(1)} %fusion.27), channel_id=1, source_target_pairs={{0,6},{1,7},{2,4},{3,5},{4,2},{5,3},{6,0},{7,1},{8,14},{9,15},{10,... | collective-permute-start | bytes 786440 | tf_op jit(solution)/shard_map/ppermute | solution.py:158
  87.5 3.2 %collective-permute-start.13 = (bf16[2,192,256]{2,1,0:T(8,128)(2,1)S(1)}, bf16[2,192,256]{2,1,0:T(8,128)(2,1)S(1)}, u32[]{:S(2)}, u32[]{:S(2)}) collective-permute-start(bf16[2,192,256]{2,1,0:T(8,128)(2,1)S(1)} %get-tuple-element.52), channel_id=1, source_target_pairs={{0,24},{1,97},{2,26},{3,99},{4,28},{5,101},{6,30},{7,103},{8,16},{... | collective-permute-start | bytes 589832 | tf_op jit(solution)/shard_map/ppermute | solution.py:149
  91.5 1.7 collective-permute-done.6
  93.3 3.8 %collective-permute-start.12 = (bf16[2,192,256]{2,1,0:T(8,128)(2,1)S(1)}, bf16[2,192,256]{2,1,0:T(8,128)(2,1)S(1)}, u32[]{:S(2)}, u32[]{:S(2)}) collective-permute-start(bf16[2,192,256]{2,1,0:T(8,128)(2,1)S(1)} %get-tuple-element.54), channel_id=1, source_target_pairs={{0,16},{1,65},{2,18},{3,67},{4,20},{5,69},{6,22},{7,71},{8,24},{9,... | collective-permute-start | bytes 589832 | tf_op jit(solution)/shard_map/ppermute | solution.py:149
  98.3 2.5 %collective-permute-done.12 = bf16[2,192,256]{2,1,0:T(8,128)(2,1)S(1)} collective-permute-done((bf16[2,192,256]{2,1,0:T(8,128)(2,1)S(1)}, bf16[2,192,256]{2,1,0:T(8,128)(2,1)S(1)}, u32[]{:S(2)}, u32[]{:S(2)}) %collective-permute-start.12) | collective-permute-done | bytes 196640 | tf_op jit(solution)/shard_map/ppermute | solution.py:149
  100.8 5.9 %collective-permute-done.20 = bf16[2,256,256]{1,2,0:T(8,128)(2,1)S(1)} collective-permute-done((bf16[2,256,256]{1,2,0:T(8,128)(2,1)S(1)}, bf16[2,256,256]{1,2,0:T(8,128)(2,1)S(1)}, u32[]{:S(2)}, u32[]{:S(2)}) %collective-permute-start.20) | collective-permute-done | bytes 262176 | tf_op jit(solution)/shard_map/ppermute | solution.py:173
  107.3 2.2 %collective-permute-start.22 = (bf16[2,192,256]{2,1,0:T(8,128)(2,1)S(1)}, bf16[2,192,256]{2,1,0:T(8,128)(2,1)S(1)}, u32[]{:S(2)}, u32[]{:S(2)}) collective-permute-start(bf16[2,192,256]{2,1,0:T(8,128)(2,1)S(1)} %fusion.28), channel_id=1, source_target_pairs={{0,16},{1,65},{2,18},{3,67},{4,20},{5,69},{6,22},{7,71},{8,24},{9,... | collective-permute-start | bytes 589832 | tf_op jit(solution)/shard_map/ppermute | solution.py:158
  109.5 1.5 collective-permute-start.21
  111.3 14.4 %collective-permute-done.23 = bf16[2,192,256]{2,1,0:T(8,128)(2,1)S(1)} collective-permute-done((bf16[2,192,256]{2,1,0:T(8,128)(2,1)S(1)}, bf16[2,192,256]{2,1,0:T(8,128)(2,1)S(1)}, u32[]{:S(2)}, u32[]{:S(2)}) %collective-permute-start.23) | collective-permute-done | bytes 196640 | tf_op jit(solution)/shard_map/ppermute | solution.py:158
  126.8 4.1 %collective-permute-start.24 = (bf16[2,4,192,256]{3,2,1,0:T(8,128)(2,1)}, bf16[2,4,192,256]{3,2,1,0:T(8,128)(2,1)}, u32[]{:S(2)}, u32[]{:S(2)}) collective-permute-start(bf16[2,4,192,256]{3,2,1,0:T(8,128)(2,1)} %pad_maximum_fusion.5), channel_id=1, source_target_pairs={{0,32},{1,9},{2,34},{3,11},{4,36},{5,13},{6,38},{7,15},{8,40},{9,1... | collective-permute-start | bytes 2359304 | tf_op jit(solution)/shard_map/ppermute | solution.py:158
  134.0 3.1 %select_convert_fusion.l2_ref = bf16[8,256,256]{2,1,0:T(8,128)(2,1)} fusion(pred[8]{0:T(512)(128)(4,1)S(1)} %get-tuple-element.69, bf16[8,1,256,256]{2,3,0,1:T(8,128)(2,1)} %bitcast.205, bf16[8,1,256,256]{2,3,0,1:T(8,128)(2,1)S(1)} %bitcast.204, bf16[8,256,256]{2,1,0:T(8,128)(2,1)S(1)} %bitcast.198, pred[8]{0:T(512)(128)(4,1)S(1)} %get-tuple-element.68, ...), kind=kOutput, calls=%fused_computation.18 | convolution fusion | flops 540540928 | bytes 4457984 | tf_op jit(solution)/shard_map/iab,bc->iac/dot_general | solution.py:179
  137.1 11.6 %collective-permute-done.26 = bf16[2,4,192,256]{3,2,1,0:T(8,128)(2,1)} collective-permute-done((bf16[2,4,192,256]{3,2,1,0:T(8,128)(2,1)}, bf16[2,4,192,256]{3,2,1,0:T(8,128)(2,1)}, u32[]{:S(2)}, u32[]{:S(2)}) %collective-permute-start.26) | collective-permute-done | bytes 786464 | tf_op jit(solution)/shard_map/ppermute | solution.py:158
  149.6 1.8 %select_bitcast_fusion.4 = bf16[2,1,4,192,256]{4,3,2,1,0:T(8,128)(2,1)S(1)} fusion(bf16[2,4,192,256]{3,2,1,0:T(8,128)(2,1)} %collective-permute-done.24, bf16[2,4,192,256]{3,2,1,0:T(8,128)(2,1)} %collective-permute-done.26, bf16[2,4,192,256]{3,2,1,0:T(8,128)(2,1)} %collective-permute-done.25, pred[2]{0:T(512)(128)(4,1)S(1)} %get-tuple-element.64, ...), kind=kLoop, calls=%fused_computation.56 | loop fusion | flops 2359296 | bytes 3932166 | tf_op jit(solution)/shard_map/stack | solution.py:161
  151.5 2.0 %select_bitcast_fusion.5 = (bf16[2,1,4,192,256]{4,3,2,1,0:T(8,128)(2,1)S(1)}, bf16[2,1,4,192,256]{4,3,2,1,0:T(8,128)(2,1)S(1)}, bf16[2,1,4,192,256]{4,3,2,1,0:T(8,128)(2,1)S(1)}) fusion(bf16[2,4,192,256]{3,2,1,0:T(8,128)(2,1)} %collective-permute-done.24, bf16[2,4,192,256]{3,2,1,0:T(8,128)(2,1)} %collective-permute-done.25, ...), kind=kLoop, calls=%fused_computation.57 | loop fusion | flops 4718592 | bytes 5505030 | tf_op jit(solution)/shard_map/stack | solution.py:161
  155.4 2.0 %fusion.4.u2_ref = bf16[12,256,256]{2,1,0:T(8,128)(2,1)} fusion(bf16[1,12,256,256]{3,2,1,0:T(8,128)(2,1)S(1)} %bitcast.200, f32[12,256,256]{1,2,0:T(8,128)S(1)} %fusion.29, pred[12]{0:T(512)(128)(4,1)S(1)} %get-tuple-element.15, pred[12]{0:T(512)(128)(4,1)S(1)} %get-tuple-element.13, bf16[256,256]{1,0:T(8,128)(2,1)S(1)} %fusion.8), kind=kLoop, calls=%fused_computation.21 | loop fusion | flops 3932160 | bytes 6422552 | tf_op jit(solution)/shard_map/squeeze | solution.py:295
  157.3 16.7 %shard_map.46 = bf16[8,12,256,256]{3,2,1,0:T(8,128)(2,1)} custom-call(s32[8,12]{1,0:T(8,128)} %select_add_fusion.codes, bf16[8,12,256,256]{3,2,1,0:T(8,128)(2,1)} %front_ref.1, bf16[8,256,256]{2,1,0:T(8,128)(2,1)} %bitcast.199, bf16[8,256,256]{2,1,0:T(8,128)(2,1)} %select_convert_fusion.l2_ref, bf16[12,256,256]{2,1,0:T(8,128)(2,1)} %bitcast.193, ...), custom_call_target="tpu_custom_call" | custom-call | tf_op jit(solution)/shard_map/pallas_call | solution.py:216
  (109 shorter events, 33.2 us)
Async XLA Ops:
  8.3 10.2 %copy-start.7 = (s32[8,16,12,8]{1,0,3,2:T(8,128)}, s32[8,16,12,8]{1,0,3,2:T(8,128)S(1)}, u32[]{:S(2)}) copy-start(s32[8,16,12,8]{1,0,3,2:T(8,128)S(1)} %reshape.615) | copy-start | bytes 147460
  11.1 25.0 %collective-permute-start.14 = (bf16[2,256,256]{1,2,0:T(8,128)(2,1)}, bf16[2,256,256]{1,2,0:T(8,128)(2,1)}, u32[]{:S(2)}, u32[]{:S(2)}) collective-permute-start(bf16[2,256,256]{1,2,0:T(8,128)(2,1)} %pad_maximum_fusion.6), channel_id=1, source_target_pairs={{0,1},{1,0},{2,3},{3,2},{4,5},{5,4},{6,7},{7,6},{8,9},{9,8},{10,11... | collective-permute-start | bytes 786440 | tf_op jit(solution)/shard_map/ppermute | solution.py:173
  14.7 3.3 %copy-start.1 = (bf16[1,2,4,256,256]{4,3,2,1,0:T(8,128)(2,1)}, bf16[1,2,4,256,256]{4,3,2,1,0:T(8,128)(2,1)S(1)}, u32[]{:S(2)}) copy-start(bf16[1,2,4,256,256]{4,3,2,1,0:T(8,128)(2,1)S(1)} %broadcast_select_fusion) | copy-start | bytes 3145732
  18.0 47.1 %collective-permute-start = (bf16[2,4,256,256]{3,2,1,0:T(8,128)(2,1)}, bf16[2,4,256,256]{3,2,1,0:T(8,128)(2,1)}, u32[]{:S(2)}, u32[]{:S(2)}) collective-permute-start(bf16[2,4,256,256]{3,2,1,0:T(8,128)(2,1)} %fusion.13), channel_id=1, source_target_pairs={{0,1},{1,0},{2,3},{3,2},{4,5},{5,4},{6,7},{7,6},{8,9},{9,8},{10,11... | collective-permute-start | bytes 3145736 | tf_op jit(solution)/shard_map/ppermute | solution.py:149
  21.3 11.4 %copy-start.4 = (s32[128,96]{0,1:T(8,128)S(1)}, s32[128,96]{0,1:T(8,128)}, u32[]{:S(2)}) copy-start(s32[128,96]{0,1:T(8,128)} %param.5) | copy-start | bytes 147460
  22.8 47.0 %collective-permute-start.10 = (bf16[2,4,192,256]{3,2,1,0:T(8,128)(2,1)}, bf16[2,4,192,256]{3,2,1,0:T(8,128)(2,1)}, u32[]{:S(2)}, u32[]{:S(2)}) collective-permute-start(bf16[2,4,192,256]{3,2,1,0:T(8,128)(2,1)} %get-tuple-element.34), channel_id=1, source_target_pairs={{0,96},{1,25},{2,98},{3,27},{4,100},{5,29},{6,102},{7,31},{8,104},... | collective-permute-start | bytes 2359304 | tf_op jit(solution)/shard_map/ppermute | solution.py:149
  26.8 43.2 %collective-permute-start.8 = (bf16[2,4,192,256]{3,2,1,0:T(8,128)(2,1)}, bf16[2,4,192,256]{3,2,1,0:T(8,128)(2,1)}, u32[]{:S(2)}, u32[]{:S(2)}) collective-permute-start(bf16[2,4,192,256]{3,2,1,0:T(8,128)(2,1)} %get-tuple-element.35), channel_id=1, source_target_pairs={{0,32},{1,9},{2,34},{3,11},{4,36},{5,13},{6,38},{7,15},{8,40},{9,1... | collective-permute-start | bytes 2359304 | tf_op jit(solution)/shard_map/ppermute | solution.py:149
  26.8 44.7 %collective-permute-start.9 = (bf16[2,4,192,256]{3,2,1,0:T(8,128)(2,1)}, bf16[2,4,192,256]{3,2,1,0:T(8,128)(2,1)}, u32[]{:S(2)}, u32[]{:S(2)}) collective-permute-start(bf16[2,4,192,256]{3,2,1,0:T(8,128)(2,1)} %get-tuple-element.36), channel_id=1, source_target_pairs={{0,64},{1,17},{2,66},{3,19},{4,68},{5,21},{6,70},{7,23},{8,72},{9,... | collective-permute-start | bytes 2359304 | tf_op jit(solution)/shard_map/ppermute | solution.py:149
  37.8 6.9 %collective-permute-start.15 = (bf16[2,256,256]{1,2,0:T(8,128)(2,1)}, bf16[2,256,256]{1,2,0:T(8,128)(2,1)}, u32[]{:S(2)}, u32[]{:S(2)}) collective-permute-start(bf16[2,256,256]{1,2,0:T(8,128)(2,1)} %broadcast_select_fusion.1), channel_id=1, source_target_pairs={{0,2},{1,3},{2,0},{3,1},{4,6},{5,7},{6,4},{7,5},{8,10},{9,11},{10,... | collective-permute-start | bytes 786440 | tf_op jit(solution)/shard_map/ppermute | solution.py:173
  46.6 8.1 %collective-permute-start.16 = (bf16[2,256,256]{1,2,0:T(8,128)(2,1)}, bf16[2,256,256]{1,2,0:T(8,128)(2,1)S(1)}, u32[]{:S(2)}, u32[]{:S(2)}) collective-permute-start(bf16[2,256,256]{1,2,0:T(8,128)(2,1)} %broadcast_select_fusion.2), channel_id=1, source_target_pairs={{0,4},{1,5},{2,6},{3,7},{4,0},{5,1},{6,2},{7,3},{8,12},{9,13},{10,... | collective-permute-start | bytes 786440 | tf_op jit(solution)/shard_map/ppermute | solution.py:173
  49.8 15.3 %copy-start.2 = (bf16[1,2,4,256,256]{4,3,2,1,0:T(8,128)(2,1)S(1)}, bf16[1,2,4,256,256]{4,3,2,1,0:T(8,128)(2,1)}, u32[]{:S(2)}) copy-start(bf16[1,2,4,256,256]{4,3,2,1,0:T(8,128)(2,1)} %copy-done.1) | copy-start | bytes 3145732
  55.7 9.2 %collective-permute-start.17 = (bf16[2,256,256]{1,2,0:T(8,128)(2,1)S(1)}, bf16[2,256,256]{1,2,0:T(8,128)(2,1)S(1)}, u32[]{:S(2)}, u32[]{:S(2)}) collective-permute-start(bf16[2,256,256]{1,2,0:T(8,128)(2,1)S(1)} %broadcast_select_fusion.3), channel_id=1, source_target_pairs={{0,8},{1,9},{2,10},{3,11},{4,12},{5,13},{6,14},{7,15},{8,0},{9,1},... | collective-permute-start | bytes 786440 | tf_op jit(solution)/shard_map/ppermute | solution.py:173
  65.0 8.3 %collective-permute-start.18 = (bf16[2,256,256]{1,2,0:T(8,128)(2,1)S(1)}, bf16[2,256,256]{1,2,0:T(8,128)(2,1)S(1)}, u32[]{:S(2)}, u32[]{:S(2)}) collective-permute-start(bf16[2,256,256]{1,2,0:T(8,128)(2,1)S(1)} %broadcast_select_fusion.4), channel_id=1, source_target_pairs={{0,16},{1,17},{2,18},{3,19},{4,20},{5,21},{6,22},{7,23},{8,24},{9,... | collective-permute-start | bytes 786440 | tf_op jit(solution)/shard_map/ppermute | solution.py:173
  66.8 8.3 %collective-permute-start.3 = (bf16[2,256,256]{2,1,0:T(8,128)(2,1)S(1)}, bf16[2,256,256]{2,1,0:T(8,128)(2,1)S(1)}, u32[]{:S(2)}, u32[]{:S(2)}) collective-permute-start(bf16[2,256,256]{2,1,0:T(8,128)(2,1)S(1)} %get-tuple-element.45), channel_id=1, source_target_pairs={{0,6},{1,7},{2,4},{3,5},{4,2},{5,3},{6,0},{7,1},{8,14},{9,15},{10,... | collective-permute-start | bytes 786440 | tf_op jit(solution)/shard_map/ppermute | solution.py:149
  69.8 8.2 %collective-permute-start.1 = (bf16[2,256,256]{2,1,0:T(8,128)(2,1)S(1)}, bf16[2,256,256]{2,1,0:T(8,128)(2,1)S(1)}, u32[]{:S(2)}, u32[]{:S(2)}) collective-permute-start(bf16[2,256,256]{2,1,0:T(8,128)(2,1)S(1)} %get-tuple-element.46), channel_id=1, source_target_pairs={{0,2},{1,3},{2,0},{3,1},{4,6},{5,7},{6,4},{7,5},{8,10},{9,11},{10,... | collective-permute-start | bytes 786440 | tf_op jit(solution)/shard_map/ppermute | solution.py:149
  70.0 10.8 %collective-permute-start.2 = (bf16[2,256,256]{2,1,0:T(8,128)(2,1)S(1)}, bf16[2,256,256]{2,1,0:T(8,128)(2,1)S(1)}, u32[]{:S(2)}, u32[]{:S(2)}) collective-permute-start(bf16[2,256,256]{2,1,0:T(8,128)(2,1)S(1)} %get-tuple-element.47), channel_id=1, source_target_pairs={{0,4},{1,5},{2,6},{3,7},{4,0},{5,1},{6,2},{7,3},{8,12},{9,13},{10,... | collective-permute-start | bytes 786440 | tf_op jit(solution)/shard_map/ppermute | solution.py:149
  73.5 17.2 %collective-permute-start.19 = (bf16[2,256,256]{1,2,0:T(8,128)(2,1)S(1)}, bf16[2,256,256]{1,2,0:T(8,128)(2,1)S(1)}, u32[]{:S(2)}, u32[]{:S(2)}) collective-permute-start(bf16[2,256,256]{1,2,0:T(8,128)(2,1)S(1)} %broadcast_select_fusion.5), channel_id=1, source_target_pairs={{0,32},{1,33},{2,34},{3,35},{4,36},{5,37},{6,38},{7,39},{8,40},{9,... | collective-permute-start | bytes 786440 | tf_op jit(solution)/shard_map/ppermute | solution.py:173
  80.9 12.4 %collective-permute-start.6 = (bf16[2,256,256]{2,1,0:T(8,128)(2,1)S(1)}, bf16[2,256,256]{2,1,0:T(8,128)(2,1)S(1)}, u32[]{:S(2)}, u32[]{:S(2)}) collective-permute-start(bf16[2,256,256]{2,1,0:T(8,128)(2,1)S(1)} %fusion.27), channel_id=1, source_target_pairs={{0,6},{1,7},{2,4},{3,5},{4,2},{5,3},{6,0},{7,1},{8,14},{9,15},{10,... | collective-permute-start | bytes 786440 | tf_op jit(solution)/shard_map/ppermute | solution.py:158
  86.6 10.5 %collective-permute-start.5 = (bf16[2,256,256]{2,1,0:T(8,128)(2,1)S(1)}, bf16[2,256,256]{2,1,0:T(8,128)(2,1)S(1)}, u32[]{:S(2)}, u32[]{:S(2)}) collective-permute-start(bf16[2,256,256]{2,1,0:T(8,128)(2,1)S(1)} %fusion.27), channel_id=1, source_target_pairs={{0,4},{1,5},{2,6},{3,7},{4,0},{5,1},{6,2},{7,3},{8,12},{9,13},{10,... | collective-permute-start | bytes 786440 | tf_op jit(solution)/shard_map/ppermute | solution.py:158
  86.6 11.2 %collective-permute-start.4 = (bf16[2,256,256]{2,1,0:T(8,128)(2,1)S(1)}, bf16[2,256,256]{2,1,0:T(8,128)(2,1)S(1)}, u32[]{:S(2)}, u32[]{:S(2)}) collective-permute-start(bf16[2,256,256]{2,1,0:T(8,128)(2,1)S(1)} %fusion.27), channel_id=1, source_target_pairs={{0,2},{1,3},{2,0},{3,1},{4,6},{5,7},{6,4},{7,5},{8,10},{9,11},{10,... | collective-permute-start | bytes 786440 | tf_op jit(solution)/shard_map/ppermute | solution.py:158
  87.5 10.7 %collective-permute-start.13 = (bf16[2,192,256]{2,1,0:T(8,128)(2,1)S(1)}, bf16[2,192,256]{2,1,0:T(8,128)(2,1)S(1)}, u32[]{:S(2)}, u32[]{:S(2)}) collective-permute-start(bf16[2,192,256]{2,1,0:T(8,128)(2,1)S(1)} %get-tuple-element.52), channel_id=1, source_target_pairs={{0,24},{1,97},{2,26},{3,99},{4,28},{5,101},{6,30},{7,103},{8,16},{... | collective-permute-start | bytes 589832 | tf_op jit(solution)/shard_map/ppermute | solution.py:149
  90.7 7.5 %collective-permute-start.11 = (bf16[2,192,256]{2,1,0:T(8,128)(2,1)S(1)}, bf16[2,192,256]{2,1,0:T(8,128)(2,1)S(1)}, u32[]{:S(2)}, u32[]{:S(2)}) collective-permute-start(bf16[2,192,256]{2,1,0:T(8,128)(2,1)S(1)} %get-tuple-element.53), channel_id=1, source_target_pairs={{0,8},{1,33},{2,10},{3,35},{4,12},{5,37},{6,14},{7,39},{8,0},{9,41... | collective-permute-start | bytes 589832 | tf_op jit(solution)/shard_map/ppermute | solution.py:149
  93.3 7.5 %collective-permute-start.12 = (bf16[2,192,256]{2,1,0:T(8,128)(2,1)S(1)}, bf16[2,192,256]{2,1,0:T(8,128)(2,1)S(1)}, u32[]{:S(2)}, u32[]{:S(2)}) collective-permute-start(bf16[2,192,256]{2,1,0:T(8,128)(2,1)S(1)} %get-tuple-element.54), channel_id=1, source_target_pairs={{0,16},{1,65},{2,18},{3,67},{4,20},{5,69},{6,22},{7,71},{8,24},{9,... | collective-permute-start | bytes 589832 | tf_op jit(solution)/shard_map/ppermute | solution.py:149
  97.1 9.7 %collective-permute-start.20 = (bf16[2,256,256]{1,2,0:T(8,128)(2,1)S(1)}, bf16[2,256,256]{1,2,0:T(8,128)(2,1)S(1)}, u32[]{:S(2)}, u32[]{:S(2)}) collective-permute-start(bf16[2,256,256]{1,2,0:T(8,128)(2,1)S(1)} %broadcast_select_fusion.6), channel_id=1, source_target_pairs={{0,64},{1,65},{2,66},{3,67},{4,68},{5,69},{6,70},{7,71},{8,72},{9,... | collective-permute-start | bytes 786440 | tf_op jit(solution)/shard_map/ppermute | solution.py:173
  98.0 13.0 %copy-start.9 = (bf16[2,256,256]{2,1,0:T(8,128)(2,1)S(1)}, bf16[2,256,256]{2,1,0:T(8,128)(2,1)}, u32[]{:S(2)}) copy-start(bf16[2,256,256]{2,1,0:T(8,128)(2,1)} %param.7) | copy-start | bytes 786436
  98.2 32.7 %collective-permute-start.7 = (bf16[2,4,256,256]{3,2,0,1:T(8,128)(2,1)S(1)}, bf16[2,4,256,256]{3,2,0,1:T(8,128)(2,1)S(1)}, u32[]{:S(2)}, u32[]{:S(2)}) collective-permute-start(bf16[2,4,256,256]{3,2,0,1:T(8,128)(2,1)S(1)} %pad_maximum_fusion.3), channel_id=1, source_target_pairs={{0,1},{1,0},{2,3},{3,2},{4,5},{5,4},{6,7},{7,6},{8,9},{9,8},{10,11... | collective-permute-start | bytes 3145736 | tf_op jit(solution)/shard_map/ppermute | solution.py:158
  106.9 18.8 %collective-permute-start.23 = (bf16[2,192,256]{2,1,0:T(8,128)(2,1)S(1)}, bf16[2,192,256]{2,1,0:T(8,128)(2,1)S(1)}, u32[]{:S(2)}, u32[]{:S(2)}) collective-permute-start(bf16[2,192,256]{2,1,0:T(8,128)(2,1)S(1)} %fusion.28), channel_id=1, source_target_pairs={{0,24},{1,97},{2,26},{3,99},{4,28},{5,101},{6,30},{7,103},{8,16},{... | collective-permute-start | bytes 589832 | tf_op jit(solution)/shard_map/ppermute | solution.py:158
  107.3 18.3 %collective-permute-start.22 = (bf16[2,192,256]{2,1,0:T(8,128)(2,1)S(1)}, bf16[2,192,256]{2,1,0:T(8,128)(2,1)S(1)}, u32[]{:S(2)}, u32[]{:S(2)}) collective-permute-start(bf16[2,192,256]{2,1,0:T(8,128)(2,1)S(1)} %fusion.28), channel_id=1, source_target_pairs={{0,16},{1,65},{2,18},{3,67},{4,20},{5,69},{6,22},{7,71},{8,24},{9,... | collective-permute-start | bytes 589832 | tf_op jit(solution)/shard_map/ppermute | solution.py:158
  109.5 16.1 %collective-permute-start.21 = (bf16[2,192,256]{2,1,0:T(8,128)(2,1)S(1)}, bf16[2,192,256]{2,1,0:T(8,128)(2,1)S(1)}, u32[]{:S(2)}, u32[]{:S(2)}) collective-permute-start(bf16[2,192,256]{2,1,0:T(8,128)(2,1)S(1)} %fusion.28), channel_id=1, source_target_pairs={{0,8},{1,33},{2,10},{3,35},{4,12},{5,37},{6,14},{7,39},{8,0},{9,41... | collective-permute-start | bytes 589832 | tf_op jit(solution)/shard_map/ppermute | solution.py:158
  126.8 21.9 %collective-permute-start.26 = (bf16[2,4,192,256]{3,2,1,0:T(8,128)(2,1)}, bf16[2,4,192,256]{3,2,1,0:T(8,128)(2,1)}, u32[]{:S(2)}, u32[]{:S(2)}) collective-permute-start(bf16[2,4,192,256]{3,2,1,0:T(8,128)(2,1)} %pad_maximum_fusion.5), channel_id=1, source_target_pairs={{0,96},{1,25},{2,98},{3,27},{4,100},{5,29},{6,102},{7,31},{8,104},... | collective-permute-start | bytes 2359304 | tf_op jit(solution)/shard_map/ppermute | solution.py:158
  126.8 21.9 %collective-permute-start.25 = (bf16[2,4,192,256]{3,2,1,0:T(8,128)(2,1)}, bf16[2,4,192,256]{3,2,1,0:T(8,128)(2,1)}, u32[]{:S(2)}, u32[]{:S(2)}) collective-permute-start(bf16[2,4,192,256]{3,2,1,0:T(8,128)(2,1)} %pad_maximum_fusion.5), channel_id=1, source_target_pairs={{0,64},{1,17},{2,66},{3,19},{4,68},{5,21},{6,70},{7,23},{8,72},{9,... | collective-permute-start | bytes 2359304 | tf_op jit(solution)/shard_map/ppermute | solution.py:158
  126.8 22.8 %collective-permute-start.24 = (bf16[2,4,192,256]{3,2,1,0:T(8,128)(2,1)}, bf16[2,4,192,256]{3,2,1,0:T(8,128)(2,1)}, u32[]{:S(2)}, u32[]{:S(2)}) collective-permute-start(bf16[2,4,192,256]{3,2,1,0:T(8,128)(2,1)} %pad_maximum_fusion.5), channel_id=1, source_target_pairs={{0,32},{1,9},{2,34},{3,11},{4,36},{5,13},{6,38},{7,15},{8,40},{9,1... | collective-permute-start | bytes 2359304 | tf_op jit(solution)/shard_map/ppermute | solution.py:158
  (5 other events, 9.7 us)

commit v12 on v8

--- a/solution.py
+++ b/solution.py
@@ -265,10 +265,10 @@
             lax.dynamic_index_in_dim(local, b, 1, keepdims=False),
         )
 
-    lower_first = lower_local(local_col(b1), pivot_inv[0], rows_first)
-    cols_sent = xor_bcast(jnp.stack([lower_first, local_col(b2)]), jnp.stack([c1, c2]), False)
+    cols_sent = xor_bcast(jnp.stack([local_col(b1), local_col(b2)]), jnp.stack([c1, c2]), False)
     rows_sent = xor_bcast(jnp.stack([local_row(a1), local_row(a2)]), jnp.stack([r1, r2]), True)
-    lower_first, second_col = cols_sent[0], cols_sent[1]
+    lower_first = lower_local(cols_sent[0], pivot_inv[0], rows_first)
+    second_col = cols_sent[1]
     upper_first, second_row = rows_sent[0], rows_sent[1]
 
     cross = all_bcast(

time: 157 us -> 154 us (0.981)
  matrix products: 5.71 us -> 3.09 us
    dot_general x3, matrix products: 5.13 us -> 2.51 us  [lower_local(): jnp.einsum('iab,bc->iac', column, inverse, preferred_element_type=jnp.flo...]
  transfers between devices with their start and end apart: 27 -> 27, of which waited for: 8 -> 8; matrix products, arithmetic and copies ran while one was open for 19% -> 18% of each run, Pallas kernels for 0% -> 0%
where the time goes in v12:
time: 154 us; the launch traced here: 153 us
  starting transfers between devices  44.8 us (29%)
  waiting for transfers between devices  43.9 us (29%)
  other arithmetic  23.3 us (15%)
  Pallas kernels  16.7 us (11%)
  between operations  11.6 us (8%)
  local copies, waits for them, and re-layouts  9.49 us (6%)
  matrix products  3.09 us (2%)
    ppermute x7, waiting for transfers between devices, all_bcast(): lax.ppermute(value, ('row', 'col'), [(d, d ^ 1 << b) for d in range(n)])  28.6 us
    ppermute x10, starting transfers between devices, xor_bcast(): lax.ppermute(groups[m], axes, digit_pairs(nrow, ncol, on_row, step, m))  18.4 us
    pallas_call x1, Pallas kernels, both_updates(): pl.pallas_call(update_kernel, grid_spec=pltpu.PrefetchScalarGridSpec(num_...  16.7 us
    ppermute x10, starting transfers between devices, xor_bcast(): lax.ppermute(buf, axes, digit_pairs(nrow, ncol, on_row, step, m))  15.8 us
    ppermute x10, waiting for transfers between devices, xor_bcast(): lax.ppermute(groups[m], axes, digit_pairs(nrow, ncol, on_row, step, m))  12.4 us
    ppermute x7, starting transfers between devices, all_bcast(): lax.ppermute(value, ('row', 'col'), [(d, d ^ 1 << b) for d in range(n)])  10.6 us
    select_n x11, other arithmetic, per_part(): return jnp.where(cond.reshape((-1,) + (1,) * (a.ndim - 1)), a, b)  8.52 us
  transfers between devices with their start and end apart: 27, of which 8 were waited for; matrix products, arithmetic and copies ran while one was open for 18% of the time, Pallas kernels for 0%

profile of v12, /device:TPU:6, one launch (start us, length us, event | category | flops | bytes accessed | tf_op | source)
XLA Modules:
  0.0 153.0 jit_solution(9244397165525365133)
XLA Ops:
  11.6 1.7 %constant_dynamic-slice_fusion.3 = (bf16[8,1,256,256]{3,2,1,0:T(8,128)(2,1)S(1)}, bf16[8,1,256,256]{3,2,1,0:T(8,128)(2,1)S(1)}) fusion(bf16[8,12,256,256]{3,2,1,0:T(8,128)(2,1)} %front_ref.1, s32[]{:T(128)S(6)} %select_n.381, s32[]{:T(128)S(6)} %select_n.385), kind=kLoop, calls=%fused_computation.107 | loop fusion | bytes 4194312 | tf_op jit(solution)/shard_map/jit(dynamic_index_in_dim)/dynamic_slice | solution.py:264
  16.0 2.2 %dynamic-slice_select_fusion = (bf16[1,12,256,256]{3,2,1,0:T(8,128)(2,1)S(1)}, bf16[1,12,256,256]{3,2,1,0:T(8,128)(2,1)S(1)}) fusion(bf16[8,12,256,256]{3,2,1,0:T(8,128)(2,1)} %front_ref.1, s32[]{:T(128)S(6)} %select_n.417, pred[12]{0:T(512)(128)(4,1)S(1)} %get-tuple-element.5, s32[]{:T(128)S(6)} %select_n.412, pred[12]{0:T(512)(128)(4,1)S(1)} %get-tuple-element.6), kind=kLoop, calls=%fused_computation.22 | loop fusion | flops 1572864 | bytes 6291488 | tf_op jit(solution)/shard_map/jit(_where)/select_n | solution.py:229
  18.1 1.5 fusion.21
  19.6 4.0 %collective-permute-start.17 = (bf16[2,4,192,256]{3,2,1,0:T(8,128)(2,1)}, bf16[2,4,192,256]{3,2,1,0:T(8,128)(2,1)}, u32[]{:S(2)}, u32[]{:S(2)}) collective-permute-start(bf16[2,4,192,256]{3,2,1,0:T(8,128)(2,1)} %get-tuple-element.32), channel_id=1, source_target_pairs={{0,96},{1,25},{2,98},{3,27},{4,100},{5,29},{6,102},{7,31},{8,104},... | collective-permute-start | bytes 2359304 | tf_op jit(solution)/shard_map/ppermute | solution.py:149
  23.7 1.5 collective-permute-start.16
  35.7 1.8 %broadcast_select_fusion.2 = bf16[2,256,256]{1,2,0:T(8,128)(2,1)} fusion(bf16[2,256,256]{1,2,0:T(8,128)(2,1)} %collective-permute-done.8, pred[2]{0:T(512)(128)(4,1)S(1)} %get-tuple-element.65, bf16[1,256,256]{1,2,0:T(8,128)(2,1)S(1)} %get-tuple-element.77, bf16[1,256,256]{1,2,0:T(8,128)(2,1)S(1)} %get-tuple-element.78), kind=kLoop, calls=%fused_computation.65 | loop fusion | flops 262144 | bytes 786434 | tf_op jit(solution)/shard_map/jit(_where)/select_n | solution.py:13
  37.4 1.6 %collective-permute-start.9 = (bf16[2,256,256]{1,2,0:T(8,128)(2,1)}, bf16[2,256,256]{1,2,0:T(8,128)(2,1)}, u32[]{:S(2)}, u32[]{:S(2)}) collective-permute-start(bf16[2,256,256]{1,2,0:T(8,128)(2,1)} %broadcast_select_fusion.2), channel_id=1, source_target_pairs={{0,2},{1,3},{2,0},{3,1},{4,6},{5,7},{6,4},{7,5},{8,10},{9,11},{10,... | collective-permute-start | bytes 786440 | tf_op jit(solution)/shard_map/ppermute | solution.py:171
  39.1 5.2 %collective-permute-done.9 = bf16[2,256,256]{1,2,0:T(8,128)(2,1)} collective-permute-done((bf16[2,256,256]{1,2,0:T(8,128)(2,1)}, bf16[2,256,256]{1,2,0:T(8,128)(2,1)}, u32[]{:S(2)}, u32[]{:S(2)}) %collective-permute-start.9) | collective-permute-done | bytes 262176 | tf_op jit(solution)/shard_map/ppermute | solution.py:171
  44.3 1.8 %broadcast_select_fusion.3 = bf16[2,256,256]{1,2,0:T(8,128)(2,1)} fusion(bf16[2,256,256]{1,2,0:T(8,128)(2,1)} %collective-permute-done.9, pred[2]{0:T(512)(128)(4,1)S(1)} %get-tuple-element.61, bf16[2,256,256]{1,2,0:T(8,128)(2,1)} %collective-permute-done.8, bf16[1,256,256]{1,2,0:T(8,128)(2,1)S(1)} %get-tuple-element.77, ...), kind=kLoop, calls=%fused_computation.66 | loop fusion | flops 393216 | bytes 1048580 | tf_op jit(solution)/shard_map/jit(_where)/select_n | solution.py:13
  46.1 3.2 %collective-permute-start.10 = (bf16[2,256,256]{1,2,0:T(8,128)(2,1)}, bf16[2,256,256]{1,2,0:T(8,128)(2,1)S(1)}, u32[]{:S(2)}, u32[]{:S(2)}) collective-permute-start(bf16[2,256,256]{1,2,0:T(8,128)(2,1)} %broadcast_select_fusion.3), channel_id=1, source_target_pairs={{0,4},{1,5},{2,6},{3,7},{4,0},{5,1},{6,2},{7,3},{8,12},{9,13},{10,... | collective-permute-start | bytes 786440 | tf_op jit(solution)/shard_map/ppermute | solution.py:171
  50.2 4.0 %collective-permute-done.10 = bf16[2,256,256]{1,2,0:T(8,128)(2,1)S(1)} collective-permute-done((bf16[2,256,256]{1,2,0:T(8,128)(2,1)}, bf16[2,256,256]{1,2,0:T(8,128)(2,1)S(1)}, u32[]{:S(2)}, u32[]{:S(2)}) %collective-permute-start.10) | collective-permute-done | bytes 262176 | tf_op jit(solution)/shard_map/ppermute | solution.py:171
  56.0 1.8 %fusion.18 = bf16[2,4,192,256]{3,2,1,0:T(8,128)(2,1)S(1)} fusion(bf16[1,4,4,192,256]{4,3,2,0,1:T(8,128)(2,1)S(1)} %bitcast.206, bf16[1,4,4,192,256]{4,3,2,0,1:T(8,128)(2,1)S(1)} %bitcast.204, bf16[2,4,192,256]{3,2,1,0:T(8,128)(2,1)} %collective-permute-done.15, bf16[2,4,192,256]{3,2,1,0:T(8,128)(2,1)} %collective-permute-done.16, ...), kind=kLoop, calls=%fused_computation.45 | loop fusion | flops 1572864 | bytes 6291462 | tf_op jit(solution)/shard_map/jit(_where)/select_n | solution.py:13
  59.4 3.2 %collective-permute-start.19 = (bf16[2,192,256]{2,1,0:T(8,128)(2,1)S(1)}, bf16[2,192,256]{2,1,0:T(8,128)(2,1)S(1)}, u32[]{:S(2)}, u32[]{:S(2)}) collective-permute-start(bf16[2,192,256]{2,1,0:T(8,128)(2,1)S(1)} %get-tuple-element.52), channel_id=1, source_target_pairs={{0,16},{1,65},{2,18},{3,67},{4,20},{5,69},{6,22},{7,71},{8,24},{9,... | collective-permute-start | bytes 589832 | tf_op jit(solution)/shard_map/ppermute | solution.py:149
  62.7 2.2 %collective-permute-done.20 = bf16[2,192,256]{2,1,0:T(8,128)(2,1)S(1)} collective-permute-done((bf16[2,192,256]{2,1,0:T(8,128)(2,1)S(1)}, bf16[2,192,256]{2,1,0:T(8,128)(2,1)S(1)}, u32[]{:S(2)}, u32[]{:S(2)}) %collective-permute-start.20) | collective-permute-done | bytes 196640 | tf_op jit(solution)/shard_map/ppermute | solution.py:149
  64.8 3.6 %collective-permute-done.19 = bf16[2,192,256]{2,1,0:T(8,128)(2,1)S(1)} collective-permute-done((bf16[2,192,256]{2,1,0:T(8,128)(2,1)S(1)}, bf16[2,192,256]{2,1,0:T(8,128)(2,1)S(1)}, u32[]{:S(2)}, u32[]{:S(2)}) %collective-permute-start.19) | collective-permute-done | bytes 196640 | tf_op jit(solution)/shard_map/ppermute | solution.py:149
  70.8 1.8 %collective-permute-start.21 = (bf16[2,192,256]{2,1,0:T(8,128)(2,1)S(1)}, bf16[2,192,256]{2,1,0:T(8,128)(2,1)S(1)}, u32[]{:S(2)}, u32[]{:S(2)}) collective-permute-start(bf16[2,192,256]{2,1,0:T(8,128)(2,1)S(1)} %fusion.23), channel_id=1, source_target_pairs={{0,8},{1,33},{2,10},{3,35},{4,12},{5,37},{6,14},{7,39},{8,0},{9,41... | collective-permute-start | bytes 589832 | tf_op jit(solution)/shard_map/ppermute | solution.py:156
  72.8 1.5 collective-permute-start.12
  75.8 3.1 %collective-permute-start.3 = (bf16[2,256,256]{2,1,0:T(8,128)(2,1)S(1)}, bf16[2,256,256]{2,1,0:T(8,128)(2,1)S(1)}, u32[]{:S(2)}, u32[]{:S(2)}) collective-permute-start(bf16[2,256,256]{2,1,0:T(8,128)(2,1)S(1)} %get-tuple-element.43), channel_id=1, source_target_pairs={{0,6},{1,7},{2,4},{3,5},{4,2},{5,3},{6,0},{7,1},{8,14},{9,15},{10,... | collective-permute-start | bytes 786440 | tf_op jit(solution)/shard_map/ppermute | solution.py:149
  78.9 1.5 collective-permute-done.23
  80.4 1.6 %collective-permute-start.1 = (bf16[2,256,256]{2,1,0:T(8,128)(2,1)S(1)}, bf16[2,256,256]{2,1,0:T(8,128)(2,1)S(1)}, u32[]{:S(2)}, u32[]{:S(2)}) collective-permute-start(bf16[2,256,256]{2,1,0:T(8,128)(2,1)S(1)} %get-tuple-element.44), channel_id=1, source_target_pairs={{0,2},{1,3},{2,0},{3,1},{4,6},{5,7},{6,4},{7,5},{8,10},{9,11},{10,... | collective-permute-start | bytes 786440 | tf_op jit(solution)/shard_map/ppermute | solution.py:149
  82.0 2.9 %collective-permute-start.2 = (bf16[2,256,256]{2,1,0:T(8,128)(2,1)S(1)}, bf16[2,256,256]{2,1,0:T(8,128)(2,1)S(1)}, u32[]{:S(2)}, u32[]{:S(2)}) collective-permute-start(bf16[2,256,256]{2,1,0:T(8,128)(2,1)S(1)} %get-tuple-element.45), channel_id=1, source_target_pairs={{0,4},{1,5},{2,6},{3,7},{4,0},{5,1},{6,2},{7,3},{8,12},{9,13},{10,... | collective-permute-start | bytes 786440 | tf_op jit(solution)/shard_map/ppermute | solution.py:149
  85.2 1.7 %collective-permute-start.13 = (bf16[2,256,256]{1,2,0:T(8,128)(2,1)S(1)}, bf16[2,256,256]{1,2,0:T(8,128)(2,1)S(1)}, u32[]{:S(2)}, u32[]{:S(2)}) collective-permute-start(bf16[2,256,256]{1,2,0:T(8,128)(2,1)S(1)} %broadcast_select_fusion.6), channel_id=1, source_target_pairs={{0,32},{1,33},{2,34},{3,35},{4,36},{5,37},{6,38},{7,39},{8,40},{9,... | collective-permute-start | bytes 786440 | tf_op jit(solution)/shard_map/ppermute | solution.py:171
  86.8 6.6 %collective-permute-done.2 = bf16[2,256,256]{2,1,0:T(8,128)(2,1)S(1)} collective-permute-done((bf16[2,256,256]{2,1,0:T(8,128)(2,1)S(1)}, bf16[2,256,256]{2,1,0:T(8,128)(2,1)S(1)}, u32[]{:S(2)}, u32[]{:S(2)}) %collective-permute-start.2) | collective-permute-done | bytes 262176 | tf_op jit(solution)/shard_map/ppermute | solution.py:149
  93.7 2.6 %collective-permute-start.5 = (bf16[2,256,256]{2,1,0:T(8,128)(2,1)S(1)}, bf16[2,256,256]{2,1,0:T(8,128)(2,1)S(1)}, u32[]{:S(2)}, u32[]{:S(2)}) collective-permute-start(bf16[2,256,256]{2,1,0:T(8,128)(2,1)S(1)} %fusion.22), channel_id=1, source_target_pairs={{0,4},{1,5},{2,6},{3,7},{4,0},{5,1},{6,2},{7,3},{8,12},{9,13},{10,... | collective-permute-start | bytes 786440 | tf_op jit(solution)/shard_map/ppermute | solution.py:156
  97.9 3.1 %collective-permute-start.26 = (bf16[2,4,192,256]{3,2,1,0:T(8,128)(2,1)S(1)}, bf16[2,4,192,256]{3,2,1,0:T(8,128)(2,1)S(1)}, u32[]{:S(2)}, u32[]{:S(2)}) collective-permute-start(bf16[2,4,192,256]{3,2,1,0:T(8,128)(2,1)S(1)} %pad_maximum_fusion.5), channel_id=1, source_target_pairs={{0,96},{1,25},{2,98},{3,27},{4,100},{5,29},{6,102},{7,31},{8,104},... | collective-permute-start | bytes 2359304 | tf_op jit(solution)/shard_map/ppermute | solution.py:156
  101.0 1.5 %collective-permute-start.25 = (bf16[2,4,192,256]{3,2,1,0:T(8,128)(2,1)S(1)}, bf16[2,4,192,256]{3,2,1,0:T(8,128)(2,1)S(1)}, u32[]{:S(2)}, u32[]{:S(2)}) collective-permute-start(bf16[2,4,192,256]{3,2,1,0:T(8,128)(2,1)S(1)} %pad_maximum_fusion.5), channel_id=1, source_target_pairs={{0,64},{1,17},{2,66},{3,19},{4,68},{5,21},{6,70},{7,23},{8,72},{9,... | collective-permute-start | bytes 2359304 | tf_op jit(solution)/shard_map/ppermute | solution.py:156
  104.1 2.5 %collective-permute-start.24 = (bf16[2,4,192,256]{3,2,1,0:T(8,128)(2,1)S(1)}, bf16[2,4,192,256]{3,2,1,0:T(8,128)(2,1)S(1)}, u32[]{:S(2)}, u32[]{:S(2)}) collective-permute-start(bf16[2,4,192,256]{3,2,1,0:T(8,128)(2,1)S(1)} %pad_maximum_fusion.5), channel_id=1, source_target_pairs={{0,32},{1,9},{2,34},{3,11},{4,36},{5,13},{6,38},{7,15},{8,40},{9,1... | collective-permute-start | bytes 2359304 | tf_op jit(solution)/shard_map/ppermute | solution.py:156
  106.6 2.0 %collective-permute-start.14 = (bf16[2,256,256]{1,2,0:T(8,128)(2,1)S(1)}, bf16[2,256,256]{1,2,0:T(8,128)(2,1)S(1)}, u32[]{:S(2)}, u32[]{:S(2)}) collective-permute-start(bf16[2,256,256]{1,2,0:T(8,128)(2,1)S(1)} %broadcast_select_fusion.7), channel_id=1, source_target_pairs={{0,64},{1,65},{2,66},{3,67},{4,68},{5,69},{6,70},{7,71},{8,72},{9,... | collective-permute-start | bytes 786440 | tf_op jit(solution)/shard_map/ppermute | solution.py:171
  109.2 19.4 %collective-permute-done.14 = bf16[2,256,256]{1,2,0:T(8,128)(2,1)S(1)} collective-permute-done((bf16[2,256,256]{1,2,0:T(8,128)(2,1)S(1)}, bf16[2,256,256]{1,2,0:T(8,128)(2,1)S(1)}, u32[]{:S(2)}, u32[]{:S(2)}) %collective-permute-start.14) | collective-permute-done | bytes 262176 | tf_op jit(solution)/shard_map/ppermute | solution.py:171
  131.5 2.0 %fusion.4.u2_ref = bf16[12,256,256]{2,1,0:T(8,128)(2,1)} fusion(bf16[1,12,256,256]{3,2,1,0:T(8,128)(2,1)S(1)} %bitcast.207, f32[12,256,256]{1,2,0:T(8,128)S(1)} %fusion.24, pred[12]{0:T(512)(128)(4,1)S(1)} %get-tuple-element.11, pred[12]{0:T(512)(128)(4,1)S(1)} %get-tuple-element.9, bf16[256,256]{1,0:T(8,128)(2,1)S(1)} %fusion.8), kind=kLoop, calls=%fused_computation.21 | loop fusion | flops 3932160 | bytes 6422552 | tf_op jit(solution)/shard_map/squeeze | solution.py:292
  134.4 1.9 %select_convert_fusion.l2_ref = bf16[8,256,256]{2,1,0:T(8,128)(2,1)} fusion(pred[8]{0:T(512)(128)(4,1)S(1)} %get-tuple-element.67, bf16[8,1,256,256]{3,2,0,1:T(8,128)(2,1)S(1)} %bitcast.210, bf16[8,256,256]{2,1,0:T(8,128)(2,1)S(1)} %select_convert_fusion.1.l1_ref, pred[8]{0:T(512)(128)(4,1)S(1)} %get-tuple-element.66, ...), kind=kOutput, calls=%fused_computation.18 | convolution fusion | flops 540540928 | bytes 4457984 | tf_op jit(solution)/shard_map/iab,bc->iac/dot_general | solution.py:177
  136.2 16.7 %shard_map.46 = bf16[8,12,256,256]{3,2,1,0:T(8,128)(2,1)} custom-call(s32[8,12]{1,0:T(8,128)} %select_add_fusion.codes, bf16[8,12,256,256]{3,2,1,0:T(8,128)(2,1)} %front_ref.1, bf16[8,256,256]{2,1,0:T(8,128)(2,1)} %copy-done.6, bf16[8,256,256]{2,1,0:T(8,128)(2,1)} %select_convert_fusion.l2_ref, bf16[12,256,256]{2,1,0:T(8,128)(2,1)} %bitcast.202, ...), custom_call_target="tpu_custom_call" | custom-call | tf_op jit(solution)/shard_map/pallas_call | solution.py:214
  (106 shorter events, 29.7 us)
Async XLA Ops:
  8.5 6.8 %copy-start.7 = (s32[8,16,12,8]{1,0,3,2:T(8,128)}, s32[8,16,12,8]{1,0,3,2:T(8,128)S(1)}, u32[]{:S(2)}) copy-start(s32[8,16,12,8]{1,0,3,2:T(8,128)S(1)} %reshape.625) | copy-start | bytes 147460
  11.3 24.3 %collective-permute-start.8 = (bf16[2,256,256]{1,2,0:T(8,128)(2,1)}, bf16[2,256,256]{1,2,0:T(8,128)(2,1)}, u32[]{:S(2)}, u32[]{:S(2)}) collective-permute-start(bf16[2,256,256]{1,2,0:T(8,128)(2,1)} %pad_maximum_fusion.6), channel_id=1, source_target_pairs={{0,1},{1,0},{2,3},{3,2},{4,5},{5,4},{6,7},{7,6},{8,9},{9,8},{10,11... | collective-permute-start | bytes 786440 | tf_op jit(solution)/shard_map/ppermute | solution.py:171
  14.8 59.5 %collective-permute-start = (bf16[2,4,256,256]{3,2,1,0:T(8,128)(2,1)}, bf16[2,4,256,256]{3,2,1,0:T(8,128)(2,1)}, u32[]{:S(2)}, u32[]{:S(2)}) collective-permute-start(bf16[2,4,256,256]{3,2,1,0:T(8,128)(2,1)} %fusion.13), channel_id=1, source_target_pairs={{0,1},{1,0},{2,3},{3,2},{4,5},{5,4},{6,7},{7,6},{8,9},{9,8},{10,11... | collective-permute-start | bytes 3145736 | tf_op jit(solution)/shard_map/ppermute | solution.py:149
  18.1 12.7 %copy-start.5 = (s32[128,96]{0,1:T(8,128)S(1)}, s32[128,96]{0,1:T(8,128)}, u32[]{:S(2)}) copy-start(s32[128,96]{0,1:T(8,128)} %param.5) | copy-start | bytes 147460
  19.6 36.4 %collective-permute-start.17 = (bf16[2,4,192,256]{3,2,1,0:T(8,128)(2,1)}, bf16[2,4,192,256]{3,2,1,0:T(8,128)(2,1)}, u32[]{:S(2)}, u32[]{:S(2)}) collective-permute-start(bf16[2,4,192,256]{3,2,1,0:T(8,128)(2,1)} %get-tuple-element.32), channel_id=1, source_target_pairs={{0,96},{1,25},{2,98},{3,27},{4,100},{5,29},{6,102},{7,31},{8,104},... | collective-permute-start | bytes 2359304 | tf_op jit(solution)/shard_map/ppermute | solution.py:149
  23.7 32.3 %collective-permute-start.15 = (bf16[2,4,192,256]{3,2,1,0:T(8,128)(2,1)}, bf16[2,4,192,256]{3,2,1,0:T(8,128)(2,1)}, u32[]{:S(2)}, u32[]{:S(2)}) collective-permute-start(bf16[2,4,192,256]{3,2,1,0:T(8,128)(2,1)} %get-tuple-element.33), channel_id=1, source_target_pairs={{0,32},{1,9},{2,34},{3,11},{4,36},{5,13},{6,38},{7,15},{8,40},{9,1... | collective-permute-start | bytes 2359304 | tf_op jit(solution)/shard_map/ppermute | solution.py:149
  23.7 32.3 %collective-permute-start.16 = (bf16[2,4,192,256]{3,2,1,0:T(8,128)(2,1)}, bf16[2,4,192,256]{3,2,1,0:T(8,128)(2,1)}, u32[]{:S(2)}, u32[]{:S(2)}) collective-permute-start(bf16[2,4,192,256]{3,2,1,0:T(8,128)(2,1)} %get-tuple-element.34), channel_id=1, source_target_pairs={{0,64},{1,17},{2,66},{3,19},{4,68},{5,21},{6,70},{7,23},{8,72},{9,... | collective-permute-start | bytes 2359304 | tf_op jit(solution)/shard_map/ppermute | solution.py:149
  37.4 6.9 %collective-permute-start.9 = (bf16[2,256,256]{1,2,0:T(8,128)(2,1)}, bf16[2,256,256]{1,2,0:T(8,128)(2,1)}, u32[]{:S(2)}, u32[]{:S(2)}) collective-permute-start(bf16[2,256,256]{1,2,0:T(8,128)(2,1)} %broadcast_select_fusion.2), channel_id=1, source_target_pairs={{0,2},{1,3},{2,0},{3,1},{4,6},{5,7},{6,4},{7,5},{8,10},{9,11},{10,... | collective-permute-start | bytes 786440 | tf_op jit(solution)/shard_map/ppermute | solution.py:171
  46.1 8.1 %collective-permute-start.10 = (bf16[2,256,256]{1,2,0:T(8,128)(2,1)}, bf16[2,256,256]{1,2,0:T(8,128)(2,1)S(1)}, u32[]{:S(2)}, u32[]{:S(2)}) collective-permute-start(bf16[2,256,256]{1,2,0:T(8,128)(2,1)} %broadcast_select_fusion.3), channel_id=1, source_target_pairs={{0,4},{1,5},{2,6},{3,7},{4,0},{5,1},{6,2},{7,3},{8,12},{9,13},{10,... | collective-permute-start | bytes 786440 | tf_op jit(solution)/shard_map/ppermute | solution.py:171
  55.3 17.4 %collective-permute-start.11 = (bf16[2,256,256]{1,2,0:T(8,128)(2,1)S(1)}, bf16[2,256,256]{1,2,0:T(8,128)(2,1)S(1)}, u32[]{:S(2)}, u32[]{:S(2)}) collective-permute-start(bf16[2,256,256]{1,2,0:T(8,128)(2,1)S(1)} %broadcast_select_fusion.4), channel_id=1, source_target_pairs={{0,8},{1,9},{2,10},{3,11},{4,12},{5,13},{6,14},{7,15},{8,0},{9,1},... | collective-permute-start | bytes 786440 | tf_op jit(solution)/shard_map/ppermute | solution.py:171
  57.8 16.5 %copy-start.2 = (bf16[1,2,4,256,256]{4,3,2,0,1:T(8,128)(2,1)S(1)}, bf16[1,2,4,256,256]{4,3,2,0,1:T(8,128)(2,1)}, u32[]{:S(2)}) copy-start(bf16[1,2,4,256,256]{4,3,2,0,1:T(8,128)(2,1)} %copy-done.1) | copy-start | bytes 3145732
  57.8 16.5 %copy-start.4 = (bf16[1,2,4,256,256]{4,3,2,0,1:T(8,128)(2,1)S(1)}, bf16[1,2,4,256,256]{4,3,2,0,1:T(8,128)(2,1)}, u32[]{:S(2)}) copy-start(bf16[1,2,4,256,256]{4,3,2,0,1:T(8,128)(2,1)} %copy-done.3) | copy-start | bytes 3145732
  57.9 7.0 %collective-permute-start.20 = (bf16[2,192,256]{2,1,0:T(8,128)(2,1)S(1)}, bf16[2,192,256]{2,1,0:T(8,128)(2,1)S(1)}, u32[]{:S(2)}, u32[]{:S(2)}) collective-permute-start(bf16[2,192,256]{2,1,0:T(8,128)(2,1)S(1)} %get-tuple-element.50), channel_id=1, source_target_pairs={{0,24},{1,97},{2,26},{3,99},{4,28},{5,101},{6,30},{7,103},{8,16},{... | collective-permute-start | bytes 589832 | tf_op jit(solution)/shard_map/ppermute | solution.py:149
  59.1 5.7 %collective-permute-start.18 = (bf16[2,192,256]{2,1,0:T(8,128)(2,1)S(1)}, bf16[2,192,256]{2,1,0:T(8,128)(2,1)S(1)}, u32[]{:S(2)}, u32[]{:S(2)}) collective-permute-start(bf16[2,192,256]{2,1,0:T(8,128)(2,1)S(1)} %get-tuple-element.51), channel_id=1, source_target_pairs={{0,8},{1,33},{2,10},{3,35},{4,12},{5,37},{6,14},{7,39},{8,0},{9,41... | collective-permute-start | bytes 589832 | tf_op jit(solution)/shard_map/ppermute | solution.py:149
  59.4 9.0 %collective-permute-start.19 = (bf16[2,192,256]{2,1,0:T(8,128)(2,1)S(1)}, bf16[2,192,256]{2,1,0:T(8,128)(2,1)S(1)}, u32[]{:S(2)}, u32[]{:S(2)}) collective-permute-start(bf16[2,192,256]{2,1,0:T(8,128)(2,1)S(1)} %get-tuple-element.52), channel_id=1, source_target_pairs={{0,16},{1,65},{2,18},{3,67},{4,20},{5,69},{6,22},{7,71},{8,24},{9,... | collective-permute-start | bytes 589832 | tf_op jit(solution)/shard_map/ppermute | solution.py:149
  68.5 11.9 %collective-permute-start.23 = (bf16[2,192,256]{2,1,0:T(8,128)(2,1)S(1)}, bf16[2,192,256]{2,1,0:T(8,128)(2,1)S(1)}, u32[]{:S(2)}, u32[]{:S(2)}) collective-permute-start(bf16[2,192,256]{2,1,0:T(8,128)(2,1)S(1)} %fusion.23), channel_id=1, source_target_pairs={{0,24},{1,97},{2,26},{3,99},{4,28},{5,101},{6,30},{7,103},{8,16},{... | collective-permute-start | bytes 589832 | tf_op jit(solution)/shard_map/ppermute | solution.py:156
  69.7 12.2 %collective-permute-start.22 = (bf16[2,192,256]{2,1,0:T(8,128)(2,1)S(1)}, bf16[2,192,256]{2,1,0:T(8,128)(2,1)S(1)}, u32[]{:S(2)}, u32[]{:S(2)}) collective-permute-start(bf16[2,192,256]{2,1,0:T(8,128)(2,1)S(1)} %fusion.23), channel_id=1, source_target_pairs={{0,16},{1,65},{2,18},{3,67},{4,20},{5,69},{6,22},{7,71},{8,24},{9,... | collective-permute-start | bytes 589832 | tf_op jit(solution)/shard_map/ppermute | solution.py:156
  70.8 14.0 %collective-permute-start.21 = (bf16[2,192,256]{2,1,0:T(8,128)(2,1)S(1)}, bf16[2,192,256]{2,1,0:T(8,128)(2,1)S(1)}, u32[]{:S(2)}, u32[]{:S(2)}) collective-permute-start(bf16[2,192,256]{2,1,0:T(8,128)(2,1)S(1)} %fusion.23), channel_id=1, source_target_pairs={{0,8},{1,33},{2,10},{3,35},{4,12},{5,37},{6,14},{7,39},{8,0},{9,41... | collective-permute-start | bytes 589832 | tf_op jit(solution)/shard_map/ppermute | solution.py:156
  72.8 12.3 %collective-permute-start.12 = (bf16[2,256,256]{1,2,0:T(8,128)(2,1)S(1)}, bf16[2,256,256]{1,2,0:T(8,128)(2,1)S(1)}, u32[]{:S(2)}, u32[]{:S(2)}) collective-permute-start(bf16[2,256,256]{1,2,0:T(8,128)(2,1)S(1)} %broadcast_select_fusion.5), channel_id=1, source_target_pairs={{0,16},{1,17},{2,18},{3,19},{4,20},{5,21},{6,22},{7,23},{8,24},{9,... | collective-permute-start | bytes 786440 | tf_op jit(solution)/shard_map/ppermute | solution.py:171
  75.8 11.0 %collective-permute-start.3 = (bf16[2,256,256]{2,1,0:T(8,128)(2,1)S(1)}, bf16[2,256,256]{2,1,0:T(8,128)(2,1)S(1)}, u32[]{:S(2)}, u32[]{:S(2)}) collective-permute-start(bf16[2,256,256]{2,1,0:T(8,128)(2,1)S(1)} %get-tuple-element.43), channel_id=1, source_target_pairs={{0,6},{1,7},{2,4},{3,5},{4,2},{5,3},{6,0},{7,1},{8,14},{9,15},{10,... | collective-permute-start | bytes 786440 | tf_op jit(solution)/shard_map/ppermute | solution.py:149
  80.4 6.4 %collective-permute-start.1 = (bf16[2,256,256]{2,1,0:T(8,128)(2,1)S(1)}, bf16[2,256,256]{2,1,0:T(8,128)(2,1)S(1)}, u32[]{:S(2)}, u32[]{:S(2)}) collective-permute-start(bf16[2,256,256]{2,1,0:T(8,128)(2,1)S(1)} %get-tuple-element.44), channel_id=1, source_target_pairs={{0,2},{1,3},{2,0},{3,1},{4,6},{5,7},{6,4},{7,5},{8,10},{9,11},{10,... | collective-permute-start | bytes 786440 | tf_op jit(solution)/shard_map/ppermute | solution.py:149
  82.0 11.5 %collective-permute-start.2 = (bf16[2,256,256]{2,1,0:T(8,128)(2,1)S(1)}, bf16[2,256,256]{2,1,0:T(8,128)(2,1)S(1)}, u32[]{:S(2)}, u32[]{:S(2)}) collective-permute-start(bf16[2,256,256]{2,1,0:T(8,128)(2,1)S(1)} %get-tuple-element.45), channel_id=1, source_target_pairs={{0,4},{1,5},{2,6},{3,7},{4,0},{5,1},{6,2},{7,3},{8,12},{9,13},{10,... | collective-permute-start | bytes 786440 | tf_op jit(solution)/shard_map/ppermute | solution.py:149
  85.2 15.9 %collective-permute-start.13 = (bf16[2,256,256]{1,2,0:T(8,128)(2,1)S(1)}, bf16[2,256,256]{1,2,0:T(8,128)(2,1)S(1)}, u32[]{:S(2)}, u32[]{:S(2)}) collective-permute-start(bf16[2,256,256]{1,2,0:T(8,128)(2,1)S(1)} %broadcast_select_fusion.6), channel_id=1, source_target_pairs={{0,32},{1,33},{2,34},{3,35},{4,36},{5,37},{6,38},{7,39},{8,40},{9,... | collective-permute-start | bytes 786440 | tf_op jit(solution)/shard_map/ppermute | solution.py:171
  93.6 10.5 %collective-permute-start.6 = (bf16[2,256,256]{2,1,0:T(8,128)(2,1)S(1)}, bf16[2,256,256]{2,1,0:T(8,128)(2,1)S(1)}, u32[]{:S(2)}, u32[]{:S(2)}) collective-permute-start(bf16[2,256,256]{2,1,0:T(8,128)(2,1)S(1)} %fusion.22), channel_id=1, source_target_pairs={{0,6},{1,7},{2,4},{3,5},{4,2},{5,3},{6,0},{7,1},{8,14},{9,15},{10,... | collective-permute-start | bytes 786440 | tf_op jit(solution)/shard_map/ppermute | solution.py:156
  93.7 12.9 %collective-permute-start.5 = (bf16[2,256,256]{2,1,0:T(8,128)(2,1)S(1)}, bf16[2,256,256]{2,1,0:T(8,128)(2,1)S(1)}, u32[]{:S(2)}, u32[]{:S(2)}) collective-permute-start(bf16[2,256,256]{2,1,0:T(8,128)(2,1)S(1)} %fusion.22), channel_id=1, source_target_pairs={{0,4},{1,5},{2,6},{3,7},{4,0},{5,1},{6,2},{7,3},{8,12},{9,13},{10,... | collective-permute-start | bytes 786440 | tf_op jit(solution)/shard_map/ppermute | solution.py:156
  96.3 12.3 %collective-permute-start.4 = (bf16[2,256,256]{2,1,0:T(8,128)(2,1)S(1)}, bf16[2,256,256]{2,1,0:T(8,128)(2,1)S(1)}, u32[]{:S(2)}, u32[]{:S(2)}) collective-permute-start(bf16[2,256,256]{2,1,0:T(8,128)(2,1)S(1)} %fusion.22), channel_id=1, source_target_pairs={{0,2},{1,3},{2,0},{3,1},{4,6},{5,7},{6,4},{7,5},{8,10},{9,11},{10,... | collective-permute-start | bytes 786440 | tf_op jit(solution)/shard_map/ppermute | solution.py:156
  97.9 31.1 %collective-permute-start.26 = (bf16[2,4,192,256]{3,2,1,0:T(8,128)(2,1)S(1)}, bf16[2,4,192,256]{3,2,1,0:T(8,128)(2,1)S(1)}, u32[]{:S(2)}, u32[]{:S(2)}) collective-permute-start(bf16[2,4,192,256]{3,2,1,0:T(8,128)(2,1)S(1)} %pad_maximum_fusion.5), channel_id=1, source_target_pairs={{0,96},{1,25},{2,98},{3,27},{4,100},{5,29},{6,102},{7,31},{8,104},... | collective-permute-start | bytes 2359304 | tf_op jit(solution)/shard_map/ppermute | solution.py:156
  101.0 27.9 %collective-permute-start.25 = (bf16[2,4,192,256]{3,2,1,0:T(8,128)(2,1)S(1)}, bf16[2,4,192,256]{3,2,1,0:T(8,128)(2,1)S(1)}, u32[]{:S(2)}, u32[]{:S(2)}) collective-permute-start(bf16[2,4,192,256]{3,2,1,0:T(8,128)(2,1)S(1)} %pad_maximum_fusion.5), channel_id=1, source_target_pairs={{0,64},{1,17},{2,66},{3,19},{4,68},{5,21},{6,70},{7,23},{8,72},{9,... | collective-permute-start | bytes 2359304 | tf_op jit(solution)/shard_map/ppermute | solution.py:156
  102.7 26.1 %copy-start.8 = (bf16[2,256,256]{2,1,0:T(8,128)(2,1)S(1)}, bf16[2,256,256]{2,1,0:T(8,128)(2,1)}, u32[]{:S(2)}) copy-start(bf16[2,256,256]{2,1,0:T(8,128)(2,1)} %param.7) | copy-start | bytes 786436
  104.1 24.9 %collective-permute-start.24 = (bf16[2,4,192,256]{3,2,1,0:T(8,128)(2,1)S(1)}, bf16[2,4,192,256]{3,2,1,0:T(8,128)(2,1)S(1)}, u32[]{:S(2)}, u32[]{:S(2)}) collective-permute-start(bf16[2,4,192,256]{3,2,1,0:T(8,128)(2,1)S(1)} %pad_maximum_fusion.5), channel_id=1, source_target_pairs={{0,32},{1,9},{2,34},{3,11},{4,36},{5,13},{6,38},{7,15},{8,40},{9,1... | collective-permute-start | bytes 2359304 | tf_op jit(solution)/shard_map/ppermute | solution.py:156
  106.6 22.0 %collective-permute-start.14 = (bf16[2,256,256]{1,2,0:T(8,128)(2,1)S(1)}, bf16[2,256,256]{1,2,0:T(8,128)(2,1)S(1)}, u32[]{:S(2)}, u32[]{:S(2)}) collective-permute-start(bf16[2,256,256]{1,2,0:T(8,128)(2,1)S(1)} %broadcast_select_fusion.7), channel_id=1, source_target_pairs={{0,64},{1,65},{2,66},{3,67},{4,68},{5,69},{6,70},{7,71},{8,72},{9,... | collective-permute-start | bytes 786440 | tf_op jit(solution)/shard_map/ppermute | solution.py:171
  108.9 24.6 %collective-permute-start.7 = (bf16[2,4,256,256]{3,2,1,0:T(8,128)(2,1)S(1)}, bf16[2,4,256,256]{3,2,1,0:T(8,128)(2,1)S(1)}, u32[]{:S(2)}, u32[]{:S(2)}) collective-permute-start(bf16[2,4,256,256]{3,2,1,0:T(8,128)(2,1)S(1)} %pad_maximum_fusion.3), channel_id=1, source_target_pairs={{0,1},{1,0},{2,3},{3,2},{4,5},{5,4},{6,7},{7,6},{8,9},{9,8},{10,11... | collective-permute-start | bytes 3145736 | tf_op jit(solution)/shard_map/ppermute | solution.py:156
  (4 other events, 7.6 us)

commit v13 on v12

--- a/solution.py
+++ b/solution.py
@@ -167,9 +167,11 @@
     ncol = lax.axis_size("col")
     n = nrow * ncol
     relative = (lax.axis_index("row") * ncol + lax.axis_index("col")) ^ root
-    for b in range(n.bit_length() - 1):
+    col_bits = (ncol.bit_length() - 1)
+    bits = list(range(col_bits, n.bit_length() - 1)) + list(range(col_bits - 1, -1, -1))
+    for b in bits:
         got = lax.ppermute(value, ("row", "col"), [(d, d ^ (1 << b)) for d in range(n)])
-        value = per_part((relative >> b) == 1, got, value)
+        value = per_part(((relative >> b) & 1) == 1, got, value)
     return value
 
 

time: 154 us -> 155 us (level)
  waiting for transfers between devices: 43.9 us -> 48.5 us
  starting transfers between devices: 44.8 us -> 40.5 us
    ppermute x10, waiting for transfers between devices: 2.92 us -> 16.9 us  [xor_bcast(): lax.ppermute(buf, axes, digit_pairs(nrow, ncol, on_row, step, m))]
    ppermute x7, waiting for transfers between devices: 28.6 us -> 16.4 us  [all_bcast(): lax.ppermute(value, ('row', 'col'), [(d, d ^ 1 << b) for d in range(n)])]
    ppermute x10, starting transfers between devices: 18.4 us -> 15.1 us  [xor_bcast(): lax.ppermute(groups[m], axes, digit_pairs(nrow, ncol, on_row, step, m))]
    ppermute x10, starting transfers between devices: 15.8 us -> 12.8 us  [xor_bcast(): lax.ppermute(buf, axes, digit_pairs(nrow, ncol, on_row, step, m))]
    ppermute x10, waiting for transfers between devices: 12.4 us -> 15.2 us  [xor_bcast(): lax.ppermute(groups[m], axes, digit_pairs(nrow, ncol, on_row, step, m))]
    ppermute x7, starting transfers between devices: 10.6 us -> 12.6 us  [all_bcast(): lax.ppermute(value, ('row', 'col'), [(d, d ^ 1 << b) for d in range(n)])]
  transfers between devices with their start and end apart: 27 -> 27, of which waited for: 8 -> 14; matrix products, arithmetic and copies ran while one was open for 18% -> 18% of each run, Pallas kernels for 0% -> 0%
where the time goes in v13:
time: 155 us; the launch traced here: 153 us
  waiting for transfers between devices  48.5 us (31%)
  starting transfers between devices  40.5 us (26%)
  other arithmetic  23.3 us (15%)
  Pallas kernels  16.7 us (11%)
  between operations  11.6 us (7%)
  local copies, waits for them, and re-layouts  9.48 us (6%)
  matrix products  3.1 us (2%)
    ppermute x10, waiting for transfers between devices, xor_bcast(): lax.ppermute(buf, axes, digit_pairs(nrow, ncol, on_row, step, m))  16.9 us
    pallas_call x1, Pallas kernels, both_updates(): pl.pallas_call(update_kernel, grid_spec=pltpu.PrefetchScalarGridSpec(num_...  16.7 us
    ppermute x7, waiting for transfers between devices, all_bcast(): lax.ppermute(value, ('row', 'col'), [(d, d ^ 1 << b) for d in range(n)])  16.4 us
    ppermute x10, waiting for transfers between devices, xor_bcast(): lax.ppermute(groups[m], axes, digit_pairs(nrow, ncol, on_row, step, m))  15.2 us
    ppermute x10, starting transfers between devices, xor_bcast(): lax.ppermute(groups[m], axes, digit_pairs(nrow, ncol, on_row, step, m))  15.1 us
    ppermute x10, starting transfers between devices, xor_bcast(): lax.ppermute(buf, axes, digit_pairs(nrow, ncol, on_row, step, m))  12.8 us
    ppermute x7, starting transfers between devices, all_bcast(): lax.ppermute(value, ('row', 'col'), [(d, d ^ 1 << b) for d in range(n)])  12.6 us
    select_n x11, other arithmetic, per_part(): return jnp.where(cond.reshape((-1,) + (1,) * (a.ndim - 1)), a, b)  8.52 us
  transfers between devices with their start and end apart: 27, of which 14 were waited for; matrix products, arithmetic and copies ran while one was open for 18% of the time, Pallas kernels for 0%

profile of v13, /device:TPU:6, one launch (start us, length us, event | category | flops | bytes accessed | tf_op | source)
XLA Modules:
  0.0 153.2 jit_solution(3623152253812753837)
XLA Ops:
  0.0 1.3 fusion.43
  12.4 1.7 %constant_dynamic-slice_fusion.3 = (bf16[8,1,256,256]{3,2,1,0:T(8,128)(2,1)S(1)}, bf16[8,1,256,256]{3,2,1,0:T(8,128)(2,1)S(1)}) fusion(bf16[8,12,256,256]{3,2,1,0:T(8,128)(2,1)} %front_ref.1, s32[]{:T(128)S(6)} %select_n.381, s32[]{:T(128)S(6)} %select_n.385), kind=kLoop, calls=%fused_computation.107 | loop fusion | bytes 4194312 | tf_op jit(solution)/shard_map/jit(dynamic_index_in_dim)/dynamic_slice | solution.py:266
  16.3 2.2 %dynamic-slice_select_fusion = (bf16[1,12,256,256]{3,2,1,0:T(8,128)(2,1)S(1)}, bf16[1,12,256,256]{3,2,1,0:T(8,128)(2,1)S(1)}) fusion(bf16[8,12,256,256]{3,2,1,0:T(8,128)(2,1)} %front_ref.1, s32[]{:T(128)S(6)} %select_n.417, pred[12]{0:T(512)(128)(4,1)S(1)} %get-tuple-element.5, s32[]{:T(128)S(6)} %select_n.412, pred[12]{0:T(512)(128)(4,1)S(1)} %get-tuple-element.6), kind=kLoop, calls=%fused_computation.22 | loop fusion | flops 1572864 | bytes 6291488 | tf_op jit(solution)/shard_map/jit(_where)/select_n | solution.py:231
  18.5 1.5 fusion.21
  19.9 4.0 %collective-permute-start.17 = (bf16[2,4,192,256]{3,2,1,0:T(8,128)(2,1)}, bf16[2,4,192,256]{3,2,1,0:T(8,128)(2,1)}, u32[]{:S(2)}, u32[]{:S(2)}) collective-permute-start(bf16[2,4,192,256]{3,2,1,0:T(8,128)(2,1)} %get-tuple-element.32), channel_id=1, source_target_pairs={{0,96},{1,25},{2,98},{3,27},{4,100},{5,29},{6,102},{7,31},{8,104},... | collective-permute-start | bytes 2359304 | tf_op jit(solution)/shard_map/ppermute | solution.py:149
  24.0 1.5 collective-permute-start.16
  36.0 1.8 %broadcast_select_fusion.2 = bf16[2,256,256]{1,2,0:T(8,128)(2,1)} fusion(bf16[2,256,256]{1,2,0:T(8,128)(2,1)} %collective-permute-done.8, pred[2]{0:T(512)(128)(4,1)S(1)} %get-tuple-element.65, bf16[1,256,256]{1,2,0:T(8,128)(2,1)S(1)} %get-tuple-element.77, bf16[1,256,256]{1,2,0:T(8,128)(2,1)S(1)} %get-tuple-element.78), kind=kLoop, calls=%fused_computation.65 | loop fusion | flops 262144 | bytes 786434 | tf_op jit(solution)/shard_map/jit(_where)/select_n | solution.py:13
  38.9 9.3 %collective-permute-done.9 = bf16[2,256,256]{1,2,0:T(8,128)(2,1)} collective-permute-done((bf16[2,256,256]{1,2,0:T(8,128)(2,1)}, bf16[2,256,256]{1,2,0:T(8,128)(2,1)}, u32[]{:S(2)}, u32[]{:S(2)}) %collective-permute-start.9) | collective-permute-done | bytes 262176 | tf_op jit(solution)/shard_map/ppermute | solution.py:173
  48.2 1.8 %broadcast_select_fusion.3 = bf16[2,256,256]{1,2,0:T(8,128)(2,1)} fusion(bf16[2,256,256]{1,2,0:T(8,128)(2,1)} %collective-permute-done.9, pred[2]{0:T(512)(128)(4,1)S(1)} %get-tuple-element.61, bf16[2,256,256]{1,2,0:T(8,128)(2,1)} %collective-permute-done.8, bf16[1,256,256]{1,2,0:T(8,128)(2,1)S(1)} %get-tuple-element.77, ...), kind=kLoop, calls=%fused_computation.66 | loop fusion | flops 393216 | bytes 1048580 | tf_op jit(solution)/shard_map/jit(_where)/select_n | solution.py:13
  52.1 6.4 %collective-permute-done.10 = bf16[2,256,256]{1,2,0:T(8,128)(2,1)S(1)} collective-permute-done((bf16[2,256,256]{1,2,0:T(8,128)(2,1)}, bf16[2,256,256]{1,2,0:T(8,128)(2,1)S(1)}, u32[]{:S(2)}, u32[]{:S(2)}) %collective-permute-start.10) | collective-permute-done | bytes 262176 | tf_op jit(solution)/shard_map/ppermute | solution.py:173
  59.5 3.8 %collective-permute-start.11 = (bf16[2,256,256]{1,2,0:T(8,128)(2,1)S(1)}, bf16[2,256,256]{1,2,0:T(8,128)(2,1)S(1)}, u32[]{:S(2)}, u32[]{:S(2)}) collective-permute-start(bf16[2,256,256]{1,2,0:T(8,128)(2,1)S(1)} %broadcast_select_fusion.4), channel_id=1, source_target_pairs={{0,64},{1,65},{2,66},{3,67},{4,68},{5,69},{6,70},{7,71},{8,72},{9,... | collective-permute-start | bytes 786440 | tf_op jit(solution)/shard_map/ppermute | solution.py:173
  63.3 1.8 %fusion.18 = bf16[2,4,192,256]{3,2,1,0:T(8,128)(2,1)S(1)} fusion(bf16[1,4,4,192,256]{4,3,2,0,1:T(8,128)(2,1)S(1)} %bitcast.206, bf16[1,4,4,192,256]{4,3,2,0,1:T(8,128)(2,1)S(1)} %bitcast.204, bf16[2,4,192,256]{3,2,1,0:T(8,128)(2,1)} %collective-permute-done.15, bf16[2,4,192,256]{3,2,1,0:T(8,128)(2,1)} %collective-permute-done.16, ...), kind=kLoop, calls=%fused_computation.45 | loop fusion | flops 1572864 | bytes 6291462 | tf_op jit(solution)/shard_map/jit(_where)/select_n | solution.py:13
  65.2 1.2 collective-permute-start.20
  66.4 3.6 %collective-permute-start.19 = (bf16[2,192,256]{2,1,0:T(8,128)(2,1)S(1)}, bf16[2,192,256]{2,1,0:T(8,128)(2,1)S(1)}, u32[]{:S(2)}, u32[]{:S(2)}) collective-permute-start(bf16[2,192,256]{2,1,0:T(8,128)(2,1)S(1)} %get-tuple-element.52), channel_id=1, source_target_pairs={{0,16},{1,65},{2,18},{3,67},{4,20},{5,69},{6,22},{7,71},{8,24},{9,... | collective-permute-start | bytes 589832 | tf_op jit(solution)/shard_map/ppermute | solution.py:149
  70.0 2.2 %collective-permute-done.20 = bf16[2,192,256]{2,1,0:T(8,128)(2,1)S(1)} collective-permute-done((bf16[2,192,256]{2,1,0:T(8,128)(2,1)S(1)}, bf16[2,192,256]{2,1,0:T(8,128)(2,1)S(1)}, u32[]{:S(2)}, u32[]{:S(2)}) %collective-permute-start.20) | collective-permute-done | bytes 196640 | tf_op jit(solution)/shard_map/ppermute | solution.py:149
  72.2 3.6 %collective-permute-done.19 = bf16[2,192,256]{2,1,0:T(8,128)(2,1)S(1)} collective-permute-done((bf16[2,192,256]{2,1,0:T(8,128)(2,1)S(1)}, bf16[2,192,256]{2,1,0:T(8,128)(2,1)S(1)}, u32[]{:S(2)}, u32[]{:S(2)}) %collective-permute-start.19) | collective-permute-done | bytes 196640 | tf_op jit(solution)/shard_map/ppermute | solution.py:149
  77.9 2.1 %collective-permute-start.21 = (bf16[2,192,256]{2,1,0:T(8,128)(2,1)S(1)}, bf16[2,192,256]{2,1,0:T(8,128)(2,1)S(1)}, u32[]{:S(2)}, u32[]{:S(2)}) collective-permute-start(bf16[2,192,256]{2,1,0:T(8,128)(2,1)S(1)} %fusion.23), channel_id=1, source_target_pairs={{0,8},{1,33},{2,10},{3,35},{4,12},{5,37},{6,14},{7,39},{8,0},{9,41... | collective-permute-start | bytes 589832 | tf_op jit(solution)/shard_map/ppermute | solution.py:156
  80.1 3.3 %collective-permute-start.12 = (bf16[2,256,256]{1,2,0:T(8,128)(2,1)S(1)}, bf16[2,256,256]{1,2,0:T(8,128)(2,1)S(1)}, u32[]{:S(2)}, u32[]{:S(2)}) collective-permute-start(bf16[2,256,256]{1,2,0:T(8,128)(2,1)S(1)} %broadcast_select_fusion.5), channel_id=1, source_target_pairs={{0,4},{1,5},{2,6},{3,7},{4,0},{5,1},{6,2},{7,3},{8,12},{9,13},{10,... | collective-permute-start | bytes 786440 | tf_op jit(solution)/shard_map/ppermute | solution.py:173
  83.4 1.4 fusion.12
  86.5 3.2 %collective-permute-start.2 = (bf16[2,256,256]{2,1,0:T(8,128)(2,1)S(1)}, bf16[2,256,256]{2,1,0:T(8,128)(2,1)S(1)}, u32[]{:S(2)}, u32[]{:S(2)}) collective-permute-start(bf16[2,256,256]{2,1,0:T(8,128)(2,1)S(1)} %get-tuple-element.45), channel_id=1, source_target_pairs={{0,4},{1,5},{2,6},{3,7},{4,0},{5,1},{6,2},{7,3},{8,12},{9,13},{10,... | collective-permute-start | bytes 786440 | tf_op jit(solution)/shard_map/ppermute | solution.py:149
  90.3 2.4 %collective-permute-start.13 = (bf16[2,256,256]{1,2,0:T(8,128)(2,1)S(1)}, bf16[2,256,256]{1,2,0:T(8,128)(2,1)S(1)}, u32[]{:S(2)}, u32[]{:S(2)}) collective-permute-start(bf16[2,256,256]{1,2,0:T(8,128)(2,1)S(1)} %broadcast_select_fusion.6), channel_id=1, source_target_pairs={{0,2},{1,3},{2,0},{3,1},{4,6},{5,7},{6,4},{7,5},{8,10},{9,11},{10,... | collective-permute-start | bytes 786440 | tf_op jit(solution)/shard_map/ppermute | solution.py:173
  92.7 3.8 %collective-permute-done.3 = bf16[2,256,256]{2,1,0:T(8,128)(2,1)S(1)} collective-permute-done((bf16[2,256,256]{2,1,0:T(8,128)(2,1)S(1)}, bf16[2,256,256]{2,1,0:T(8,128)(2,1)S(1)}, u32[]{:S(2)}, u32[]{:S(2)}) %collective-permute-start.3) | collective-permute-done | bytes 262176 | tf_op jit(solution)/shard_map/ppermute | solution.py:149
  96.8 5.3 %collective-permute-done.2 = bf16[2,256,256]{2,1,0:T(8,128)(2,1)S(1)} collective-permute-done((bf16[2,256,256]{2,1,0:T(8,128)(2,1)S(1)}, bf16[2,256,256]{2,1,0:T(8,128)(2,1)S(1)}, u32[]{:S(2)}, u32[]{:S(2)}) %collective-permute-start.2) | collective-permute-done | bytes 262176 | tf_op jit(solution)/shard_map/ppermute | solution.py:149
  102.3 3.1 %collective-permute-start.6 = (bf16[2,256,256]{2,1,0:T(8,128)(2,1)S(1)}, bf16[2,256,256]{2,1,0:T(8,128)(2,1)S(1)}, u32[]{:S(2)}, u32[]{:S(2)}) collective-permute-start(bf16[2,256,256]{2,1,0:T(8,128)(2,1)S(1)} %fusion.22), channel_id=1, source_target_pairs={{0,6},{1,7},{2,4},{3,5},{4,2},{5,3},{6,0},{7,1},{8,14},{9,15},{10,... | collective-permute-start | bytes 786440 | tf_op jit(solution)/shard_map/ppermute | solution.py:156
  108.1 1.7 %collective-permute-start.25 = (bf16[2,4,192,256]{3,2,1,0:T(8,128)(2,1)S(1)}, bf16[2,4,192,256]{3,2,1,0:T(8,128)(2,1)S(1)}, u32[]{:S(2)}, u32[]{:S(2)}) collective-permute-start(bf16[2,4,192,256]{3,2,1,0:T(8,128)(2,1)S(1)} %pad_maximum_fusion.5), channel_id=1, source_target_pairs={{0,64},{1,17},{2,66},{3,19},{4,68},{5,21},{6,70},{7,23},{8,72},{9,... | collective-permute-start | bytes 2359304 | tf_op jit(solution)/shard_map/ppermute | solution.py:156
  109.9 1.7 %collective-permute-done.6 = bf16[2,256,256]{2,1,0:T(8,128)(2,1)S(1)} collective-permute-done((bf16[2,256,256]{2,1,0:T(8,128)(2,1)S(1)}, bf16[2,256,256]{2,1,0:T(8,128)(2,1)S(1)}, u32[]{:S(2)}, u32[]{:S(2)}) %collective-permute-start.6) | collective-permute-done | bytes 262176 | tf_op jit(solution)/shard_map/ppermute | solution.py:156
  111.7 1.4 collective-permute-start.24
  113.4 3.0 %collective-permute-done.4 = bf16[2,256,256]{2,1,0:T(8,128)(2,1)S(1)} collective-permute-done((bf16[2,256,256]{2,1,0:T(8,128)(2,1)S(1)}, bf16[2,256,256]{2,1,0:T(8,128)(2,1)S(1)}, u32[]{:S(2)}, u32[]{:S(2)}) %collective-permute-start.4) | collective-permute-done | bytes 262176 | tf_op jit(solution)/shard_map/ppermute | solution.py:156
  117.3 10.9 %collective-permute-done.26 = bf16[2,4,192,256]{3,2,1,0:T(8,128)(2,1)S(1)} collective-permute-done((bf16[2,4,192,256]{3,2,1,0:T(8,128)(2,1)S(1)}, bf16[2,4,192,256]{3,2,1,0:T(8,128)(2,1)S(1)}, u32[]{:S(2)}, u32[]{:S(2)}) %collective-permute-start.26) | collective-permute-done | bytes 786464 | tf_op jit(solution)/shard_map/ppermute | solution.py:156
  131.7 2.0 %fusion.4.u2_ref = bf16[12,256,256]{2,1,0:T(8,128)(2,1)} fusion(bf16[1,12,256,256]{3,2,1,0:T(8,128)(2,1)S(1)} %bitcast.207, f32[12,256,256]{1,2,0:T(8,128)S(1)} %fusion.24, pred[12]{0:T(512)(128)(4,1)S(1)} %get-tuple-element.11, pred[12]{0:T(512)(128)(4,1)S(1)} %get-tuple-element.9, bf16[256,256]{1,0:T(8,128)(2,1)S(1)} %fusion.8), kind=kLoop, calls=%fused_computation.21 | loop fusion | flops 3932160 | bytes 6422552 | tf_op jit(solution)/shard_map/squeeze | solution.py:294
  134.6 1.9 %select_convert_fusion.l2_ref = bf16[8,256,256]{2,1,0:T(8,128)(2,1)} fusion(pred[8]{0:T(512)(128)(4,1)S(1)} %get-tuple-element.67, bf16[8,1,256,256]{3,2,0,1:T(8,128)(2,1)S(1)} %bitcast.210, bf16[8,256,256]{2,1,0:T(8,128)(2,1)S(1)} %select_convert_fusion.1.l1_ref, pred[8]{0:T(512)(128)(4,1)S(1)} %get-tuple-element.66, ...), kind=kOutput, calls=%fused_computation.18 | convolution fusion | flops 540540928 | bytes 4457984 | tf_op jit(solution)/shard_map/iab,bc->iac/dot_general | solution.py:179
  136.5 16.7 %shard_map.46 = bf16[8,12,256,256]{3,2,1,0:T(8,128)(2,1)} custom-call(s32[8,12]{1,0:T(8,128)} %select_add_fusion.codes, bf16[8,12,256,256]{3,2,1,0:T(8,128)(2,1)} %front_ref.1, bf16[8,256,256]{2,1,0:T(8,128)(2,1)} %copy-done.6, bf16[8,256,256]{2,1,0:T(8,128)(2,1)} %select_convert_fusion.l2_ref, bf16[12,256,256]{2,1,0:T(8,128)(2,1)} %bitcast.202, ...), custom_call_target="tpu_custom_call" | custom-call | tf_op jit(solution)/shard_map/pallas_call | solution.py:216
  (106 shorter events, 30.1 us)
Async XLA Ops:
  8.5 7.1 %copy-start.7 = (s32[8,16,12,8]{1,0,3,2:T(8,128)}, s32[8,16,12,8]{1,0,3,2:T(8,128)S(1)}, u32[]{:S(2)}) copy-start(s32[8,16,12,8]{1,0,3,2:T(8,128)S(1)} %reshape.632) | copy-start | bytes 147460
  11.3 24.6 %collective-permute-start.8 = (bf16[2,256,256]{1,2,0:T(8,128)(2,1)}, bf16[2,256,256]{1,2,0:T(8,128)(2,1)}, u32[]{:S(2)}, u32[]{:S(2)}) collective-permute-start(bf16[2,256,256]{1,2,0:T(8,128)(2,1)} %pad_maximum_fusion.6), channel_id=1, source_target_pairs={{0,8},{1,9},{2,10},{3,11},{4,12},{5,13},{6,14},{7,15},{8,0},{9,1},... | collective-permute-start | bytes 786440 | tf_op jit(solution)/shard_map/ppermute | solution.py:173
  15.7 67.7 %collective-permute-start = (bf16[2,4,256,256]{3,2,1,0:T(8,128)(2,1)}, bf16[2,4,256,256]{3,2,1,0:T(8,128)(2,1)}, u32[]{:S(2)}, u32[]{:S(2)}) collective-permute-start(bf16[2,4,256,256]{3,2,1,0:T(8,128)(2,1)} %fusion.13), channel_id=1, source_target_pairs={{0,1},{1,0},{2,3},{3,2},{4,5},{5,4},{6,7},{7,6},{8,9},{9,8},{10,11... | collective-permute-start | bytes 3145736 | tf_op jit(solution)/shard_map/ppermute | solution.py:149
  18.4 12.7 %copy-start.5 = (s32[128,96]{0,1:T(8,128)S(1)}, s32[128,96]{0,1:T(8,128)}, u32[]{:S(2)}) copy-start(s32[128,96]{0,1:T(8,128)} %param.5) | copy-start | bytes 147460
  19.9 43.4 %collective-permute-start.17 = (bf16[2,4,192,256]{3,2,1,0:T(8,128)(2,1)}, bf16[2,4,192,256]{3,2,1,0:T(8,128)(2,1)}, u32[]{:S(2)}, u32[]{:S(2)}) collective-permute-start(bf16[2,4,192,256]{3,2,1,0:T(8,128)(2,1)} %get-tuple-element.32), channel_id=1, source_target_pairs={{0,96},{1,25},{2,98},{3,27},{4,100},{5,29},{6,102},{7,31},{8,104},... | collective-permute-start | bytes 2359304 | tf_op jit(solution)/shard_map/ppermute | solution.py:149
  24.0 39.3 %collective-permute-start.15 = (bf16[2,4,192,256]{3,2,1,0:T(8,128)(2,1)}, bf16[2,4,192,256]{3,2,1,0:T(8,128)(2,1)}, u32[]{:S(2)}, u32[]{:S(2)}) collective-permute-start(bf16[2,4,192,256]{3,2,1,0:T(8,128)(2,1)} %get-tuple-element.33), channel_id=1, source_target_pairs={{0,32},{1,9},{2,34},{3,11},{4,36},{5,13},{6,38},{7,15},{8,40},{9,1... | collective-permute-start | bytes 2359304 | tf_op jit(solution)/shard_map/ppermute | solution.py:149
  24.0 39.3 %collective-permute-start.16 = (bf16[2,4,192,256]{3,2,1,0:T(8,128)(2,1)}, bf16[2,4,192,256]{3,2,1,0:T(8,128)(2,1)}, u32[]{:S(2)}, u32[]{:S(2)}) collective-permute-start(bf16[2,4,192,256]{3,2,1,0:T(8,128)(2,1)} %get-tuple-element.34), channel_id=1, source_target_pairs={{0,64},{1,17},{2,66},{3,19},{4,68},{5,21},{6,70},{7,23},{8,72},{9,... | collective-permute-start | bytes 2359304 | tf_op jit(solution)/shard_map/ppermute | solution.py:149
  37.7 10.5 %collective-permute-start.9 = (bf16[2,256,256]{1,2,0:T(8,128)(2,1)}, bf16[2,256,256]{1,2,0:T(8,128)(2,1)}, u32[]{:S(2)}, u32[]{:S(2)}) collective-permute-start(bf16[2,256,256]{1,2,0:T(8,128)(2,1)} %broadcast_select_fusion.2), channel_id=1, source_target_pairs={{0,16},{1,17},{2,18},{3,19},{4,20},{5,21},{6,22},{7,23},{8,24},{9,... | collective-permute-start | bytes 786440 | tf_op jit(solution)/shard_map/ppermute | solution.py:173
  50.1 8.4 %collective-permute-start.10 = (bf16[2,256,256]{1,2,0:T(8,128)(2,1)}, bf16[2,256,256]{1,2,0:T(8,128)(2,1)S(1)}, u32[]{:S(2)}, u32[]{:S(2)}) collective-permute-start(bf16[2,256,256]{1,2,0:T(8,128)(2,1)} %broadcast_select_fusion.3), channel_id=1, source_target_pairs={{0,32},{1,33},{2,34},{3,35},{4,36},{5,37},{6,38},{7,39},{8,40},{9,... | collective-permute-start | bytes 786440 | tf_op jit(solution)/shard_map/ppermute | solution.py:173
  59.5 20.5 %collective-permute-start.11 = (bf16[2,256,256]{1,2,0:T(8,128)(2,1)S(1)}, bf16[2,256,256]{1,2,0:T(8,128)(2,1)S(1)}, u32[]{:S(2)}, u32[]{:S(2)}) collective-permute-start(bf16[2,256,256]{1,2,0:T(8,128)(2,1)S(1)} %broadcast_select_fusion.4), channel_id=1, source_target_pairs={{0,64},{1,65},{2,66},{3,67},{4,68},{5,69},{6,70},{7,71},{8,72},{9,... | collective-permute-start | bytes 786440 | tf_op jit(solution)/shard_map/ppermute | solution.py:173
  65.1 18.3 %copy-start.2 = (bf16[1,2,4,256,256]{4,3,2,0,1:T(8,128)(2,1)S(1)}, bf16[1,2,4,256,256]{4,3,2,0,1:T(8,128)(2,1)}, u32[]{:S(2)}) copy-start(bf16[1,2,4,256,256]{4,3,2,0,1:T(8,128)(2,1)} %copy-done.1) | copy-start | bytes 3145732
  65.1 18.3 %copy-start.4 = (bf16[1,2,4,256,256]{4,3,2,0,1:T(8,128)(2,1)S(1)}, bf16[1,2,4,256,256]{4,3,2,0,1:T(8,128)(2,1)}, u32[]{:S(2)}) copy-start(bf16[1,2,4,256,256]{4,3,2,0,1:T(8,128)(2,1)} %copy-done.3) | copy-start | bytes 3145732
  65.2 7.0 %collective-permute-start.20 = (bf16[2,192,256]{2,1,0:T(8,128)(2,1)S(1)}, bf16[2,192,256]{2,1,0:T(8,128)(2,1)S(1)}, u32[]{:S(2)}, u32[]{:S(2)}) collective-permute-start(bf16[2,192,256]{2,1,0:T(8,128)(2,1)S(1)} %get-tuple-element.50), channel_id=1, source_target_pairs={{0,24},{1,97},{2,26},{3,99},{4,28},{5,101},{6,30},{7,103},{8,16},{... | collective-permute-start | bytes 589832 | tf_op jit(solution)/shard_map/ppermute | solution.py:149
  66.4 5.7 %collective-permute-start.18 = (bf16[2,192,256]{2,1,0:T(8,128)(2,1)S(1)}, bf16[2,192,256]{2,1,0:T(8,128)(2,1)S(1)}, u32[]{:S(2)}, u32[]{:S(2)}) collective-permute-start(bf16[2,192,256]{2,1,0:T(8,128)(2,1)S(1)} %get-tuple-element.51), channel_id=1, source_target_pairs={{0,8},{1,33},{2,10},{3,35},{4,12},{5,37},{6,14},{7,39},{8,0},{9,41... | collective-permute-start | bytes 589832 | tf_op jit(solution)/shard_map/ppermute | solution.py:149
  66.4 9.3 %collective-permute-start.19 = (bf16[2,192,256]{2,1,0:T(8,128)(2,1)S(1)}, bf16[2,192,256]{2,1,0:T(8,128)(2,1)S(1)}, u32[]{:S(2)}, u32[]{:S(2)}) collective-permute-start(bf16[2,192,256]{2,1,0:T(8,128)(2,1)S(1)} %get-tuple-element.52), channel_id=1, source_target_pairs={{0,16},{1,65},{2,18},{3,67},{4,20},{5,69},{6,22},{7,71},{8,24},{9,... | collective-permute-start | bytes 589832 | tf_op jit(solution)/shard_map/ppermute | solution.py:149
  75.8 10.2 %collective-permute-start.23 = (bf16[2,192,256]{2,1,0:T(8,128)(2,1)S(1)}, bf16[2,192,256]{2,1,0:T(8,128)(2,1)S(1)}, u32[]{:S(2)}, u32[]{:S(2)}) collective-permute-start(bf16[2,192,256]{2,1,0:T(8,128)(2,1)S(1)} %fusion.23), channel_id=1, source_target_pairs={{0,24},{1,97},{2,26},{3,99},{4,28},{5,101},{6,30},{7,103},{8,16},{... | collective-permute-start | bytes 589832 | tf_op jit(solution)/shard_map/ppermute | solution.py:156
  77.1 9.4 %collective-permute-start.22 = (bf16[2,192,256]{2,1,0:T(8,128)(2,1)S(1)}, bf16[2,192,256]{2,1,0:T(8,128)(2,1)S(1)}, u32[]{:S(2)}, u32[]{:S(2)}) collective-permute-start(bf16[2,192,256]{2,1,0:T(8,128)(2,1)S(1)} %fusion.23), channel_id=1, source_target_pairs={{0,16},{1,65},{2,18},{3,67},{4,20},{5,69},{6,22},{7,71},{8,24},{9,... | collective-permute-start | bytes 589832 | tf_op jit(solution)/shard_map/ppermute | solution.py:156
  77.9 11.8 %collective-permute-start.21 = (bf16[2,192,256]{2,1,0:T(8,128)(2,1)S(1)}, bf16[2,192,256]{2,1,0:T(8,128)(2,1)S(1)}, u32[]{:S(2)}, u32[]{:S(2)}) collective-permute-start(bf16[2,192,256]{2,1,0:T(8,128)(2,1)S(1)} %fusion.23), channel_id=1, source_target_pairs={{0,8},{1,33},{2,10},{3,35},{4,12},{5,37},{6,14},{7,39},{8,0},{9,41... | collective-permute-start | bytes 589832 | tf_op jit(solution)/shard_map/ppermute | solution.py:156
  80.1 10.1 %collective-permute-start.12 = (bf16[2,256,256]{1,2,0:T(8,128)(2,1)S(1)}, bf16[2,256,256]{1,2,0:T(8,128)(2,1)S(1)}, u32[]{:S(2)}, u32[]{:S(2)}) collective-permute-start(bf16[2,256,256]{1,2,0:T(8,128)(2,1)S(1)} %broadcast_select_fusion.5), channel_id=1, source_target_pairs={{0,4},{1,5},{2,6},{3,7},{4,0},{5,1},{6,2},{7,3},{8,12},{9,13},{10,... | collective-permute-start | bytes 786440 | tf_op jit(solution)/shard_map/ppermute | solution.py:173
  84.9 11.6 %collective-permute-start.3 = (bf16[2,256,256]{2,1,0:T(8,128)(2,1)S(1)}, bf16[2,256,256]{2,1,0:T(8,128)(2,1)S(1)}, u32[]{:S(2)}, u32[]{:S(2)}) collective-permute-start(bf16[2,256,256]{2,1,0:T(8,128)(2,1)S(1)} %get-tuple-element.43), channel_id=1, source_target_pairs={{0,6},{1,7},{2,4},{3,5},{4,2},{5,3},{6,0},{7,1},{8,14},{9,15},{10,... | collective-permute-start | bytes 786440 | tf_op jit(solution)/shard_map/ppermute | solution.py:149
  86.0 10.8 %collective-permute-start.1 = (bf16[2,256,256]{2,1,0:T(8,128)(2,1)S(1)}, bf16[2,256,256]{2,1,0:T(8,128)(2,1)S(1)}, u32[]{:S(2)}, u32[]{:S(2)}) collective-permute-start(bf16[2,256,256]{2,1,0:T(8,128)(2,1)S(1)} %get-tuple-element.44), channel_id=1, source_target_pairs={{0,2},{1,3},{2,0},{3,1},{4,6},{5,7},{6,4},{7,5},{8,10},{9,11},{10,... | collective-permute-start | bytes 786440 | tf_op jit(solution)/shard_map/ppermute | solution.py:149
  86.5 15.7 %collective-permute-start.2 = (bf16[2,256,256]{2,1,0:T(8,128)(2,1)S(1)}, bf16[2,256,256]{2,1,0:T(8,128)(2,1)S(1)}, u32[]{:S(2)}, u32[]{:S(2)}) collective-permute-start(bf16[2,256,256]{2,1,0:T(8,128)(2,1)S(1)} %get-tuple-element.45), channel_id=1, source_target_pairs={{0,4},{1,5},{2,6},{3,7},{4,0},{5,1},{6,2},{7,3},{8,12},{9,13},{10,... | collective-permute-start | bytes 786440 | tf_op jit(solution)/shard_map/ppermute | solution.py:149
  90.3 17.8 %collective-permute-start.13 = (bf16[2,256,256]{1,2,0:T(8,128)(2,1)S(1)}, bf16[2,256,256]{1,2,0:T(8,128)(2,1)S(1)}, u32[]{:S(2)}, u32[]{:S(2)}) collective-permute-start(bf16[2,256,256]{1,2,0:T(8,128)(2,1)S(1)} %broadcast_select_fusion.6), channel_id=1, source_target_pairs={{0,2},{1,3},{2,0},{3,1},{4,6},{5,7},{6,4},{7,5},{8,10},{9,11},{10,... | collective-permute-start | bytes 786440 | tf_op jit(solution)/shard_map/ppermute | solution.py:173
  102.3 9.4 %collective-permute-start.6 = (bf16[2,256,256]{2,1,0:T(8,128)(2,1)S(1)}, bf16[2,256,256]{2,1,0:T(8,128)(2,1)S(1)}, u32[]{:S(2)}, u32[]{:S(2)}) collective-permute-start(bf16[2,256,256]{2,1,0:T(8,128)(2,1)S(1)} %fusion.22), channel_id=1, source_target_pairs={{0,6},{1,7},{2,4},{3,5},{4,2},{5,3},{6,0},{7,1},{8,14},{9,15},{10,... | collective-permute-start | bytes 786440 | tf_op jit(solution)/shard_map/ppermute | solution.py:156
  105.4 8.0 %collective-permute-start.5 = (bf16[2,256,256]{2,1,0:T(8,128)(2,1)S(1)}, bf16[2,256,256]{2,1,0:T(8,128)(2,1)S(1)}, u32[]{:S(2)}, u32[]{:S(2)}) collective-permute-start(bf16[2,256,256]{2,1,0:T(8,128)(2,1)S(1)} %fusion.22), channel_id=1, source_target_pairs={{0,4},{1,5},{2,6},{3,7},{4,0},{5,1},{6,2},{7,3},{8,12},{9,13},{10,... | collective-permute-start | bytes 786440 | tf_op jit(solution)/shard_map/ppermute | solution.py:156
  106.0 10.4 %collective-permute-start.4 = (bf16[2,256,256]{2,1,0:T(8,128)(2,1)S(1)}, bf16[2,256,256]{2,1,0:T(8,128)(2,1)S(1)}, u32[]{:S(2)}, u32[]{:S(2)}) collective-permute-start(bf16[2,256,256]{2,1,0:T(8,128)(2,1)S(1)} %fusion.22), channel_id=1, source_target_pairs={{0,2},{1,3},{2,0},{3,1},{4,6},{5,7},{6,4},{7,5},{8,10},{9,11},{10,... | collective-permute-start | bytes 786440 | tf_op jit(solution)/shard_map/ppermute | solution.py:156
  106.6 21.7 %collective-permute-start.26 = (bf16[2,4,192,256]{3,2,1,0:T(8,128)(2,1)S(1)}, bf16[2,4,192,256]{3,2,1,0:T(8,128)(2,1)S(1)}, u32[]{:S(2)}, u32[]{:S(2)}) collective-permute-start(bf16[2,4,192,256]{3,2,1,0:T(8,128)(2,1)S(1)} %pad_maximum_fusion.5), channel_id=1, source_target_pairs={{0,96},{1,25},{2,98},{3,27},{4,100},{5,29},{6,102},{7,31},{8,104},... | collective-permute-start | bytes 2359304 | tf_op jit(solution)/shard_map/ppermute | solution.py:156
  108.1 20.2 %collective-permute-start.25 = (bf16[2,4,192,256]{3,2,1,0:T(8,128)(2,1)S(1)}, bf16[2,4,192,256]{3,2,1,0:T(8,128)(2,1)S(1)}, u32[]{:S(2)}, u32[]{:S(2)}) collective-permute-start(bf16[2,4,192,256]{3,2,1,0:T(8,128)(2,1)S(1)} %pad_maximum_fusion.5), channel_id=1, source_target_pairs={{0,64},{1,17},{2,66},{3,19},{4,68},{5,21},{6,70},{7,23},{8,72},{9,... | collective-permute-start | bytes 2359304 | tf_op jit(solution)/shard_map/ppermute | solution.py:156
  109.9 7.2 %copy-start.8 = (bf16[2,256,256]{2,1,0:T(8,128)(2,1)S(1)}, bf16[2,256,256]{2,1,0:T(8,128)(2,1)}, u32[]{:S(2)}) copy-start(bf16[2,256,256]{2,1,0:T(8,128)(2,1)} %param.7) | copy-start | bytes 786436
  111.7 17.5 %collective-permute-start.24 = (bf16[2,4,192,256]{3,2,1,0:T(8,128)(2,1)S(1)}, bf16[2,4,192,256]{3,2,1,0:T(8,128)(2,1)S(1)}, u32[]{:S(2)}, u32[]{:S(2)}) collective-permute-start(bf16[2,4,192,256]{3,2,1,0:T(8,128)(2,1)S(1)} %pad_maximum_fusion.5), channel_id=1, source_target_pairs={{0,32},{1,9},{2,34},{3,11},{4,36},{5,13},{6,38},{7,15},{8,40},{9,1... | collective-permute-start | bytes 2359304 | tf_op jit(solution)/shard_map/ppermute | solution.py:156
  113.4 3.6 %collective-permute-start.14 = (bf16[2,256,256]{1,2,0:T(8,128)(2,1)S(1)}, bf16[2,256,256]{1,2,0:T(8,128)(2,1)S(1)}, u32[]{:S(2)}, u32[]{:S(2)}) collective-permute-start(bf16[2,256,256]{1,2,0:T(8,128)(2,1)S(1)} %broadcast_select_fusion.7), channel_id=1, source_target_pairs={{0,1},{1,0},{2,3},{3,2},{4,5},{5,4},{6,7},{7,6},{8,9},{9,8},{10,11... | collective-permute-start | bytes 786440 | tf_op jit(solution)/shard_map/ppermute | solution.py:173
  116.7 17.0 %collective-permute-start.7 = (bf16[2,4,256,256]{3,2,1,0:T(8,128)(2,1)S(1)}, bf16[2,4,256,256]{3,2,1,0:T(8,128)(2,1)S(1)}, u32[]{:S(2)}, u32[]{:S(2)}) collective-permute-start(bf16[2,4,256,256]{3,2,1,0:T(8,128)(2,1)S(1)} %pad_maximum_fusion.3), channel_id=1, source_target_pairs={{0,1},{1,0},{2,3},{3,2},{4,5},{5,4},{6,7},{7,6},{8,9},{9,8},{10,11... | collective-permute-start | bytes 3145736 | tf_op jit(solution)/shard_map/ppermute | solution.py:156
  (4 other events, 6.6 us)

commit v14 on v12

--- a/solution.py
+++ b/solution.py
@@ -187,10 +187,19 @@
     return jnp.where(place[:, :, None, None], lower[:, None], result)
 
 
-def update_kernel(codes, front_ref, l1_ref, l2_ref, u1_ref, u2_ref, out_ref):
+def update_kernel(
+    codes, row_codes, front_ref, c1_ref, c2_ref, x_ref, p1_ref, p2_ref, u1_ref, u2_ref, out_ref
+):
     i = pl.program_id(0)
-    lower1 = l1_ref[0]
-    lower2 = l2_ref[0]
+    row_code = row_codes[i]
+    lower1 = jnp.dot(c1_ref[0], p1_ref[...], preferred_element_type=jnp.float32).astype(jnp.bfloat16)
+    lower1 = jnp.where((row_code & 1) != 0, lower1, jnp.zeros_like(lower1))
+    column = c2_ref[0]
+    product = jnp.dot(lower1, x_ref[...], preferred_element_type=jnp.float32)
+    changed = (column.astype(jnp.float32) - product).astype(jnp.bfloat16)
+    column = jnp.where((row_code & 4) != 0, changed, column)
+    lower2 = jnp.dot(column, p2_ref[...], preferred_element_type=jnp.float32).astype(jnp.bfloat16)
+    lower2 = jnp.where((row_code & 2) != 0, lower2, jnp.zeros_like(lower2))
     for j in range(front_ref.shape[1]):
         code = codes[i, j]
         block = front_ref[0, j]
@@ -206,22 +215,26 @@
         out_ref[0, j] = block
 
 
-def both_updates(front, codes, lower1, lower2, upper1, upper2):
+def both_updates(front, codes, row_codes, column1, column2, cross, inverse, upper1, upper2):
     rows, cols, bs, _ = front.shape
-    row_block = pl.BlockSpec((1, cols, bs, bs), lambda i, c: (i, 0, 0, 0))
-    lower_block = pl.BlockSpec((1, bs, bs), lambda i, c: (i, 0, 0))
-    upper_block = pl.BlockSpec((cols, bs, bs), lambda i, c: (0, 0, 0))
+    row_block = pl.BlockSpec((1, cols, bs, bs), lambda i, c, r: (i, 0, 0, 0))
+    lower_block = pl.BlockSpec((1, bs, bs), lambda i, c, r: (i, 0, 0))
+    one_block = pl.BlockSpec((bs, bs), lambda i, c, r: (0, 0))
+    upper_block = pl.BlockSpec((cols, bs, bs), lambda i, c, r: (0, 0, 0))
     return pl.pallas_call(
         update_kernel,
         grid_spec=pltpu.PrefetchScalarGridSpec(
-            num_scalar_prefetch=1,
+            num_scalar_prefetch=2,
             grid=(rows,),
-            in_specs=[row_block, lower_block, lower_block, upper_block, upper_block],
+            in_specs=[
+                row_block, lower_block, lower_block, one_block, one_block, one_block,
+                upper_block, upper_block,
+            ],
             out_specs=row_block,
         ),
         out_shape=jax.ShapeDtypeStruct(front.shape, front.dtype),
         compiler_params=pltpu.CompilerParams(dimension_semantics=("arbitrary",)),
-    )(codes, front, lower1, lower2, upper1, upper2)
+    )(codes, row_codes, front, column1, column2, cross, inverse[0], inverse[1], upper1, upper2)
 
 
 def masked(blocks, keep):
@@ -267,7 +280,6 @@
 
     cols_sent = xor_bcast(jnp.stack([local_col(b1), local_col(b2)]), jnp.stack([c1, c2]), False)
     rows_sent = xor_bcast(jnp.stack([local_row(a1), local_row(a2)]), jnp.stack([r1, r2]), True)
-    lower_first = lower_local(cols_sent[0], pivot_inv[0], rows_first)
     second_col = cols_sent[1]
     upper_first, second_row = rows_sent[0], rows_sent[1]
 
@@ -290,17 +302,11 @@
         front_cols,
     )
     upper_second = row_after[0]
-    col_after = eliminate(
-        second_col[:, None],
-        lower_first,
-        first_at_second[None],
-        first,
-        rows_first,
-        second_ok,
-        pattern[front_rows, second][:, None],
-        second[None],
-    )
-    lower_second = lower_local(col_after[:, 0], pivot_inv[1], rows_second)
+    row_codes = (
+        rows_first.astype(jnp.int32)
+        + 2 * rows_second.astype(jnp.int32)
+        + 4 * (rows_first & second_ok[0] & (pattern[front_rows, second] > 0)).astype(jnp.int32)
+    )
 
     keep = local > 0
     update_first = rows_first[:, None] & cols_first[None, :] & keep
@@ -314,7 +320,10 @@
         + 8 * update_second.astype(jnp.int32)
         + 16 * place_second.astype(jnp.int32)
     )
-    return both_updates(front, codes, lower_first, lower_second, upper_first, upper_second)
+    return both_updates(
+        front, codes, row_codes, cols_sent[0], second_col, first_at_second, pivot_inv,
+        upper_first, upper_second,
+    )
 
 
 def solution(mesh):

time: 154 us -> 151 us (0.981)
  matrix products: 3.09 us -> 0.77 us
  starting transfers between devices: 44.8 us -> 43.1 us
    ppermute x7, waiting for transfers between devices: 28.6 us -> 25.8 us  [all_bcast(): lax.ppermute(value, ('row', 'col'), [(d, d ^ 1 << b) for d in range(n)])]
    ppermute x10, starting transfers between devices: 15.8 us -> 13.4 us  [xor_bcast(): lax.ppermute(buf, axes, digit_pairs(nrow, ncol, on_row, step, m))]
    squeeze x0 -> x2, local copies, waits for them, and re-layouts: none -> 2.36 us  [the longest x1 1.69 us: both_updates(): inverse[1]]
    dot_general x3 -> x1, matrix products: 2.51 us -> 0.19 us  [lower_local(): jnp.einsum('iab,bc->iac', column, inverse, preferred_element_type=jnp.flo...]
    add x0 -> x1, other arithmetic: none -> 1.77 us  [body(): rows_first.astype(jnp.int32) + 2 * rows_second.astype(jnp.int32)]
    select_n x11, other arithmetic: 8.52 us -> 6.85 us  [per_part(): return jnp.where(cond.reshape((-1,) + (1,) * (a.ndim - 1)), a, b)]
  transfers between devices with their start and end apart: 27 -> 27, of which waited for: 8 -> 8; matrix products, arithmetic and copies ran while one was open for 18% -> 19% of each run, Pallas kernels for 0% -> 0%
where the time goes in v14:
time: 151 us
  starting transfers between devices  43.1 us (29%)
  waiting for transfers between devices  42.9 us (28%)
  other arithmetic  24.5 us (16%)
  Pallas kernels  18.1 us (12%)
  local copies, waits for them, and re-layouts  10.6 us (7%)
  between operations  10.5 us (7%)
    ppermute x7, waiting for transfers between devices, all_bcast(): lax.ppermute(value, ('row', 'col'), [(d, d ^ 1 << b) for d in range(n)])  25.8 us
    ppermute x10, starting transfers between devices, xor_bcast(): lax.ppermute(groups[m], axes, digit_pairs(nrow, ncol, on_row, step, m))  19.6 us
    pallas_call x1, Pallas kernels, both_updates(): pl.pallas_call(update_kernel, grid_spec=pltpu.PrefetchScalarGridSpec(num_...  18.1 us
    ppermute x10, waiting for transfers between devices, xor_bcast(): lax.ppermute(groups[m], axes, digit_pairs(nrow, ncol, on_row, step, m))  13.6 us
    ppermute x10, starting transfers between devices, xor_bcast(): lax.ppermute(buf, axes, digit_pairs(nrow, ncol, on_row, step, m))  13.4 us
    ppermute x7, starting transfers between devices, all_bcast(): lax.ppermute(value, ('row', 'col'), [(d, d ^ 1 << b) for d in range(n)])  10.1 us
    select_n x11, other arithmetic, per_part(): return jnp.where(cond.reshape((-1,) + (1,) * (a.ndim - 1)), a, b)  6.85 us
    ppermute x10, waiting for transfers between devices, xor_bcast(): lax.ppermute(buf, axes, digit_pairs(nrow, ncol, on_row, step, m))  3.53 us
  transfers between devices with their start and end apart: 27, of which 8 were waited for; matrix products, arithmetic and copies ran while one was open for 19% of the time, Pallas kernels for 0%

profile of v14, /device:TPU:6, one launch (start us, length us, event | category | flops | bytes accessed | tf_op | source)
XLA Modules:
  0.0 150.5 jit_solution(16988029482654907949)
XLA Ops:
  11.2 1.7 %constant_dynamic-slice_fusion.1 = (bf16[8,1,256,256]{3,2,1,0:T(8,128)(2,1)S(1)}, bf16[8,1,256,256]{3,2,1,0:T(8,128)(2,1)S(1)}) fusion(bf16[8,12,256,256]{3,2,1,0:T(8,128)(2,1)} %front_ref.1, s32[]{:T(128)S(6)} %select_n.369, s32[]{:T(128)S(6)} %select_n.373), kind=kLoop, calls=%fused_computation.94 | loop fusion | bytes 4194312 | tf_op jit(solution)/shard_map/jit(dynamic_index_in_dim)/dynamic_slice | solution.py:277
  15.6 2.2 %dynamic-slice_select_fusion = (bf16[1,12,256,256]{3,2,1,0:T(8,128)(2,1)S(1)}, bf16[1,12,256,256]{3,2,1,0:T(8,128)(2,1)S(1)}) fusion(bf16[8,12,256,256]{3,2,1,0:T(8,128)(2,1)} %front_ref.1, s32[]{:T(128)S(6)} %select_n.402, pred[12]{0:T(512)(128)(4,1)S(1)} %get-tuple-element.5, s32[]{:T(128)S(6)} %select_n.397, pred[12]{0:T(512)(128)(4,1)S(1)} %get-tuple-element.6), kind=kLoop, calls=%fused_computation.18 | loop fusion | flops 1572864 | bytes 6291488 | tf_op jit(solution)/shard_map/jit(_where)/select_n | solution.py:242
  17.8 1.5 fusion.17
  19.3 4.0 %collective-permute-start.17 = (bf16[2,4,192,256]{3,2,1,0:T(8,128)(2,1)}, bf16[2,4,192,256]{3,2,1,0:T(8,128)(2,1)}, u32[]{:S(2)}, u32[]{:S(2)}) collective-permute-start(bf16[2,4,192,256]{3,2,1,0:T(8,128)(2,1)} %get-tuple-element.33), channel_id=1, source_target_pairs={{0,96},{1,25},{2,98},{3,27},{4,100},{5,29},{6,102},{7,31},{8,104},... | collective-permute-start | bytes 2359304 | tf_op jit(solution)/shard_map/ppermute | solution.py:149
  23.3 1.5 collective-permute-start.16
  30.3 1.8 %add_add_fusion = (s32[8]{0:T(128)}, pred[8]{0:T(512)(128)(4,1)S(1)}, pred[8]{0:T(512)(128)(4,1)S(1)}) fusion(s32[8]{0:T(128)S(1)} %gather_fusion, pred[]{:T(512)S(6)} %ne.98, s32[]{:T(128)} %bitcast.2, s32[]{:T(128)S(6)} %axis_index.15, s32[]{:T(128)} %bitcast.1), kind=kLoop, calls=%fused_computation.122 | loop fusion | flops 104 | bytes 93 | tf_op jit(solution)/shard_map/add | solution.py:306
  34.3 1.8 %broadcast_select_fusion.2 = bf16[2,256,256]{2,1,0:T(8,128)(2,1)} fusion(bf16[2,256,256]{2,1,0:T(8,128)(2,1)} %collective-permute-done.8, pred[2]{0:T(512)(128)(4,1)S(1)} %get-tuple-element.68, bf16[1,256,256]{2,1,0:T(8,128)(2,1)S(1)} %get-tuple-element.25, bf16[1,256,256]{2,1,0:T(8,128)(2,1)S(1)} %get-tuple-element.24), kind=kLoop, calls=%fused_computation.58 | loop fusion | flops 262144 | bytes 786434 | tf_op jit(solution)/shard_map/jit(_where)/select_n | solution.py:13
  36.0 1.6 %collective-permute-start.9 = (bf16[2,256,256]{2,1,0:T(8,128)(2,1)}, bf16[2,256,256]{2,1,0:T(8,128)(2,1)}, u32[]{:S(2)}, u32[]{:S(2)}) collective-permute-start(bf16[2,256,256]{2,1,0:T(8,128)(2,1)} %broadcast_select_fusion.2), channel_id=1, source_target_pairs={{0,2},{1,3},{2,0},{3,1},{4,6},{5,7},{6,4},{7,5},{8,10},{9,11},{10,... | collective-permute-start | bytes 786440 | tf_op jit(solution)/shard_map/ppermute | solution.py:171
  39.0 3.9 %collective-permute-done.9 = bf16[2,256,256]{2,1,0:T(8,128)(2,1)} collective-permute-done((bf16[2,256,256]{2,1,0:T(8,128)(2,1)}, bf16[2,256,256]{2,1,0:T(8,128)(2,1)}, u32[]{:S(2)}, u32[]{:S(2)}) %collective-permute-start.9) | collective-permute-done | bytes 262176 | tf_op jit(solution)/shard_map/ppermute | solution.py:171
  44.0 3.3 %collective-permute-start.10 = (bf16[2,256,256]{2,1,0:T(8,128)(2,1)S(1)}, bf16[2,256,256]{2,1,0:T(8,128)(2,1)S(1)}, u32[]{:S(2)}, u32[]{:S(2)}) collective-permute-start(bf16[2,256,256]{2,1,0:T(8,128)(2,1)S(1)} %broadcast_select_fusion.3), channel_id=1, source_target_pairs={{0,4},{1,5},{2,6},{3,7},{4,0},{5,1},{6,2},{7,3},{8,12},{9,13},{10,... | collective-permute-start | bytes 786440 | tf_op jit(solution)/shard_map/ppermute | solution.py:171
  47.4 1.7 %slice_bitcast_fusion.11 = (bf16[256,256]{1,0:T(8,128)(2,1)}, bf16[256,256]{1,0:T(8,128)(2,1)}) fusion(bf16[2,256,256]{2,1,0:T(8,128)(2,1)} %param.7), kind=kLoop, calls=%fused_computation.78 | loop fusion | bytes 524288 | tf_op jit(solution)/shard_map/squeeze | solution.py:237
  49.1 2.9 %collective-permute-done.10 = bf16[2,256,256]{2,1,0:T(8,128)(2,1)S(1)} collective-permute-done((bf16[2,256,256]{2,1,0:T(8,128)(2,1)S(1)}, bf16[2,256,256]{2,1,0:T(8,128)(2,1)S(1)}, u32[]{:S(2)}, u32[]{:S(2)}) %collective-permute-start.10) | collective-permute-done | bytes 262176 | tf_op jit(solution)/shard_map/ppermute | solution.py:171
  52.8 1.8 %fusion.14 = bf16[2,4,192,256]{3,2,1,0:T(8,128)(2,1)S(1)} fusion(bf16[1,4,4,192,256]{4,3,2,0,1:T(8,128)(2,1)S(1)} %bitcast.173, bf16[1,4,4,192,256]{4,3,2,0,1:T(8,128)(2,1)S(1)} %bitcast.171, bf16[2,4,192,256]{3,2,1,0:T(8,128)(2,1)} %collective-permute-done.15, bf16[2,4,192,256]{3,2,1,0:T(8,128)(2,1)} %collective-permute-done.16, ...), kind=kLoop, calls=%fused_computation.38 | loop fusion | flops 1572864 | bytes 6291462 | tf_op jit(solution)/shard_map/jit(_where)/select_n | solution.py:13
  56.3 3.2 %collective-permute-start.19 = (bf16[2,192,256]{2,1,0:T(8,128)(2,1)S(1)}, bf16[2,192,256]{2,1,0:T(8,128)(2,1)S(1)}, u32[]{:S(2)}, u32[]{:S(2)}) collective-permute-start(bf16[2,192,256]{2,1,0:T(8,128)(2,1)S(1)} %get-tuple-element.53), channel_id=1, source_target_pairs={{0,16},{1,65},{2,18},{3,67},{4,20},{5,69},{6,22},{7,71},{8,24},{9,... | collective-permute-start | bytes 589832 | tf_op jit(solution)/shard_map/ppermute | solution.py:149
  59.5 2.2 %collective-permute-done.20 = bf16[2,192,256]{2,1,0:T(8,128)(2,1)S(1)} collective-permute-done((bf16[2,192,256]{2,1,0:T(8,128)(2,1)S(1)}, bf16[2,192,256]{2,1,0:T(8,128)(2,1)S(1)}, u32[]{:S(2)}, u32[]{:S(2)}) %collective-permute-start.20) | collective-permute-done | bytes 196640 | tf_op jit(solution)/shard_map/ppermute | solution.py:149
  61.7 3.6 %collective-permute-done.19 = bf16[2,192,256]{2,1,0:T(8,128)(2,1)S(1)} collective-permute-done((bf16[2,192,256]{2,1,0:T(8,128)(2,1)S(1)}, bf16[2,192,256]{2,1,0:T(8,128)(2,1)S(1)}, u32[]{:S(2)}, u32[]{:S(2)}) %collective-permute-start.19) | collective-permute-done | bytes 196640 | tf_op jit(solution)/shard_map/ppermute | solution.py:149
  67.7 1.8 %collective-permute-start.21 = (bf16[2,192,256]{2,1,0:T(8,128)(2,1)S(1)}, bf16[2,192,256]{2,1,0:T(8,128)(2,1)S(1)}, u32[]{:S(2)}, u32[]{:S(2)}) collective-permute-start(bf16[2,192,256]{2,1,0:T(8,128)(2,1)S(1)} %fusion.19), channel_id=1, source_target_pairs={{0,8},{1,33},{2,10},{3,35},{4,12},{5,37},{6,14},{7,39},{8,0},{9,41... | collective-permute-start | bytes 589832 | tf_op jit(solution)/shard_map/ppermute | solution.py:156
  69.6 1.5 collective-permute-start.12
  72.6 3.7 %collective-permute-start.3 = (bf16[2,256,256]{2,1,0:T(8,128)(2,1)S(1)}, bf16[2,256,256]{2,1,0:T(8,128)(2,1)S(1)}, u32[]{:S(2)}, u32[]{:S(2)}) collective-permute-start(bf16[2,256,256]{2,1,0:T(8,128)(2,1)S(1)} %get-tuple-element.44), channel_id=1, source_target_pairs={{0,6},{1,7},{2,4},{3,5},{4,2},{5,3},{6,0},{7,1},{8,14},{9,15},{10,... | collective-permute-start | bytes 786440 | tf_op jit(solution)/shard_map/ppermute | solution.py:149
  77.2 1.6 %collective-permute-start.1 = (bf16[2,256,256]{2,1,0:T(8,128)(2,1)S(1)}, bf16[2,256,256]{2,1,0:T(8,128)(2,1)S(1)}, u32[]{:S(2)}, u32[]{:S(2)}) collective-permute-start(bf16[2,256,256]{2,1,0:T(8,128)(2,1)S(1)} %get-tuple-element.45), channel_id=1, source_target_pairs={{0,2},{1,3},{2,0},{3,1},{4,6},{5,7},{6,4},{7,5},{8,10},{9,11},{10,... | collective-permute-start | bytes 786440 | tf_op jit(solution)/shard_map/ppermute | solution.py:149
  78.8 3.5 %collective-permute-start.2 = (bf16[2,256,256]{2,1,0:T(8,128)(2,1)S(1)}, bf16[2,256,256]{2,1,0:T(8,128)(2,1)S(1)}, u32[]{:S(2)}, u32[]{:S(2)}) collective-permute-start(bf16[2,256,256]{2,1,0:T(8,128)(2,1)S(1)} %get-tuple-element.46), channel_id=1, source_target_pairs={{0,4},{1,5},{2,6},{3,7},{4,0},{5,1},{6,2},{7,3},{8,12},{9,13},{10,... | collective-permute-start | bytes 786440 | tf_op jit(solution)/shard_map/ppermute | solution.py:149
  83.7 7.8 %collective-permute-done.2 = bf16[2,256,256]{2,1,0:T(8,128)(2,1)S(1)} collective-permute-done((bf16[2,256,256]{2,1,0:T(8,128)(2,1)S(1)}, bf16[2,256,256]{2,1,0:T(8,128)(2,1)S(1)}, u32[]{:S(2)}, u32[]{:S(2)}) %collective-permute-start.2) | collective-permute-done | bytes 262176 | tf_op jit(solution)/shard_map/ppermute | solution.py:149
  91.7 1.4 collective-permute-start.5
  93.2 2.7 %collective-permute-start.4 = (bf16[2,256,256]{2,1,0:T(8,128)(2,1)S(1)}, bf16[2,256,256]{2,1,0:T(8,128)(2,1)S(1)}, u32[]{:S(2)}, u32[]{:S(2)}) collective-permute-start(bf16[2,256,256]{2,1,0:T(8,128)(2,1)S(1)} %fusion.18), channel_id=1, source_target_pairs={{0,2},{1,3},{2,0},{3,1},{4,6},{5,7},{6,4},{7,5},{8,10},{9,11},{10,... | collective-permute-start | bytes 786440 | tf_op jit(solution)/shard_map/ppermute | solution.py:156
  95.9 1.9 %collective-permute-start.26 = (bf16[2,4,192,256]{3,2,1,0:T(8,128)(2,1)S(1)}, bf16[2,4,192,256]{3,2,1,0:T(8,128)(2,1)S(1)}, u32[]{:S(2)}, u32[]{:S(2)}) collective-permute-start(bf16[2,4,192,256]{3,2,1,0:T(8,128)(2,1)S(1)} %pad_maximum_fusion.5), channel_id=1, source_target_pairs={{0,96},{1,25},{2,98},{3,27},{4,100},{5,29},{6,102},{7,31},{8,104},... | collective-permute-start | bytes 2359304 | tf_op jit(solution)/shard_map/ppermute | solution.py:156
  97.8 1.5 %collective-permute-start.25 = (bf16[2,4,192,256]{3,2,1,0:T(8,128)(2,1)S(1)}, bf16[2,4,192,256]{3,2,1,0:T(8,128)(2,1)S(1)}, u32[]{:S(2)}, u32[]{:S(2)}) collective-permute-start(bf16[2,4,192,256]{3,2,1,0:T(8,128)(2,1)S(1)} %pad_maximum_fusion.5), channel_id=1, source_target_pairs={{0,64},{1,17},{2,66},{3,19},{4,68},{5,21},{6,70},{7,23},{8,72},{9,... | collective-permute-start | bytes 2359304 | tf_op jit(solution)/shard_map/ppermute | solution.py:156
  99.5 2.6 %collective-permute-done.6 = bf16[2,256,256]{2,1,0:T(8,128)(2,1)S(1)} collective-permute-done((bf16[2,256,256]{2,1,0:T(8,128)(2,1)S(1)}, bf16[2,256,256]{2,1,0:T(8,128)(2,1)S(1)}, u32[]{:S(2)}, u32[]{:S(2)}) %collective-permute-start.6) | collective-permute-done | bytes 262176 | tf_op jit(solution)/shard_map/ppermute | solution.py:156
  103.4 2.0 %collective-permute-start.14 = (bf16[2,256,256]{2,1,0:T(8,128)(2,1)S(1)}, bf16[2,256,256]{2,1,0:T(8,128)(2,1)S(1)}, u32[]{:S(2)}, u32[]{:S(2)}) collective-permute-start(bf16[2,256,256]{2,1,0:T(8,128)(2,1)S(1)} %broadcast_select_fusion.7), channel_id=1, source_target_pairs={{0,64},{1,65},{2,66},{3,67},{4,68},{5,69},{6,70},{7,71},{8,72},{9,... | collective-permute-start | bytes 786440 | tf_op jit(solution)/shard_map/ppermute | solution.py:171
  106.1 19.0 %collective-permute-done.14 = bf16[2,256,256]{2,1,0:T(8,128)(2,1)S(1)} collective-permute-done((bf16[2,256,256]{2,1,0:T(8,128)(2,1)S(1)}, bf16[2,256,256]{2,1,0:T(8,128)(2,1)S(1)}, u32[]{:S(2)}, u32[]{:S(2)}) %collective-permute-start.14) | collective-permute-done | bytes 262176 | tf_op jit(solution)/shard_map/ppermute | solution.py:171
  128.6 2.0 %fusion.3.u2_ref = bf16[12,256,256]{2,1,0:T(8,128)(2,1)} fusion(bf16[1,12,256,256]{3,2,1,0:T(8,128)(2,1)S(1)} %bitcast.174, f32[12,256,256]{1,2,0:T(8,128)S(1)} %fusion.20, pred[12]{0:T(512)(128)(4,1)S(1)} %get-tuple-element.11, pred[12]{0:T(512)(128)(4,1)S(1)} %get-tuple-element.9, bf16[256,256]{1,0:T(8,128)(2,1)S(1)} %fusion.4), kind=kLoop, calls=%fused_computation.17 | loop fusion | flops 3932160 | bytes 6422552 | tf_op jit(solution)/shard_map/squeeze | solution.py:304
  130.8 1.5 %pad_maximum_fusion.1 = (bf16[1,2,4,256,256]{4,3,2,1,0:T(8,128)(2,1)}, bf16[1,2,4,256,256]{4,3,2,1,0:T(8,128)(2,1)}) fusion(bf16[2,1,4,256,256]{4,3,2,1,0:T(8,128)(2,1)S(1)} %get-tuple-element.36, bf16[2,1,4,256,256]{4,3,2,1,0:T(8,128)(2,1)S(1)} %get-tuple-element.37), kind=kLoop, calls=%fused_computation.26 | loop fusion | flops 1048576 | bytes 4194304 | tf_op jit(solution)/shard_map/stack | solution.py:159
  132.4 18.1 %shard_map.46 = bf16[8,12,256,256]{3,2,1,0:T(8,128)(2,1)} custom-call(s32[8,12]{1,0:T(8,128)} %select_add_fusion.codes, s32[8]{0:T(128)} %get-tuple-element.19.row_codes, bf16[8,12,256,256]{3,2,1,0:T(8,128)(2,1)} %front_ref.1, bf16[8,256,256]{2,1,0:T(8,128)(2,1)} %bitcast.178, bf16[8,256,256]{2,1,0:T(8,128)(2,1)} %bitcast.177, ...), custom_call_target="tpu_custom_call" | custom-call | tf_op jit(solution)/shard_map/pallas_call | solution.py:224
  (100 shorter events, 28.7 us)
Async XLA Ops:
  7.4 7.6 %copy-start.6 = (s32[8,16,12,8]{1,0,3,2:T(8,128)}, s32[8,16,12,8]{1,0,3,2:T(8,128)S(1)}, u32[]{:S(2)}) copy-start(s32[8,16,12,8]{1,0,3,2:T(8,128)S(1)} %reshape.568) | copy-start | bytes 147460
  11.0 23.3 %collective-permute-start.8 = (bf16[2,256,256]{2,1,0:T(8,128)(2,1)}, bf16[2,256,256]{2,1,0:T(8,128)(2,1)}, u32[]{:S(2)}, u32[]{:S(2)}) collective-permute-start(bf16[2,256,256]{2,1,0:T(8,128)(2,1)} %pad_maximum_fusion.6), channel_id=1, source_target_pairs={{0,1},{1,0},{2,3},{3,2},{4,5},{5,4},{6,7},{7,6},{8,9},{9,8},{10,11... | collective-permute-start | bytes 786440 | tf_op jit(solution)/shard_map/ppermute | solution.py:171
  14.5 56.6 %collective-permute-start = (bf16[2,4,256,256]{3,2,1,0:T(8,128)(2,1)}, bf16[2,4,256,256]{3,2,1,0:T(8,128)(2,1)}, u32[]{:S(2)}, u32[]{:S(2)}) collective-permute-start(bf16[2,4,256,256]{3,2,1,0:T(8,128)(2,1)} %fusion.9), channel_id=1, source_target_pairs={{0,1},{1,0},{2,3},{3,2},{4,5},{5,4},{6,7},{7,6},{8,9},{9,8},{10,11... | collective-permute-start | bytes 3145736 | tf_op jit(solution)/shard_map/ppermute | solution.py:149
  17.8 11.7 %copy-start.5 = (s32[128,96]{0,1:T(8,128)S(1)}, s32[128,96]{0,1:T(8,128)}, u32[]{:S(2)}) copy-start(s32[128,96]{0,1:T(8,128)} %param.5) | copy-start | bytes 147460
  19.3 33.5 %collective-permute-start.17 = (bf16[2,4,192,256]{3,2,1,0:T(8,128)(2,1)}, bf16[2,4,192,256]{3,2,1,0:T(8,128)(2,1)}, u32[]{:S(2)}, u32[]{:S(2)}) collective-permute-start(bf16[2,4,192,256]{3,2,1,0:T(8,128)(2,1)} %get-tuple-element.33), channel_id=1, source_target_pairs={{0,96},{1,25},{2,98},{3,27},{4,100},{5,29},{6,102},{7,31},{8,104},... | collective-permute-start | bytes 2359304 | tf_op jit(solution)/shard_map/ppermute | solution.py:149
  23.3 29.5 %collective-permute-start.15 = (bf16[2,4,192,256]{3,2,1,0:T(8,128)(2,1)}, bf16[2,4,192,256]{3,2,1,0:T(8,128)(2,1)}, u32[]{:S(2)}, u32[]{:S(2)}) collective-permute-start(bf16[2,4,192,256]{3,2,1,0:T(8,128)(2,1)} %get-tuple-element.34), channel_id=1, source_target_pairs={{0,32},{1,9},{2,34},{3,11},{4,36},{5,13},{6,38},{7,15},{8,40},{9,1... | collective-permute-start | bytes 2359304 | tf_op jit(solution)/shard_map/ppermute | solution.py:149
  23.3 29.5 %collective-permute-start.16 = (bf16[2,4,192,256]{3,2,1,0:T(8,128)(2,1)}, bf16[2,4,192,256]{3,2,1,0:T(8,128)(2,1)}, u32[]{:S(2)}, u32[]{:S(2)}) collective-permute-start(bf16[2,4,192,256]{3,2,1,0:T(8,128)(2,1)} %get-tuple-element.35), channel_id=1, source_target_pairs={{0,64},{1,17},{2,66},{3,19},{4,68},{5,21},{6,70},{7,23},{8,72},{9,... | collective-permute-start | bytes 2359304 | tf_op jit(solution)/shard_map/ppermute | solution.py:149
  36.0 6.9 %collective-permute-start.9 = (bf16[2,256,256]{2,1,0:T(8,128)(2,1)}, bf16[2,256,256]{2,1,0:T(8,128)(2,1)}, u32[]{:S(2)}, u32[]{:S(2)}) collective-permute-start(bf16[2,256,256]{2,1,0:T(8,128)(2,1)} %broadcast_select_fusion.2), channel_id=1, source_target_pairs={{0,2},{1,3},{2,0},{3,1},{4,6},{5,7},{6,4},{7,5},{8,10},{9,11},{10,... | collective-permute-start | bytes 786440 | tf_op jit(solution)/shard_map/ppermute | solution.py:171
  44.0 8.0 %collective-permute-start.10 = (bf16[2,256,256]{2,1,0:T(8,128)(2,1)S(1)}, bf16[2,256,256]{2,1,0:T(8,128)(2,1)S(1)}, u32[]{:S(2)}, u32[]{:S(2)}) collective-permute-start(bf16[2,256,256]{2,1,0:T(8,128)(2,1)S(1)} %broadcast_select_fusion.3), channel_id=1, source_target_pairs={{0,4},{1,5},{2,6},{3,7},{4,0},{5,1},{6,2},{7,3},{8,12},{9,13},{10,... | collective-permute-start | bytes 786440 | tf_op jit(solution)/shard_map/ppermute | solution.py:171
  52.1 17.4 %collective-permute-start.11 = (bf16[2,256,256]{2,1,0:T(8,128)(2,1)S(1)}, bf16[2,256,256]{2,1,0:T(8,128)(2,1)S(1)}, u32[]{:S(2)}, u32[]{:S(2)}) collective-permute-start(bf16[2,256,256]{2,1,0:T(8,128)(2,1)S(1)} %broadcast_select_fusion.4), channel_id=1, source_target_pairs={{0,8},{1,9},{2,10},{3,11},{4,12},{5,13},{6,14},{7,15},{8,0},{9,1},... | collective-permute-start | bytes 786440 | tf_op jit(solution)/shard_map/ppermute | solution.py:171
  54.6 16.5 %copy-start.2 = (bf16[1,2,4,256,256]{4,3,2,0,1:T(8,128)(2,1)S(1)}, bf16[1,2,4,256,256]{4,3,2,0,1:T(8,128)(2,1)}, u32[]{:S(2)}) copy-start(bf16[1,2,4,256,256]{4,3,2,0,1:T(8,128)(2,1)} %copy-done.1) | copy-start | bytes 3145732
  54.6 16.5 %copy-start.4 = (bf16[1,2,4,256,256]{4,3,2,0,1:T(8,128)(2,1)S(1)}, bf16[1,2,4,256,256]{4,3,2,0,1:T(8,128)(2,1)}, u32[]{:S(2)}) copy-start(bf16[1,2,4,256,256]{4,3,2,0,1:T(8,128)(2,1)} %copy-done.3) | copy-start | bytes 3145732
  54.7 7.0 %collective-permute-start.20 = (bf16[2,192,256]{2,1,0:T(8,128)(2,1)S(1)}, bf16[2,192,256]{2,1,0:T(8,128)(2,1)S(1)}, u32[]{:S(2)}, u32[]{:S(2)}) collective-permute-start(bf16[2,192,256]{2,1,0:T(8,128)(2,1)S(1)} %get-tuple-element.51), channel_id=1, source_target_pairs={{0,24},{1,97},{2,26},{3,99},{4,28},{5,101},{6,30},{7,103},{8,16},{... | collective-permute-start | bytes 589832 | tf_op jit(solution)/shard_map/ppermute | solution.py:149
  55.9 5.7 %collective-permute-start.18 = (bf16[2,192,256]{2,1,0:T(8,128)(2,1)S(1)}, bf16[2,192,256]{2,1,0:T(8,128)(2,1)S(1)}, u32[]{:S(2)}, u32[]{:S(2)}) collective-permute-start(bf16[2,192,256]{2,1,0:T(8,128)(2,1)S(1)} %get-tuple-element.52), channel_id=1, source_target_pairs={{0,8},{1,33},{2,10},{3,35},{4,12},{5,37},{6,14},{7,39},{8,0},{9,41... | collective-permute-start | bytes 589832 | tf_op jit(solution)/shard_map/ppermute | solution.py:149
  56.3 9.0 %collective-permute-start.19 = (bf16[2,192,256]{2,1,0:T(8,128)(2,1)S(1)}, bf16[2,192,256]{2,1,0:T(8,128)(2,1)S(1)}, u32[]{:S(2)}, u32[]{:S(2)}) collective-permute-start(bf16[2,192,256]{2,1,0:T(8,128)(2,1)S(1)} %get-tuple-element.53), channel_id=1, source_target_pairs={{0,16},{1,65},{2,18},{3,67},{4,20},{5,69},{6,22},{7,71},{8,24},{9,... | collective-permute-start | bytes 589832 | tf_op jit(solution)/shard_map/ppermute | solution.py:149
  65.3 11.9 %collective-permute-start.23 = (bf16[2,192,256]{2,1,0:T(8,128)(2,1)S(1)}, bf16[2,192,256]{2,1,0:T(8,128)(2,1)S(1)}, u32[]{:S(2)}, u32[]{:S(2)}) collective-permute-start(bf16[2,192,256]{2,1,0:T(8,128)(2,1)S(1)} %fusion.19), channel_id=1, source_target_pairs={{0,24},{1,97},{2,26},{3,99},{4,28},{5,101},{6,30},{7,103},{8,16},{... | collective-permute-start | bytes 589832 | tf_op jit(solution)/shard_map/ppermute | solution.py:156
  66.6 12.2 %collective-permute-start.22 = (bf16[2,192,256]{2,1,0:T(8,128)(2,1)S(1)}, bf16[2,192,256]{2,1,0:T(8,128)(2,1)S(1)}, u32[]{:S(2)}, u32[]{:S(2)}) collective-permute-start(bf16[2,192,256]{2,1,0:T(8,128)(2,1)S(1)} %fusion.19), channel_id=1, source_target_pairs={{0,16},{1,65},{2,18},{3,67},{4,20},{5,69},{6,22},{7,71},{8,24},{9,... | collective-permute-start | bytes 589832 | tf_op jit(solution)/shard_map/ppermute | solution.py:156
  67.7 14.6 %collective-permute-start.21 = (bf16[2,192,256]{2,1,0:T(8,128)(2,1)S(1)}, bf16[2,192,256]{2,1,0:T(8,128)(2,1)S(1)}, u32[]{:S(2)}, u32[]{:S(2)}) collective-permute-start(bf16[2,192,256]{2,1,0:T(8,128)(2,1)S(1)} %fusion.19), channel_id=1, source_target_pairs={{0,8},{1,33},{2,10},{3,35},{4,12},{5,37},{6,14},{7,39},{8,0},{9,41... | collective-permute-start | bytes 589832 | tf_op jit(solution)/shard_map/ppermute | solution.py:156
  69.6 12.9 %collective-permute-start.12 = (bf16[2,256,256]{2,1,0:T(8,128)(2,1)S(1)}, bf16[2,256,256]{2,1,0:T(8,128)(2,1)S(1)}, u32[]{:S(2)}, u32[]{:S(2)}) collective-permute-start(bf16[2,256,256]{2,1,0:T(8,128)(2,1)S(1)} %broadcast_select_fusion.5), channel_id=1, source_target_pairs={{0,16},{1,17},{2,18},{3,19},{4,20},{5,21},{6,22},{7,23},{8,24},{9,... | collective-permute-start | bytes 786440 | tf_op jit(solution)/shard_map/ppermute | solution.py:171
  72.6 11.0 %collective-permute-start.3 = (bf16[2,256,256]{2,1,0:T(8,128)(2,1)S(1)}, bf16[2,256,256]{2,1,0:T(8,128)(2,1)S(1)}, u32[]{:S(2)}, u32[]{:S(2)}) collective-permute-start(bf16[2,256,256]{2,1,0:T(8,128)(2,1)S(1)} %get-tuple-element.44), channel_id=1, source_target_pairs={{0,6},{1,7},{2,4},{3,5},{4,2},{5,3},{6,0},{7,1},{8,14},{9,15},{10,... | collective-permute-start | bytes 786440 | tf_op jit(solution)/shard_map/ppermute | solution.py:149
  77.2 6.4 %collective-permute-start.1 = (bf16[2,256,256]{2,1,0:T(8,128)(2,1)S(1)}, bf16[2,256,256]{2,1,0:T(8,128)(2,1)S(1)}, u32[]{:S(2)}, u32[]{:S(2)}) collective-permute-start(bf16[2,256,256]{2,1,0:T(8,128)(2,1)S(1)} %get-tuple-element.45), channel_id=1, source_target_pairs={{0,2},{1,3},{2,0},{3,1},{4,6},{5,7},{6,4},{7,5},{8,10},{9,11},{10,... | collective-permute-start | bytes 786440 | tf_op jit(solution)/shard_map/ppermute | solution.py:149
  78.8 12.7 %collective-permute-start.2 = (bf16[2,256,256]{2,1,0:T(8,128)(2,1)S(1)}, bf16[2,256,256]{2,1,0:T(8,128)(2,1)S(1)}, u32[]{:S(2)}, u32[]{:S(2)}) collective-permute-start(bf16[2,256,256]{2,1,0:T(8,128)(2,1)S(1)} %get-tuple-element.46), channel_id=1, source_target_pairs={{0,4},{1,5},{2,6},{3,7},{4,0},{5,1},{6,2},{7,3},{8,12},{9,13},{10,... | collective-permute-start | bytes 786440 | tf_op jit(solution)/shard_map/ppermute | solution.py:149
  82.6 15.3 %collective-permute-start.13 = (bf16[2,256,256]{2,1,0:T(8,128)(2,1)S(1)}, bf16[2,256,256]{2,1,0:T(8,128)(2,1)S(1)}, u32[]{:S(2)}, u32[]{:S(2)}) collective-permute-start(bf16[2,256,256]{2,1,0:T(8,128)(2,1)S(1)} %broadcast_select_fusion.6), channel_id=1, source_target_pairs={{0,32},{1,33},{2,34},{3,35},{4,36},{5,37},{6,38},{7,39},{8,40},{9,... | collective-permute-start | bytes 786440 | tf_op jit(solution)/shard_map/ppermute | solution.py:171
  91.6 10.5 %collective-permute-start.6 = (bf16[2,256,256]{2,1,0:T(8,128)(2,1)S(1)}, bf16[2,256,256]{2,1,0:T(8,128)(2,1)S(1)}, u32[]{:S(2)}, u32[]{:S(2)}) collective-permute-start(bf16[2,256,256]{2,1,0:T(8,128)(2,1)S(1)} %fusion.18), channel_id=1, source_target_pairs={{0,6},{1,7},{2,4},{3,5},{4,2},{5,3},{6,0},{7,1},{8,14},{9,15},{10,... | collective-permute-start | bytes 786440 | tf_op jit(solution)/shard_map/ppermute | solution.py:156
  91.7 11.7 %collective-permute-start.5 = (bf16[2,256,256]{2,1,0:T(8,128)(2,1)S(1)}, bf16[2,256,256]{2,1,0:T(8,128)(2,1)S(1)}, u32[]{:S(2)}, u32[]{:S(2)}) collective-permute-start(bf16[2,256,256]{2,1,0:T(8,128)(2,1)S(1)} %fusion.18), channel_id=1, source_target_pairs={{0,4},{1,5},{2,6},{3,7},{4,0},{5,1},{6,2},{7,3},{8,12},{9,13},{10,... | collective-permute-start | bytes 786440 | tf_op jit(solution)/shard_map/ppermute | solution.py:156
  93.2 12.3 %collective-permute-start.4 = (bf16[2,256,256]{2,1,0:T(8,128)(2,1)S(1)}, bf16[2,256,256]{2,1,0:T(8,128)(2,1)S(1)}, u32[]{:S(2)}, u32[]{:S(2)}) collective-permute-start(bf16[2,256,256]{2,1,0:T(8,128)(2,1)S(1)} %fusion.18), channel_id=1, source_target_pairs={{0,2},{1,3},{2,0},{3,1},{4,6},{5,7},{6,4},{7,5},{8,10},{9,11},{10,... | collective-permute-start | bytes 786440 | tf_op jit(solution)/shard_map/ppermute | solution.py:156
  95.9 30.1 %collective-permute-start.26 = (bf16[2,4,192,256]{3,2,1,0:T(8,128)(2,1)S(1)}, bf16[2,4,192,256]{3,2,1,0:T(8,128)(2,1)S(1)}, u32[]{:S(2)}, u32[]{:S(2)}) collective-permute-start(bf16[2,4,192,256]{3,2,1,0:T(8,128)(2,1)S(1)} %pad_maximum_fusion.5), channel_id=1, source_target_pairs={{0,96},{1,25},{2,98},{3,27},{4,100},{5,29},{6,102},{7,31},{8,104},... | collective-permute-start | bytes 2359304 | tf_op jit(solution)/shard_map/ppermute | solution.py:156
  97.8 28.2 %collective-permute-start.25 = (bf16[2,4,192,256]{3,2,1,0:T(8,128)(2,1)S(1)}, bf16[2,4,192,256]{3,2,1,0:T(8,128)(2,1)S(1)}, u32[]{:S(2)}, u32[]{:S(2)}) collective-permute-start(bf16[2,4,192,256]{3,2,1,0:T(8,128)(2,1)S(1)} %pad_maximum_fusion.5), channel_id=1, source_target_pairs={{0,64},{1,17},{2,66},{3,19},{4,68},{5,21},{6,70},{7,23},{8,72},{9,... | collective-permute-start | bytes 2359304 | tf_op jit(solution)/shard_map/ppermute | solution.py:156
  102.1 24.0 %collective-permute-start.24 = (bf16[2,4,192,256]{3,2,1,0:T(8,128)(2,1)S(1)}, bf16[2,4,192,256]{3,2,1,0:T(8,128)(2,1)S(1)}, u32[]{:S(2)}, u32[]{:S(2)}) collective-permute-start(bf16[2,4,192,256]{3,2,1,0:T(8,128)(2,1)S(1)} %pad_maximum_fusion.5), channel_id=1, source_target_pairs={{0,32},{1,9},{2,34},{3,11},{4,36},{5,13},{6,38},{7,15},{8,40},{9,1... | collective-permute-start | bytes 2359304 | tf_op jit(solution)/shard_map/ppermute | solution.py:156
  103.4 21.7 %collective-permute-start.14 = (bf16[2,256,256]{2,1,0:T(8,128)(2,1)S(1)}, bf16[2,256,256]{2,1,0:T(8,128)(2,1)S(1)}, u32[]{:S(2)}, u32[]{:S(2)}) collective-permute-start(bf16[2,256,256]{2,1,0:T(8,128)(2,1)S(1)} %broadcast_select_fusion.7), channel_id=1, source_target_pairs={{0,64},{1,65},{2,66},{3,67},{4,68},{5,69},{6,70},{7,71},{8,72},{9,... | collective-permute-start | bytes 786440 | tf_op jit(solution)/shard_map/ppermute | solution.py:171
  105.6 20.2 %copy-start.7 = (bf16[2,256,256]{2,1,0:T(8,128)(2,1)S(1)}, bf16[2,256,256]{2,1,0:T(8,128)(2,1)}, u32[]{:S(2)}) copy-start(bf16[2,256,256]{2,1,0:T(8,128)(2,1)} %param.7) | copy-start | bytes 786436
  105.8 24.8 %collective-permute-start.7 = (bf16[2,4,256,256]{3,2,1,0:T(8,128)(2,1)S(1)}, bf16[2,4,256,256]{3,2,1,0:T(8,128)(2,1)S(1)}, u32[]{:S(2)}, u32[]{:S(2)}) collective-permute-start(bf16[2,4,256,256]{3,2,1,0:T(8,128)(2,1)S(1)} %pad_maximum_fusion.3), channel_id=1, source_target_pairs={{0,1},{1,0},{2,3},{3,2},{4,5},{5,4},{6,7},{7,6},{8,9},{9,8},{10,11... | collective-permute-start | bytes 3145736 | tf_op jit(solution)/shard_map/ppermute | solution.py:156
  (3 other events, 5.8 us)

commit v15 on v14

--- a/solution.py
+++ b/solution.py
@@ -188,9 +188,22 @@
 
 
 def update_kernel(
-    codes, row_codes, front_ref, c1_ref, c2_ref, x_ref, p1_ref, p2_ref, u1_ref, u2_ref, out_ref
+    codes, row_codes, col_codes, front_ref, c1_ref, c2_ref, x_ref, y_ref, p1_ref, p2_ref, u1_ref,
+    r2_ref, out_ref, u2_ref,
 ):
     i = pl.program_id(0)
+
+    @pl.when(i == 0)
+    def _():
+        lower = jnp.dot(y_ref[...], p1_ref[...], preferred_element_type=jnp.float32).astype(jnp.bfloat16)
+        for j in range(r2_ref.shape[0]):
+            code = col_codes[j]
+            block = r2_ref[j]
+            product = jnp.dot(lower, u1_ref[j], preferred_element_type=jnp.float32)
+            changed = (block.astype(jnp.float32) - product).astype(jnp.bfloat16)
+            block = jnp.where((code & 1) != 0, changed, block)
+            u2_ref[j] = jnp.where((code & 2) != 0, lower, block)
+
     row_code = row_codes[i]
     lower1 = jnp.dot(c1_ref[0], p1_ref[...], preferred_element_type=jnp.float32).astype(jnp.bfloat16)
     lower1 = jnp.where((row_code & 1) != 0, lower1, jnp.zeros_like(lower1))
@@ -215,26 +228,30 @@
         out_ref[0, j] = block
 
 
-def both_updates(front, codes, row_codes, column1, column2, cross, inverse, upper1, upper2):
+def both_updates(front, codes, row_codes, col_codes, column1, column2, cross, inverse, upper1, row2):
     rows, cols, bs, _ = front.shape
-    row_block = pl.BlockSpec((1, cols, bs, bs), lambda i, c, r: (i, 0, 0, 0))
-    lower_block = pl.BlockSpec((1, bs, bs), lambda i, c, r: (i, 0, 0))
-    one_block = pl.BlockSpec((bs, bs), lambda i, c, r: (0, 0))
-    upper_block = pl.BlockSpec((cols, bs, bs), lambda i, c, r: (0, 0, 0))
+    row_block = pl.BlockSpec((1, cols, bs, bs), lambda i, c, r, k: (i, 0, 0, 0))
+    lower_block = pl.BlockSpec((1, bs, bs), lambda i, c, r, k: (i, 0, 0))
+    one_block = pl.BlockSpec((bs, bs), lambda i, c, r, k: (0, 0))
+    upper_block = pl.BlockSpec((cols, bs, bs), lambda i, c, r, k: (0, 0, 0))
     return pl.pallas_call(
         update_kernel,
         grid_spec=pltpu.PrefetchScalarGridSpec(
-            num_scalar_prefetch=2,
+            num_scalar_prefetch=3,
             grid=(rows,),
             in_specs=[
-                row_block, lower_block, lower_block, one_block, one_block, one_block,
+                row_block, lower_block, lower_block, one_block, one_block, one_block, one_block,
                 upper_block, upper_block,
             ],
             out_specs=row_block,
+            scratch_shapes=[pltpu.VMEM((cols, bs, bs), front.dtype)],
         ),
         out_shape=jax.ShapeDtypeStruct(front.shape, front.dtype),
         compiler_params=pltpu.CompilerParams(dimension_semantics=("arbitrary",)),
-    )(codes, row_codes, front, column1, column2, cross, inverse[0], inverse[1], upper1, upper2)
+    )(
+        codes, row_codes, col_codes, front, column1, column2, cross[0], cross[1], inverse[0],
+        inverse[1], upper1, row2,
+    )
 
 
 def masked(blocks, keep):
@@ -290,18 +307,10 @@
     first_at_second, second_at_first = cross[0], cross[1]
 
     second_ok = (second != first)[None]
-    lower_first_at_second = lower_local(second_at_first[None], pivot_inv[0], second_ok)
-    row_after = eliminate(
-        second_row[None],
-        lower_first_at_second,
-        upper_first,
-        first,
-        second_ok,
-        cols_first,
-        pattern[second][front_cols][None],
-        front_cols,
-    )
-    upper_second = row_after[0]
+    col_codes = (
+        (second_ok[0] & cols_first & (pattern[second][front_cols] > 0)).astype(jnp.int32)
+        + 2 * (second_ok[0] & (front_cols == first)).astype(jnp.int32)
+    )
     row_codes = (
         rows_first.astype(jnp.int32)
         + 2 * rows_second.astype(jnp.int32)
@@ -321,8 +330,8 @@
         + 16 * place_second.astype(jnp.int32)
     )
     return both_updates(
-        front, codes, row_codes, cols_sent[0], second_col, first_at_second, pivot_inv,
-        upper_first, upper_second,
+        front, codes, row_codes, col_codes, cols_sent[0], second_col, cross, pivot_inv,
+        upper_first, second_row,
     )
 
 

time: 151 us -> 152 us (level)
  other arithmetic: 24.5 us -> 22.8 us
    squeeze x1 -> x0, other arithmetic: 2 us -> none  [body(): upper_second = row_after[0]]
    slice x1, local copies, waits for them, and re-layouts: 0.27 us -> 1.98 us  [body(): upper_first, second_row = (rows_sent[0], rows_sent[1])]
where the time goes in v15:
time: 152 us; the launch traced here: 151 us
  starting transfers between devices  43.1 us (28%)
  waiting for transfers between devices  42.7 us (28%)
  other arithmetic  22.8 us (15%)
  Pallas kernels  19 us (12%)
  local copies, waits for them, and re-layouts  11.9 us (8%)
  between operations  11.4 us (8%)
    ppermute x7, waiting for transfers between devices, all_bcast(): lax.ppermute(value, ('row', 'col'), [(d, d ^ 1 << b) for d in range(n)])  25.6 us
    ppermute x10, starting transfers between devices, xor_bcast(): lax.ppermute(groups[m], axes, digit_pairs(nrow, ncol, on_row, step, m))  19.6 us
    pallas_call x1, Pallas kernels, both_updates(): pl.pallas_call(update_kernel, grid_spec=pltpu.PrefetchScalarGridSpec(num_...  19 us
    ppermute x10, waiting for transfers between devices, xor_bcast(): lax.ppermute(groups[m], axes, digit_pairs(nrow, ncol, on_row, step, m))  13.6 us
    ppermute x10, starting transfers between devices, xor_bcast(): lax.ppermute(buf, axes, digit_pairs(nrow, ncol, on_row, step, m))  13.4 us
    ppermute x7, starting transfers between devices, all_bcast(): lax.ppermute(value, ('row', 'col'), [(d, d ^ 1 << b) for d in range(n)])  10.1 us
    select_n x11, other arithmetic, per_part(): return jnp.where(cond.reshape((-1,) + (1,) * (a.ndim - 1)), a, b)  6.95 us
    ppermute x10, waiting for transfers between devices, xor_bcast(): lax.ppermute(buf, axes, digit_pairs(nrow, ncol, on_row, step, m))  3.53 us
  transfers between devices with their start and end apart: 27, of which 8 were waited for; matrix products, arithmetic and copies ran while one was open for 19% of the time, Pallas kernels for 0%

profile of v15, /device:TPU:6, one launch (start us, length us, event | category | flops | bytes accessed | tf_op | source)
XLA Modules:
  0.0 150.9 jit_solution(9562752124272590363)
XLA Ops:
  12.0 1.7 %constant_dynamic-slice_fusion.1 = (bf16[8,1,256,256]{3,2,1,0:T(8,128)(2,1)S(1)}, bf16[8,1,256,256]{3,2,1,0:T(8,128)(2,1)S(1)}) fusion(bf16[8,12,256,256]{3,2,1,0:T(8,128)(2,1)} %front_ref.1, s32[]{:T(128)S(6)} %select_n.358, s32[]{:T(128)S(6)} %select_n.362), kind=kLoop, calls=%fused_computation.85 | loop fusion | bytes 4194312 | tf_op jit(solution)/shard_map/jit(dynamic_index_in_dim)/dynamic_slice | solution.py:294
  16.4 2.2 %dynamic-slice_select_fusion = (bf16[1,12,256,256]{3,2,1,0:T(8,128)(2,1)S(1)}, bf16[1,12,256,256]{3,2,1,0:T(8,128)(2,1)S(1)}) fusion(bf16[8,12,256,256]{3,2,1,0:T(8,128)(2,1)} %front_ref.1, s32[]{:T(128)S(6)} %select_n.391, pred[12]{0:T(512)(128)(4,1)S(1)} %get-tuple-element.5, s32[]{:T(128)S(6)} %select_n.386, pred[12]{0:T(512)(128)(4,1)S(1)} %get-tuple-element.6), kind=kLoop, calls=%fused_computation.13 | loop fusion | flops 1572864 | bytes 6291488 | tf_op jit(solution)/shard_map/jit(_where)/select_n | solution.py:259
  18.6 1.5 fusion.12
  20.1 4.0 %collective-permute-start.17 = (bf16[2,4,192,256]{3,2,1,0:T(8,128)(2,1)}, bf16[2,4,192,256]{3,2,1,0:T(8,128)(2,1)}, u32[]{:S(2)}, u32[]{:S(2)}) collective-permute-start(bf16[2,4,192,256]{3,2,1,0:T(8,128)(2,1)} %get-tuple-element.32), channel_id=1, source_target_pairs={{0,96},{1,25},{2,98},{3,27},{4,100},{5,29},{6,102},{7,31},{8,104},... | collective-permute-start | bytes 2359304 | tf_op jit(solution)/shard_map/ppermute | solution.py:149
  24.1 1.5 collective-permute-start.16
  30.6 1.9 %add_add_fusion = (s32[8]{0:T(128)}, pred[8]{0:T(512)(128)(4,1)S(1)}, pred[8]{0:T(512)(128)(4,1)S(1)}) fusion(s32[8]{0:T(128)S(1)} %gather_fusion, pred[]{:T(512)S(6)} %ne.93, s32[]{:T(128)} %bitcast.2, s32[]{:T(128)S(6)} %axis_index.15, s32[]{:T(128)} %bitcast.1), kind=kLoop, calls=%fused_computation.114 | loop fusion | flops 104 | bytes 93 | tf_op jit(solution)/shard_map/add | solution.py:315
  35.3 1.7 %broadcast_select_fusion.2 = bf16[2,256,256]{2,1,0:T(8,128)(2,1)} fusion(bf16[2,256,256]{2,1,0:T(8,128)(2,1)} %collective-permute-done.8, pred[2]{0:T(512)(128)(4,1)S(1)} %get-tuple-element.69, bf16[1,256,256]{2,1,0:T(8,128)(2,1)S(1)} %get-tuple-element.24, bf16[1,256,256]{2,1,0:T(8,128)(2,1)S(1)} %get-tuple-element.23), kind=kLoop, calls=%fused_computation.51 | loop fusion | flops 262144 | bytes 786434 | tf_op jit(solution)/shard_map/jit(_where)/select_n | solution.py:13
  37.1 1.6 %collective-permute-start.9 = (bf16[2,256,256]{2,1,0:T(8,128)(2,1)}, bf16[2,256,256]{2,1,0:T(8,128)(2,1)}, u32[]{:S(2)}, u32[]{:S(2)}) collective-permute-start(bf16[2,256,256]{2,1,0:T(8,128)(2,1)} %broadcast_select_fusion.2), channel_id=1, source_target_pairs={{0,2},{1,3},{2,0},{3,1},{4,6},{5,7},{6,4},{7,5},{8,10},{9,11},{10,... | collective-permute-start | bytes 786440 | tf_op jit(solution)/shard_map/ppermute | solution.py:171
  40.3 3.6 %collective-permute-done.9 = bf16[2,256,256]{2,1,0:T(8,128)(2,1)} collective-permute-done((bf16[2,256,256]{2,1,0:T(8,128)(2,1)}, bf16[2,256,256]{2,1,0:T(8,128)(2,1)}, u32[]{:S(2)}, u32[]{:S(2)}) %collective-permute-start.9) | collective-permute-done | bytes 262176 | tf_op jit(solution)/shard_map/ppermute | solution.py:171
  45.1 3.3 %collective-permute-start.10 = (bf16[2,256,256]{2,1,0:T(8,128)(2,1)S(1)}, bf16[2,256,256]{2,1,0:T(8,128)(2,1)S(1)}, u32[]{:S(2)}, u32[]{:S(2)}) collective-permute-start(bf16[2,256,256]{2,1,0:T(8,128)(2,1)S(1)} %broadcast_select_fusion.3), channel_id=1, source_target_pairs={{0,4},{1,5},{2,6},{3,7},{4,0},{5,1},{6,2},{7,3},{8,12},{9,13},{10,... | collective-permute-start | bytes 786440 | tf_op jit(solution)/shard_map/ppermute | solution.py:171
  48.4 1.7 %slice_bitcast_fusion.10 = (bf16[256,256]{1,0:T(8,128)(2,1)}, bf16[256,256]{1,0:T(8,128)(2,1)}) fusion(bf16[2,256,256]{2,1,0:T(8,128)(2,1)} %param.7), kind=kLoop, calls=%fused_computation.69 | loop fusion | bytes 524288 | tf_op jit(solution)/shard_map/squeeze | solution.py:253
  50.1 2.9 %collective-permute-done.10 = bf16[2,256,256]{2,1,0:T(8,128)(2,1)S(1)} collective-permute-done((bf16[2,256,256]{2,1,0:T(8,128)(2,1)S(1)}, bf16[2,256,256]{2,1,0:T(8,128)(2,1)S(1)}, u32[]{:S(2)}, u32[]{:S(2)}) %collective-permute-start.10) | collective-permute-done | bytes 262176 | tf_op jit(solution)/shard_map/ppermute | solution.py:171
  53.9 2.0 %fusion.9 = bf16[2,4,192,256]{3,2,1,0:T(8,128)(2,1)S(1)} fusion(bf16[1,4,4,192,256]{4,3,2,0,1:T(8,128)(2,1)S(1)} %bitcast.151, bf16[1,4,4,192,256]{4,3,2,0,1:T(8,128)(2,1)S(1)} %bitcast.149, bf16[2,4,192,256]{3,2,1,0:T(8,128)(2,1)} %collective-permute-done.15, bf16[2,4,192,256]{3,2,1,0:T(8,128)(2,1)} %collective-permute-done.16, ...), kind=kLoop, calls=%fused_computation.31 | loop fusion | flops 1572864 | bytes 6291462 | tf_op jit(solution)/shard_map/jit(_where)/select_n | solution.py:13
  57.5 3.2 %collective-permute-start.19 = (bf16[2,192,256]{2,1,0:T(8,128)(2,1)S(1)}, bf16[2,192,256]{2,1,0:T(8,128)(2,1)S(1)}, u32[]{:S(2)}, u32[]{:S(2)}) collective-permute-start(bf16[2,192,256]{2,1,0:T(8,128)(2,1)S(1)} %get-tuple-element.52), channel_id=1, source_target_pairs={{0,16},{1,65},{2,18},{3,67},{4,20},{5,69},{6,22},{7,71},{8,24},{9,... | collective-permute-start | bytes 589832 | tf_op jit(solution)/shard_map/ppermute | solution.py:149
  60.7 2.2 %collective-permute-done.20 = bf16[2,192,256]{2,1,0:T(8,128)(2,1)S(1)} collective-permute-done((bf16[2,192,256]{2,1,0:T(8,128)(2,1)S(1)}, bf16[2,192,256]{2,1,0:T(8,128)(2,1)S(1)}, u32[]{:S(2)}, u32[]{:S(2)}) %collective-permute-start.20) | collective-permute-done | bytes 196640 | tf_op jit(solution)/shard_map/ppermute | solution.py:149
  62.8 3.6 %collective-permute-done.19 = bf16[2,192,256]{2,1,0:T(8,128)(2,1)S(1)} collective-permute-done((bf16[2,192,256]{2,1,0:T(8,128)(2,1)S(1)}, bf16[2,192,256]{2,1,0:T(8,128)(2,1)S(1)}, u32[]{:S(2)}, u32[]{:S(2)}) %collective-permute-start.19) | collective-permute-done | bytes 196640 | tf_op jit(solution)/shard_map/ppermute | solution.py:149
  68.9 1.8 %collective-permute-start.21 = (bf16[2,192,256]{2,1,0:T(8,128)(2,1)S(1)}, bf16[2,192,256]{2,1,0:T(8,128)(2,1)S(1)}, u32[]{:S(2)}, u32[]{:S(2)}) collective-permute-start(bf16[2,192,256]{2,1,0:T(8,128)(2,1)S(1)} %fusion.14), channel_id=1, source_target_pairs={{0,8},{1,33},{2,10},{3,35},{4,12},{5,37},{6,14},{7,39},{8,0},{9,41... | collective-permute-start | bytes 589832 | tf_op jit(solution)/shard_map/ppermute | solution.py:156
  70.8 1.5 collective-permute-start.12
  73.8 3.7 %collective-permute-start.3 = (bf16[2,256,256]{2,1,0:T(8,128)(2,1)S(1)}, bf16[2,256,256]{2,1,0:T(8,128)(2,1)S(1)}, u32[]{:S(2)}, u32[]{:S(2)}) collective-permute-start(bf16[2,256,256]{2,1,0:T(8,128)(2,1)S(1)} %get-tuple-element.43), channel_id=1, source_target_pairs={{0,6},{1,7},{2,4},{3,5},{4,2},{5,3},{6,0},{7,1},{8,14},{9,15},{10,... | collective-permute-start | bytes 786440 | tf_op jit(solution)/shard_map/ppermute | solution.py:149
  78.4 1.6 %collective-permute-start.1 = (bf16[2,256,256]{2,1,0:T(8,128)(2,1)S(1)}, bf16[2,256,256]{2,1,0:T(8,128)(2,1)S(1)}, u32[]{:S(2)}, u32[]{:S(2)}) collective-permute-start(bf16[2,256,256]{2,1,0:T(8,128)(2,1)S(1)} %get-tuple-element.44), channel_id=1, source_target_pairs={{0,2},{1,3},{2,0},{3,1},{4,6},{5,7},{6,4},{7,5},{8,10},{9,11},{10,... | collective-permute-start | bytes 786440 | tf_op jit(solution)/shard_map/ppermute | solution.py:149
  80.0 3.5 %collective-permute-start.2 = (bf16[2,256,256]{2,1,0:T(8,128)(2,1)S(1)}, bf16[2,256,256]{2,1,0:T(8,128)(2,1)S(1)}, u32[]{:S(2)}, u32[]{:S(2)}) collective-permute-start(bf16[2,256,256]{2,1,0:T(8,128)(2,1)S(1)} %get-tuple-element.45), channel_id=1, source_target_pairs={{0,4},{1,5},{2,6},{3,7},{4,0},{5,1},{6,2},{7,3},{8,12},{9,13},{10,... | collective-permute-start | bytes 786440 | tf_op jit(solution)/shard_map/ppermute | solution.py:149
  84.9 7.8 %collective-permute-done.2 = bf16[2,256,256]{2,1,0:T(8,128)(2,1)S(1)} collective-permute-done((bf16[2,256,256]{2,1,0:T(8,128)(2,1)S(1)}, bf16[2,256,256]{2,1,0:T(8,128)(2,1)S(1)}, u32[]{:S(2)}, u32[]{:S(2)}) %collective-permute-start.2) | collective-permute-done | bytes 262176 | tf_op jit(solution)/shard_map/ppermute | solution.py:149
  92.9 1.4 collective-permute-start.5
  94.3 2.7 %collective-permute-start.4 = (bf16[2,256,256]{2,1,0:T(8,128)(2,1)S(1)}, bf16[2,256,256]{2,1,0:T(8,128)(2,1)S(1)}, u32[]{:S(2)}, u32[]{:S(2)}) collective-permute-start(bf16[2,256,256]{2,1,0:T(8,128)(2,1)S(1)} %fusion.13), channel_id=1, source_target_pairs={{0,2},{1,3},{2,0},{3,1},{4,6},{5,7},{6,4},{7,5},{8,10},{9,11},{10,... | collective-permute-start | bytes 786440 | tf_op jit(solution)/shard_map/ppermute | solution.py:156
  97.1 1.9 %collective-permute-start.26 = (bf16[2,4,192,256]{3,2,1,0:T(8,128)(2,1)S(1)}, bf16[2,4,192,256]{3,2,1,0:T(8,128)(2,1)S(1)}, u32[]{:S(2)}, u32[]{:S(2)}) collective-permute-start(bf16[2,4,192,256]{3,2,1,0:T(8,128)(2,1)S(1)} %pad_maximum_fusion.5), channel_id=1, source_target_pairs={{0,96},{1,25},{2,98},{3,27},{4,100},{5,29},{6,102},{7,31},{8,104},... | collective-permute-start | bytes 2359304 | tf_op jit(solution)/shard_map/ppermute | solution.py:156
  99.0 1.5 %collective-permute-start.25 = (bf16[2,4,192,256]{3,2,1,0:T(8,128)(2,1)S(1)}, bf16[2,4,192,256]{3,2,1,0:T(8,128)(2,1)S(1)}, u32[]{:S(2)}, u32[]{:S(2)}) collective-permute-start(bf16[2,4,192,256]{3,2,1,0:T(8,128)(2,1)S(1)} %pad_maximum_fusion.5), channel_id=1, source_target_pairs={{0,64},{1,17},{2,66},{3,19},{4,68},{5,21},{6,70},{7,23},{8,72},{9,... | collective-permute-start | bytes 2359304 | tf_op jit(solution)/shard_map/ppermute | solution.py:156
  100.7 2.6 %collective-permute-done.6 = bf16[2,256,256]{2,1,0:T(8,128)(2,1)S(1)} collective-permute-done((bf16[2,256,256]{2,1,0:T(8,128)(2,1)S(1)}, bf16[2,256,256]{2,1,0:T(8,128)(2,1)S(1)}, u32[]{:S(2)}, u32[]{:S(2)}) %collective-permute-start.6) | collective-permute-done | bytes 262176 | tf_op jit(solution)/shard_map/ppermute | solution.py:156
  104.6 2.0 %collective-permute-start.14 = (bf16[2,256,256]{2,1,0:T(8,128)(2,1)S(1)}, bf16[2,256,256]{2,1,0:T(8,128)(2,1)S(1)}, u32[]{:S(2)}, u32[]{:S(2)}) collective-permute-start(bf16[2,256,256]{2,1,0:T(8,128)(2,1)S(1)} %broadcast_select_fusion.7), channel_id=1, source_target_pairs={{0,64},{1,65},{2,66},{3,67},{4,68},{5,69},{6,70},{7,71},{8,72},{9,... | collective-permute-start | bytes 786440 | tf_op jit(solution)/shard_map/ppermute | solution.py:171
  107.2 19.0 %collective-permute-done.14 = bf16[2,256,256]{2,1,0:T(8,128)(2,1)S(1)} collective-permute-done((bf16[2,256,256]{2,1,0:T(8,128)(2,1)S(1)}, bf16[2,256,256]{2,1,0:T(8,128)(2,1)S(1)}, u32[]{:S(2)}, u32[]{:S(2)}) %collective-permute-start.14) | collective-permute-done | bytes 262176 | tf_op jit(solution)/shard_map/ppermute | solution.py:171
  128.2 2.0 %fusion.25 = (bf16[1,4,4,192,256]{4,3,2,1,0:T(8,128)(2,1)}, bf16[1,4,4,192,256]{4,3,2,1,0:T(8,128)(2,1)}) fusion(bf16[2,4,4,192,256]{4,3,2,1,0:T(8,128)(2,1)S(1)} %pad_maximum_fusion), kind=kLoop, calls=%fused_computation.130 | loop fusion | bytes 6291456 | tf_op jit(solution)/shard_map/slice | solution.py:301
  130.4 1.5 %pad_maximum_fusion.1 = (bf16[1,2,4,256,256]{4,3,2,1,0:T(8,128)(2,1)}, bf16[1,2,4,256,256]{4,3,2,1,0:T(8,128)(2,1)}) fusion(bf16[2,1,4,256,256]{4,3,2,1,0:T(8,128)(2,1)S(1)} %get-tuple-element.35, bf16[2,1,4,256,256]{4,3,2,1,0:T(8,128)(2,1)S(1)} %get-tuple-element.36), kind=kLoop, calls=%fused_computation.19 | loop fusion | flops 1048576 | bytes 4194304 | tf_op jit(solution)/shard_map/stack | solution.py:159
  131.9 19.0 %shard_map.46 = bf16[8,12,256,256]{3,2,1,0:T(8,128)(2,1)} custom-call(s32[8,12]{1,0:T(8,128)} %select_add_fusion.codes, s32[8]{0:T(128)} %get-tuple-element.18.row_codes, s32[12]{0:T(128)} %get-tuple-element.15.col_codes, bf16[8,12,256,256]{3,2,1,0:T(8,128)(2,1)} %front_ref.1, bf16[8,256,256]{2,1,0:T(8,128)(2,1)} %bitcast.157, ...), custom_call_target="tpu_custom_call" | custom-call | tf_op jit(solution)/shard_map/pallas_call | solution.py:237
  (92 shorter events, 27.3 us)
Async XLA Ops:
  8.0 7.8 %copy-start.5 = (s32[8,16,12,8]{1,0,3,2:T(8,128)}, s32[8,16,12,8]{1,0,3,2:T(8,128)S(1)}, u32[]{:S(2)}) copy-start(s32[8,16,12,8]{1,0,3,2:T(8,128)S(1)} %reshape.512) | copy-start | bytes 147460
  11.8 23.5 %collective-permute-start.8 = (bf16[2,256,256]{2,1,0:T(8,128)(2,1)}, bf16[2,256,256]{2,1,0:T(8,128)(2,1)}, u32[]{:S(2)}, u32[]{:S(2)}) collective-permute-start(bf16[2,256,256]{2,1,0:T(8,128)(2,1)} %pad_maximum_fusion.6), channel_id=1, source_target_pairs={{0,1},{1,0},{2,3},{3,2},{4,5},{5,4},{6,7},{7,6},{8,9},{9,8},{10,11... | collective-permute-start | bytes 786440 | tf_op jit(solution)/shard_map/ppermute | solution.py:171
  14.1 2.3 %copy-start = (bf16[1,2,4,256,256]{4,3,2,0,1:T(8,128)(2,1)}, bf16[1,2,4,256,256]{4,3,2,0,1:T(8,128)(2,1)S(1)}, u32[]{:S(2)}) copy-start(bf16[1,2,4,256,256]{4,3,2,0,1:T(8,128)(2,1)S(1)} %get-tuple-element.77) | copy-start | bytes 3145732
  15.3 57.0 %collective-permute-start = (bf16[2,4,256,256]{3,2,1,0:T(8,128)(2,1)}, bf16[2,4,256,256]{3,2,1,0:T(8,128)(2,1)}, u32[]{:S(2)}, u32[]{:S(2)}) collective-permute-start(bf16[2,4,256,256]{3,2,1,0:T(8,128)(2,1)} %fusion.4), channel_id=1, source_target_pairs={{0,1},{1,0},{2,3},{3,2},{4,5},{5,4},{6,7},{7,6},{8,9},{9,8},{10,11... | collective-permute-start | bytes 3145736 | tf_op jit(solution)/shard_map/ppermute | solution.py:149
  18.6 11.2 %copy-start.4 = (s32[128,96]{0,1:T(8,128)S(1)}, s32[128,96]{0,1:T(8,128)}, u32[]{:S(2)}) copy-start(s32[128,96]{0,1:T(8,128)} %param.5) | copy-start | bytes 147460
  20.1 33.8 %collective-permute-start.17 = (bf16[2,4,192,256]{3,2,1,0:T(8,128)(2,1)}, bf16[2,4,192,256]{3,2,1,0:T(8,128)(2,1)}, u32[]{:S(2)}, u32[]{:S(2)}) collective-permute-start(bf16[2,4,192,256]{3,2,1,0:T(8,128)(2,1)} %get-tuple-element.32), channel_id=1, source_target_pairs={{0,96},{1,25},{2,98},{3,27},{4,100},{5,29},{6,102},{7,31},{8,104},... | collective-permute-start | bytes 2359304 | tf_op jit(solution)/shard_map/ppermute | solution.py:149
  24.1 29.7 %collective-permute-start.15 = (bf16[2,4,192,256]{3,2,1,0:T(8,128)(2,1)}, bf16[2,4,192,256]{3,2,1,0:T(8,128)(2,1)}, u32[]{:S(2)}, u32[]{:S(2)}) collective-permute-start(bf16[2,4,192,256]{3,2,1,0:T(8,128)(2,1)} %get-tuple-element.33), channel_id=1, source_target_pairs={{0,32},{1,9},{2,34},{3,11},{4,36},{5,13},{6,38},{7,15},{8,40},{9,1... | collective-permute-start | bytes 2359304 | tf_op jit(solution)/shard_map/ppermute | solution.py:149
  24.1 29.7 %collective-permute-start.16 = (bf16[2,4,192,256]{3,2,1,0:T(8,128)(2,1)}, bf16[2,4,192,256]{3,2,1,0:T(8,128)(2,1)}, u32[]{:S(2)}, u32[]{:S(2)}) collective-permute-start(bf16[2,4,192,256]{3,2,1,0:T(8,128)(2,1)} %get-tuple-element.34), channel_id=1, source_target_pairs={{0,64},{1,17},{2,66},{3,19},{4,68},{5,21},{6,70},{7,23},{8,72},{9,... | collective-permute-start | bytes 2359304 | tf_op jit(solution)/shard_map/ppermute | solution.py:149
  37.1 6.9 %collective-permute-start.9 = (bf16[2,256,256]{2,1,0:T(8,128)(2,1)}, bf16[2,256,256]{2,1,0:T(8,128)(2,1)}, u32[]{:S(2)}, u32[]{:S(2)}) collective-permute-start(bf16[2,256,256]{2,1,0:T(8,128)(2,1)} %broadcast_select_fusion.2), channel_id=1, source_target_pairs={{0,2},{1,3},{2,0},{3,1},{4,6},{5,7},{6,4},{7,5},{8,10},{9,11},{10,... | collective-permute-start | bytes 786440 | tf_op jit(solution)/shard_map/ppermute | solution.py:171
  45.1 8.0 %collective-permute-start.10 = (bf16[2,256,256]{2,1,0:T(8,128)(2,1)S(1)}, bf16[2,256,256]{2,1,0:T(8,128)(2,1)S(1)}, u32[]{:S(2)}, u32[]{:S(2)}) collective-permute-start(bf16[2,256,256]{2,1,0:T(8,128)(2,1)S(1)} %broadcast_select_fusion.3), channel_id=1, source_target_pairs={{0,4},{1,5},{2,6},{3,7},{4,0},{5,1},{6,2},{7,3},{8,12},{9,13},{10,... | collective-permute-start | bytes 786440 | tf_op jit(solution)/shard_map/ppermute | solution.py:171
  53.1 17.6 %collective-permute-start.11 = (bf16[2,256,256]{2,1,0:T(8,128)(2,1)S(1)}, bf16[2,256,256]{2,1,0:T(8,128)(2,1)S(1)}, u32[]{:S(2)}, u32[]{:S(2)}) collective-permute-start(bf16[2,256,256]{2,1,0:T(8,128)(2,1)S(1)} %broadcast_select_fusion.4), channel_id=1, source_target_pairs={{0,8},{1,9},{2,10},{3,11},{4,12},{5,13},{6,14},{7,15},{8,0},{9,1},... | collective-permute-start | bytes 786440 | tf_op jit(solution)/shard_map/ppermute | solution.py:171
  53.9 18.5 %copy-start.1 = (bf16[1,2,4,256,256]{4,3,2,0,1:T(8,128)(2,1)S(1)}, bf16[1,2,4,256,256]{4,3,2,0,1:T(8,128)(2,1)}, u32[]{:S(2)}) copy-start(bf16[1,2,4,256,256]{4,3,2,0,1:T(8,128)(2,1)} %copy-done) | copy-start | bytes 3145732
  53.9 18.5 %copy-start.3 = (bf16[1,2,4,256,256]{4,3,2,0,1:T(8,128)(2,1)S(1)}, bf16[1,2,4,256,256]{4,3,2,0,1:T(8,128)(2,1)}, u32[]{:S(2)}) copy-start(bf16[1,2,4,256,256]{4,3,2,0,1:T(8,128)(2,1)} %copy-done.2) | copy-start | bytes 3145732
  55.9 7.0 %collective-permute-start.20 = (bf16[2,192,256]{2,1,0:T(8,128)(2,1)S(1)}, bf16[2,192,256]{2,1,0:T(8,128)(2,1)S(1)}, u32[]{:S(2)}, u32[]{:S(2)}) collective-permute-start(bf16[2,192,256]{2,1,0:T(8,128)(2,1)S(1)} %get-tuple-element.50), channel_id=1, source_target_pairs={{0,24},{1,97},{2,26},{3,99},{4,28},{5,101},{6,30},{7,103},{8,16},{... | collective-permute-start | bytes 589832 | tf_op jit(solution)/shard_map/ppermute | solution.py:149
  57.1 5.7 %collective-permute-start.18 = (bf16[2,192,256]{2,1,0:T(8,128)(2,1)S(1)}, bf16[2,192,256]{2,1,0:T(8,128)(2,1)S(1)}, u32[]{:S(2)}, u32[]{:S(2)}) collective-permute-start(bf16[2,192,256]{2,1,0:T(8,128)(2,1)S(1)} %get-tuple-element.51), channel_id=1, source_target_pairs={{0,8},{1,33},{2,10},{3,35},{4,12},{5,37},{6,14},{7,39},{8,0},{9,41... | collective-permute-start | bytes 589832 | tf_op jit(solution)/shard_map/ppermute | solution.py:149
  57.5 9.0 %collective-permute-start.19 = (bf16[2,192,256]{2,1,0:T(8,128)(2,1)S(1)}, bf16[2,192,256]{2,1,0:T(8,128)(2,1)S(1)}, u32[]{:S(2)}, u32[]{:S(2)}) collective-permute-start(bf16[2,192,256]{2,1,0:T(8,128)(2,1)S(1)} %get-tuple-element.52), channel_id=1, source_target_pairs={{0,16},{1,65},{2,18},{3,67},{4,20},{5,69},{6,22},{7,71},{8,24},{9,... | collective-permute-start | bytes 589832 | tf_op jit(solution)/shard_map/ppermute | solution.py:149
  66.5 11.9 %collective-permute-start.23 = (bf16[2,192,256]{2,1,0:T(8,128)(2,1)S(1)}, bf16[2,192,256]{2,1,0:T(8,128)(2,1)S(1)}, u32[]{:S(2)}, u32[]{:S(2)}) collective-permute-start(bf16[2,192,256]{2,1,0:T(8,128)(2,1)S(1)} %fusion.14), channel_id=1, source_target_pairs={{0,24},{1,97},{2,26},{3,99},{4,28},{5,101},{6,30},{7,103},{8,16},{... | collective-permute-start | bytes 589832 | tf_op jit(solution)/shard_map/ppermute | solution.py:156
  67.8 12.2 %collective-permute-start.22 = (bf16[2,192,256]{2,1,0:T(8,128)(2,1)S(1)}, bf16[2,192,256]{2,1,0:T(8,128)(2,1)S(1)}, u32[]{:S(2)}, u32[]{:S(2)}) collective-permute-start(bf16[2,192,256]{2,1,0:T(8,128)(2,1)S(1)} %fusion.14), channel_id=1, source_target_pairs={{0,16},{1,65},{2,18},{3,67},{4,20},{5,69},{6,22},{7,71},{8,24},{9,... | collective-permute-start | bytes 589832 | tf_op jit(solution)/shard_map/ppermute | solution.py:156
  68.9 14.6 %collective-permute-start.21 = (bf16[2,192,256]{2,1,0:T(8,128)(2,1)S(1)}, bf16[2,192,256]{2,1,0:T(8,128)(2,1)S(1)}, u32[]{:S(2)}, u32[]{:S(2)}) collective-permute-start(bf16[2,192,256]{2,1,0:T(8,128)(2,1)S(1)} %fusion.14), channel_id=1, source_target_pairs={{0,8},{1,33},{2,10},{3,35},{4,12},{5,37},{6,14},{7,39},{8,0},{9,41... | collective-permute-start | bytes 589832 | tf_op jit(solution)/shard_map/ppermute | solution.py:156
  70.8 12.9 %collective-permute-start.12 = (bf16[2,256,256]{2,1,0:T(8,128)(2,1)S(1)}, bf16[2,256,256]{2,1,0:T(8,128)(2,1)S(1)}, u32[]{:S(2)}, u32[]{:S(2)}) collective-permute-start(bf16[2,256,256]{2,1,0:T(8,128)(2,1)S(1)} %broadcast_select_fusion.5), channel_id=1, source_target_pairs={{0,16},{1,17},{2,18},{3,19},{4,20},{5,21},{6,22},{7,23},{8,24},{9,... | collective-permute-start | bytes 786440 | tf_op jit(solution)/shard_map/ppermute | solution.py:171
  73.8 11.0 %collective-permute-start.3 = (bf16[2,256,256]{2,1,0:T(8,128)(2,1)S(1)}, bf16[2,256,256]{2,1,0:T(8,128)(2,1)S(1)}, u32[]{:S(2)}, u32[]{:S(2)}) collective-permute-start(bf16[2,256,256]{2,1,0:T(8,128)(2,1)S(1)} %get-tuple-element.43), channel_id=1, source_target_pairs={{0,6},{1,7},{2,4},{3,5},{4,2},{5,3},{6,0},{7,1},{8,14},{9,15},{10,... | collective-permute-start | bytes 786440 | tf_op jit(solution)/shard_map/ppermute | solution.py:149
  78.4 6.4 %collective-permute-start.1 = (bf16[2,256,256]{2,1,0:T(8,128)(2,1)S(1)}, bf16[2,256,256]{2,1,0:T(8,128)(2,1)S(1)}, u32[]{:S(2)}, u32[]{:S(2)}) collective-permute-start(bf16[2,256,256]{2,1,0:T(8,128)(2,1)S(1)} %get-tuple-element.44), channel_id=1, source_target_pairs={{0,2},{1,3},{2,0},{3,1},{4,6},{5,7},{6,4},{7,5},{8,10},{9,11},{10,... | collective-permute-start | bytes 786440 | tf_op jit(solution)/shard_map/ppermute | solution.py:149
  80.0 12.7 %collective-permute-start.2 = (bf16[2,256,256]{2,1,0:T(8,128)(2,1)S(1)}, bf16[2,256,256]{2,1,0:T(8,128)(2,1)S(1)}, u32[]{:S(2)}, u32[]{:S(2)}) collective-permute-start(bf16[2,256,256]{2,1,0:T(8,128)(2,1)S(1)} %get-tuple-element.45), channel_id=1, source_target_pairs={{0,4},{1,5},{2,6},{3,7},{4,0},{5,1},{6,2},{7,3},{8,12},{9,13},{10,... | collective-permute-start | bytes 786440 | tf_op jit(solution)/shard_map/ppermute | solution.py:149
  83.8 15.3 %collective-permute-start.13 = (bf16[2,256,256]{2,1,0:T(8,128)(2,1)S(1)}, bf16[2,256,256]{2,1,0:T(8,128)(2,1)S(1)}, u32[]{:S(2)}, u32[]{:S(2)}) collective-permute-start(bf16[2,256,256]{2,1,0:T(8,128)(2,1)S(1)} %broadcast_select_fusion.6), channel_id=1, source_target_pairs={{0,32},{1,33},{2,34},{3,35},{4,36},{5,37},{6,38},{7,39},{8,40},{9,... | collective-permute-start | bytes 786440 | tf_op jit(solution)/shard_map/ppermute | solution.py:171
  92.8 10.5 %collective-permute-start.6 = (bf16[2,256,256]{2,1,0:T(8,128)(2,1)S(1)}, bf16[2,256,256]{2,1,0:T(8,128)(2,1)S(1)}, u32[]{:S(2)}, u32[]{:S(2)}) collective-permute-start(bf16[2,256,256]{2,1,0:T(8,128)(2,1)S(1)} %fusion.13), channel_id=1, source_target_pairs={{0,6},{1,7},{2,4},{3,5},{4,2},{5,3},{6,0},{7,1},{8,14},{9,15},{10,... | collective-permute-start | bytes 786440 | tf_op jit(solution)/shard_map/ppermute | solution.py:156
  92.9 11.7 %collective-permute-start.5 = (bf16[2,256,256]{2,1,0:T(8,128)(2,1)S(1)}, bf16[2,256,256]{2,1,0:T(8,128)(2,1)S(1)}, u32[]{:S(2)}, u32[]{:S(2)}) collective-permute-start(bf16[2,256,256]{2,1,0:T(8,128)(2,1)S(1)} %fusion.13), channel_id=1, source_target_pairs={{0,4},{1,5},{2,6},{3,7},{4,0},{5,1},{6,2},{7,3},{8,12},{9,13},{10,... | collective-permute-start | bytes 786440 | tf_op jit(solution)/shard_map/ppermute | solution.py:156
  94.3 12.3 %collective-permute-start.4 = (bf16[2,256,256]{2,1,0:T(8,128)(2,1)S(1)}, bf16[2,256,256]{2,1,0:T(8,128)(2,1)S(1)}, u32[]{:S(2)}, u32[]{:S(2)}) collective-permute-start(bf16[2,256,256]{2,1,0:T(8,128)(2,1)S(1)} %fusion.13), channel_id=1, source_target_pairs={{0,2},{1,3},{2,0},{3,1},{4,6},{5,7},{6,4},{7,5},{8,10},{9,11},{10,... | collective-permute-start | bytes 786440 | tf_op jit(solution)/shard_map/ppermute | solution.py:156
  97.1 30.0 %collective-permute-start.26 = (bf16[2,4,192,256]{3,2,1,0:T(8,128)(2,1)S(1)}, bf16[2,4,192,256]{3,2,1,0:T(8,128)(2,1)S(1)}, u32[]{:S(2)}, u32[]{:S(2)}) collective-permute-start(bf16[2,4,192,256]{3,2,1,0:T(8,128)(2,1)S(1)} %pad_maximum_fusion.5), channel_id=1, source_target_pairs={{0,96},{1,25},{2,98},{3,27},{4,100},{5,29},{6,102},{7,31},{8,104},... | collective-permute-start | bytes 2359304 | tf_op jit(solution)/shard_map/ppermute | solution.py:156
  99.0 28.1 %collective-permute-start.25 = (bf16[2,4,192,256]{3,2,1,0:T(8,128)(2,1)S(1)}, bf16[2,4,192,256]{3,2,1,0:T(8,128)(2,1)S(1)}, u32[]{:S(2)}, u32[]{:S(2)}) collective-permute-start(bf16[2,4,192,256]{3,2,1,0:T(8,128)(2,1)S(1)} %pad_maximum_fusion.5), channel_id=1, source_target_pairs={{0,64},{1,17},{2,66},{3,19},{4,68},{5,21},{6,70},{7,23},{8,72},{9,... | collective-permute-start | bytes 2359304 | tf_op jit(solution)/shard_map/ppermute | solution.py:156
  103.3 23.8 %collective-permute-start.24 = (bf16[2,4,192,256]{3,2,1,0:T(8,128)(2,1)S(1)}, bf16[2,4,192,256]{3,2,1,0:T(8,128)(2,1)S(1)}, u32[]{:S(2)}, u32[]{:S(2)}) collective-permute-start(bf16[2,4,192,256]{3,2,1,0:T(8,128)(2,1)S(1)} %pad_maximum_fusion.5), channel_id=1, source_target_pairs={{0,32},{1,9},{2,34},{3,11},{4,36},{5,13},{6,38},{7,15},{8,40},{9,1... | collective-permute-start | bytes 2359304 | tf_op jit(solution)/shard_map/ppermute | solution.py:156
  104.6 21.6 %collective-permute-start.14 = (bf16[2,256,256]{2,1,0:T(8,128)(2,1)S(1)}, bf16[2,256,256]{2,1,0:T(8,128)(2,1)S(1)}, u32[]{:S(2)}, u32[]{:S(2)}) collective-permute-start(bf16[2,256,256]{2,1,0:T(8,128)(2,1)S(1)} %broadcast_select_fusion.7), channel_id=1, source_target_pairs={{0,64},{1,65},{2,66},{3,67},{4,68},{5,69},{6,70},{7,71},{8,72},{9,... | collective-permute-start | bytes 786440 | tf_op jit(solution)/shard_map/ppermute | solution.py:171
  107.0 23.2 %collective-permute-start.7 = (bf16[2,4,256,256]{3,2,1,0:T(8,128)(2,1)S(1)}, bf16[2,4,256,256]{3,2,1,0:T(8,128)(2,1)S(1)}, u32[]{:S(2)}, u32[]{:S(2)}) collective-permute-start(bf16[2,4,256,256]{3,2,1,0:T(8,128)(2,1)S(1)} %pad_maximum_fusion.3), channel_id=1, source_target_pairs={{0,1},{1,0},{2,3},{3,2},{4,5},{5,4},{6,7},{7,6},{8,9},{9,8},{10,11... | collective-permute-start | bytes 3145736 | tf_op jit(solution)/shard_map/ppermute | solution.py:156
  (1 other events, 2.3 us)

commit v16 on v14

--- a/solution.py
+++ b/solution.py
@@ -190,42 +190,47 @@
 def update_kernel(
     codes, row_codes, front_ref, c1_ref, c2_ref, x_ref, p1_ref, p2_ref, u1_ref, u2_ref, out_ref
 ):
-    i = pl.program_id(0)
-    row_code = row_codes[i]
-    lower1 = jnp.dot(c1_ref[0], p1_ref[...], preferred_element_type=jnp.float32).astype(jnp.bfloat16)
-    lower1 = jnp.where((row_code & 1) != 0, lower1, jnp.zeros_like(lower1))
-    column = c2_ref[0]
-    product = jnp.dot(lower1, x_ref[...], preferred_element_type=jnp.float32)
-    changed = (column.astype(jnp.float32) - product).astype(jnp.bfloat16)
-    column = jnp.where((row_code & 4) != 0, changed, column)
-    lower2 = jnp.dot(column, p2_ref[...], preferred_element_type=jnp.float32).astype(jnp.bfloat16)
-    lower2 = jnp.where((row_code & 2) != 0, lower2, jnp.zeros_like(lower2))
-    for j in range(front_ref.shape[1]):
-        code = codes[i, j]
-        block = front_ref[0, j]
-        block = jnp.where((code & 1) != 0, block, jnp.zeros_like(block))
-        product = jnp.dot(lower1, u1_ref[j], preferred_element_type=jnp.float32)
-        changed = (block.astype(jnp.float32) - product).astype(jnp.bfloat16)
-        block = jnp.where((code & 2) != 0, changed, block)
-        block = jnp.where((code & 4) != 0, lower1, block)
-        product = jnp.dot(lower2, u2_ref[j], preferred_element_type=jnp.float32)
-        changed = (block.astype(jnp.float32) - product).astype(jnp.bfloat16)
-        block = jnp.where((code & 8) != 0, changed, block)
-        block = jnp.where((code & 16) != 0, lower2, block)
-        out_ref[0, j] = block
+    for r in range(front_ref.shape[0]):
+        i = pl.program_id(0) * front_ref.shape[0] + r
+        row_code = row_codes[i]
+        lower1 = jnp.dot(c1_ref[r], p1_ref[...], preferred_element_type=jnp.float32).astype(jnp.bfloat16)
+        lower1 = jnp.where((row_code & 1) != 0, lower1, jnp.zeros_like(lower1))
+        column = c2_ref[r]
+        product = jnp.dot(lower1, x_ref[...], preferred_element_type=jnp.float32)
+        changed = (column.astype(jnp.float32) - product).astype(jnp.bfloat16)
+        column = jnp.where((row_code & 4) != 0, changed, column)
+        lower2 = jnp.dot(column, p2_ref[...], preferred_element_type=jnp.float32).astype(jnp.bfloat16)
+        lower2 = jnp.where((row_code & 2) != 0, lower2, jnp.zeros_like(lower2))
+        for j in range(front_ref.shape[1]):
+            code = codes[i, j]
+            block = front_ref[r, j]
+            block = jnp.where((code & 1) != 0, block, jnp.zeros_like(block))
+            product = jnp.dot(lower1, u1_ref[j], preferred_element_type=jnp.float32)
+            changed = (block.astype(jnp.float32) - product).astype(jnp.bfloat16)
+            block = jnp.where((code & 2) != 0, changed, block)
+            block = jnp.where((code & 4) != 0, lower1, block)
+            product = jnp.dot(lower2, u2_ref[j], preferred_element_type=jnp.float32)
+            changed = (block.astype(jnp.float32) - product).astype(jnp.bfloat16)
+            block = jnp.where((code & 8) != 0, changed, block)
+            block = jnp.where((code & 16) != 0, lower2, block)
+            out_ref[r, j] = block
+
+
+ROWS_PER_STEP = 2
 
 
 def both_updates(front, codes, row_codes, column1, column2, cross, inverse, upper1, upper2):
     rows, cols, bs, _ = front.shape
-    row_block = pl.BlockSpec((1, cols, bs, bs), lambda i, c, r: (i, 0, 0, 0))
-    lower_block = pl.BlockSpec((1, bs, bs), lambda i, c, r: (i, 0, 0))
+    step = ROWS_PER_STEP
+    row_block = pl.BlockSpec((step, cols, bs, bs), lambda i, c, r: (i, 0, 0, 0))
+    lower_block = pl.BlockSpec((step, bs, bs), lambda i, c, r: (i, 0, 0))
     one_block = pl.BlockSpec((bs, bs), lambda i, c, r: (0, 0))
     upper_block = pl.BlockSpec((cols, bs, bs), lambda i, c, r: (0, 0, 0))
     return pl.pallas_call(
         update_kernel,
         grid_spec=pltpu.PrefetchScalarGridSpec(
             num_scalar_prefetch=2,
-            grid=(rows,),
+            grid=(rows // step,),
             in_specs=[
                 row_block, lower_block, lower_block, one_block, one_block, one_block,
                 upper_block, upper_block,

time: 151 us -> 150 us (level)
  no operation moved by 1% of the time
where the time goes in v16:
time: 150 us; the launch traced here: 149 us
  starting transfers between devices  43.1 us (29%)
  waiting for transfers between devices  42.9 us (29%)
  other arithmetic  24.5 us (16%)
  Pallas kernels  16.7 us (11%)
  local copies, waits for them, and re-layouts  10.6 us (7%)
  between operations  10.5 us (7%)
    ppermute x7, waiting for transfers between devices, all_bcast(): lax.ppermute(value, ('row', 'col'), [(d, d ^ 1 << b) for d in range(n)])  25.8 us
    ppermute x10, starting transfers between devices, xor_bcast(): lax.ppermute(groups[m], axes, digit_pairs(nrow, ncol, on_row, step, m))  19.6 us
    pallas_call x1, Pallas kernels, both_updates(): pl.pallas_call(update_kernel, grid_spec=pltpu.PrefetchScalarGridSpec(num_...  16.7 us
    ppermute x10, waiting for transfers between devices, xor_bcast(): lax.ppermute(groups[m], axes, digit_pairs(nrow, ncol, on_row, step, m))  13.6 us
    ppermute x10, starting transfers between devices, xor_bcast(): lax.ppermute(buf, axes, digit_pairs(nrow, ncol, on_row, step, m))  13.4 us
    ppermute x7, starting transfers between devices, all_bcast(): lax.ppermute(value, ('row', 'col'), [(d, d ^ 1 << b) for d in range(n)])  10.1 us
    select_n x11, other arithmetic, per_part(): return jnp.where(cond.reshape((-1,) + (1,) * (a.ndim - 1)), a, b)  6.85 us
    ppermute x10, waiting for transfers between devices, xor_bcast(): lax.ppermute(buf, axes, digit_pairs(nrow, ncol, on_row, step, m))  3.53 us
  transfers between devices with their start and end apart: 27, of which 8 were waited for; matrix products, arithmetic and copies ran while one was open for 19% of the time, Pallas kernels for 0%

profile of v16, /device:TPU:6, one launch (start us, length us, event | category | flops | bytes accessed | tf_op | source)
XLA Modules:
  0.0 149.0 jit_solution(17132317983546630411)
XLA Ops:
  11.2 1.7 %constant_dynamic-slice_fusion.1 = (bf16[8,1,256,256]{3,2,1,0:T(8,128)(2,1)S(1)}, bf16[8,1,256,256]{3,2,1,0:T(8,128)(2,1)S(1)}) fusion(bf16[8,12,256,256]{3,2,1,0:T(8,128)(2,1)} %front_ref.1, s32[]{:T(128)S(6)} %select_n.369, s32[]{:T(128)S(6)} %select_n.373), kind=kLoop, calls=%fused_computation.94 | loop fusion | bytes 4194312 | tf_op jit(solution)/shard_map/jit(dynamic_index_in_dim)/dynamic_slice | solution.py:282
  15.6 2.2 %dynamic-slice_select_fusion = (bf16[1,12,256,256]{3,2,1,0:T(8,128)(2,1)S(1)}, bf16[1,12,256,256]{3,2,1,0:T(8,128)(2,1)S(1)}) fusion(bf16[8,12,256,256]{3,2,1,0:T(8,128)(2,1)} %front_ref.1, s32[]{:T(128)S(6)} %select_n.402, pred[12]{0:T(512)(128)(4,1)S(1)} %get-tuple-element.5, s32[]{:T(128)S(6)} %select_n.397, pred[12]{0:T(512)(128)(4,1)S(1)} %get-tuple-element.6), kind=kLoop, calls=%fused_computation.18 | loop fusion | flops 1572864 | bytes 6291488 | tf_op jit(solution)/shard_map/jit(_where)/select_n | solution.py:247
  17.8 1.5 %fusion.17 = (bf16[2,4,192,256]{3,2,1,0:T(8,128)(2,1)}, bf16[2,4,192,256]{3,2,1,0:T(8,128)(2,1)}, bf16[2,4,192,256]{3,2,1,0:T(8,128)(2,1)}) fusion(bf16[1,4,4,192,256]{4,3,2,0,1:T(8,128)(2,1)S(1)} %bitcast.170, bf16[1,4,4,192,256]{4,3,2,0,1:T(8,128)(2,1)S(1)} %bitcast.172), kind=kLoop, calls=%fused_computation.42 | loop fusion | flops 1179648 | bytes 5505024 | tf_op jit(solution)/shard_map/squeeze | solution.py:147
  19.3 4.0 %collective-permute-start.17 = (bf16[2,4,192,256]{3,2,1,0:T(8,128)(2,1)}, bf16[2,4,192,256]{3,2,1,0:T(8,128)(2,1)}, u32[]{:S(2)}, u32[]{:S(2)}) collective-permute-start(bf16[2,4,192,256]{3,2,1,0:T(8,128)(2,1)} %get-tuple-element.33), channel_id=1, source_target_pairs={{0,96},{1,25},{2,98},{3,27},{4,100},{5,29},{6,102},{7,31},{8,104},... | collective-permute-start | bytes 2359304 | tf_op jit(solution)/shard_map/ppermute | solution.py:149
  23.3 1.5 collective-permute-start.16
  30.3 1.8 %add_add_fusion = (s32[8]{0:T(128)}, pred[8]{0:T(512)(128)(4,1)S(1)}, pred[8]{0:T(512)(128)(4,1)S(1)}) fusion(s32[8]{0:T(128)S(1)} %gather_fusion, pred[]{:T(512)S(6)} %ne.98, s32[]{:T(128)} %bitcast.2, s32[]{:T(128)S(6)} %axis_index.15, s32[]{:T(128)} %bitcast.1), kind=kLoop, calls=%fused_computation.122 | loop fusion | flops 104 | bytes 93 | tf_op jit(solution)/shard_map/add | solution.py:311
  34.3 1.8 %broadcast_select_fusion.2 = bf16[2,256,256]{2,1,0:T(8,128)(2,1)} fusion(bf16[2,256,256]{2,1,0:T(8,128)(2,1)} %collective-permute-done.8, pred[2]{0:T(512)(128)(4,1)S(1)} %get-tuple-element.68, bf16[1,256,256]{2,1,0:T(8,128)(2,1)S(1)} %get-tuple-element.25, bf16[1,256,256]{2,1,0:T(8,128)(2,1)S(1)} %get-tuple-element.24), kind=kLoop, calls=%fused_computation.58 | loop fusion | flops 262144 | bytes 786434 | tf_op jit(solution)/shard_map/jit(_where)/select_n | solution.py:13
  36.0 1.6 %collective-permute-start.9 = (bf16[2,256,256]{2,1,0:T(8,128)(2,1)}, bf16[2,256,256]{2,1,0:T(8,128)(2,1)}, u32[]{:S(2)}, u32[]{:S(2)}) collective-permute-start(bf16[2,256,256]{2,1,0:T(8,128)(2,1)} %broadcast_select_fusion.2), channel_id=1, source_target_pairs={{0,2},{1,3},{2,0},{3,1},{4,6},{5,7},{6,4},{7,5},{8,10},{9,11},{10,... | collective-permute-start | bytes 786440 | tf_op jit(solution)/shard_map/ppermute | solution.py:171
  39.0 3.9 %collective-permute-done.9 = bf16[2,256,256]{2,1,0:T(8,128)(2,1)} collective-permute-done((bf16[2,256,256]{2,1,0:T(8,128)(2,1)}, bf16[2,256,256]{2,1,0:T(8,128)(2,1)}, u32[]{:S(2)}, u32[]{:S(2)}) %collective-permute-start.9) | collective-permute-done | bytes 262176 | tf_op jit(solution)/shard_map/ppermute | solution.py:171
  44.0 3.3 %collective-permute-start.10 = (bf16[2,256,256]{2,1,0:T(8,128)(2,1)S(1)}, bf16[2,256,256]{2,1,0:T(8,128)(2,1)S(1)}, u32[]{:S(2)}, u32[]{:S(2)}) collective-permute-start(bf16[2,256,256]{2,1,0:T(8,128)(2,1)S(1)} %broadcast_select_fusion.3), channel_id=1, source_target_pairs={{0,4},{1,5},{2,6},{3,7},{4,0},{5,1},{6,2},{7,3},{8,12},{9,13},{10,... | collective-permute-start | bytes 786440 | tf_op jit(solution)/shard_map/ppermute | solution.py:171
  47.4 1.7 %slice_bitcast_fusion.11 = (bf16[256,256]{1,0:T(8,128)(2,1)}, bf16[256,256]{1,0:T(8,128)(2,1)}) fusion(bf16[2,256,256]{2,1,0:T(8,128)(2,1)} %param.7), kind=kLoop, calls=%fused_computation.78 | loop fusion | bytes 524288 | tf_op jit(solution)/shard_map/squeeze | solution.py:242
  49.1 2.9 %collective-permute-done.10 = bf16[2,256,256]{2,1,0:T(8,128)(2,1)S(1)} collective-permute-done((bf16[2,256,256]{2,1,0:T(8,128)(2,1)S(1)}, bf16[2,256,256]{2,1,0:T(8,128)(2,1)S(1)}, u32[]{:S(2)}, u32[]{:S(2)}) %collective-permute-start.10) | collective-permute-done | bytes 262176 | tf_op jit(solution)/shard_map/ppermute | solution.py:171
  52.8 1.8 %fusion.14 = bf16[2,4,192,256]{3,2,1,0:T(8,128)(2,1)S(1)} fusion(bf16[1,4,4,192,256]{4,3,2,0,1:T(8,128)(2,1)S(1)} %bitcast.173, bf16[1,4,4,192,256]{4,3,2,0,1:T(8,128)(2,1)S(1)} %bitcast.171, bf16[2,4,192,256]{3,2,1,0:T(8,128)(2,1)} %collective-permute-done.15, bf16[2,4,192,256]{3,2,1,0:T(8,128)(2,1)} %collective-permute-done.16, ...), kind=kLoop, calls=%fused_computation.38 | loop fusion | flops 1572864 | bytes 6291462 | tf_op jit(solution)/shard_map/jit(_where)/select_n | solution.py:13
  56.3 3.2 %collective-permute-start.19 = (bf16[2,192,256]{2,1,0:T(8,128)(2,1)S(1)}, bf16[2,192,256]{2,1,0:T(8,128)(2,1)S(1)}, u32[]{:S(2)}, u32[]{:S(2)}) collective-permute-start(bf16[2,192,256]{2,1,0:T(8,128)(2,1)S(1)} %get-tuple-element.53), channel_id=1, source_target_pairs={{0,16},{1,65},{2,18},{3,67},{4,20},{5,69},{6,22},{7,71},{8,24},{9,... | collective-permute-start | bytes 589832 | tf_op jit(solution)/shard_map/ppermute | solution.py:149
  59.5 2.2 %collective-permute-done.20 = bf16[2,192,256]{2,1,0:T(8,128)(2,1)S(1)} collective-permute-done((bf16[2,192,256]{2,1,0:T(8,128)(2,1)S(1)}, bf16[2,192,256]{2,1,0:T(8,128)(2,1)S(1)}, u32[]{:S(2)}, u32[]{:S(2)}) %collective-permute-start.20) | collective-permute-done | bytes 196640 | tf_op jit(solution)/shard_map/ppermute | solution.py:149
  61.7 3.6 %collective-permute-done.19 = bf16[2,192,256]{2,1,0:T(8,128)(2,1)S(1)} collective-permute-done((bf16[2,192,256]{2,1,0:T(8,128)(2,1)S(1)}, bf16[2,192,256]{2,1,0:T(8,128)(2,1)S(1)}, u32[]{:S(2)}, u32[]{:S(2)}) %collective-permute-start.19) | collective-permute-done | bytes 196640 | tf_op jit(solution)/shard_map/ppermute | solution.py:149
  67.7 1.8 %collective-permute-start.21 = (bf16[2,192,256]{2,1,0:T(8,128)(2,1)S(1)}, bf16[2,192,256]{2,1,0:T(8,128)(2,1)S(1)}, u32[]{:S(2)}, u32[]{:S(2)}) collective-permute-start(bf16[2,192,256]{2,1,0:T(8,128)(2,1)S(1)} %fusion.19), channel_id=1, source_target_pairs={{0,8},{1,33},{2,10},{3,35},{4,12},{5,37},{6,14},{7,39},{8,0},{9,41... | collective-permute-start | bytes 589832 | tf_op jit(solution)/shard_map/ppermute | solution.py:156
  69.6 1.5 %collective-permute-start.12 = (bf16[2,256,256]{2,1,0:T(8,128)(2,1)S(1)}, bf16[2,256,256]{2,1,0:T(8,128)(2,1)S(1)}, u32[]{:S(2)}, u32[]{:S(2)}) collective-permute-start(bf16[2,256,256]{2,1,0:T(8,128)(2,1)S(1)} %broadcast_select_fusion.5), channel_id=1, source_target_pairs={{0,16},{1,17},{2,18},{3,19},{4,20},{5,21},{6,22},{7,23},{8,24},{9,... | collective-permute-start | bytes 786440 | tf_op jit(solution)/shard_map/ppermute | solution.py:171
  72.6 3.7 %collective-permute-start.3 = (bf16[2,256,256]{2,1,0:T(8,128)(2,1)S(1)}, bf16[2,256,256]{2,1,0:T(8,128)(2,1)S(1)}, u32[]{:S(2)}, u32[]{:S(2)}) collective-permute-start(bf16[2,256,256]{2,1,0:T(8,128)(2,1)S(1)} %get-tuple-element.44), channel_id=1, source_target_pairs={{0,6},{1,7},{2,4},{3,5},{4,2},{5,3},{6,0},{7,1},{8,14},{9,15},{10,... | collective-permute-start | bytes 786440 | tf_op jit(solution)/shard_map/ppermute | solution.py:149
  77.2 1.6 %collective-permute-start.1 = (bf16[2,256,256]{2,1,0:T(8,128)(2,1)S(1)}, bf16[2,256,256]{2,1,0:T(8,128)(2,1)S(1)}, u32[]{:S(2)}, u32[]{:S(2)}) collective-permute-start(bf16[2,256,256]{2,1,0:T(8,128)(2,1)S(1)} %get-tuple-element.45), channel_id=1, source_target_pairs={{0,2},{1,3},{2,0},{3,1},{4,6},{5,7},{6,4},{7,5},{8,10},{9,11},{10,... | collective-permute-start | bytes 786440 | tf_op jit(solution)/shard_map/ppermute | solution.py:149
  78.8 3.5 %collective-permute-start.2 = (bf16[2,256,256]{2,1,0:T(8,128)(2,1)S(1)}, bf16[2,256,256]{2,1,0:T(8,128)(2,1)S(1)}, u32[]{:S(2)}, u32[]{:S(2)}) collective-permute-start(bf16[2,256,256]{2,1,0:T(8,128)(2,1)S(1)} %get-tuple-element.46), channel_id=1, source_target_pairs={{0,4},{1,5},{2,6},{3,7},{4,0},{5,1},{6,2},{7,3},{8,12},{9,13},{10,... | collective-permute-start | bytes 786440 | tf_op jit(solution)/shard_map/ppermute | solution.py:149
  83.7 7.8 %collective-permute-done.2 = bf16[2,256,256]{2,1,0:T(8,128)(2,1)S(1)} collective-permute-done((bf16[2,256,256]{2,1,0:T(8,128)(2,1)S(1)}, bf16[2,256,256]{2,1,0:T(8,128)(2,1)S(1)}, u32[]{:S(2)}, u32[]{:S(2)}) %collective-permute-start.2) | collective-permute-done | bytes 262176 | tf_op jit(solution)/shard_map/ppermute | solution.py:149
  91.7 1.4 collective-permute-start.5
  93.2 2.7 %collective-permute-start.4 = (bf16[2,256,256]{2,1,0:T(8,128)(2,1)S(1)}, bf16[2,256,256]{2,1,0:T(8,128)(2,1)S(1)}, u32[]{:S(2)}, u32[]{:S(2)}) collective-permute-start(bf16[2,256,256]{2,1,0:T(8,128)(2,1)S(1)} %fusion.18), channel_id=1, source_target_pairs={{0,2},{1,3},{2,0},{3,1},{4,6},{5,7},{6,4},{7,5},{8,10},{9,11},{10,... | collective-permute-start | bytes 786440 | tf_op jit(solution)/shard_map/ppermute | solution.py:156
  95.9 1.9 %collective-permute-start.26 = (bf16[2,4,192,256]{3,2,1,0:T(8,128)(2,1)S(1)}, bf16[2,4,192,256]{3,2,1,0:T(8,128)(2,1)S(1)}, u32[]{:S(2)}, u32[]{:S(2)}) collective-permute-start(bf16[2,4,192,256]{3,2,1,0:T(8,128)(2,1)S(1)} %pad_maximum_fusion.5), channel_id=1, source_target_pairs={{0,96},{1,25},{2,98},{3,27},{4,100},{5,29},{6,102},{7,31},{8,104},... | collective-permute-start | bytes 2359304 | tf_op jit(solution)/shard_map/ppermute | solution.py:156
  97.9 1.5 %collective-permute-start.25 = (bf16[2,4,192,256]{3,2,1,0:T(8,128)(2,1)S(1)}, bf16[2,4,192,256]{3,2,1,0:T(8,128)(2,1)S(1)}, u32[]{:S(2)}, u32[]{:S(2)}) collective-permute-start(bf16[2,4,192,256]{3,2,1,0:T(8,128)(2,1)S(1)} %pad_maximum_fusion.5), channel_id=1, source_target_pairs={{0,64},{1,17},{2,66},{3,19},{4,68},{5,21},{6,70},{7,23},{8,72},{9,... | collective-permute-start | bytes 2359304 | tf_op jit(solution)/shard_map/ppermute | solution.py:156
  99.5 2.6 %collective-permute-done.6 = bf16[2,256,256]{2,1,0:T(8,128)(2,1)S(1)} collective-permute-done((bf16[2,256,256]{2,1,0:T(8,128)(2,1)S(1)}, bf16[2,256,256]{2,1,0:T(8,128)(2,1)S(1)}, u32[]{:S(2)}, u32[]{:S(2)}) %collective-permute-start.6) | collective-permute-done | bytes 262176 | tf_op jit(solution)/shard_map/ppermute | solution.py:156
  103.4 2.0 %collective-permute-start.14 = (bf16[2,256,256]{2,1,0:T(8,128)(2,1)S(1)}, bf16[2,256,256]{2,1,0:T(8,128)(2,1)S(1)}, u32[]{:S(2)}, u32[]{:S(2)}) collective-permute-start(bf16[2,256,256]{2,1,0:T(8,128)(2,1)S(1)} %broadcast_select_fusion.7), channel_id=1, source_target_pairs={{0,64},{1,65},{2,66},{3,67},{4,68},{5,69},{6,70},{7,71},{8,72},{9,... | collective-permute-start | bytes 786440 | tf_op jit(solution)/shard_map/ppermute | solution.py:171
  106.1 19.0 %collective-permute-done.14 = bf16[2,256,256]{2,1,0:T(8,128)(2,1)S(1)} collective-permute-done((bf16[2,256,256]{2,1,0:T(8,128)(2,1)S(1)}, bf16[2,256,256]{2,1,0:T(8,128)(2,1)S(1)}, u32[]{:S(2)}, u32[]{:S(2)}) %collective-permute-start.14) | collective-permute-done | bytes 262176 | tf_op jit(solution)/shard_map/ppermute | solution.py:171
  128.6 2.0 %fusion.3.u2_ref = bf16[12,256,256]{2,1,0:T(8,128)(2,1)} fusion(bf16[1,12,256,256]{3,2,1,0:T(8,128)(2,1)S(1)} %bitcast.174, f32[12,256,256]{1,2,0:T(8,128)S(1)} %fusion.20, pred[12]{0:T(512)(128)(4,1)S(1)} %get-tuple-element.11, pred[12]{0:T(512)(128)(4,1)S(1)} %get-tuple-element.9, bf16[256,256]{1,0:T(8,128)(2,1)S(1)} %fusion.4), kind=kLoop, calls=%fused_computation.17 | loop fusion | flops 3932160 | bytes 6422552 | tf_op jit(solution)/shard_map/squeeze | solution.py:309
  130.8 1.5 %pad_maximum_fusion.1 = (bf16[1,2,4,256,256]{4,3,2,1,0:T(8,128)(2,1)}, bf16[1,2,4,256,256]{4,3,2,1,0:T(8,128)(2,1)}) fusion(bf16[2,1,4,256,256]{4,3,2,1,0:T(8,128)(2,1)S(1)} %get-tuple-element.36, bf16[2,1,4,256,256]{4,3,2,1,0:T(8,128)(2,1)S(1)} %get-tuple-element.37), kind=kLoop, calls=%fused_computation.26 | loop fusion | flops 1048576 | bytes 4194304 | tf_op jit(solution)/shard_map/stack | solution.py:159
  132.4 16.7 %shard_map.46 = bf16[8,12,256,256]{3,2,1,0:T(8,128)(2,1)} custom-call(s32[8,12]{1,0:T(8,128)} %select_add_fusion.codes, s32[8]{0:T(128)} %get-tuple-element.19.row_codes, bf16[8,12,256,256]{3,2,1,0:T(8,128)(2,1)} %front_ref.1, bf16[8,256,256]{2,1,0:T(8,128)(2,1)} %bitcast.178, bf16[8,256,256]{2,1,0:T(8,128)(2,1)} %bitcast.177, ...), custom_call_target="tpu_custom_call" | custom-call | tf_op jit(solution)/shard_map/pallas_call | solution.py:229
  (100 shorter events, 28.8 us)
Async XLA Ops:
  7.4 7.6 %copy-start.6 = (s32[8,16,12,8]{1,0,3,2:T(8,128)}, s32[8,16,12,8]{1,0,3,2:T(8,128)S(1)}, u32[]{:S(2)}) copy-start(s32[8,16,12,8]{1,0,3,2:T(8,128)S(1)} %reshape.568) | copy-start | bytes 147460
  11.0 23.3 %collective-permute-start.8 = (bf16[2,256,256]{2,1,0:T(8,128)(2,1)}, bf16[2,256,256]{2,1,0:T(8,128)(2,1)}, u32[]{:S(2)}, u32[]{:S(2)}) collective-permute-start(bf16[2,256,256]{2,1,0:T(8,128)(2,1)} %pad_maximum_fusion.6), channel_id=1, source_target_pairs={{0,1},{1,0},{2,3},{3,2},{4,5},{5,4},{6,7},{7,6},{8,9},{9,8},{10,11... | collective-permute-start | bytes 786440 | tf_op jit(solution)/shard_map/ppermute | solution.py:171
  14.5 56.6 %collective-permute-start = (bf16[2,4,256,256]{3,2,1,0:T(8,128)(2,1)}, bf16[2,4,256,256]{3,2,1,0:T(8,128)(2,1)}, u32[]{:S(2)}, u32[]{:S(2)}) collective-permute-start(bf16[2,4,256,256]{3,2,1,0:T(8,128)(2,1)} %fusion.9), channel_id=1, source_target_pairs={{0,1},{1,0},{2,3},{3,2},{4,5},{5,4},{6,7},{7,6},{8,9},{9,8},{10,11... | collective-permute-start | bytes 3145736 | tf_op jit(solution)/shard_map/ppermute | solution.py:149
  17.8 11.7 %copy-start.5 = (s32[128,96]{0,1:T(8,128)S(1)}, s32[128,96]{0,1:T(8,128)}, u32[]{:S(2)}) copy-start(s32[128,96]{0,1:T(8,128)} %param.5) | copy-start | bytes 147460
  19.3 33.5 %collective-permute-start.17 = (bf16[2,4,192,256]{3,2,1,0:T(8,128)(2,1)}, bf16[2,4,192,256]{3,2,1,0:T(8,128)(2,1)}, u32[]{:S(2)}, u32[]{:S(2)}) collective-permute-start(bf16[2,4,192,256]{3,2,1,0:T(8,128)(2,1)} %get-tuple-element.33), channel_id=1, source_target_pairs={{0,96},{1,25},{2,98},{3,27},{4,100},{5,29},{6,102},{7,31},{8,104},... | collective-permute-start | bytes 2359304 | tf_op jit(solution)/shard_map/ppermute | solution.py:149
  23.3 29.5 %collective-permute-start.15 = (bf16[2,4,192,256]{3,2,1,0:T(8,128)(2,1)}, bf16[2,4,192,256]{3,2,1,0:T(8,128)(2,1)}, u32[]{:S(2)}, u32[]{:S(2)}) collective-permute-start(bf16[2,4,192,256]{3,2,1,0:T(8,128)(2,1)} %get-tuple-element.34), channel_id=1, source_target_pairs={{0,32},{1,9},{2,34},{3,11},{4,36},{5,13},{6,38},{7,15},{8,40},{9,1... | collective-permute-start | bytes 2359304 | tf_op jit(solution)/shard_map/ppermute | solution.py:149
  23.3 29.5 %collective-permute-start.16 = (bf16[2,4,192,256]{3,2,1,0:T(8,128)(2,1)}, bf16[2,4,192,256]{3,2,1,0:T(8,128)(2,1)}, u32[]{:S(2)}, u32[]{:S(2)}) collective-permute-start(bf16[2,4,192,256]{3,2,1,0:T(8,128)(2,1)} %get-tuple-element.35), channel_id=1, source_target_pairs={{0,64},{1,17},{2,66},{3,19},{4,68},{5,21},{6,70},{7,23},{8,72},{9,... | collective-permute-start | bytes 2359304 | tf_op jit(solution)/shard_map/ppermute | solution.py:149
  36.0 6.9 %collective-permute-start.9 = (bf16[2,256,256]{2,1,0:T(8,128)(2,1)}, bf16[2,256,256]{2,1,0:T(8,128)(2,1)}, u32[]{:S(2)}, u32[]{:S(2)}) collective-permute-start(bf16[2,256,256]{2,1,0:T(8,128)(2,1)} %broadcast_select_fusion.2), channel_id=1, source_target_pairs={{0,2},{1,3},{2,0},{3,1},{4,6},{5,7},{6,4},{7,5},{8,10},{9,11},{10,... | collective-permute-start | bytes 786440 | tf_op jit(solution)/shard_map/ppermute | solution.py:171
  44.0 8.0 %collective-permute-start.10 = (bf16[2,256,256]{2,1,0:T(8,128)(2,1)S(1)}, bf16[2,256,256]{2,1,0:T(8,128)(2,1)S(1)}, u32[]{:S(2)}, u32[]{:S(2)}) collective-permute-start(bf16[2,256,256]{2,1,0:T(8,128)(2,1)S(1)} %broadcast_select_fusion.3), channel_id=1, source_target_pairs={{0,4},{1,5},{2,6},{3,7},{4,0},{5,1},{6,2},{7,3},{8,12},{9,13},{10,... | collective-permute-start | bytes 786440 | tf_op jit(solution)/shard_map/ppermute | solution.py:171
  52.1 17.4 %collective-permute-start.11 = (bf16[2,256,256]{2,1,0:T(8,128)(2,1)S(1)}, bf16[2,256,256]{2,1,0:T(8,128)(2,1)S(1)}, u32[]{:S(2)}, u32[]{:S(2)}) collective-permute-start(bf16[2,256,256]{2,1,0:T(8,128)(2,1)S(1)} %broadcast_select_fusion.4), channel_id=1, source_target_pairs={{0,8},{1,9},{2,10},{3,11},{4,12},{5,13},{6,14},{7,15},{8,0},{9,1},... | collective-permute-start | bytes 786440 | tf_op jit(solution)/shard_map/ppermute | solution.py:171
  54.6 16.5 %copy-start.2 = (bf16[1,2,4,256,256]{4,3,2,0,1:T(8,128)(2,1)S(1)}, bf16[1,2,4,256,256]{4,3,2,0,1:T(8,128)(2,1)}, u32[]{:S(2)}) copy-start(bf16[1,2,4,256,256]{4,3,2,0,1:T(8,128)(2,1)} %copy-done.1) | copy-start | bytes 3145732
  54.6 16.5 %copy-start.4 = (bf16[1,2,4,256,256]{4,3,2,0,1:T(8,128)(2,1)S(1)}, bf16[1,2,4,256,256]{4,3,2,0,1:T(8,128)(2,1)}, u32[]{:S(2)}) copy-start(bf16[1,2,4,256,256]{4,3,2,0,1:T(8,128)(2,1)} %copy-done.3) | copy-start | bytes 3145732
  54.7 7.0 %collective-permute-start.20 = (bf16[2,192,256]{2,1,0:T(8,128)(2,1)S(1)}, bf16[2,192,256]{2,1,0:T(8,128)(2,1)S(1)}, u32[]{:S(2)}, u32[]{:S(2)}) collective-permute-start(bf16[2,192,256]{2,1,0:T(8,128)(2,1)S(1)} %get-tuple-element.51), channel_id=1, source_target_pairs={{0,24},{1,97},{2,26},{3,99},{4,28},{5,101},{6,30},{7,103},{8,16},{... | collective-permute-start | bytes 589832 | tf_op jit(solution)/shard_map/ppermute | solution.py:149
  55.9 5.7 %collective-permute-start.18 = (bf16[2,192,256]{2,1,0:T(8,128)(2,1)S(1)}, bf16[2,192,256]{2,1,0:T(8,128)(2,1)S(1)}, u32[]{:S(2)}, u32[]{:S(2)}) collective-permute-start(bf16[2,192,256]{2,1,0:T(8,128)(2,1)S(1)} %get-tuple-element.52), channel_id=1, source_target_pairs={{0,8},{1,33},{2,10},{3,35},{4,12},{5,37},{6,14},{7,39},{8,0},{9,41... | collective-permute-start | bytes 589832 | tf_op jit(solution)/shard_map/ppermute | solution.py:149
  56.3 9.0 %collective-permute-start.19 = (bf16[2,192,256]{2,1,0:T(8,128)(2,1)S(1)}, bf16[2,192,256]{2,1,0:T(8,128)(2,1)S(1)}, u32[]{:S(2)}, u32[]{:S(2)}) collective-permute-start(bf16[2,192,256]{2,1,0:T(8,128)(2,1)S(1)} %get-tuple-element.53), channel_id=1, source_target_pairs={{0,16},{1,65},{2,18},{3,67},{4,20},{5,69},{6,22},{7,71},{8,24},{9,... | collective-permute-start | bytes 589832 | tf_op jit(solution)/shard_map/ppermute | solution.py:149
  65.4 11.9 %collective-permute-start.23 = (bf16[2,192,256]{2,1,0:T(8,128)(2,1)S(1)}, bf16[2,192,256]{2,1,0:T(8,128)(2,1)S(1)}, u32[]{:S(2)}, u32[]{:S(2)}) collective-permute-start(bf16[2,192,256]{2,1,0:T(8,128)(2,1)S(1)} %fusion.19), channel_id=1, source_target_pairs={{0,24},{1,97},{2,26},{3,99},{4,28},{5,101},{6,30},{7,103},{8,16},{... | collective-permute-start | bytes 589832 | tf_op jit(solution)/shard_map/ppermute | solution.py:156
  66.6 12.2 %collective-permute-start.22 = (bf16[2,192,256]{2,1,0:T(8,128)(2,1)S(1)}, bf16[2,192,256]{2,1,0:T(8,128)(2,1)S(1)}, u32[]{:S(2)}, u32[]{:S(2)}) collective-permute-start(bf16[2,192,256]{2,1,0:T(8,128)(2,1)S(1)} %fusion.19), channel_id=1, source_target_pairs={{0,16},{1,65},{2,18},{3,67},{4,20},{5,69},{6,22},{7,71},{8,24},{9,... | collective-permute-start | bytes 589832 | tf_op jit(solution)/shard_map/ppermute | solution.py:156
  67.7 14.6 %collective-permute-start.21 = (bf16[2,192,256]{2,1,0:T(8,128)(2,1)S(1)}, bf16[2,192,256]{2,1,0:T(8,128)(2,1)S(1)}, u32[]{:S(2)}, u32[]{:S(2)}) collective-permute-start(bf16[2,192,256]{2,1,0:T(8,128)(2,1)S(1)} %fusion.19), channel_id=1, source_target_pairs={{0,8},{1,33},{2,10},{3,35},{4,12},{5,37},{6,14},{7,39},{8,0},{9,41... | collective-permute-start | bytes 589832 | tf_op jit(solution)/shard_map/ppermute | solution.py:156
  69.6 12.9 %collective-permute-start.12 = (bf16[2,256,256]{2,1,0:T(8,128)(2,1)S(1)}, bf16[2,256,256]{2,1,0:T(8,128)(2,1)S(1)}, u32[]{:S(2)}, u32[]{:S(2)}) collective-permute-start(bf16[2,256,256]{2,1,0:T(8,128)(2,1)S(1)} %broadcast_select_fusion.5), channel_id=1, source_target_pairs={{0,16},{1,17},{2,18},{3,19},{4,20},{5,21},{6,22},{7,23},{8,24},{9,... | collective-permute-start | bytes 786440 | tf_op jit(solution)/shard_map/ppermute | solution.py:171
  72.6 11.0 %collective-permute-start.3 = (bf16[2,256,256]{2,1,0:T(8,128)(2,1)S(1)}, bf16[2,256,256]{2,1,0:T(8,128)(2,1)S(1)}, u32[]{:S(2)}, u32[]{:S(2)}) collective-permute-start(bf16[2,256,256]{2,1,0:T(8,128)(2,1)S(1)} %get-tuple-element.44), channel_id=1, source_target_pairs={{0,6},{1,7},{2,4},{3,5},{4,2},{5,3},{6,0},{7,1},{8,14},{9,15},{10,... | collective-permute-start | bytes 786440 | tf_op jit(solution)/shard_map/ppermute | solution.py:149
  77.2 6.4 %collective-permute-start.1 = (bf16[2,256,256]{2,1,0:T(8,128)(2,1)S(1)}, bf16[2,256,256]{2,1,0:T(8,128)(2,1)S(1)}, u32[]{:S(2)}, u32[]{:S(2)}) collective-permute-start(bf16[2,256,256]{2,1,0:T(8,128)(2,1)S(1)} %get-tuple-element.45), channel_id=1, source_target_pairs={{0,2},{1,3},{2,0},{3,1},{4,6},{5,7},{6,4},{7,5},{8,10},{9,11},{10,... | collective-permute-start | bytes 786440 | tf_op jit(solution)/shard_map/ppermute | solution.py:149
  78.8 12.7 %collective-permute-start.2 = (bf16[2,256,256]{2,1,0:T(8,128)(2,1)S(1)}, bf16[2,256,256]{2,1,0:T(8,128)(2,1)S(1)}, u32[]{:S(2)}, u32[]{:S(2)}) collective-permute-start(bf16[2,256,256]{2,1,0:T(8,128)(2,1)S(1)} %get-tuple-element.46), channel_id=1, source_target_pairs={{0,4},{1,5},{2,6},{3,7},{4,0},{5,1},{6,2},{7,3},{8,12},{9,13},{10,... | collective-permute-start | bytes 786440 | tf_op jit(solution)/shard_map/ppermute | solution.py:149
  82.6 15.3 %collective-permute-start.13 = (bf16[2,256,256]{2,1,0:T(8,128)(2,1)S(1)}, bf16[2,256,256]{2,1,0:T(8,128)(2,1)S(1)}, u32[]{:S(2)}, u32[]{:S(2)}) collective-permute-start(bf16[2,256,256]{2,1,0:T(8,128)(2,1)S(1)} %broadcast_select_fusion.6), channel_id=1, source_target_pairs={{0,32},{1,33},{2,34},{3,35},{4,36},{5,37},{6,38},{7,39},{8,40},{9,... | collective-permute-start | bytes 786440 | tf_op jit(solution)/shard_map/ppermute | solution.py:171
  91.6 10.5 %collective-permute-start.6 = (bf16[2,256,256]{2,1,0:T(8,128)(2,1)S(1)}, bf16[2,256,256]{2,1,0:T(8,128)(2,1)S(1)}, u32[]{:S(2)}, u32[]{:S(2)}) collective-permute-start(bf16[2,256,256]{2,1,0:T(8,128)(2,1)S(1)} %fusion.18), channel_id=1, source_target_pairs={{0,6},{1,7},{2,4},{3,5},{4,2},{5,3},{6,0},{7,1},{8,14},{9,15},{10,... | collective-permute-start | bytes 786440 | tf_op jit(solution)/shard_map/ppermute | solution.py:156
  91.7 11.7 %collective-permute-start.5 = (bf16[2,256,256]{2,1,0:T(8,128)(2,1)S(1)}, bf16[2,256,256]{2,1,0:T(8,128)(2,1)S(1)}, u32[]{:S(2)}, u32[]{:S(2)}) collective-permute-start(bf16[2,256,256]{2,1,0:T(8,128)(2,1)S(1)} %fusion.18), channel_id=1, source_target_pairs={{0,4},{1,5},{2,6},{3,7},{4,0},{5,1},{6,2},{7,3},{8,12},{9,13},{10,... | collective-permute-start | bytes 786440 | tf_op jit(solution)/shard_map/ppermute | solution.py:156
  93.2 12.3 %collective-permute-start.4 = (bf16[2,256,256]{2,1,0:T(8,128)(2,1)S(1)}, bf16[2,256,256]{2,1,0:T(8,128)(2,1)S(1)}, u32[]{:S(2)}, u32[]{:S(2)}) collective-permute-start(bf16[2,256,256]{2,1,0:T(8,128)(2,1)S(1)} %fusion.18), channel_id=1, source_target_pairs={{0,2},{1,3},{2,0},{3,1},{4,6},{5,7},{6,4},{7,5},{8,10},{9,11},{10,... | collective-permute-start | bytes 786440 | tf_op jit(solution)/shard_map/ppermute | solution.py:156
  95.9 30.1 %collective-permute-start.26 = (bf16[2,4,192,256]{3,2,1,0:T(8,128)(2,1)S(1)}, bf16[2,4,192,256]{3,2,1,0:T(8,128)(2,1)S(1)}, u32[]{:S(2)}, u32[]{:S(2)}) collective-permute-start(bf16[2,4,192,256]{3,2,1,0:T(8,128)(2,1)S(1)} %pad_maximum_fusion.5), channel_id=1, source_target_pairs={{0,96},{1,25},{2,98},{3,27},{4,100},{5,29},{6,102},{7,31},{8,104},... | collective-permute-start | bytes 2359304 | tf_op jit(solution)/shard_map/ppermute | solution.py:156
  97.9 28.2 %collective-permute-start.25 = (bf16[2,4,192,256]{3,2,1,0:T(8,128)(2,1)S(1)}, bf16[2,4,192,256]{3,2,1,0:T(8,128)(2,1)S(1)}, u32[]{:S(2)}, u32[]{:S(2)}) collective-permute-start(bf16[2,4,192,256]{3,2,1,0:T(8,128)(2,1)S(1)} %pad_maximum_fusion.5), channel_id=1, source_target_pairs={{0,64},{1,17},{2,66},{3,19},{4,68},{5,21},{6,70},{7,23},{8,72},{9,... | collective-permute-start | bytes 2359304 | tf_op jit(solution)/shard_map/ppermute | solution.py:156
  102.1 24.0 %collective-permute-start.24 = (bf16[2,4,192,256]{3,2,1,0:T(8,128)(2,1)S(1)}, bf16[2,4,192,256]{3,2,1,0:T(8,128)(2,1)S(1)}, u32[]{:S(2)}, u32[]{:S(2)}) collective-permute-start(bf16[2,4,192,256]{3,2,1,0:T(8,128)(2,1)S(1)} %pad_maximum_fusion.5), channel_id=1, source_target_pairs={{0,32},{1,9},{2,34},{3,11},{4,36},{5,13},{6,38},{7,15},{8,40},{9,1... | collective-permute-start | bytes 2359304 | tf_op jit(solution)/shard_map/ppermute | solution.py:156
  103.4 21.7 %collective-permute-start.14 = (bf16[2,256,256]{2,1,0:T(8,128)(2,1)S(1)}, bf16[2,256,256]{2,1,0:T(8,128)(2,1)S(1)}, u32[]{:S(2)}, u32[]{:S(2)}) collective-permute-start(bf16[2,256,256]{2,1,0:T(8,128)(2,1)S(1)} %broadcast_select_fusion.7), channel_id=1, source_target_pairs={{0,64},{1,65},{2,66},{3,67},{4,68},{5,69},{6,70},{7,71},{8,72},{9,... | collective-permute-start | bytes 786440 | tf_op jit(solution)/shard_map/ppermute | solution.py:171
  105.6 20.2 %copy-start.7 = (bf16[2,256,256]{2,1,0:T(8,128)(2,1)S(1)}, bf16[2,256,256]{2,1,0:T(8,128)(2,1)}, u32[]{:S(2)}) copy-start(bf16[2,256,256]{2,1,0:T(8,128)(2,1)} %param.7) | copy-start | bytes 786436
  105.8 24.8 %collective-permute-start.7 = (bf16[2,4,256,256]{3,2,1,0:T(8,128)(2,1)S(1)}, bf16[2,4,256,256]{3,2,1,0:T(8,128)(2,1)S(1)}, u32[]{:S(2)}, u32[]{:S(2)}) collective-permute-start(bf16[2,4,256,256]{3,2,1,0:T(8,128)(2,1)S(1)} %pad_maximum_fusion.3), channel_id=1, source_target_pairs={{0,1},{1,0},{2,3},{3,2},{4,5},{5,4},{6,7},{7,6},{8,9},{9,8},{10,11... | collective-permute-start | bytes 3145736 | tf_op jit(solution)/shard_map/ppermute | solution.py:156
  (3 other events, 5.8 us)

commit v17 on v16

--- a/solution.py
+++ b/solution.py
@@ -216,7 +216,7 @@
             out_ref[r, j] = block
 
 
-ROWS_PER_STEP = 2
+ROWS_PER_STEP = 4
 
 
 def both_updates(front, codes, row_codes, column1, column2, cross, inverse, upper1, upper2):

time: 150 us -> 151 us (level)
  no operation moved by 1% of the time
where the time goes in v17:
time: 151 us; the launch traced here: 150 us
  starting transfers between devices  43.1 us (29%)
  waiting for transfers between devices  42.9 us (28%)
  other arithmetic  24.5 us (16%)
  Pallas kernels  17.6 us (12%)
  local copies, waits for them, and re-layouts  10.6 us (7%)
  between operations  10.5 us (7%)
    ppermute x7, waiting for transfers between devices, all_bcast(): lax.ppermute(value, ('row', 'col'), [(d, d ^ 1 << b) for d in range(n)])  25.8 us
    ppermute x10, starting transfers between devices, xor_bcast(): lax.ppermute(groups[m], axes, digit_pairs(nrow, ncol, on_row, step, m))  19.6 us
    pallas_call x1, Pallas kernels, both_updates(): pl.pallas_call(update_kernel, grid_spec=pltpu.PrefetchScalarGridSpec(num_...  17.6 us
    ppermute x10, waiting for transfers between devices, xor_bcast(): lax.ppermute(groups[m], axes, digit_pairs(nrow, ncol, on_row, step, m))  13.6 us
    ppermute x10, starting transfers between devices, xor_bcast(): lax.ppermute(buf, axes, digit_pairs(nrow, ncol, on_row, step, m))  13.4 us
    ppermute x7, starting transfers between devices, all_bcast(): lax.ppermute(value, ('row', 'col'), [(d, d ^ 1 << b) for d in range(n)])  10.1 us
    select_n x11, other arithmetic, per_part(): return jnp.where(cond.reshape((-1,) + (1,) * (a.ndim - 1)), a, b)  6.85 us
    ppermute x10, waiting for transfers between devices, xor_bcast(): lax.ppermute(buf, axes, digit_pairs(nrow, ncol, on_row, step, m))  3.53 us
  transfers between devices with their start and end apart: 27, of which 8 were waited for; matrix products, arithmetic and copies ran while one was open for 19% of the time, Pallas kernels for 0%

profile of v17, /device:TPU:6, one launch (start us, length us, event | category | flops | bytes accessed | tf_op | source)
XLA Modules:
  0.0 150.0 jit_solution(14893431646271569559)
XLA Ops:
  11.2 1.7 %constant_dynamic-slice_fusion.1 = (bf16[8,1,256,256]{3,2,1,0:T(8,128)(2,1)S(1)}, bf16[8,1,256,256]{3,2,1,0:T(8,128)(2,1)S(1)}) fusion(bf16[8,12,256,256]{3,2,1,0:T(8,128)(2,1)} %front_ref.1, s32[]{:T(128)S(6)} %select_n.369, s32[]{:T(128)S(6)} %select_n.373), kind=kLoop, calls=%fused_computation.94 | loop fusion | bytes 4194312 | tf_op jit(solution)/shard_map/jit(dynamic_index_in_dim)/dynamic_slice | solution.py:282
  15.6 2.2 %dynamic-slice_select_fusion = (bf16[1,12,256,256]{3,2,1,0:T(8,128)(2,1)S(1)}, bf16[1,12,256,256]{3,2,1,0:T(8,128)(2,1)S(1)}) fusion(bf16[8,12,256,256]{3,2,1,0:T(8,128)(2,1)} %front_ref.1, s32[]{:T(128)S(6)} %select_n.402, pred[12]{0:T(512)(128)(4,1)S(1)} %get-tuple-element.5, s32[]{:T(128)S(6)} %select_n.397, pred[12]{0:T(512)(128)(4,1)S(1)} %get-tuple-element.6), kind=kLoop, calls=%fused_computation.18 | loop fusion | flops 1572864 | bytes 6291488 | tf_op jit(solution)/shard_map/jit(_where)/select_n | solution.py:247
  17.8 1.5 fusion.17
  19.3 4.0 %collective-permute-start.17 = (bf16[2,4,192,256]{3,2,1,0:T(8,128)(2,1)}, bf16[2,4,192,256]{3,2,1,0:T(8,128)(2,1)}, u32[]{:S(2)}, u32[]{:S(2)}) collective-permute-start(bf16[2,4,192,256]{3,2,1,0:T(8,128)(2,1)} %get-tuple-element.33), channel_id=1, source_target_pairs={{0,96},{1,25},{2,98},{3,27},{4,100},{5,29},{6,102},{7,31},{8,104},... | collective-permute-start | bytes 2359304 | tf_op jit(solution)/shard_map/ppermute | solution.py:149
  23.3 1.5 collective-permute-start.16
  30.3 1.8 %add_add_fusion = (s32[8]{0:T(128)}, pred[8]{0:T(512)(128)(4,1)S(1)}, pred[8]{0:T(512)(128)(4,1)S(1)}) fusion(s32[8]{0:T(128)S(1)} %gather_fusion, pred[]{:T(512)S(6)} %ne.98, s32[]{:T(128)} %bitcast.2, s32[]{:T(128)S(6)} %axis_index.15, s32[]{:T(128)} %bitcast.1), kind=kLoop, calls=%fused_computation.122 | loop fusion | flops 104 | bytes 93 | tf_op jit(solution)/shard_map/add | solution.py:311
  34.3 1.8 %broadcast_select_fusion.2 = bf16[2,256,256]{2,1,0:T(8,128)(2,1)} fusion(bf16[2,256,256]{2,1,0:T(8,128)(2,1)} %collective-permute-done.8, pred[2]{0:T(512)(128)(4,1)S(1)} %get-tuple-element.68, bf16[1,256,256]{2,1,0:T(8,128)(2,1)S(1)} %get-tuple-element.25, bf16[1,256,256]{2,1,0:T(8,128)(2,1)S(1)} %get-tuple-element.24), kind=kLoop, calls=%fused_computation.58 | loop fusion | flops 262144 | bytes 786434 | tf_op jit(solution)/shard_map/jit(_where)/select_n | solution.py:13
  36.0 1.6 %collective-permute-start.9 = (bf16[2,256,256]{2,1,0:T(8,128)(2,1)}, bf16[2,256,256]{2,1,0:T(8,128)(2,1)}, u32[]{:S(2)}, u32[]{:S(2)}) collective-permute-start(bf16[2,256,256]{2,1,0:T(8,128)(2,1)} %broadcast_select_fusion.2), channel_id=1, source_target_pairs={{0,2},{1,3},{2,0},{3,1},{4,6},{5,7},{6,4},{7,5},{8,10},{9,11},{10,... | collective-permute-start | bytes 786440 | tf_op jit(solution)/shard_map/ppermute | solution.py:171
  39.0 3.9 %collective-permute-done.9 = bf16[2,256,256]{2,1,0:T(8,128)(2,1)} collective-permute-done((bf16[2,256,256]{2,1,0:T(8,128)(2,1)}, bf16[2,256,256]{2,1,0:T(8,128)(2,1)}, u32[]{:S(2)}, u32[]{:S(2)}) %collective-permute-start.9) | collective-permute-done | bytes 262176 | tf_op jit(solution)/shard_map/ppermute | solution.py:171
  44.0 3.3 %collective-permute-start.10 = (bf16[2,256,256]{2,1,0:T(8,128)(2,1)S(1)}, bf16[2,256,256]{2,1,0:T(8,128)(2,1)S(1)}, u32[]{:S(2)}, u32[]{:S(2)}) collective-permute-start(bf16[2,256,256]{2,1,0:T(8,128)(2,1)S(1)} %broadcast_select_fusion.3), channel_id=1, source_target_pairs={{0,4},{1,5},{2,6},{3,7},{4,0},{5,1},{6,2},{7,3},{8,12},{9,13},{10,... | collective-permute-start | bytes 786440 | tf_op jit(solution)/shard_map/ppermute | solution.py:171
  47.4 1.7 %slice_bitcast_fusion.11 = (bf16[256,256]{1,0:T(8,128)(2,1)}, bf16[256,256]{1,0:T(8,128)(2,1)}) fusion(bf16[2,256,256]{2,1,0:T(8,128)(2,1)} %param.7), kind=kLoop, calls=%fused_computation.78 | loop fusion | bytes 524288 | tf_op jit(solution)/shard_map/squeeze | solution.py:242
  49.1 2.9 %collective-permute-done.10 = bf16[2,256,256]{2,1,0:T(8,128)(2,1)S(1)} collective-permute-done((bf16[2,256,256]{2,1,0:T(8,128)(2,1)S(1)}, bf16[2,256,256]{2,1,0:T(8,128)(2,1)S(1)}, u32[]{:S(2)}, u32[]{:S(2)}) %collective-permute-start.10) | collective-permute-done | bytes 262176 | tf_op jit(solution)/shard_map/ppermute | solution.py:171
  52.8 1.8 %fusion.14 = bf16[2,4,192,256]{3,2,1,0:T(8,128)(2,1)S(1)} fusion(bf16[1,4,4,192,256]{4,3,2,0,1:T(8,128)(2,1)S(1)} %bitcast.173, bf16[1,4,4,192,256]{4,3,2,0,1:T(8,128)(2,1)S(1)} %bitcast.171, bf16[2,4,192,256]{3,2,1,0:T(8,128)(2,1)} %collective-permute-done.15, bf16[2,4,192,256]{3,2,1,0:T(8,128)(2,1)} %collective-permute-done.16, ...), kind=kLoop, calls=%fused_computation.38 | loop fusion | flops 1572864 | bytes 6291462 | tf_op jit(solution)/shard_map/jit(_where)/select_n | solution.py:13
  56.3 3.2 %collective-permute-start.19 = (bf16[2,192,256]{2,1,0:T(8,128)(2,1)S(1)}, bf16[2,192,256]{2,1,0:T(8,128)(2,1)S(1)}, u32[]{:S(2)}, u32[]{:S(2)}) collective-permute-start(bf16[2,192,256]{2,1,0:T(8,128)(2,1)S(1)} %get-tuple-element.53), channel_id=1, source_target_pairs={{0,16},{1,65},{2,18},{3,67},{4,20},{5,69},{6,22},{7,71},{8,24},{9,... | collective-permute-start | bytes 589832 | tf_op jit(solution)/shard_map/ppermute | solution.py:149
  59.5 2.2 %collective-permute-done.20 = bf16[2,192,256]{2,1,0:T(8,128)(2,1)S(1)} collective-permute-done((bf16[2,192,256]{2,1,0:T(8,128)(2,1)S(1)}, bf16[2,192,256]{2,1,0:T(8,128)(2,1)S(1)}, u32[]{:S(2)}, u32[]{:S(2)}) %collective-permute-start.20) | collective-permute-done | bytes 196640 | tf_op jit(solution)/shard_map/ppermute | solution.py:149
  61.7 3.6 %collective-permute-done.19 = bf16[2,192,256]{2,1,0:T(8,128)(2,1)S(1)} collective-permute-done((bf16[2,192,256]{2,1,0:T(8,128)(2,1)S(1)}, bf16[2,192,256]{2,1,0:T(8,128)(2,1)S(1)}, u32[]{:S(2)}, u32[]{:S(2)}) %collective-permute-start.19) | collective-permute-done | bytes 196640 | tf_op jit(solution)/shard_map/ppermute | solution.py:149
  67.7 1.8 %collective-permute-start.21 = (bf16[2,192,256]{2,1,0:T(8,128)(2,1)S(1)}, bf16[2,192,256]{2,1,0:T(8,128)(2,1)S(1)}, u32[]{:S(2)}, u32[]{:S(2)}) collective-permute-start(bf16[2,192,256]{2,1,0:T(8,128)(2,1)S(1)} %fusion.19), channel_id=1, source_target_pairs={{0,8},{1,33},{2,10},{3,35},{4,12},{5,37},{6,14},{7,39},{8,0},{9,41... | collective-permute-start | bytes 589832 | tf_op jit(solution)/shard_map/ppermute | solution.py:156
  69.6 1.5 %collective-permute-start.12 = (bf16[2,256,256]{2,1,0:T(8,128)(2,1)S(1)}, bf16[2,256,256]{2,1,0:T(8,128)(2,1)S(1)}, u32[]{:S(2)}, u32[]{:S(2)}) collective-permute-start(bf16[2,256,256]{2,1,0:T(8,128)(2,1)S(1)} %broadcast_select_fusion.5), channel_id=1, source_target_pairs={{0,16},{1,17},{2,18},{3,19},{4,20},{5,21},{6,22},{7,23},{8,24},{9,... | collective-permute-start | bytes 786440 | tf_op jit(solution)/shard_map/ppermute | solution.py:171
  72.6 3.7 %collective-permute-start.3 = (bf16[2,256,256]{2,1,0:T(8,128)(2,1)S(1)}, bf16[2,256,256]{2,1,0:T(8,128)(2,1)S(1)}, u32[]{:S(2)}, u32[]{:S(2)}) collective-permute-start(bf16[2,256,256]{2,1,0:T(8,128)(2,1)S(1)} %get-tuple-element.44), channel_id=1, source_target_pairs={{0,6},{1,7},{2,4},{3,5},{4,2},{5,3},{6,0},{7,1},{8,14},{9,15},{10,... | collective-permute-start | bytes 786440 | tf_op jit(solution)/shard_map/ppermute | solution.py:149
  77.2 1.6 %collective-permute-start.1 = (bf16[2,256,256]{2,1,0:T(8,128)(2,1)S(1)}, bf16[2,256,256]{2,1,0:T(8,128)(2,1)S(1)}, u32[]{:S(2)}, u32[]{:S(2)}) collective-permute-start(bf16[2,256,256]{2,1,0:T(8,128)(2,1)S(1)} %get-tuple-element.45), channel_id=1, source_target_pairs={{0,2},{1,3},{2,0},{3,1},{4,6},{5,7},{6,4},{7,5},{8,10},{9,11},{10,... | collective-permute-start | bytes 786440 | tf_op jit(solution)/shard_map/ppermute | solution.py:149
  78.8 3.5 %collective-permute-start.2 = (bf16[2,256,256]{2,1,0:T(8,128)(2,1)S(1)}, bf16[2,256,256]{2,1,0:T(8,128)(2,1)S(1)}, u32[]{:S(2)}, u32[]{:S(2)}) collective-permute-start(bf16[2,256,256]{2,1,0:T(8,128)(2,1)S(1)} %get-tuple-element.46), channel_id=1, source_target_pairs={{0,4},{1,5},{2,6},{3,7},{4,0},{5,1},{6,2},{7,3},{8,12},{9,13},{10,... | collective-permute-start | bytes 786440 | tf_op jit(solution)/shard_map/ppermute | solution.py:149
  83.7 7.8 %collective-permute-done.2 = bf16[2,256,256]{2,1,0:T(8,128)(2,1)S(1)} collective-permute-done((bf16[2,256,256]{2,1,0:T(8,128)(2,1)S(1)}, bf16[2,256,256]{2,1,0:T(8,128)(2,1)S(1)}, u32[]{:S(2)}, u32[]{:S(2)}) %collective-permute-start.2) | collective-permute-done | bytes 262176 | tf_op jit(solution)/shard_map/ppermute | solution.py:149
  91.7 1.4 collective-permute-start.5
  93.2 2.7 %collective-permute-start.4 = (bf16[2,256,256]{2,1,0:T(8,128)(2,1)S(1)}, bf16[2,256,256]{2,1,0:T(8,128)(2,1)S(1)}, u32[]{:S(2)}, u32[]{:S(2)}) collective-permute-start(bf16[2,256,256]{2,1,0:T(8,128)(2,1)S(1)} %fusion.18), channel_id=1, source_target_pairs={{0,2},{1,3},{2,0},{3,1},{4,6},{5,7},{6,4},{7,5},{8,10},{9,11},{10,... | collective-permute-start | bytes 786440 | tf_op jit(solution)/shard_map/ppermute | solution.py:156
  95.9 1.9 %collective-permute-start.26 = (bf16[2,4,192,256]{3,2,1,0:T(8,128)(2,1)S(1)}, bf16[2,4,192,256]{3,2,1,0:T(8,128)(2,1)S(1)}, u32[]{:S(2)}, u32[]{:S(2)}) collective-permute-start(bf16[2,4,192,256]{3,2,1,0:T(8,128)(2,1)S(1)} %pad_maximum_fusion.5), channel_id=1, source_target_pairs={{0,96},{1,25},{2,98},{3,27},{4,100},{5,29},{6,102},{7,31},{8,104},... | collective-permute-start | bytes 2359304 | tf_op jit(solution)/shard_map/ppermute | solution.py:156
  97.9 1.5 %collective-permute-start.25 = (bf16[2,4,192,256]{3,2,1,0:T(8,128)(2,1)S(1)}, bf16[2,4,192,256]{3,2,1,0:T(8,128)(2,1)S(1)}, u32[]{:S(2)}, u32[]{:S(2)}) collective-permute-start(bf16[2,4,192,256]{3,2,1,0:T(8,128)(2,1)S(1)} %pad_maximum_fusion.5), channel_id=1, source_target_pairs={{0,64},{1,17},{2,66},{3,19},{4,68},{5,21},{6,70},{7,23},{8,72},{9,... | collective-permute-start | bytes 2359304 | tf_op jit(solution)/shard_map/ppermute | solution.py:156
  99.5 2.6 %collective-permute-done.6 = bf16[2,256,256]{2,1,0:T(8,128)(2,1)S(1)} collective-permute-done((bf16[2,256,256]{2,1,0:T(8,128)(2,1)S(1)}, bf16[2,256,256]{2,1,0:T(8,128)(2,1)S(1)}, u32[]{:S(2)}, u32[]{:S(2)}) %collective-permute-start.6) | collective-permute-done | bytes 262176 | tf_op jit(solution)/shard_map/ppermute | solution.py:156
  103.4 2.0 %collective-permute-start.14 = (bf16[2,256,256]{2,1,0:T(8,128)(2,1)S(1)}, bf16[2,256,256]{2,1,0:T(8,128)(2,1)S(1)}, u32[]{:S(2)}, u32[]{:S(2)}) collective-permute-start(bf16[2,256,256]{2,1,0:T(8,128)(2,1)S(1)} %broadcast_select_fusion.7), channel_id=1, source_target_pairs={{0,64},{1,65},{2,66},{3,67},{4,68},{5,69},{6,70},{7,71},{8,72},{9,... | collective-permute-start | bytes 786440 | tf_op jit(solution)/shard_map/ppermute | solution.py:171
  106.1 19.0 %collective-permute-done.14 = bf16[2,256,256]{2,1,0:T(8,128)(2,1)S(1)} collective-permute-done((bf16[2,256,256]{2,1,0:T(8,128)(2,1)S(1)}, bf16[2,256,256]{2,1,0:T(8,128)(2,1)S(1)}, u32[]{:S(2)}, u32[]{:S(2)}) %collective-permute-start.14) | collective-permute-done | bytes 262176 | tf_op jit(solution)/shard_map/ppermute | solution.py:171
  128.6 2.0 %fusion.3.u2_ref = bf16[12,256,256]{2,1,0:T(8,128)(2,1)} fusion(bf16[1,12,256,256]{3,2,1,0:T(8,128)(2,1)S(1)} %bitcast.174, f32[12,256,256]{1,2,0:T(8,128)S(1)} %fusion.20, pred[12]{0:T(512)(128)(4,1)S(1)} %get-tuple-element.11, pred[12]{0:T(512)(128)(4,1)S(1)} %get-tuple-element.9, bf16[256,256]{1,0:T(8,128)(2,1)S(1)} %fusion.4), kind=kLoop, calls=%fused_computation.17 | loop fusion | flops 3932160 | bytes 6422552 | tf_op jit(solution)/shard_map/squeeze | solution.py:309
  130.8 1.5 %pad_maximum_fusion.1 = (bf16[1,2,4,256,256]{4,3,2,1,0:T(8,128)(2,1)}, bf16[1,2,4,256,256]{4,3,2,1,0:T(8,128)(2,1)}) fusion(bf16[2,1,4,256,256]{4,3,2,1,0:T(8,128)(2,1)S(1)} %get-tuple-element.36, bf16[2,1,4,256,256]{4,3,2,1,0:T(8,128)(2,1)S(1)} %get-tuple-element.37), kind=kLoop, calls=%fused_computation.26 | loop fusion | flops 1048576 | bytes 4194304 | tf_op jit(solution)/shard_map/stack | solution.py:159
  132.4 17.6 %shard_map.46 = bf16[8,12,256,256]{3,2,1,0:T(8,128)(2,1)} custom-call(s32[8,12]{1,0:T(8,128)} %select_add_fusion.codes, s32[8]{0:T(128)} %get-tuple-element.19.row_codes, bf16[8,12,256,256]{3,2,1,0:T(8,128)(2,1)} %front_ref.1, bf16[8,256,256]{2,1,0:T(8,128)(2,1)} %bitcast.178, bf16[8,256,256]{2,1,0:T(8,128)(2,1)} %bitcast.177, ...), custom_call_target="tpu_custom_call" | custom-call | tf_op jit(solution)/shard_map/pallas_call | solution.py:229
  (100 shorter events, 28.8 us)
Async XLA Ops:
  7.4 7.6 %copy-start.6 = (s32[8,16,12,8]{1,0,3,2:T(8,128)}, s32[8,16,12,8]{1,0,3,2:T(8,128)S(1)}, u32[]{:S(2)}) copy-start(s32[8,16,12,8]{1,0,3,2:T(8,128)S(1)} %reshape.568) | copy-start | bytes 147460
  11.0 23.3 %collective-permute-start.8 = (bf16[2,256,256]{2,1,0:T(8,128)(2,1)}, bf16[2,256,256]{2,1,0:T(8,128)(2,1)}, u32[]{:S(2)}, u32[]{:S(2)}) collective-permute-start(bf16[2,256,256]{2,1,0:T(8,128)(2,1)} %pad_maximum_fusion.6), channel_id=1, source_target_pairs={{0,1},{1,0},{2,3},{3,2},{4,5},{5,4},{6,7},{7,6},{8,9},{9,8},{10,11... | collective-permute-start | bytes 786440 | tf_op jit(solution)/shard_map/ppermute | solution.py:171
  14.5 56.6 %collective-permute-start = (bf16[2,4,256,256]{3,2,1,0:T(8,128)(2,1)}, bf16[2,4,256,256]{3,2,1,0:T(8,128)(2,1)}, u32[]{:S(2)}, u32[]{:S(2)}) collective-permute-start(bf16[2,4,256,256]{3,2,1,0:T(8,128)(2,1)} %fusion.9), channel_id=1, source_target_pairs={{0,1},{1,0},{2,3},{3,2},{4,5},{5,4},{6,7},{7,6},{8,9},{9,8},{10,11... | collective-permute-start | bytes 3145736 | tf_op jit(solution)/shard_map/ppermute | solution.py:149
  17.8 11.7 %copy-start.5 = (s32[128,96]{0,1:T(8,128)S(1)}, s32[128,96]{0,1:T(8,128)}, u32[]{:S(2)}) copy-start(s32[128,96]{0,1:T(8,128)} %param.5) | copy-start | bytes 147460
  19.3 33.5 %collective-permute-start.17 = (bf16[2,4,192,256]{3,2,1,0:T(8,128)(2,1)}, bf16[2,4,192,256]{3,2,1,0:T(8,128)(2,1)}, u32[]{:S(2)}, u32[]{:S(2)}) collective-permute-start(bf16[2,4,192,256]{3,2,1,0:T(8,128)(2,1)} %get-tuple-element.33), channel_id=1, source_target_pairs={{0,96},{1,25},{2,98},{3,27},{4,100},{5,29},{6,102},{7,31},{8,104},... | collective-permute-start | bytes 2359304 | tf_op jit(solution)/shard_map/ppermute | solution.py:149
  23.3 29.5 %collective-permute-start.15 = (bf16[2,4,192,256]{3,2,1,0:T(8,128)(2,1)}, bf16[2,4,192,256]{3,2,1,0:T(8,128)(2,1)}, u32[]{:S(2)}, u32[]{:S(2)}) collective-permute-start(bf16[2,4,192,256]{3,2,1,0:T(8,128)(2,1)} %get-tuple-element.34), channel_id=1, source_target_pairs={{0,32},{1,9},{2,34},{3,11},{4,36},{5,13},{6,38},{7,15},{8,40},{9,1... | collective-permute-start | bytes 2359304 | tf_op jit(solution)/shard_map/ppermute | solution.py:149
  23.3 29.5 %collective-permute-start.16 = (bf16[2,4,192,256]{3,2,1,0:T(8,128)(2,1)}, bf16[2,4,192,256]{3,2,1,0:T(8,128)(2,1)}, u32[]{:S(2)}, u32[]{:S(2)}) collective-permute-start(bf16[2,4,192,256]{3,2,1,0:T(8,128)(2,1)} %get-tuple-element.35), channel_id=1, source_target_pairs={{0,64},{1,17},{2,66},{3,19},{4,68},{5,21},{6,70},{7,23},{8,72},{9,... | collective-permute-start | bytes 2359304 | tf_op jit(solution)/shard_map/ppermute | solution.py:149
  36.0 6.9 %collective-permute-start.9 = (bf16[2,256,256]{2,1,0:T(8,128)(2,1)}, bf16[2,256,256]{2,1,0:T(8,128)(2,1)}, u32[]{:S(2)}, u32[]{:S(2)}) collective-permute-start(bf16[2,256,256]{2,1,0:T(8,128)(2,1)} %broadcast_select_fusion.2), channel_id=1, source_target_pairs={{0,2},{1,3},{2,0},{3,1},{4,6},{5,7},{6,4},{7,5},{8,10},{9,11},{10,... | collective-permute-start | bytes 786440 | tf_op jit(solution)/shard_map/ppermute | solution.py:171
  44.0 8.0 %collective-permute-start.10 = (bf16[2,256,256]{2,1,0:T(8,128)(2,1)S(1)}, bf16[2,256,256]{2,1,0:T(8,128)(2,1)S(1)}, u32[]{:S(2)}, u32[]{:S(2)}) collective-permute-start(bf16[2,256,256]{2,1,0:T(8,128)(2,1)S(1)} %broadcast_select_fusion.3), channel_id=1, source_target_pairs={{0,4},{1,5},{2,6},{3,7},{4,0},{5,1},{6,2},{7,3},{8,12},{9,13},{10,... | collective-permute-start | bytes 786440 | tf_op jit(solution)/shard_map/ppermute | solution.py:171
  52.1 17.4 %collective-permute-start.11 = (bf16[2,256,256]{2,1,0:T(8,128)(2,1)S(1)}, bf16[2,256,256]{2,1,0:T(8,128)(2,1)S(1)}, u32[]{:S(2)}, u32[]{:S(2)}) collective-permute-start(bf16[2,256,256]{2,1,0:T(8,128)(2,1)S(1)} %broadcast_select_fusion.4), channel_id=1, source_target_pairs={{0,8},{1,9},{2,10},{3,11},{4,12},{5,13},{6,14},{7,15},{8,0},{9,1},... | collective-permute-start | bytes 786440 | tf_op jit(solution)/shard_map/ppermute | solution.py:171
  54.6 16.5 %copy-start.2 = (bf16[1,2,4,256,256]{4,3,2,0,1:T(8,128)(2,1)S(1)}, bf16[1,2,4,256,256]{4,3,2,0,1:T(8,128)(2,1)}, u32[]{:S(2)}) copy-start(bf16[1,2,4,256,256]{4,3,2,0,1:T(8,128)(2,1)} %copy-done.1) | copy-start | bytes 3145732
  54.6 16.5 %copy-start.4 = (bf16[1,2,4,256,256]{4,3,2,0,1:T(8,128)(2,1)S(1)}, bf16[1,2,4,256,256]{4,3,2,0,1:T(8,128)(2,1)}, u32[]{:S(2)}) copy-start(bf16[1,2,4,256,256]{4,3,2,0,1:T(8,128)(2,1)} %copy-done.3) | copy-start | bytes 3145732
  54.7 7.0 %collective-permute-start.20 = (bf16[2,192,256]{2,1,0:T(8,128)(2,1)S(1)}, bf16[2,192,256]{2,1,0:T(8,128)(2,1)S(1)}, u32[]{:S(2)}, u32[]{:S(2)}) collective-permute-start(bf16[2,192,256]{2,1,0:T(8,128)(2,1)S(1)} %get-tuple-element.51), channel_id=1, source_target_pairs={{0,24},{1,97},{2,26},{3,99},{4,28},{5,101},{6,30},{7,103},{8,16},{... | collective-permute-start | bytes 589832 | tf_op jit(solution)/shard_map/ppermute | solution.py:149
  55.9 5.7 %collective-permute-start.18 = (bf16[2,192,256]{2,1,0:T(8,128)(2,1)S(1)}, bf16[2,192,256]{2,1,0:T(8,128)(2,1)S(1)}, u32[]{:S(2)}, u32[]{:S(2)}) collective-permute-start(bf16[2,192,256]{2,1,0:T(8,128)(2,1)S(1)} %get-tuple-element.52), channel_id=1, source_target_pairs={{0,8},{1,33},{2,10},{3,35},{4,12},{5,37},{6,14},{7,39},{8,0},{9,41... | collective-permute-start | bytes 589832 | tf_op jit(solution)/shard_map/ppermute | solution.py:149
  56.3 9.0 %collective-permute-start.19 = (bf16[2,192,256]{2,1,0:T(8,128)(2,1)S(1)}, bf16[2,192,256]{2,1,0:T(8,128)(2,1)S(1)}, u32[]{:S(2)}, u32[]{:S(2)}) collective-permute-start(bf16[2,192,256]{2,1,0:T(8,128)(2,1)S(1)} %get-tuple-element.53), channel_id=1, source_target_pairs={{0,16},{1,65},{2,18},{3,67},{4,20},{5,69},{6,22},{7,71},{8,24},{9,... | collective-permute-start | bytes 589832 | tf_op jit(solution)/shard_map/ppermute | solution.py:149
  65.4 11.9 %collective-permute-start.23 = (bf16[2,192,256]{2,1,0:T(8,128)(2,1)S(1)}, bf16[2,192,256]{2,1,0:T(8,128)(2,1)S(1)}, u32[]{:S(2)}, u32[]{:S(2)}) collective-permute-start(bf16[2,192,256]{2,1,0:T(8,128)(2,1)S(1)} %fusion.19), channel_id=1, source_target_pairs={{0,24},{1,97},{2,26},{3,99},{4,28},{5,101},{6,30},{7,103},{8,16},{... | collective-permute-start | bytes 589832 | tf_op jit(solution)/shard_map/ppermute | solution.py:156
  66.6 12.2 %collective-permute-start.22 = (bf16[2,192,256]{2,1,0:T(8,128)(2,1)S(1)}, bf16[2,192,256]{2,1,0:T(8,128)(2,1)S(1)}, u32[]{:S(2)}, u32[]{:S(2)}) collective-permute-start(bf16[2,192,256]{2,1,0:T(8,128)(2,1)S(1)} %fusion.19), channel_id=1, source_target_pairs={{0,16},{1,65},{2,18},{3,67},{4,20},{5,69},{6,22},{7,71},{8,24},{9,... | collective-permute-start | bytes 589832 | tf_op jit(solution)/shard_map/ppermute | solution.py:156
  67.7 14.6 %collective-permute-start.21 = (bf16[2,192,256]{2,1,0:T(8,128)(2,1)S(1)}, bf16[2,192,256]{2,1,0:T(8,128)(2,1)S(1)}, u32[]{:S(2)}, u32[]{:S(2)}) collective-permute-start(bf16[2,192,256]{2,1,0:T(8,128)(2,1)S(1)} %fusion.19), channel_id=1, source_target_pairs={{0,8},{1,33},{2,10},{3,35},{4,12},{5,37},{6,14},{7,39},{8,0},{9,41... | collective-permute-start | bytes 589832 | tf_op jit(solution)/shard_map/ppermute | solution.py:156
  69.6 12.9 %collective-permute-start.12 = (bf16[2,256,256]{2,1,0:T(8,128)(2,1)S(1)}, bf16[2,256,256]{2,1,0:T(8,128)(2,1)S(1)}, u32[]{:S(2)}, u32[]{:S(2)}) collective-permute-start(bf16[2,256,256]{2,1,0:T(8,128)(2,1)S(1)} %broadcast_select_fusion.5), channel_id=1, source_target_pairs={{0,16},{1,17},{2,18},{3,19},{4,20},{5,21},{6,22},{7,23},{8,24},{9,... | collective-permute-start | bytes 786440 | tf_op jit(solution)/shard_map/ppermute | solution.py:171
  72.6 11.0 %collective-permute-start.3 = (bf16[2,256,256]{2,1,0:T(8,128)(2,1)S(1)}, bf16[2,256,256]{2,1,0:T(8,128)(2,1)S(1)}, u32[]{:S(2)}, u32[]{:S(2)}) collective-permute-start(bf16[2,256,256]{2,1,0:T(8,128)(2,1)S(1)} %get-tuple-element.44), channel_id=1, source_target_pairs={{0,6},{1,7},{2,4},{3,5},{4,2},{5,3},{6,0},{7,1},{8,14},{9,15},{10,... | collective-permute-start | bytes 786440 | tf_op jit(solution)/shard_map/ppermute | solution.py:149
  77.2 6.4 %collective-permute-start.1 = (bf16[2,256,256]{2,1,0:T(8,128)(2,1)S(1)}, bf16[2,256,256]{2,1,0:T(8,128)(2,1)S(1)}, u32[]{:S(2)}, u32[]{:S(2)}) collective-permute-start(bf16[2,256,256]{2,1,0:T(8,128)(2,1)S(1)} %get-tuple-element.45), channel_id=1, source_target_pairs={{0,2},{1,3},{2,0},{3,1},{4,6},{5,7},{6,4},{7,5},{8,10},{9,11},{10,... | collective-permute-start | bytes 786440 | tf_op jit(solution)/shard_map/ppermute | solution.py:149
  78.8 12.7 %collective-permute-start.2 = (bf16[2,256,256]{2,1,0:T(8,128)(2,1)S(1)}, bf16[2,256,256]{2,1,0:T(8,128)(2,1)S(1)}, u32[]{:S(2)}, u32[]{:S(2)}) collective-permute-start(bf16[2,256,256]{2,1,0:T(8,128)(2,1)S(1)} %get-tuple-element.46), channel_id=1, source_target_pairs={{0,4},{1,5},{2,6},{3,7},{4,0},{5,1},{6,2},{7,3},{8,12},{9,13},{10,... | collective-permute-start | bytes 786440 | tf_op jit(solution)/shard_map/ppermute | solution.py:149
  82.6 15.3 %collective-permute-start.13 = (bf16[2,256,256]{2,1,0:T(8,128)(2,1)S(1)}, bf16[2,256,256]{2,1,0:T(8,128)(2,1)S(1)}, u32[]{:S(2)}, u32[]{:S(2)}) collective-permute-start(bf16[2,256,256]{2,1,0:T(8,128)(2,1)S(1)} %broadcast_select_fusion.6), channel_id=1, source_target_pairs={{0,32},{1,33},{2,34},{3,35},{4,36},{5,37},{6,38},{7,39},{8,40},{9,... | collective-permute-start | bytes 786440 | tf_op jit(solution)/shard_map/ppermute | solution.py:171
  91.6 10.5 %collective-permute-start.6 = (bf16[2,256,256]{2,1,0:T(8,128)(2,1)S(1)}, bf16[2,256,256]{2,1,0:T(8,128)(2,1)S(1)}, u32[]{:S(2)}, u32[]{:S(2)}) collective-permute-start(bf16[2,256,256]{2,1,0:T(8,128)(2,1)S(1)} %fusion.18), channel_id=1, source_target_pairs={{0,6},{1,7},{2,4},{3,5},{4,2},{5,3},{6,0},{7,1},{8,14},{9,15},{10,... | collective-permute-start | bytes 786440 | tf_op jit(solution)/shard_map/ppermute | solution.py:156
  91.7 11.7 %collective-permute-start.5 = (bf16[2,256,256]{2,1,0:T(8,128)(2,1)S(1)}, bf16[2,256,256]{2,1,0:T(8,128)(2,1)S(1)}, u32[]{:S(2)}, u32[]{:S(2)}) collective-permute-start(bf16[2,256,256]{2,1,0:T(8,128)(2,1)S(1)} %fusion.18), channel_id=1, source_target_pairs={{0,4},{1,5},{2,6},{3,7},{4,0},{5,1},{6,2},{7,3},{8,12},{9,13},{10,... | collective-permute-start | bytes 786440 | tf_op jit(solution)/shard_map/ppermute | solution.py:156
  93.2 12.3 %collective-permute-start.4 = (bf16[2,256,256]{2,1,0:T(8,128)(2,1)S(1)}, bf16[2,256,256]{2,1,0:T(8,128)(2,1)S(1)}, u32[]{:S(2)}, u32[]{:S(2)}) collective-permute-start(bf16[2,256,256]{2,1,0:T(8,128)(2,1)S(1)} %fusion.18), channel_id=1, source_target_pairs={{0,2},{1,3},{2,0},{3,1},{4,6},{5,7},{6,4},{7,5},{8,10},{9,11},{10,... | collective-permute-start | bytes 786440 | tf_op jit(solution)/shard_map/ppermute | solution.py:156
  95.9 30.1 %collective-permute-start.26 = (bf16[2,4,192,256]{3,2,1,0:T(8,128)(2,1)S(1)}, bf16[2,4,192,256]{3,2,1,0:T(8,128)(2,1)S(1)}, u32[]{:S(2)}, u32[]{:S(2)}) collective-permute-start(bf16[2,4,192,256]{3,2,1,0:T(8,128)(2,1)S(1)} %pad_maximum_fusion.5), channel_id=1, source_target_pairs={{0,96},{1,25},{2,98},{3,27},{4,100},{5,29},{6,102},{7,31},{8,104},... | collective-permute-start | bytes 2359304 | tf_op jit(solution)/shard_map/ppermute | solution.py:156
  97.9 28.2 %collective-permute-start.25 = (bf16[2,4,192,256]{3,2,1,0:T(8,128)(2,1)S(1)}, bf16[2,4,192,256]{3,2,1,0:T(8,128)(2,1)S(1)}, u32[]{:S(2)}, u32[]{:S(2)}) collective-permute-start(bf16[2,4,192,256]{3,2,1,0:T(8,128)(2,1)S(1)} %pad_maximum_fusion.5), channel_id=1, source_target_pairs={{0,64},{1,17},{2,66},{3,19},{4,68},{5,21},{6,70},{7,23},{8,72},{9,... | collective-permute-start | bytes 2359304 | tf_op jit(solution)/shard_map/ppermute | solution.py:156
  102.1 24.0 %collective-permute-start.24 = (bf16[2,4,192,256]{3,2,1,0:T(8,128)(2,1)S(1)}, bf16[2,4,192,256]{3,2,1,0:T(8,128)(2,1)S(1)}, u32[]{:S(2)}, u32[]{:S(2)}) collective-permute-start(bf16[2,4,192,256]{3,2,1,0:T(8,128)(2,1)S(1)} %pad_maximum_fusion.5), channel_id=1, source_target_pairs={{0,32},{1,9},{2,34},{3,11},{4,36},{5,13},{6,38},{7,15},{8,40},{9,1... | collective-permute-start | bytes 2359304 | tf_op jit(solution)/shard_map/ppermute | solution.py:156
  103.4 21.7 %collective-permute-start.14 = (bf16[2,256,256]{2,1,0:T(8,128)(2,1)S(1)}, bf16[2,256,256]{2,1,0:T(8,128)(2,1)S(1)}, u32[]{:S(2)}, u32[]{:S(2)}) collective-permute-start(bf16[2,256,256]{2,1,0:T(8,128)(2,1)S(1)} %broadcast_select_fusion.7), channel_id=1, source_target_pairs={{0,64},{1,65},{2,66},{3,67},{4,68},{5,69},{6,70},{7,71},{8,72},{9,... | collective-permute-start | bytes 786440 | tf_op jit(solution)/shard_map/ppermute | solution.py:171
  105.6 20.2 %copy-start.7 = (bf16[2,256,256]{2,1,0:T(8,128)(2,1)S(1)}, bf16[2,256,256]{2,1,0:T(8,128)(2,1)}, u32[]{:S(2)}) copy-start(bf16[2,256,256]{2,1,0:T(8,128)(2,1)} %param.7) | copy-start | bytes 786436
  105.8 24.8 %collective-permute-start.7 = (bf16[2,4,256,256]{3,2,1,0:T(8,128)(2,1)S(1)}, bf16[2,4,256,256]{3,2,1,0:T(8,128)(2,1)S(1)}, u32[]{:S(2)}, u32[]{:S(2)}) collective-permute-start(bf16[2,4,256,256]{3,2,1,0:T(8,128)(2,1)S(1)} %pad_maximum_fusion.3), channel_id=1, source_target_pairs={{0,1},{1,0},{2,3},{3,2},{4,5},{5,4},{6,7},{7,6},{8,9},{9,8},{10,11... | collective-permute-start | bytes 3145736 | tf_op jit(solution)/shard_map/ppermute | solution.py:156
  (3 other events, 5.8 us)
